TPU v7x, 32 devices: a whole 2x2x4 slice. The times are simulated.
32 devices in a mesh: groups: 2 (over y), ctx: 4 (over z), head: 2 (over x), dp: 2 (over core).
Axes of the slice: x: 2, y: 2, z: 4, core: 2. Of those that a mesh axis runs over, the one named last changes fastest.
Arguments:
- query_rows: bfloat16 [8192, 4096], P(('groups', 'ctx', 'dp'), 'head'), parts along dimension 0, may hold values from -6 to 6
- key_rows: bfloat16 [8192, 4096], P(('groups', 'ctx', 'dp'), 'head'), parts along dimension 0, may hold values from -6 to 6
- value_rows: bfloat16 [8192, 4096], P(('groups', 'ctx', 'dp'), 'head'), parts along dimension 0, may hold values from -6 to 6
- cotangent: bfloat16 [8192, 4096], P(('groups', 'ctx', 'dp'), 'head'), parts along dimension 0, may hold values from -6 to 6
- log_decay: float32 [8192, 32], P(('groups', 'ctx', 'dp'), 'head'), parts along dimension 0, may hold values from -0.7 to 0, as said below
- norm_gain: float32 [4096], P('head'), may hold values from 0.1 to 1.9
Outputs:
- query_grad: bfloat16 [8192, 4096], P(('groups', 'ctx', 'dp'), 'head'), parts along dimension 0
- key_grad: bfloat16 [8192, 4096], P(('groups', 'ctx', 'dp'), 'head'), parts along dimension 0
- value_grad: bfloat16 [8192, 4096], P(('groups', 'ctx', 'dp'), 'head'), parts along dimension 0
- gain_grad: float32 [8192], P(('groups', 'head')), parts along dimension 0
There are 2 independent parts, one for each index of `groups`. A program takes and returns all parts, laid end to end along the dimension named above; an argument that names none is the same for every part. Nothing has to cross between parts.
Inputs may be any that keep to these rules, and one draw needn't show every extreme that they name: `log_decay`: every entry is negative.
All inputs are finite; a program needn't handle non-finite values.
Results may differ from a plain program's by a relative error of at most 0.0062.
Values sent between devices are 32-bit elements; how exact they have to be, the bound alone decides.
No kernel may reach another device: no remote copies, remote signals or barrier semaphores. Data moves between devices by JAX's collectives and lax.ppermute only.
A program may use at most 128 MiB of HBM per device.

v0:
```python
import math

import jax
import jax.numpy as jnp
from jax import lax
from jax.sharding import PartitionSpec as P

DH = 128


epsilon = 1e-06


def carried_in(array, axis, combine, identity):
    peers, index = (lax.axis_size(axis), lax.axis_index(axis))
    everything = jax.tree.map(lambda part: lax.all_gather(part, axis), array)
    start = jax.tree.map(
        lambda part, zero: jnp.broadcast_to(jnp.asarray(zero, part.dtype), part.shape),
        array,
        identity,
    )

    def turn(k, before):
        at = peers - 1 - k
        reached = at > index
        new = combine(before, jax.tree.map(lambda part: part[at], everything))
        return jax.tree.map(lambda a, b: jnp.where(reached, a, b), new, before)

    return lax.fori_loop(0, peers, turn, start)


def decay_parts(decay_log):
    cumulated = jnp.cumsum(decay_log, axis=0)
    final_log = cumulated[-1]
    by_head = cumulated.T
    spread = by_head[:, :, None] - by_head[:, None, :]
    length = decay_log.shape[0]
    causal = (jnp.arange(length)[:, None] >= jnp.arange(length)[None, :])[None]
    decay_mat = jnp.where(causal, jnp.exp(jnp.where(causal, spread, 0.0)), 0.0)
    return (cumulated, final_log, decay_mat)


def chain_combine(earlier, later):
    return (later[1] * earlier[0] + later[0], earlier[1] * later[1])


def gathered_prefix(local_state, final_log):
    totals = lax.all_gather(final_log[None, :], ("ctx", "dp"), axis=0, tiled=True)
    before = jnp.cumsum(totals, axis=0) - totals
    position = lax.axis_index(("ctx", "dp"))
    count = totals.shape[0]
    here = (jnp.arange(count) == position)[:, None]
    mine = jnp.sum(jnp.where(here, before, 0.0), axis=0)
    piece = lax.all_gather(local_state[None], ("ctx", "dp"), axis=0, tiled=True)
    rows_here = piece.shape[0]
    index = jnp.arange(rows_here)
    valid = (index < position)[:, None]
    weight = jnp.where(valid, jnp.exp(jnp.where(valid, mine[None, :] - before - totals, 0.0)), 0.0)
    return jnp.einsum("rh,rhde->hde", weight, piece, precision=lax.Precision.HIGHEST)


def on_device(query_rows, key_rows, value_rows, cotangent, log_decay, norm_gain):
    length = query_rows.shape[0]
    heads = log_decay.shape[1]
    shaped = (length, heads, DH)
    query_blk = query_rows.reshape(shaped)
    key_blk = key_rows.reshape(shaped)
    value_blk = value_rows.reshape(shaped)
    grad_blk = cotangent.reshape(shaped)
    gain_heads = norm_gain.reshape(heads, DH)
    f32 = jnp.float32
    bf16 = jnp.bfloat16
    cumulated, final_log, decay_mat = decay_parts(log_decay)
    to_end = jnp.exp(final_log[None, :] - cumulated)
    grow_from = jnp.exp(cumulated)
    scores = jnp.einsum("thd,shd->hts", query_blk, key_blk, preferred_element_type=f32)
    masked = (scores * decay_mat).astype(bf16)
    intra = jnp.einsum("hts,she->the", masked, value_blk, preferred_element_type=f32)
    key_scaled = (key_blk.astype(f32) * to_end[:, :, None]).astype(bf16)
    local_state = jnp.einsum("shd,she->hde", key_scaled, value_blk, preferred_element_type=f32)
    total = jnp.exp(final_log)[:, None, None]
    identity = (jnp.zeros_like(local_state), jnp.ones_like(total))
    state_in = gathered_prefix(local_state, final_log)
    state_low = state_in.astype(bf16)
    attended = intra + grow_from[:, :, None] * jnp.einsum(
        "thd,hde->the", query_blk, state_low, preferred_element_type=f32
    )
    root_mean = jnp.sqrt(jnp.mean(attended * attended, axis=-1, keepdims=True) + epsilon)
    normed = attended / root_mean
    grad_f = grad_blk.astype(f32)
    scaled = gain_heads[None] * grad_f
    projected = jnp.sum(scaled * attended, axis=-1, keepdims=True)
    out_grad = ((scaled - attended * projected / (DH * root_mean * root_mean)) / root_mean).astype(
        bf16
    )
    gain_part = jnp.sum(grad_f * normed, axis=0).reshape(heads * DH)
    query_scaled = (query_blk.astype(f32) * grow_from[:, :, None]).astype(bf16)
    moment = jnp.einsum("thd,the->hde", query_scaled, out_grad, preferred_element_type=f32)
    grad_state, _ = carried_in((moment, total), ("ctx", "dp"), chain_combine, identity)
    grad_low = grad_state.astype(bf16)
    seq_total = length * lax.axis_size(("ctx", "dp"))
    gain_grad = lax.psum(gain_part, ("ctx", "dp")) * (1.0 / math.sqrt(seq_total))
    dots = jnp.einsum("the,she->hts", out_grad, value_blk, preferred_element_type=f32)
    rgrad = (dots * decay_mat).astype(bf16)
    query_grad = jnp.einsum("hts,shd->thd", rgrad, key_blk, preferred_element_type=f32) + grow_from[
        :, :, None
    ] * jnp.einsum("the,hde->thd", out_grad, state_low, preferred_element_type=f32)
    key_grad = jnp.einsum("hts,thd->shd", rgrad, query_blk, preferred_element_type=f32) + to_end[
        :, :, None
    ] * jnp.einsum("she,hde->shd", value_blk, grad_low, preferred_element_type=f32)
    value_grad = jnp.einsum("hts,the->she", masked, out_grad, preferred_element_type=f32) + to_end[
        :, :, None
    ] * jnp.einsum("shd,hde->she", key_blk, grad_low, preferred_element_type=f32)
    flat = (length, heads * DH)
    return (
        query_grad.astype(bf16).reshape(flat),
        key_grad.astype(bf16).reshape(flat),
        value_grad.astype(bf16).reshape(flat),
        gain_grad,
    )


def solution(mesh):
    return jax.shard_map(
        on_device,
        mesh=mesh,
        in_specs=(
            P(("groups", "ctx", "dp"), "head"),
            P(("groups", "ctx", "dp"), "head"),
            P(("groups", "ctx", "dp"), "head"),
            P(("groups", "ctx", "dp"), "head"),
            P(("groups", "ctx", "dp"), "head"),
            P("head"),
        ),
        out_specs=(
            P(("groups", "ctx", "dp"), "head"),
            P(("groups", "ctx", "dp"), "head"),
            P(("groups", "ctx", "dp"), "head"),
            P(("groups", "head")),
        ),
        check_vma=False,
    )
```

profile of v0, /device:TPU:0, one launch (start us, length us, event | category | flops | bytes accessed | tf_op | source)
XLA Modules:
  0.0 248.4 jit_solution(7484581878501972760)
XLA Ops:
  9.8 3.9 %copy.81 = bf16[512,2048]{0,1:T(8,128)(2,1)} copy(bf16[512,2048]{1,0:T(8,128)(2,1)} %param.9) | data formatting | bytes 4194304 | tf_op args[1]
  13.8 3.3 %fusion.15 = f32[16,128,128]{2,1,0:T(8,128)} fusion(bf16[512,16,128]{0,2,1:T(8,128)(2,1)} %bitcast.124, f32[512,16]{0,1:T(8,128)S(1)} %get-tuple-element.207, bf16[512,2048]{1,0:T(8,128)(2,1)S(1)} %copy-done), kind=kOutput, calls=%fused_computation.28 | convolution fusion | flops 271581184 | bytes 5275648 | tf_op jit(solution)/shard_map/shd,she->hde/dot_general | solution.py:80
  17.2 13.4 %all-gather.3 = f32[8,1,16]{2,1,0:T(1,128)S(1)} all-gather(f32[1,1,16]{2,1,0:T(1,128)S(1)} %bitcast.141), channel_id=1, replica_groups=mesh['groups'=2,'ctx'=4,'head'=2,'dp'=2] {'ctx','dp'}, dimensions={0}, use_global_device_ids=true | all-gather | bytes 576 | tf_op jit(solution)/shard_map/all_gather | solution.py:48
  30.8 3.9 %copy.80 = bf16[512,2048]{0,1:T(8,128)(2,1)} copy(bf16[512,2048]{1,0:T(8,128)(2,1)} %param.8) | data formatting | bytes 4194304 | tf_op args[0]
  34.8 4.2 %copy.79 = f32[512,2048]{0,1:T(8,128)} copy(bf16[512,2048]{1,0:T(8,128)(2,1)} %param.11) | data formatting | bytes 6291456 | tf_op jit(solution)/shard_map/convert_element_type | solution.py:90
  39.0 7.5 %multiply_convert_fusion.1 = bf16[16,512,512]{2,1,0:T(8,128)(2,1)S(1)} fusion(bf16[512,16,128]{0,2,1:T(8,128)(2,1)} %bitcast.120, bf16[512,16,128]{0,2,1:T(8,128)(2,1)} %bitcast.125, f32[16,512]{1,0:T(8,128)S(1)} %get-tuple-element.210, pred[512,512]{1,0:T(8,128)(4,1)S(1)} %iota_compare_fusion), kind=kOutput, calls=%fused_computation.5 | convolution fusion | flops 1094713344 | bytes 12877824 | tf_op jit(solution)/shard_map/thd,shd->hts/dot_general | solution.py:76
  46.5 3.2 %copy-done.1 = bf16[16,512,512]{2,1,0:T(8,128)(2,1)} copy-done((bf16[16,512,512]{2,1,0:T(8,128)(2,1)}, bf16[16,512,512]{2,1,0:T(8,128)(2,1)S(1)}, u32[]{:S(2)}) %copy-start.1) | copy-done | bytes 8388632
  49.7 4.8 %fusion.17 = f32[16,512,128]{1,2,0:T(8,128)} fusion(bf16[16,512,512]{2,1,0:T(8,128)(2,1)S(1)} %multiply_convert_fusion.1, bf16[512,2048]{1,0:T(8,128)(2,1)S(1)} %copy-done), kind=kOutput, calls=%fused_computation.30 | convolution fusion | flops 1073741824 | bytes 14680064 | tf_op jit(solution)/shard_map/hts,she->the/dot_general | solution.py:78
  54.6 47.5 %all-gather.8.cloned.1.call-done = f32[128,128,128]{2,1,0:T(8,128)} async-done(((f32[16,128,128]{2,1,0:T(8,128)}), f32[128,128,128]{2,1,0:T(8,128)}) %all-gather.8.cloned.1.call-update) | async-done | bytes 8388624 | tf_op jit(solution)/shard_map/all_gather | solution.py:54
  102.0 15.5 %fusion.2 = f32[16,1,128,128]{3,1,2,0:T(1,128)S(1)} fusion(f32[8,16,1,1]{0,2,3,1:T(1,128)S(1)} %copy.103, f32[8,16,128,128]{3,2,1,0:T(8,128)} %bitcast.132), kind=kOutput, calls=%fused_computation.7 | convolution fusion | flops 25165824 | bytes 9437696 | tf_op jit(solution)/shard_map/rh,rhde->hde/dot_general | solution.py:59
  118.6 2.9 %copy-done.9 = f32[512,2048]{0,1:T(8,128)S(1)} copy-done((f32[512,2048]{0,1:T(8,128)S(1)}, f32[512,2048]{0,1:T(8,128)}, u32[]{:S(2)}) %copy-start.9) | copy-done | bytes 4194328
  126.1 8.9 %all-gather.4 = f32[8,1,16]{2,1,0:T(1,128)S(1)} all-gather(f32[1,1,16]{2,1,0:T(1,128)S(1)} %bitcast.143), channel_id=3, replica_groups=mesh['groups'=2,'ctx'=4,'head'=2,'dp'=2] {'ctx','dp'}, dimensions={0}, use_global_device_ids=true | all-gather | bytes 576 | tf_op jit(solution)/shard_map/all_gather | solution.py:16
  135.0 7.1 %multiply_convert_fusion = bf16[16,512,512]{2,1,0:T(8,128)(2,1)S(1)} fusion(bf16[512,16,128]{0,2,1:T(8,128)(2,1)} %copy-done.5, f32[16,512]{1,0:T(8,128)S(1)} %get-tuple-element.210, pred[512,512]{1,0:T(8,128)(4,1)S(1)} %iota_compare_fusion, bf16[512,2048]{1,0:T(8,128)(2,1)S(1)} %copy-done), kind=kOutput, calls=%fused_computation.4 | convolution fusion | flops 1094713344 | bytes 12877824 | tf_op jit(solution)/shard_map/the,she->hts/dot_general | solution.py:103
  142.2 4.9 %fusion.35 = f32[16,512,128]{1,2,0:T(8,128)} fusion(bf16[16,512,512]{2,1,0:T(8,128)(2,1)S(1)} %multiply_convert_fusion, bf16[512,16,128]{0,2,1:T(8,128)(2,1)S(1)} %bitcast.126), kind=kOutput, calls=%fused_computation.64 | convolution fusion | flops 1073741824 | bytes 14680064 | tf_op jit(solution)/shard_map/hts,shd->thd/dot_general | solution.py:105
  147.1 4.6 %fusion.9 = bf16[512,16,128]{0,2,1:T(8,128)(2,1)} fusion(f32[16,512,128]{1,2,0:T(8,128)} %fusion.35, bf16[512,16,128]{0,2,1:T(8,128)(2,1)S(1)} %copy-done.6, f32[512,16]{0,1:T(8,128)S(1)} %get-tuple-element.208, f32[16,128,128]{2,1,0:T(8,128)} %bitcast.131), kind=kOutput, calls=%fused_computation.17 | convolution fusion | flops 271843328 | bytes 9469952 | tf_op jit(solution)/shard_map/the,hde->thd/dot_general | solution.py:107
  151.7 3.9 %copy.98 = bf16[512,2048]{1,0:T(8,128)(2,1)} copy(bf16[512,2048]{0,1:T(8,128)(2,1)} %bitcast.133) | data formatting | bytes 4194304
  155.6 4.1 %multiply_reduce_fusion = f32[16,128]{1,0:T(8,128)S(1)} fusion(f32[512,16,128]{0,2,1:T(8,128)} %bitcast.128, f32[512,16,128]{0,2,1:T(8,128)} %copy-done.11, f32[512,16]{0,1:T(8,128)S(1)} %get-tuple-element.206), kind=kLoop, calls=%fused_computation.20 | loop fusion | flops 3143680 | bytes 8429568 | tf_op jit(solution)/shard_map/reduce_sum | solution.py:96
  159.7 16.1 %psum.7 = f32[2048]{0:T(1024)S(1)} all-reduce(f32[2048]{0:T(1024)S(1)} %bitcast.140), channel_id=1, replica_groups=mesh['groups'=2,'ctx'=4,'head'=2,'dp'=2] {'ctx','dp'}, use_global_device_ids=true, to_apply=%region_9.10 | all-reduce | flops 2048 | bytes 16384 | tf_op jit(solution)/shard_map/psum | solution.py:102
  176.4 7.4 %fusion.36 = f32[16,128,512]{2,1,0:T(8,128)} fusion(bf16[512,16,128]{0,2,1:T(8,128)(2,1)} %copy-done.5, bf16[16,512,512]{2,1,0:T(8,128)(2,1)} %copy-done.1), kind=kOutput, calls=%fused_computation.65 | convolution fusion | flops 1073741824 | bytes 14680064 | tf_op jit(solution)/shard_map/hts,the->she/dot_general | solution.py:111
  183.8 23.6 %all-gather.10.cloned.1.call-done = f32[128,128,128]{2,1,0:T(8,128)} async-done(((f32[16,128,128]{2,1,0:T(8,128)}), f32[128,128,128]{2,1,0:T(8,128)}) %all-gather.10.cloned.1.call-update) | async-done | bytes 8388624 | tf_op jit(solution)/shard_map/all_gather | solution.py:16
  207.4 12.0 %while.16 = (s32[]{:T(128)}, f32[16,128,128]{2,1,0:T(8,128)S(1)}, s32[]{:T(128)}, f32[8,16,1,1]{1,3,2,0:T(1,128)S(1)}, f32[8,16,128,128]{3,2,1,0:T(8,128)}, /*index=5*/s32[]{:T(128)}, s32[]{:T(128)}, s32[]{:T(128)}, s32[]{:T(128)}) while((s32[]{:T(128)}, f32[16,128,128]{2,1,0:T(8,128)S(1)}, s32[]{:T(128)}, ...), condition=%wide.region_7.8_spmd.clone, body=%wide.region_6.7_spmd.clone.sunk | while | flops 1048584 | bytes 3146095 | solution.py:29
  225.9 3.9 %copy.100 = bf16[512,2048]{1,0:T(8,128)(2,1)} copy(bf16[512,2048]{0,1:T(8,128)(2,1)} %bitcast.134) | data formatting | bytes 4194304
  229.8 7.8 %fusion.7 = bf16[512,16,128]{0,2,1:T(8,128)(2,1)} fusion(f32[16,128,512]{2,1,0:T(8,128)} %fusion.19, bf16[512,16,128]{0,2,1:T(8,128)(2,1)} %bitcast.121, bf16[16,512,512]{2,1,0:T(8,128)(2,1)} %copy-done.2, f32[512,16]{0,1:T(8,128)S(1)} %get-tuple-element.207), kind=kOutput, calls=%fused_computation.14 | convolution fusion | flops 1076887552 | bytes 16809984 | tf_op jit(solution)/shard_map/hts,thd->shd/dot_general | solution.py:108
  237.6 3.9 %copy.99 = bf16[512,2048]{1,0:T(8,128)(2,1)} copy(bf16[512,2048]{0,1:T(8,128)(2,1)} %bitcast.135) | data formatting | bytes 4194304
  (68 shorter events, 27.5 us)
Async XLA Ops:
  7.2 6.6 %copy-start = (bf16[512,2048]{1,0:T(8,128)(2,1)S(1)}, bf16[512,2048]{1,0:T(8,128)(2,1)}, u32[]{:S(2)}) copy-start(bf16[512,2048]{1,0:T(8,128)(2,1)} %param.10) | copy-start | bytes 6291460
  7.2 94.9 %all-gather.8.cloned.1.call-start = ((), (), s32[]{:S(2)}) async-start(), calls=%async_computation | async-start | bytes 9437184 | tf_op jit(solution)/shard_map/all_gather | solution.py:54
  17.1 190.2 %all-gather.10.cloned.1.call-start = ((), (), s32[]{:S(2)}) async-start(), calls=%async_computation.1 | async-start | bytes 9437184 | tf_op jit(solution)/shard_map/all_gather | solution.py:16
  46.5 3.2 %copy-start.1 = (bf16[16,512,512]{2,1,0:T(8,128)(2,1)}, bf16[16,512,512]{2,1,0:T(8,128)(2,1)S(1)}, u32[]{:S(2)}) copy-start(bf16[16,512,512]{2,1,0:T(8,128)(2,1)S(1)} %multiply_convert_fusion.1) | copy-start | bytes 25165828
  102.0 15.5 %copy-start.3 = (bf16[512,2048]{0,1:T(8,128)(2,1)S(1)}, bf16[512,2048]{0,1:T(8,128)(2,1)}, u32[]{:S(2)}) copy-start(bf16[512,2048]{0,1:T(8,128)(2,1)} %copy.80) | copy-start | bytes 6291460
  102.0 15.5 %copy-start.10 = (f32[16,512,128]{1,2,0:T(8,128)S(1)}, f32[16,512,128]{1,2,0:T(8,128)}, u32[]{:S(2)}) copy-start(f32[16,512,128]{1,2,0:T(8,128)} %fusion.17) | copy-start | bytes 12582916
  117.5 1.1 copy-start.12
  117.5 4.0 %copy-start.9 = (f32[512,2048]{0,1:T(8,128)S(1)}, f32[512,2048]{0,1:T(8,128)}, u32[]{:S(2)}) copy-start(f32[512,2048]{0,1:T(8,128)} %copy.79) | copy-start | bytes 12582916
  117.5 4.0 %copy-start.13 = (f32[2048]{0:T(1024)S(1)}, f32[2048]{0:T(1024)}, u32[]{:S(2)}) copy-start(f32[2048]{0:T(1024)} %param.13) | copy-start | bytes 24580
  118.6 4.5 %copy-start.11 = (f32[512,16,128]{0,2,1:T(8,128)}, f32[512,16,128]{0,2,1:T(8,128)S(1)}, u32[]{:S(2)}) copy-start(f32[512,16,128]{0,2,1:T(8,128)S(1)} %get-tuple-element.212) | copy-start | bytes 12582916
  123.0 1.3 copy-start.5
  135.0 7.2 %copy-start.7 = (bf16[512,2048]{0,1:T(8,128)(2,1)S(1)}, bf16[512,2048]{0,1:T(8,128)(2,1)}, u32[]{:S(2)}) copy-start(bf16[512,2048]{0,1:T(8,128)(2,1)} %copy.81) | copy-start | bytes 6291460
  142.2 4.9 %copy-start.2 = (bf16[16,512,512]{2,1,0:T(8,128)(2,1)}, bf16[16,512,512]{2,1,0:T(8,128)(2,1)S(1)}, u32[]{:S(2)}) copy-start(bf16[16,512,512]{2,1,0:T(8,128)(2,1)S(1)} %multiply_convert_fusion) | copy-start | bytes 25165828
  142.2 4.9 %copy-start.6 = (bf16[512,16,128]{0,2,1:T(8,128)(2,1)S(1)}, bf16[512,16,128]{0,2,1:T(8,128)(2,1)}, u32[]{:S(2)}) copy-start(bf16[512,16,128]{0,2,1:T(8,128)(2,1)} %copy-done.5) | copy-start | bytes 6291460
  219.4 3.4 %copy-start.4 = (f32[16,128,512]{2,1,0:T(8,128)S(1)}, f32[16,128,512]{2,1,0:T(8,128)}, u32[]{:S(2)}) copy-start(f32[16,128,512]{2,1,0:T(8,128)} %fusion.36) | copy-start | bytes 12582916
  219.4 4.4 %copy-start.8 = (bf16[512,2048]{0,1:T(8,128)(2,1)S(1)}, bf16[512,2048]{0,1:T(8,128)(2,1)}, u32[]{:S(2)}) copy-start(bf16[512,2048]{0,1:T(8,128)(2,1)} %copy.81) | copy-start | bytes 6291460
Sparse Core Ops, SparseCore 0:
  17.2 84.7 all-gather.7
  126.2 81.1 all-gather.9
where the time goes:
time: 249 us; the launch traced here: 248 us
  waiting for transfers between devices  71.1 us (29%)
  matrix products  70.6 us (28%)
  blocking collectives  38.4 us (15%)
  local copies, waits for them, and re-layouts  34.2 us (14%)
  other arithmetic  19.5 us (8%)
  between operations  14.3 us (6%)
    all_gather x1, waiting for transfers between devices, gathered_prefix(): piece = lax.all_gather(local_state[None], ('ctx', 'dp'), axis=0, tiled=True)  47.5 us
    unnamed x33, local copies, waits for them, and re-layouts  28.6 us
    all_gather x1, waiting for transfers between devices, carried_in(): everything = jax.tree.map(lambda part: lax.all_gather(part, axis), array)  23.6 us
    psum x1, blocking collectives, on_device(): lax.psum(gain_part, ('ctx', 'dp')) * (1.0 / math.sqrt(seq_total))  16.1 us
    dot_general x1, matrix products, gathered_prefix(): jnp.einsum('rh,rhde->hde', weight, piece, precision=lax.Precision.HIGHEST)  15.5 us
    all_gather x1, blocking collectives, gathered_prefix(): lax.all_gather(final_log[None, :], ('ctx', 'dp'), axis=0, tiled=True)  13.4 us
    select_n x8, other arithmetic, turn(): return jax.tree.map(lambda a, b: jnp.where(reached, a, b), new, before)  11.7 us
    all_gather x1, blocking collectives, carried_in(): everything = jax.tree.map(lambda part: lax.all_gather(part, axis), array)  8.92 us
  transfers between devices with their start and end apart: 2, of which 2 were waited for; matrix products, arithmetic and copies ran while one was open for 21% of the time, Pallas kernels for 0%

commit v1 on v0

--- a/solution.py
+++ b/solution.py
@@ -6,27 +6,10 @@
 from jax.sharding import PartitionSpec as P
 
 DH = 128
+PAD = 8
 
 
 epsilon = 1e-06
-
-
-def carried_in(array, axis, combine, identity):
-    peers, index = (lax.axis_size(axis), lax.axis_index(axis))
-    everything = jax.tree.map(lambda part: lax.all_gather(part, axis), array)
-    start = jax.tree.map(
-        lambda part, zero: jnp.broadcast_to(jnp.asarray(zero, part.dtype), part.shape),
-        array,
-        identity,
-    )
-
-    def turn(k, before):
-        at = peers - 1 - k
-        reached = at > index
-        new = combine(before, jax.tree.map(lambda part: part[at], everything))
-        return jax.tree.map(lambda a, b: jnp.where(reached, a, b), new, before)
-
-    return lax.fori_loop(0, peers, turn, start)
 
 
 def decay_parts(decay_log):
@@ -40,23 +23,90 @@
     return (cumulated, final_log, decay_mat)
 
 
-def chain_combine(earlier, later):
-    return (later[1] * earlier[0] + later[0], earlier[1] * later[1])
+def swap_dp(x):
+    return lax.ppermute(x, "dp", perm=[(0, 1), (1, 0)])
 
 
-def gathered_prefix(local_state, final_log):
-    totals = lax.all_gather(final_log[None, :], ("ctx", "dp"), axis=0, tiled=True)
-    before = jnp.cumsum(totals, axis=0) - totals
-    position = lax.axis_index(("ctx", "dp"))
-    count = totals.shape[0]
-    here = (jnp.arange(count) == position)[:, None]
-    mine = jnp.sum(jnp.where(here, before, 0.0), axis=0)
-    piece = lax.all_gather(local_state[None], ("ctx", "dp"), axis=0, tiled=True)
-    rows_here = piece.shape[0]
-    index = jnp.arange(rows_here)
-    valid = (index < position)[:, None]
-    weight = jnp.where(valid, jnp.exp(jnp.where(valid, mine[None, :] - before - totals, 0.0)), 0.0)
-    return jnp.einsum("rh,rhde->hde", weight, piece, precision=lax.Precision.HIGHEST)
+def pack_rows(core, *rows):
+    heads = core.shape[0]
+    pad = [jnp.broadcast_to(r.reshape(heads, 1, -1), (heads, 1, DH)) for r in rows]
+    fill = jnp.zeros((heads, PAD - len(rows), DH), jnp.float32)
+    return jnp.concatenate([core] + pad + [fill], axis=1)
+
+
+def chip_prefix(message, later):
+    gathered = lax.all_gather(message, "ctx")
+    chips = gathered.shape[0]
+    z = lax.axis_index("ctx")
+    decay = gathered[:, :, DH, 0]
+    before = jnp.cumsum(decay, axis=0) - decay
+    index = jnp.arange(chips)[:, None]
+    mine = jnp.sum(jnp.where(index == z, before, 0.0), axis=0)
+    mine_decay = jnp.sum(jnp.where(index == z, decay, 0.0), axis=0)
+    if later:
+        valid = index > z
+        spread = before - mine[None] - mine_decay[None]
+    else:
+        valid = index < z
+        spread = mine[None] - before - decay
+    weight = jnp.where(valid, jnp.exp(jnp.where(valid, spread, 0.0)), 0.0)
+    total = jnp.sum(weight[:, :, None, None] * gathered[:, :, :DH, :], axis=0)
+    return total, gathered
+
+
+def halves(x, c):
+    half = x.shape[0] // 2
+    return lax.dynamic_slice_in_dim(x, c * half, half, axis=0)
+
+
+def join_halves(mine, other, c):
+    first = jnp.where(c == 0, mine, other)
+    second = jnp.where(c == 0, other, mine)
+    return jnp.concatenate([first, second], axis=0)
+
+
+def forward_states(local_state, final_log):
+    c = lax.axis_index("dp")
+    message = pack_rows(local_state, final_log)
+    other = swap_dp(message)
+    own_state, other_state = local_state, other[:, :DH, :]
+    own_fin, other_fin = final_log, other[:, DH, 0]
+    first = jnp.where(c == 0, own_state, other_state)
+    second = jnp.where(c == 0, other_state, own_state)
+    fin_first = jnp.where(c == 0, own_fin, other_fin)
+    fin_second = jnp.where(c == 0, other_fin, own_fin)
+    chip_state = jnp.exp(fin_second)[:, None, None] * first + second
+    chip_decay = fin_first + fin_second
+    prefix_half, _ = chip_prefix(pack_rows(halves(chip_state, c), halves(chip_decay, c)), later=False)
+    prefix = join_halves(prefix_half, swap_dp(prefix_half), c)
+    core_one = jnp.exp(fin_first)[:, None, None] * prefix + first
+    return jnp.where(c == 0, prefix, core_one)
+
+
+def backward_states(moment, final_log, gain_part):
+    c = lax.axis_index("dp")
+    heads = moment.shape[0]
+    gain_rows = gain_part.reshape(heads, DH)
+    message = pack_rows(moment, final_log, gain_rows)
+    other = swap_dp(message)
+    own_m, other_m = moment, other[:, :DH, :]
+    own_fin, other_fin = final_log, other[:, DH, 0]
+    first = jnp.where(c == 0, own_m, other_m)
+    second = jnp.where(c == 0, other_m, own_m)
+    fin_first = jnp.where(c == 0, own_fin, other_fin)
+    fin_second = jnp.where(c == 0, other_fin, own_fin)
+    chip_gain = gain_rows + other[:, DH + 1, :]
+    chip_state = first + jnp.exp(fin_first)[:, None, None] * second
+    chip_decay = fin_first + fin_second
+    suffix_half, gathered = chip_prefix(
+        pack_rows(halves(chip_state, c), halves(chip_decay, c), halves(chip_gain, c)), later=True
+    )
+    gain_half = jnp.sum(gathered[:, :, DH + 1, :], axis=0)
+    back = swap_dp(pack_rows(suffix_half, gain_half))
+    suffix = join_halves(suffix_half, back[:, :DH, :], c)
+    gain_total = join_halves(gain_half, back[:, DH, :], c)
+    core_zero = second + jnp.exp(fin_second)[:, None, None] * suffix
+    return jnp.where(c == 0, core_zero, suffix), gain_total.reshape(heads * DH)
 
 
 def on_device(query_rows, key_rows, value_rows, cotangent, log_decay, norm_gain):
@@ -78,9 +128,7 @@
     intra = jnp.einsum("hts,she->the", masked, value_blk, preferred_element_type=f32)
     key_scaled = (key_blk.astype(f32) * to_end[:, :, None]).astype(bf16)
     local_state = jnp.einsum("shd,she->hde", key_scaled, value_blk, preferred_element_type=f32)
-    total = jnp.exp(final_log)[:, None, None]
-    identity = (jnp.zeros_like(local_state), jnp.ones_like(total))
-    state_in = gathered_prefix(local_state, final_log)
+    state_in = forward_states(local_state, final_log)
     state_low = state_in.astype(bf16)
     attended = intra + grow_from[:, :, None] * jnp.einsum(
         "thd,hde->the", query_blk, state_low, preferred_element_type=f32
@@ -96,10 +144,10 @@
     gain_part = jnp.sum(grad_f * normed, axis=0).reshape(heads * DH)
     query_scaled = (query_blk.astype(f32) * grow_from[:, :, None]).astype(bf16)
     moment = jnp.einsum("thd,the->hde", query_scaled, out_grad, preferred_element_type=f32)
-    grad_state, _ = carried_in((moment, total), ("ctx", "dp"), chain_combine, identity)
+    grad_state, gain_sum = backward_states(moment, final_log, gain_part)
     grad_low = grad_state.astype(bf16)
     seq_total = length * lax.axis_size(("ctx", "dp"))
-    gain_grad = lax.psum(gain_part, ("ctx", "dp")) * (1.0 / math.sqrt(seq_total))
+    gain_grad = gain_sum * (1.0 / math.sqrt(seq_total))
     dots = jnp.einsum("the,she->hts", out_grad, value_blk, preferred_element_type=f32)
     rgrad = (dots * decay_mat).astype(bf16)
     query_grad = jnp.einsum("hts,shd->thd", rgrad, key_blk, preferred_element_type=f32) + grow_from[

time: 249 us -> 188 us (0.76)
  blocking collectives: 38.4 us -> 0 us
  matrix products: 70.6 us -> 53.7 us
  waiting for transfers between devices: 71.1 us -> 64.1 us
    all_gather x2 -> x0, blocking collectives: 22.3 us -> none  [the longest x1 13.4 us: gathered_prefix(): lax.all_gather(final_log[None, :], ('ctx', 'dp'), axis=0, tiled=True)]
    psum x1 -> x0, blocking collectives: 16.1 us -> none  [on_device(): lax.psum(gain_part, ('ctx', 'dp')) * (1.0 / math.sqrt(seq_total))]
    dot_general x1 -> x0, matrix products: 15.5 us -> none  [gathered_prefix(): jnp.einsum('rh,rhde->hde', weight, piece, precision=lax.Precision.HIGHEST)]
    all_gather x2, waiting for transfers between devices: 71.1 us -> 59.2 us  [chip_prefix(): gathered = lax.all_gather(message, 'ctx')]
    select_n x9 -> x5, other arithmetic: 11.8 us -> 2.65 us  [the longest x2 2.44 us: chip_prefix(): weight = jnp.where(valid, jnp.exp(jnp.where(valid, spread, 0.0)), 0.0)]
    reduce_sum x1 -> x5, other arithmetic: 0.09 us -> 5.36 us  [the longest x2 3.75 us: chip_prefix(): total = jnp.sum(weight[:, :, None, None] * gathered[:, :, :DH, :], axis=0)]
    ppermute x0 -> x4, waiting for transfers between devices: none -> 4.9 us  [swap_dp(): return lax.ppermute(x, 'dp', perm=[(0, 1), (1, 0)])]
    unnamed x33 -> x51, local copies, waits for them, and re-layouts: 28.6 us -> 24.2 us
  transfers between devices with their start and end apart: 2 -> 6, of which waited for: 2 -> 4; matrix products, arithmetic and copies ran while one was open for 21% -> 27% of each run, Pallas kernels for 0% -> 0%
where the time goes in v1:
time: 188 us; the launch traced here: 187 us
  waiting for transfers between devices  64.1 us (34%)
  matrix products  53.7 us (29%)
  local copies, waits for them, and re-layouts  32.5 us (17%)
  other arithmetic  20.4 us (11%)
  between operations  14.5 us (8%)
    all_gather x2, waiting for transfers between devices, chip_prefix(): gathered = lax.all_gather(message, 'ctx')  59.2 us
    unnamed x51, local copies, waits for them, and re-layouts  24.2 us
    dot_general x1, matrix products, on_device(): jnp.einsum('thd,shd->hts', query_blk, key_blk, preferred_element_type=f32)  9.58 us
    dot_general x1, matrix products, on_device(): jnp.einsum('hts,thd->shd', rgrad, query_blk, preferred_element_type=f32)  7.79 us
    dot_general x1, matrix products, on_device(): jnp.einsum('the,she->hts', out_grad, value_blk, preferred_element_type=f32)  7.35 us
    dot_general x1, matrix products, on_device(): jnp.einsum('hts,she->the', masked, value_blk, preferred_element_type=f32)  6.25 us
    ppermute x4, waiting for transfers between devices, swap_dp(): return lax.ppermute(x, 'dp', perm=[(0, 1), (1, 0)])  4.9 us
    dot_general x1, matrix products, on_device(): jnp.einsum('hts,shd->thd', rgrad, key_blk, preferred_element_type=f32)  4.74 us
  transfers between devices with their start and end apart: 6, of which 4 were waited for; matrix products, arithmetic and copies ran while one was open for 27% of the time, Pallas kernels for 0%

profile of v1, /device:TPU:0, one launch (start us, length us, event | category | flops | bytes accessed | tf_op | source)
XLA Modules:
  0.0 186.7 jit_solution(91512117220855926)
XLA Ops:
  10.4 3.9 %copy.160 = bf16[512,2048]{0,1:T(8,128)(2,1)} copy(bf16[512,2048]{1,0:T(8,128)(2,1)} %param.7) | data formatting | bytes 4194304 | tf_op args[1]
  14.4 2.4 %fusion.12 = f32[16,128,128]{2,1,0:T(8,128)S(1)} fusion(bf16[512,16,128]{0,2,1:T(8,128)(2,1)} %bitcast.123, f32[512,16]{0,1:T(8,128)S(1)} %get-tuple-element.47, bf16[512,2048]{1,0:T(8,128)(2,1)S(1)} %copy-done), kind=kOutput, calls=%fused_computation.23 | convolution fusion | flops 271581184 | bytes 5275648 | tf_op jit(solution)/shard_map/shd,she->hde/dot_general | solution.py:130
  18.4 2.5 %collective-permute-done = f32[16,136,128]{2,1,0:T(8,128)} collective-permute-done((f32[16,136,128]{2,1,0:T(8,128)S(1)}, f32[16,136,128]{2,1,0:T(8,128)}, u32[]{:S(2)}, u32[]{:S(2)}) %collective-permute-start) | collective-permute-done | bytes 1114144 | tf_op jit(solution)/shard_map/ppermute | solution.py:27
  22.7 1.8 fusion.49
  26.0 3.9 %copy.159 = bf16[512,2048]{0,1:T(8,128)(2,1)} copy(bf16[512,2048]{1,0:T(8,128)(2,1)} %param.6) | data formatting | bytes 4194304 | tf_op args[0]
  29.9 4.1 %copy.158 = f32[512,2048]{0,1:T(8,128)} copy(bf16[512,2048]{1,0:T(8,128)(2,1)} %param.9) | data formatting | bytes 6291456 | tf_op jit(solution)/shard_map/convert_element_type | solution.py:138
  34.8 9.6 %multiply_convert_fusion.1 = bf16[16,512,512]{2,1,0:T(8,128)(2,1)} fusion(bf16[512,16,128]{0,2,1:T(8,128)(2,1)} %bitcast.119, bf16[512,16,128]{0,2,1:T(8,128)(2,1)} %bitcast.124, f32[16,512]{1,0:T(8,128)S(1)} %copy-done.12, pred[512,512]{1,0:T(8,128)(4,1)S(1)} %iota_compare_fusion), kind=kOutput, calls=%fused_computation.2 | convolution fusion | flops 1094713344 | bytes 12877824 | tf_op jit(solution)/shard_map/thd,shd->hts/dot_general | solution.py:126
  44.4 32.5 %all-gather.5.cloned.1.call-done = f32[32,136,128]{2,1,0:T(8,128)} async-done(((f32[8,136,128]{2,1,0:T(8,128)}), f32[32,136,128]{2,1,0:T(8,128)}) %all-gather.5.cloned.1.call-update) | async-done | bytes 2228240 | tf_op jit(solution)/shard_map/all_gather | solution.py:38
  79.8 1.9 fusion.21
  81.7 6.2 %fusion.14 = f32[16,512,128]{1,2,0:T(8,128)S(1)} fusion(bf16[16,512,512]{2,1,0:T(8,128)(2,1)} %multiply_convert_fusion.1, bf16[512,2048]{1,0:T(8,128)(2,1)S(1)} %copy-done), kind=kOutput, calls=%fused_computation.25 | convolution fusion | flops 1073741824 | bytes 14680064 | tf_op jit(solution)/shard_map/hts,she->the/dot_general | solution.py:128
  92.5 1.7 divide_convert_fusion
  96.2 2.4 %collective-permute-done.2 = f32[16,136,128]{2,1,0:T(8,128)S(1)} collective-permute-done((f32[16,136,128]{2,1,0:T(8,128)S(1)}, f32[16,136,128]{2,1,0:T(8,128)S(1)}, u32[]{:S(2)}, u32[]{:S(2)}) %collective-permute-start.2) | collective-permute-done | bytes 1114144 | tf_op jit(solution)/shard_map/ppermute | solution.py:27
  100.9 7.3 %multiply_convert_fusion = bf16[16,512,512]{2,1,0:T(8,128)(2,1)S(1)} fusion(bf16[512,16,128]{0,2,1:T(8,128)(2,1)} %copy-done.3, f32[16,512]{1,0:T(8,128)S(1)} %copy-done.12, pred[512,512]{1,0:T(8,128)(4,1)S(1)} %iota_compare_fusion, bf16[512,2048]{1,0:T(8,128)(2,1)S(1)} %copy-done), kind=kOutput, calls=%fused_computation.1 | convolution fusion | flops 1094713344 | bytes 12877824 | tf_op jit(solution)/shard_map/the,she->hts/dot_general | solution.py:151
  108.2 4.7 %fusion.51 = f32[16,512,128]{1,2,0:T(8,128)} fusion(bf16[16,512,512]{2,1,0:T(8,128)(2,1)S(1)} %multiply_convert_fusion, bf16[512,16,128]{0,2,1:T(8,128)(2,1)S(1)} %bitcast.125), kind=kOutput, calls=%fused_computation.120 | convolution fusion | flops 1073741824 | bytes 14680064 | tf_op jit(solution)/shard_map/hts,shd->thd/dot_general | solution.py:153
  113.0 4.5 %fusion.6 = bf16[512,16,128]{0,2,1:T(8,128)(2,1)} fusion(f32[16,512,128]{1,2,0:T(8,128)} %fusion.51, bf16[16,128,128]{2,1,0:T(8,128)(2,1)} %copy-done.11, bf16[512,16,128]{0,2,1:T(8,128)(2,1)S(1)} %copy-done.4, f32[512,16]{0,1:T(8,128)S(1)} %get-tuple-element.46), kind=kOutput, calls=%fused_computation.12 | convolution fusion | flops 271581184 | bytes 8945664 | tf_op jit(solution)/shard_map/the,hde->thd/dot_general | solution.py:155
  117.5 3.9 %copy.184 = bf16[512,2048]{1,0:T(8,128)(2,1)} copy(bf16[512,2048]{0,1:T(8,128)(2,1)} %bitcast.129) | data formatting | bytes 4194304
  121.5 26.7 %all-gather.7.cloned.1.call-done = f32[32,136,128]{2,1,0:T(8,128)} async-done(((f32[8,136,128]{2,1,0:T(8,128)}), f32[32,136,128]{2,1,0:T(8,128)}) %all-gather.7.cloned.1.call-update) | async-done | bytes 2228240 | tf_op jit(solution)/shard_map/all_gather | solution.py:38
  151.7 1.9 %fusion.20 = f32[8,128,128]{2,1,0:T(8,128)S(1)} fusion(f32[4,8,136,128]{3,2,1,0:T(8,128)} %bitcast.135, f32[4,8]{1,0:T(4,128)S(1)} %fusion.35), kind=kLoop, calls=%fused_computation.32 | loop fusion | flops 917504 | bytes 2621568 | tf_op jit(solution)/shard_map/reduce_sum | solution.py:53
  153.8 4.7 %fusion.52 = f32[16,128,512]{2,1,0:T(8,128)S(1)} fusion(bf16[512,16,128]{0,2,1:T(8,128)(2,1)S(1)} %copy-done.5, bf16[16,512,512]{2,1,0:T(8,128)(2,1)} %multiply_convert_fusion.1), kind=kOutput, calls=%fused_computation.121 | convolution fusion | flops 1073741824 | bytes 14680064 | tf_op jit(solution)/shard_map/hts,the->she/dot_general | solution.py:159
  158.9 2.7 %fusion.16 = f32[16,128,512]{2,1,0:T(8,128)} fusion(bf16[16,128,128]{2,1,0:T(8,128)(2,1)S(1)} %select_convert_fusion, bf16[512,2048]{1,0:T(8,128)(2,1)S(1)} %copy-done), kind=kOutput, calls=%fused_computation.27 | convolution fusion | flops 268435456 | bytes 6815744 | tf_op jit(solution)/shard_map/she,hde->shd/dot_general | solution.py:158
  161.5 2.1 %fusion.2 = bf16[512,16,128]{0,2,1:T(8,128)(2,1)} fusion(f32[16,128,512]{2,1,0:T(8,128)S(1)} %fusion.52, bf16[16,128,128]{2,1,0:T(8,128)(2,1)S(1)} %select_convert_fusion, bf16[512,16,128]{0,2,1:T(8,128)(2,1)S(1)} %bitcast.126, f32[512,16]{0,1:T(8,128)S(1)} %get-tuple-element.47), kind=kOutput, calls=%fused_computation.6 | convolution fusion | flops 271581184 | bytes 8945664 | tf_op jit(solution)/shard_map/shd,hde->she/dot_general | solution.py:161
  163.6 3.9 %copy.186 = bf16[512,2048]{1,0:T(8,128)(2,1)} copy(bf16[512,2048]{0,1:T(8,128)(2,1)} %bitcast.130) | data formatting | bytes 4194304
  167.6 7.8 %fusion.4 = bf16[512,16,128]{0,2,1:T(8,128)(2,1)} fusion(f32[16,128,512]{2,1,0:T(8,128)} %fusion.16, bf16[512,16,128]{0,2,1:T(8,128)(2,1)} %bitcast.120, bf16[16,512,512]{2,1,0:T(8,128)(2,1)} %copy-done.1, f32[512,16]{0,1:T(8,128)S(1)} %get-tuple-element.47), kind=kOutput, calls=%fused_computation.9 | convolution fusion | flops 1076887552 | bytes 16809984 | tf_op jit(solution)/shard_map/hts,thd->shd/dot_general | solution.py:156
  175.3 3.9 %copy.185 = bf16[512,2048]{1,0:T(8,128)(2,1)} copy(bf16[512,2048]{0,1:T(8,128)(2,1)} %bitcast.131) | data formatting | bytes 4194304
  (114 shorter events, 25.2 us)
Async XLA Ops:
  7.2 7.3 %copy-start = (bf16[512,2048]{1,0:T(8,128)(2,1)S(1)}, bf16[512,2048]{1,0:T(8,128)(2,1)}, u32[]{:S(2)}) copy-start(bf16[512,2048]{1,0:T(8,128)(2,1)} %param.8) | copy-start | bytes 6291460
  7.2 69.7 %all-gather.5.cloned.1.call-start = ((), (), s32[]{:S(2)}) async-start(), calls=%async_computation | async-start | bytes 2785280 | tf_op jit(solution)/shard_map/all_gather | solution.py:38
  10.3 12.2 %copy-start.15 = (f32[16]{0:T(128)}, f32[16]{0:T(128)S(1)}, u32[]{:S(2)}) copy-start(f32[16]{0:T(128)S(1)} %get-tuple-element.49) | copy-start | bytes 196
  14.4 10.3 %copy-start.13 = (f32[136]{0:T(256)}, f32[136]{0:T(256)S(1)}, u32[]{:S(2)}) copy-start(f32[136]{0:T(256)S(1)} %pad.22.clone) | copy-start | bytes 1636
  17.9 3.0 %collective-permute-start = (f32[16,136,128]{2,1,0:T(8,128)S(1)}, f32[16,136,128]{2,1,0:T(8,128)}, u32[]{:S(2)}, u32[]{:S(2)}) collective-permute-start(f32[16,136,128]{2,1,0:T(8,128)S(1)} %fusion.29), channel_id=1, source_target_pairs={{0,1},{1,0},{2,3},{3,2},{4,5},{5,4},{6,7},{7,6},{8,9},{9,8},{10,11... | collective-permute-start | bytes 3342344 | tf_op jit(solution)/shard_map/ppermute | solution.py:27
  22.7 1.9 copy-start.10
  25.7 122.4 %all-gather.7.cloned.1.call-start = ((), (), s32[]{:S(2)}) async-start(), calls=%async_computation.1 | async-start | bytes 2785280 | tf_op jit(solution)/shard_map/all_gather | solution.py:38
  29.9 4.9 %copy-start.12 = (f32[16,512]{1,0:T(8,128)S(1)}, f32[16,512]{1,0:T(8,128)}, u32[]{:S(2)}) copy-start(f32[16,512]{1,0:T(8,128)} %get-tuple-element.51) | copy-start | bytes 98308
  34.1 61.4 %copy-start.17 = (f32[136]{0:T(256)}, f32[136]{0:T(256)S(1)}, u32[]{:S(2)}) copy-start(f32[136]{0:T(256)S(1)} %pad.14.clone) | copy-start | bytes 1636
  34.7 43.2 %copy-start.20 = (pred[4]{0:T(512)(128)(4,1)}, pred[4]{0:T(512)(128)(4,1)S(1)}, u32[]{:S(2)}) copy-start(pred[4]{0:T(512)(128)(4,1)S(1)} %get-tuple-element.56) | copy-start | bytes 16
  81.6 6.4 %collective-permute-start.1 = (f32[8,128,128]{2,1,0:T(8,128)S(1)}, f32[8,128,128]{2,1,0:T(8,128)S(1)}, u32[]{:S(2)}, u32[]{:S(2)}) collective-permute-start(f32[8,128,128]{2,1,0:T(8,128)S(1)} %fusion.21), channel_id=1, source_target_pairs={{0,1},{1,0},{2,3},{3,2},{4,5},{5,4},{6,7},{7,6},{8,9},{9,8},{10,11... | collective-permute-start | bytes 1572872 | tf_op jit(solution)/shard_map/ppermute | solution.py:27
  88.0 1.6 copy-start.2
  88.9 1.7 copy-start.11
  89.6 2.2 %copy-start.8 = (f32[512,2048]{0,1:T(8,128)S(1)}, f32[512,2048]{0,1:T(8,128)}, u32[]{:S(2)}) copy-start(f32[512,2048]{0,1:T(8,128)} %copy.158) | copy-start | bytes 12582916
  95.5 3.4 %copy-start.16 = (f32[16]{0:T(128)S(1)}, f32[16]{0:T(128)}, u32[]{:S(2)}) copy-start(f32[16]{0:T(128)} %copy-done.15) | copy-start | bytes 196
  95.6 2.9 %collective-permute-start.2 = (f32[16,136,128]{2,1,0:T(8,128)S(1)}, f32[16,136,128]{2,1,0:T(8,128)S(1)}, u32[]{:S(2)}, u32[]{:S(2)}) collective-permute-start(f32[16,136,128]{2,1,0:T(8,128)S(1)} %fusion.31), channel_id=1, source_target_pairs={{0,1},{1,0},{2,3},{3,2},{4,5},{5,4},{6,7},{7,6},{8,9},{9,8},{10,11... | collective-permute-start | bytes 3342344 | tf_op jit(solution)/shard_map/ppermute | solution.py:27
  100.8 7.4 %copy-start.6 = (bf16[512,2048]{0,1:T(8,128)(2,1)S(1)}, bf16[512,2048]{0,1:T(8,128)(2,1)}, u32[]{:S(2)}) copy-start(bf16[512,2048]{0,1:T(8,128)(2,1)} %copy.160) | copy-start | bytes 6291460
  108.2 4.8 %copy-start.1 = (bf16[16,512,512]{2,1,0:T(8,128)(2,1)}, bf16[16,512,512]{2,1,0:T(8,128)(2,1)S(1)}, u32[]{:S(2)}) copy-start(bf16[16,512,512]{2,1,0:T(8,128)(2,1)S(1)} %multiply_convert_fusion) | copy-start | bytes 25165828
  108.2 4.8 %copy-start.4 = (bf16[512,16,128]{0,2,1:T(8,128)(2,1)S(1)}, bf16[512,16,128]{0,2,1:T(8,128)(2,1)}, u32[]{:S(2)}) copy-start(bf16[512,16,128]{0,2,1:T(8,128)(2,1)} %copy-done.3) | copy-start | bytes 6291460
  117.5 32.7 %copy-start.21 = (pred[4]{0:T(512)(128)(4,1)S(1)}, pred[4]{0:T(512)(128)(4,1)}, u32[]{:S(2)}) copy-start(pred[4]{0:T(512)(128)(4,1)} %copy-done.20) | copy-start | bytes 16
  121.5 32.1 %copy-start.14 = (f32[136]{0:T(256)S(1)}, f32[136]{0:T(256)}, u32[]{:S(2)}) copy-start(f32[136]{0:T(256)} %copy-done.13) | copy-start | bytes 1636
  150.4 3.4 %copy-start.5 = (bf16[512,16,128]{0,2,1:T(8,128)(2,1)S(1)}, bf16[512,16,128]{0,2,1:T(8,128)(2,1)}, u32[]{:S(2)}) copy-start(bf16[512,16,128]{0,2,1:T(8,128)(2,1)} %copy-done.3) | copy-start | bytes 6291460
  153.7 4.8 %collective-permute-start.3 = (f32[8,136,128]{2,1,0:T(8,128)S(1)}, f32[8,136,128]{2,1,0:T(8,128)S(1)}, u32[]{:S(2)}, u32[]{:S(2)}) collective-permute-start(f32[8,136,128]{2,1,0:T(8,128)S(1)} %maximum_maximum_fusion.2), channel_id=1, source_target_pairs={{0,1},{1,0},{2,3},{3,2},{4,5},{5,4},{6,7},{7,6},{8,9},{9,8},{10,11... | collective-permute-start | bytes 1671176 | tf_op jit(solution)/shard_map/ppermute | solution.py:27
  158.8 2.7 %copy-start.7 = (bf16[512,2048]{0,1:T(8,128)(2,1)S(1)}, bf16[512,2048]{0,1:T(8,128)(2,1)}, u32[]{:S(2)}) copy-start(bf16[512,2048]{0,1:T(8,128)(2,1)} %copy.160) | copy-start | bytes 6291460
  (5 other events, 4.4 us)
Sparse Core Ops, SparseCore 0:
  25.9 50.9 all-gather.4
  101.0 47.1 all-gather.6

commit v2 on v1

--- a/solution.py
+++ b/solution.py
@@ -3,6 +3,7 @@
 import jax
 import jax.numpy as jnp
 from jax import lax
+from jax.experimental import pallas as pl
 from jax.sharding import PartitionSpec as P
 
 DH = 128
@@ -10,17 +11,6 @@
 
 
 epsilon = 1e-06
-
-
-def decay_parts(decay_log):
-    cumulated = jnp.cumsum(decay_log, axis=0)
-    final_log = cumulated[-1]
-    by_head = cumulated.T
-    spread = by_head[:, :, None] - by_head[:, None, :]
-    length = decay_log.shape[0]
-    causal = (jnp.arange(length)[:, None] >= jnp.arange(length)[None, :])[None]
-    decay_mat = jnp.where(causal, jnp.exp(jnp.where(causal, spread, 0.0)), 0.0)
-    return (cumulated, final_log, decay_mat)
 
 
 def swap_dp(x):
@@ -109,63 +99,165 @@
     return jnp.where(c == 0, core_zero, suffix), gain_total.reshape(heads * DH)
 
 
+def _dot(a, b, contract):
+    return lax.dot_general(a, b, (contract, ((), ())), preferred_element_type=jnp.float32)
+
+
+def _nn(a, b):
+    return _dot(a, b, ((1,), (0,)))
+
+
+def _nt(a, b):
+    return _dot(a, b, ((1,), (1,)))
+
+
+def _tn(a, b):
+    return _dot(a, b, ((0,), (0,)))
+
+
+def _decay(cum_col, cum_row):
+    length = cum_col.shape[0]
+    t = lax.broadcasted_iota(jnp.int32, (length, length), 0)
+    s = lax.broadcasted_iota(jnp.int32, (length, length), 1)
+    causal = t >= s
+    spread = cum_col - cum_row
+    return jnp.where(causal, jnp.exp(jnp.where(causal, spread, 0.0)), 0.0)
+
+
+def _masked(q, k, decay):
+    return (_nt(q, k) * decay).astype(jnp.bfloat16)
+
+
+def local_state_kernel(k_ref, v_ref, toend_ref, s_ref):
+    scaled = (k_ref[...].astype(jnp.float32) * toend_ref[0]).astype(jnp.bfloat16)
+    s_ref[0] = _tn(scaled, v_ref[...])
+
+
+def intra_kernel(q_ref, k_ref, v_ref, col_ref, row_ref, out_ref):
+    decay = _decay(col_ref[0], row_ref[0])
+    out_ref[...] = _nn(_masked(q_ref[...], k_ref[...], decay), v_ref[...])
+
+
+def norm_kernel(q_ref, g_ref, intra_ref, st_ref, grow_ref, gain_ref, og_ref, m_ref, gp_ref):
+    grow = grow_ref[0]
+    q = q_ref[...]
+    attended = intra_ref[...] + grow * _nn(q, st_ref[0])
+    width = attended.shape[-1]
+    root_mean = jnp.sqrt(jnp.sum(attended * attended, axis=-1, keepdims=True) / width + epsilon)
+    normed = attended / root_mean
+    grad_f = g_ref[...].astype(jnp.float32)
+    scaled = gain_ref[0] * grad_f
+    projected = jnp.sum(scaled * attended, axis=-1, keepdims=True)
+    out_grad = ((scaled - attended * projected / (width * root_mean * root_mean)) / root_mean).astype(
+        jnp.bfloat16
+    )
+    og_ref[...] = out_grad
+    gp_ref[0] = jnp.sum(grad_f * normed, axis=0, keepdims=True)
+    q_scaled = (q.astype(jnp.float32) * grow).astype(jnp.bfloat16)
+    m_ref[0] = _tn(q_scaled, out_grad)
+
+
+def grads_kernel(q_ref, k_ref, v_ref, og_ref, col_ref, row_ref, grow_ref, st_ref, qg_ref, kg_ref, vg_ref):
+    decay = _decay(col_ref[0], row_ref[0])
+    q, k, v, og = q_ref[...], k_ref[...], v_ref[...], og_ref[...]
+    masked = _masked(q, k, decay)
+    rgrad = (_nt(og, v) * decay).astype(jnp.bfloat16)
+    qg_ref[...] = (_nn(rgrad, k) + grow_ref[0] * _nt(og, st_ref[0])).astype(jnp.bfloat16)
+    kg_ref[...] = _tn(rgrad, q)
+    vg_ref[...] = _tn(masked, og)
+
+
+def finish_kernel(k_ref, v_ref, kg_ref, vg_ref, gl_ref, toend_ref, ko_ref, vo_ref):
+    toend = toend_ref[0]
+    grad_low = gl_ref[0]
+    ko_ref[...] = (kg_ref[...] + toend * _nt(v_ref[...], grad_low)).astype(jnp.bfloat16)
+    vo_ref[...] = (vg_ref[...] + toend * _nn(k_ref[...], grad_low)).astype(jnp.bfloat16)
+
+
+def _per_head(kernel, ins, outs, heads, length, flops, nbytes, exps=0):
+    def spec(kind):
+        if kind == "rows":
+            return pl.BlockSpec((length, DH), lambda h: (0, h))
+        if kind == "col":
+            return pl.BlockSpec((1, length, 1), lambda h: (h, 0, 0))
+        if kind == "row":
+            return pl.BlockSpec((1, 1, length), lambda h: (h, 0, 0))
+        if kind == "gain":
+            return pl.BlockSpec((1, 1, DH), lambda h: (h, 0, 0))
+        return pl.BlockSpec((1, DH, DH), lambda h: (h, 0, 0))
+
+    shapes = {
+        "rows": (length, heads * DH),
+        "gain": (heads, 1, DH),
+        "square": (heads, DH, DH),
+    }
+    out_shape = [jax.ShapeDtypeStruct(shapes[kind], dtype) for kind, dtype in outs]
+    return pl.pallas_call(
+        kernel,
+        grid=(heads,),
+        in_specs=[spec(kind) for kind, _ in ins],
+        out_specs=[spec(kind) for kind, _ in outs],
+        out_shape=out_shape,
+        cost_estimate=pl.CostEstimate(flops=flops, transcendentals=exps, bytes_accessed=nbytes),
+    )(*[x for _, x in ins])
+
+
 def on_device(query_rows, key_rows, value_rows, cotangent, log_decay, norm_gain):
     length = query_rows.shape[0]
     heads = log_decay.shape[1]
-    shaped = (length, heads, DH)
-    query_blk = query_rows.reshape(shaped)
-    key_blk = key_rows.reshape(shaped)
-    value_blk = value_rows.reshape(shaped)
-    grad_blk = cotangent.reshape(shaped)
-    gain_heads = norm_gain.reshape(heads, DH)
     f32 = jnp.float32
     bf16 = jnp.bfloat16
-    cumulated, final_log, decay_mat = decay_parts(log_decay)
-    to_end = jnp.exp(final_log[None, :] - cumulated)
-    grow_from = jnp.exp(cumulated)
-    scores = jnp.einsum("thd,shd->hts", query_blk, key_blk, preferred_element_type=f32)
-    masked = (scores * decay_mat).astype(bf16)
-    intra = jnp.einsum("hts,she->the", masked, value_blk, preferred_element_type=f32)
-    key_scaled = (key_blk.astype(f32) * to_end[:, :, None]).astype(bf16)
-    local_state = jnp.einsum("shd,she->hde", key_scaled, value_blk, preferred_element_type=f32)
+    cumulated = jnp.cumsum(log_decay, axis=0)
+    final_log = cumulated[-1]
+    by_head = cumulated.T
+    cum_col = by_head[:, :, None]
+    cum_row = by_head[:, None, :]
+    grow_col = jnp.exp(cum_col)
+    toend_col = jnp.exp(final_log[:, None, None] - cum_col)
+    gain_rows = norm_gain.reshape(heads, 1, DH)
+    q, k, v, g = query_rows, key_rows, value_rows, cotangent
+    big = length * length * DH * 2 * heads
+    small = length * DH * DH * 2 * heads
+    rows_bytes = length * heads * DH * 2
+    (local_state,) = _per_head(
+        local_state_kernel,
+        [("rows", k), ("rows", v), ("col", toend_col)],
+        [("square", f32)],
+        heads, length, small, 2 * rows_bytes,
+    )
     state_in = forward_states(local_state, final_log)
+    (intra,) = _per_head(
+        intra_kernel,
+        [("rows", q), ("rows", k), ("rows", v), ("col", cum_col), ("row", cum_row)],
+        [("rows", f32)],
+        heads, length, 2 * big, 5 * rows_bytes, heads * length * length,
+    )
     state_low = state_in.astype(bf16)
-    attended = intra + grow_from[:, :, None] * jnp.einsum(
-        "thd,hde->the", query_blk, state_low, preferred_element_type=f32
-    )
-    root_mean = jnp.sqrt(jnp.mean(attended * attended, axis=-1, keepdims=True) + epsilon)
-    normed = attended / root_mean
-    grad_f = grad_blk.astype(f32)
-    scaled = gain_heads[None] * grad_f
-    projected = jnp.sum(scaled * attended, axis=-1, keepdims=True)
-    out_grad = ((scaled - attended * projected / (DH * root_mean * root_mean)) / root_mean).astype(
-        bf16
-    )
-    gain_part = jnp.sum(grad_f * normed, axis=0).reshape(heads * DH)
-    query_scaled = (query_blk.astype(f32) * grow_from[:, :, None]).astype(bf16)
-    moment = jnp.einsum("thd,the->hde", query_scaled, out_grad, preferred_element_type=f32)
-    grad_state, gain_sum = backward_states(moment, final_log, gain_part)
+    out_grad, moment, gain_part = _per_head(
+        norm_kernel,
+        [("rows", q), ("rows", g), ("rows", intra), ("square", state_low), ("col", grow_col), ("gain", gain_rows)],
+        [("rows", bf16), ("square", f32), ("gain", f32)],
+        heads, length, 2 * small, 5 * rows_bytes,
+    )
+    grad_state, gain_sum = backward_states(moment, final_log, gain_part.reshape(heads * DH))
+    query_grad, key_part, value_part = _per_head(
+        grads_kernel,
+        [("rows", q), ("rows", k), ("rows", v), ("rows", out_grad), ("col", cum_col), ("row", cum_row),
+         ("col", grow_col), ("square", state_low)],
+        [("rows", bf16), ("rows", f32), ("rows", f32)],
+        heads, length, 5 * big + small, 9 * rows_bytes, heads * length * length,
+    )
     grad_low = grad_state.astype(bf16)
+    key_grad, value_grad = _per_head(
+        finish_kernel,
+        [("rows", k), ("rows", v), ("rows", key_part), ("rows", value_part), ("square", grad_low),
+         ("col", toend_col)],
+        [("rows", bf16), ("rows", bf16)],
+        heads, length, 2 * small, 8 * rows_bytes,
+    )
     seq_total = length * lax.axis_size(("ctx", "dp"))
     gain_grad = gain_sum * (1.0 / math.sqrt(seq_total))
-    dots = jnp.einsum("the,she->hts", out_grad, value_blk, preferred_element_type=f32)
-    rgrad = (dots * decay_mat).astype(bf16)
-    query_grad = jnp.einsum("hts,shd->thd", rgrad, key_blk, preferred_element_type=f32) + grow_from[
-        :, :, None
-    ] * jnp.einsum("the,hde->thd", out_grad, state_low, preferred_element_type=f32)
-    key_grad = jnp.einsum("hts,thd->shd", rgrad, query_blk, preferred_element_type=f32) + to_end[
-        :, :, None
-    ] * jnp.einsum("she,hde->shd", value_blk, grad_low, preferred_element_type=f32)
-    value_grad = jnp.einsum("hts,the->she", masked, out_grad, preferred_element_type=f32) + to_end[
-        :, :, None
-    ] * jnp.einsum("shd,hde->she", key_blk, grad_low, preferred_element_type=f32)
-    flat = (length, heads * DH)
-    return (
-        query_grad.astype(bf16).reshape(flat),
-        key_grad.astype(bf16).reshape(flat),
-        value_grad.astype(bf16).reshape(flat),
-        gain_grad,
-    )
+    return (query_grad, key_grad, value_grad, gain_grad)
 
 
 def solution(mesh):

time: 188 us -> 237 us (1.26)
  Pallas kernels: 0 us -> 81 us
  matrix products: 53.7 us -> 0 us
  waiting for transfers between devices: 64.1 us -> 103 us
  local copies, waits for them, and re-layouts: 32.5 us -> 9.38 us
  other arithmetic: 20.4 us -> 25.9 us
    pallas_call x0 -> x5, Pallas kernels: none -> 81 us  [_per_head(): pl.pallas_call(kernel, grid=(heads,), in_specs=[spec(kind) for kind, _ in...]
    dot_general x12 -> x0, matrix products: 53.7 us -> none  [the longest x1 9.58 us: on_device(): jnp.einsum('thd,shd->hts', query_blk, key_blk, preferred_element_type=f32)]
    all_gather x2, waiting for transfers between devices: 59.2 us -> 98.4 us  [chip_prefix(): gathered = lax.all_gather(message, 'ctx')]
    unnamed x51 -> x10, local copies, waits for them, and re-layouts: 24.2 us -> 0.73 us
    exp x1, other arithmetic: 0.09 us -> 6.49 us  [on_device(): grow_col = jnp.exp(cum_col)]
    another operation x1 -> x3, local copies, waits for them, and re-layouts: 0.01 us -> 5.32 us
    convert_element_type x1 -> x0, local copies, waits for them, and re-layouts: 4.13 us -> none  [on_device(): grad_f = grad_blk.astype(f32)]
    concatenate x5, other arithmetic: 2.23 us -> 4.85 us  [pack_rows(): return jnp.concatenate([core] + pad + [fill], axis=1)]
  transfers between devices with their start and end apart: 6 -> 6, of which waited for: 4 -> 4; matrix products, arithmetic and copies ran while one was open for 27% -> 0% of each run, Pallas kernels for 0% -> 16%
where the time goes in v2:
time: 237 us; the launch traced here: 235 us
  waiting for transfers between devices  103 us (43%)
  Pallas kernels  81 us (34%)
  other arithmetic  25.9 us (11%)
  between operations  14.3 us (6%)
  local copies, waits for them, and re-layouts  9.38 us (4%)
    all_gather x2, waiting for transfers between devices, chip_prefix(): gathered = lax.all_gather(message, 'ctx')  98.4 us
    pallas_call x5, Pallas kernels, _per_head(): pl.pallas_call(kernel, grid=(heads,), in_specs=[spec(kind) for kind, _ in...  81 us
    exp x1, other arithmetic, on_device(): grow_col = jnp.exp(cum_col)  6.49 us
    another operation x3, local copies, waits for them, and re-layouts  5.32 us
    ppermute x4, waiting for transfers between devices, swap_dp(): return lax.ppermute(x, 'dp', perm=[(0, 1), (1, 0)])  4.9 us
    concatenate x5, other arithmetic, pack_rows(): return jnp.concatenate([core] + pad + [fill], axis=1)  4.85 us
  transfers between devices with their start and end apart: 6, of which 4 were waited for; matrix products, arithmetic and copies ran while one was open for 0% of the time, Pallas kernels for 16%

profile of v2, /device:TPU:0, one launch (start us, length us, event | category | flops | bytes accessed | tf_op | source)
XLA Modules:
  0.0 235.2 jit_solution(7781322693293296262)
XLA Ops:
  7.9 1.1 reduce-window.6
  9.6 5.3 %reduce_window_sum.72.col_ref = f32[16,512,1]{2,1,0:T(8,128)} reshape(f32[16,4,128]{2,1,0:T(4,128)S(1)} %copy.96) | data formatting | bytes 65536 | tf_op jit(solution)/shard_map/reduce_window_sum
  14.9 6.5 %fusion.20 = (f32[16,512,1]{2,1,0:T(8,128)}, f32[16,512,1]{2,1,0:T(8,128)}) fusion(f32[16,512,1]{2,1,0:T(8,128)} %reduce_window_sum.72.col_ref, f32[16]{0:T(128)S(1)} %get-tuple-element.39), kind=kLoop, calls=%fused_computation.74 | loop fusion | flops 8192 | bytes 98368 | tf_op jit(solution)/shard_map/exp | solution.py:215
  21.5 12.9 %shard_map.94 = f32[16,128,128]{2,1,0:T(8,128)} custom-call(bf16[512,2048]{1,0:T(8,128)(2,1)} %k_ref.7, bf16[512,2048]{1,0:T(8,128)(2,1)} %v_ref.7, f32[16,512,1]{2,1,0:T(8,128)} %get-tuple-element.29.toend_ref), custom_call_target="tpu_custom_call" | custom-call | flops 268435456 | bytes 4194304 | tf_op jit(solution)/shard_map/pallas_call | solution.py:195
  34.5 1.4 fusion.2
  36.5 2.5 %collective-permute-done = f32[16,136,128]{2,1,0:T(8,128)} collective-permute-done((f32[16,136,128]{2,1,0:T(8,128)S(1)}, f32[16,136,128]{2,1,0:T(8,128)}, u32[]{:S(2)}, u32[]{:S(2)}) %collective-permute-start) | collective-permute-done | bytes 1114144 | tf_op jit(solution)/shard_map/ppermute | solution.py:17
  39.0 1.1 fusion.16
  40.2 1.4 fusion.22
  42.8 51.0 %all-gather.5.cloned.1.call-done = f32[32,136,128]{2,1,0:T(8,128)} async-done(((f32[8,136,128]{2,1,0:T(8,128)}), f32[32,136,128]{2,1,0:T(8,128)}) %all-gather.5.cloned.1.call-update) | async-done | bytes 2228240 | tf_op jit(solution)/shard_map/all_gather | solution.py:28
  93.8 1.0 slice_reduce_fusion.3
  95.1 1.2 fusion.7
  96.3 1.9 fusion.1
  98.3 15.4 %shard_map.93.intra_ref = f32[512,2048]{1,0:T(8,128)} custom-call(bf16[512,2048]{1,0:T(8,128)(2,1)} %q_ref.5, bf16[512,2048]{1,0:T(8,128)(2,1)} %k_ref.7, bf16[512,2048]{1,0:T(8,128)(2,1)} %v_ref.7, f32[16,512,1]{2,1,0:T(8,128)} %reduce_window_sum.72.col_ref, f32[16,1,512]{2,1,0:T(1,128)} %bitcast.33), custom_call_target="tpu_custom_call" | custom-call | flops 2147483648 | bytes 10485760 | tf_op jit(solution)/shard_map/pallas_call | solution.py:195
  113.8 1.0 select_convert_fusion.1.st_ref
  114.9 17.0 %shard_map.95 = (bf16[512,2048]{1,0:T(8,128)(2,1)}, f32[16,128,128]{2,1,0:T(8,128)}, f32[16,1,128]{2,1,0:T(1,128)}) custom-call(bf16[512,2048]{1,0:T(8,128)(2,1)} %q_ref.5, bf16[512,2048]{1,0:T(8,128)(2,1)} %g_ref.1, f32[512,2048]{1,0:T(8,128)} %shard_map.93.intra_ref, bf16[16,128,128]{2,1,0:T(8,128)(2,1)} %select_convert_fusion.1.st_ref, ...), custom_call_target="tpu_custom_call" | custom-call | flops 536870912 | bytes 10485760 | tf_op jit(solution)/shard_map/pallas_call | solution.py:195
  131.9 1.5 fusion.4
  133.9 2.4 %collective-permute-done.2 = f32[16,136,128]{2,1,0:T(8,128)S(1)} collective-permute-done((f32[16,136,128]{2,1,0:T(8,128)S(1)}, f32[16,136,128]{2,1,0:T(8,128)S(1)}, u32[]{:S(2)}, u32[]{:S(2)}) %collective-permute-start.2) | collective-permute-done | bytes 1114144 | tf_op jit(solution)/shard_map/ppermute | solution.py:17
  138.1 47.3 %all-gather.7.cloned.1.call-done = f32[32,136,128]{2,1,0:T(8,128)} async-done(((f32[8,136,128]{2,1,0:T(8,128)}), f32[32,136,128]{2,1,0:T(8,128)}) %all-gather.7.cloned.1.call-update) | async-done | bytes 2228240 | tf_op jit(solution)/shard_map/all_gather | solution.py:28
  185.4 1.0 slice_reduce_fusion.2
  187.6 1.1 fusion.8
  188.8 1.9 fusion
  190.8 21.6 %shard_map.96 = (bf16[512,2048]{1,0:T(8,128)(2,1)}, f32[512,2048]{1,0:T(8,128)}, f32[512,2048]{1,0:T(8,128)}) custom-call(bf16[512,2048]{1,0:T(8,128)(2,1)} %q_ref.5, bf16[512,2048]{1,0:T(8,128)(2,1)} %k_ref.7, bf16[512,2048]{1,0:T(8,128)(2,1)} %v_ref.7, bf16[512,2048]{1,0:T(8,128)(2,1)} %get-tuple-element.12.og_ref, ...), custom_call_target="tpu_custom_call" | custom-call | flops 5637144576 | bytes 18874368 | tf_op jit(solution)/shard_map/pallas_call | solution.py:195
  213.2 1.0 select_convert_fusion.gl_ref
  214.2 14.1 %shard_map.97 = (bf16[512,2048]{1,0:T(8,128)(2,1)}, bf16[512,2048]{1,0:T(8,128)(2,1)}) custom-call(bf16[512,2048]{1,0:T(8,128)(2,1)} %k_ref.7, bf16[512,2048]{1,0:T(8,128)(2,1)} %v_ref.7, f32[512,2048]{1,0:T(8,128)} %get-tuple-element.14.kg_ref, f32[512,2048]{1,0:T(8,128)} %get-tuple-element.15.vg_ref, bf16[16,128,128]{2,1,0:T(8,128)(2,1)} %select_convert_fusion.gl_ref, ...), custom_call_target="tpu_custom_call" | custom-call | flops 536870912 | bytes 16777216 | tf_op jit(solution)/shard_map/pallas_call | solution.py:195
  (64 shorter events, 8.1 us)
Async XLA Ops:
  7.2 0.8 copy-start
  7.2 86.7 %all-gather.5.cloned.1.call-start = ((), (), s32[]{:S(2)}) async-start(), calls=%async_computation | async-start | bytes 2785280 | tf_op jit(solution)/shard_map/all_gather | solution.py:28
  9.6 5.3 %copy-start.3 = (f32[16,4,128]{2,1,0:T(4,128)}, f32[16,4,128]{2,1,0:T(4,128)S(1)}, u32[]{:S(2)}) copy-start(f32[16,4,128]{2,1,0:T(4,128)S(1)} %copy.96) | copy-start | bytes 98308
  34.4 5.8 %copy-start.1 = (f32[16,128,128]{2,1,0:T(8,128)S(1)}, f32[16,128,128]{2,1,0:T(8,128)}, u32[]{:S(2)}) copy-start(f32[16,128,128]{2,1,0:T(8,128)} %shard_map.94) | copy-start | bytes 3145732
  36.0 3.0 %collective-permute-start = (f32[16,136,128]{2,1,0:T(8,128)S(1)}, f32[16,136,128]{2,1,0:T(8,128)}, u32[]{:S(2)}, u32[]{:S(2)}) collective-permute-start(f32[16,136,128]{2,1,0:T(8,128)S(1)} %fusion.2), channel_id=1, source_target_pairs={{0,1},{1,0},{2,3},{3,2},{4,5},{5,4},{6,7},{7,6},{8,9},{9,8},{10,11... | collective-permute-start | bytes 3342344 | tf_op jit(solution)/shard_map/ppermute | solution.py:17
  42.7 142.7 %all-gather.7.cloned.1.call-start = ((), (), s32[]{:S(2)}) async-start(), calls=%async_computation.1 | async-start | bytes 2785280 | tf_op jit(solution)/shard_map/all_gather | solution.py:28
  98.2 15.6 %collective-permute-start.1 = (f32[8,128,128]{2,1,0:T(8,128)S(1)}, f32[8,128,128]{2,1,0:T(8,128)S(1)}, u32[]{:S(2)}, u32[]{:S(2)}) collective-permute-start(f32[8,128,128]{2,1,0:T(8,128)S(1)} %fusion.1), channel_id=1, source_target_pairs={{0,1},{1,0},{2,3},{3,2},{4,5},{5,4},{6,7},{7,6},{8,9},{9,8},{10,11... | collective-permute-start | bytes 1572872 | tf_op jit(solution)/shard_map/ppermute | solution.py:17
  131.8 4.7 %copy-start.4 = (f32[16,1,128]{2,1,0:T(1,128)S(1)}, f32[16,1,128]{2,1,0:T(1,128)}, u32[]{:S(2)}) copy-start(f32[16,1,128]{2,1,0:T(1,128)} %get-tuple-element.17) | copy-start | bytes 24580
  131.8 4.9 %copy-start.2 = (f32[16,128,128]{2,1,0:T(8,128)S(1)}, f32[16,128,128]{2,1,0:T(8,128)}, u32[]{:S(2)}) copy-start(f32[16,128,128]{2,1,0:T(8,128)} %get-tuple-element.16) | copy-start | bytes 3145732
  133.3 2.9 %collective-permute-start.2 = (f32[16,136,128]{2,1,0:T(8,128)S(1)}, f32[16,136,128]{2,1,0:T(8,128)S(1)}, u32[]{:S(2)}, u32[]{:S(2)}) collective-permute-start(f32[16,136,128]{2,1,0:T(8,128)S(1)} %fusion.4), channel_id=1, source_target_pairs={{0,1},{1,0},{2,3},{3,2},{4,5},{5,4},{6,7},{7,6},{8,9},{9,8},{10,11... | collective-permute-start | bytes 3342344 | tf_op jit(solution)/shard_map/ppermute | solution.py:17
  190.8 21.7 %collective-permute-start.3 = (f32[8,136,128]{2,1,0:T(8,128)S(1)}, f32[8,136,128]{2,1,0:T(8,128)S(1)}, u32[]{:S(2)}, u32[]{:S(2)}) collective-permute-start(f32[8,136,128]{2,1,0:T(8,128)S(1)} %maximum_maximum_fusion.2), channel_id=1, source_target_pairs={{0,1},{1,0},{2,3},{3,2},{4,5},{5,4},{6,7},{7,6},{8,9},{9,8},{10,11... | collective-permute-start | bytes 1671176 | tf_op jit(solution)/shard_map/ppermute | solution.py:17
Sparse Core Ops, SparseCore 0:
  42.9 50.9 all-gather.4
  138.2 47.1 all-gather.6

commit v3 on v2

--- a/solution.py
+++ b/solution.py
@@ -8,6 +8,7 @@
 
 DH = 128
 PAD = 8
+CHUNKS = 4
 
 
 epsilon = 1e-06
@@ -24,26 +25,6 @@
     return jnp.concatenate([core] + pad + [fill], axis=1)
 
 
-def chip_prefix(message, later):
-    gathered = lax.all_gather(message, "ctx")
-    chips = gathered.shape[0]
-    z = lax.axis_index("ctx")
-    decay = gathered[:, :, DH, 0]
-    before = jnp.cumsum(decay, axis=0) - decay
-    index = jnp.arange(chips)[:, None]
-    mine = jnp.sum(jnp.where(index == z, before, 0.0), axis=0)
-    mine_decay = jnp.sum(jnp.where(index == z, decay, 0.0), axis=0)
-    if later:
-        valid = index > z
-        spread = before - mine[None] - mine_decay[None]
-    else:
-        valid = index < z
-        spread = mine[None] - before - decay
-    weight = jnp.where(valid, jnp.exp(jnp.where(valid, spread, 0.0)), 0.0)
-    total = jnp.sum(weight[:, :, None, None] * gathered[:, :, :DH, :], axis=0)
-    return total, gathered
-
-
 def halves(x, c):
     half = x.shape[0] // 2
     return lax.dynamic_slice_in_dim(x, c * half, half, axis=0)
@@ -53,6 +34,31 @@
     first = jnp.where(c == 0, mine, other)
     second = jnp.where(c == 0, other, mine)
     return jnp.concatenate([first, second], axis=0)
+
+
+def chain_scan(chip_state, chip_decay, later):
+    chips = lax.axis_size("ctx")
+    z = lax.axis_index("ctx")
+    heads = chip_state.shape[0]
+    count = min(CHUNKS, heads)
+    size = heads // count
+    pieces = chip_state.reshape(count, size, DH, DH)
+    factor = jnp.exp(chip_decay).reshape(count, size, 1, 1)
+    rank = (chips - 1 - z) if later else z
+    if later:
+        perm = [(i, i - 1) for i in range(1, chips)]
+    else:
+        perm = [(i, i + 1) for i in range(chips - 1)]
+    prefix = jnp.zeros_like(pieces)
+    for step in range(count + chips - 2):
+        send = jnp.clip(step - rank, 0, count - 1)
+        outgoing = factor[send] * prefix[send] + pieces[send]
+        arrived = lax.ppermute(outgoing, "ctx", perm=perm)
+        where_to = step - rank + 1
+        valid = (where_to >= 0) & (where_to < count) & (rank >= 1)
+        slot = jnp.clip(where_to, 0, count - 1)
+        prefix = prefix.at[slot].set(jnp.where(valid, arrived, prefix[slot]))
+    return prefix.reshape(heads, DH, DH)
 
 
 def forward_states(local_state, final_log):
@@ -67,7 +73,7 @@
     fin_second = jnp.where(c == 0, other_fin, own_fin)
     chip_state = jnp.exp(fin_second)[:, None, None] * first + second
     chip_decay = fin_first + fin_second
-    prefix_half, _ = chip_prefix(pack_rows(halves(chip_state, c), halves(chip_decay, c)), later=False)
+    prefix_half = chain_scan(halves(chip_state, c), halves(chip_decay, c), later=False)
     prefix = join_halves(prefix_half, swap_dp(prefix_half), c)
     core_one = jnp.exp(fin_first)[:, None, None] * prefix + first
     return jnp.where(c == 0, prefix, core_one)
@@ -88,10 +94,8 @@
     chip_gain = gain_rows + other[:, DH + 1, :]
     chip_state = first + jnp.exp(fin_first)[:, None, None] * second
     chip_decay = fin_first + fin_second
-    suffix_half, gathered = chip_prefix(
-        pack_rows(halves(chip_state, c), halves(chip_decay, c), halves(chip_gain, c)), later=True
-    )
-    gain_half = jnp.sum(gathered[:, :, DH + 1, :], axis=0)
+    gain_half = jnp.sum(lax.all_gather(halves(chip_gain, c), "ctx"), axis=0)
+    suffix_half = chain_scan(halves(chip_state, c), halves(chip_decay, c), later=True)
     back = swap_dp(pack_rows(suffix_half, gain_half))
     suffix = join_halves(suffix_half, back[:, :DH, :], c)
     gain_total = join_halves(gain_half, back[:, DH, :], c)

time: 237 us -> 218 us (0.920)
  waiting for transfers between devices: 103 us -> 44.4 us
  starting transfers between devices: 1.3 us -> 35.6 us
  blocking collectives: 0 us -> 14.7 us
  between operations: 14.3 us -> 1.25 us
  other arithmetic: 25.9 us -> 29.9 us
    all_gather x2 -> x0, waiting for transfers between devices: 98.4 us -> none  [chip_prefix(): gathered = lax.all_gather(message, 'ctx')]
    ppermute x0 -> x12, waiting for transfers between devices: none -> 39.5 us  [chain_scan(): arrived = lax.ppermute(outgoing, 'ctx', perm=perm)]
    ppermute x0 -> x12, starting transfers between devices: none -> 34.4 us  [chain_scan(): arrived = lax.ppermute(outgoing, 'ctx', perm=perm)]
    all_gather x0 -> x1, blocking collectives: none -> 14.7 us  [backward_states(): gain_half = jnp.sum(lax.all_gather(halves(chip_gain, c), 'ctx'), axis=0)]
    scatter x0 -> x12, other arithmetic: none -> 7.59 us  [chain_scan(): prefix = prefix.at[slot].set(jnp.where(valid, arrived, prefix[slot]))]
    reduce_sum x5 -> x1, other arithmetic: 4.85 us -> 0.01 us  [backward_states(): gain_half = jnp.sum(lax.all_gather(halves(chip_gain, c), 'ctx'), axis=0)]
    another operation x6 -> x10, other arithmetic: 1.41 us -> 5.74 us
    concatenate x5 -> x3, other arithmetic: 4.85 us -> 3.03 us  [pack_rows(): return jnp.concatenate([core] + pad + [fill], axis=1)]
  transfers between devices with their start and end apart: 6 -> 16, of which waited for: 4 -> 13; matrix products, arithmetic and copies ran while one was open for 0% -> 3% of each run, Pallas kernels for 16% -> 17%
where the time goes in v3:
time: 218 us; the launch traced here: 215 us
  Pallas kernels  81 us (37%)
  waiting for transfers between devices  44.4 us (20%)
  starting transfers between devices  35.6 us (16%)
  other arithmetic  29.9 us (14%)
  blocking collectives  14.7 us (7%)
  local copies, waits for them, and re-layouts  8.21 us (4%)
    pallas_call x5, Pallas kernels, _per_head(): pl.pallas_call(kernel, grid=(heads,), in_specs=[spec(kind) for kind, _ in...  81 us
    ppermute x12, waiting for transfers between devices, chain_scan(): arrived = lax.ppermute(outgoing, 'ctx', perm=perm)  39.5 us
    ppermute x12, starting transfers between devices, chain_scan(): arrived = lax.ppermute(outgoing, 'ctx', perm=perm)  34.4 us
    all_gather x1, blocking collectives, backward_states(): gain_half = jnp.sum(lax.all_gather(halves(chip_gain, c), 'ctx'), axis=0)  14.7 us
    scatter x12, other arithmetic, chain_scan(): prefix = prefix.at[slot].set(jnp.where(valid, arrived, prefix[slot]))  7.59 us
    exp x1, other arithmetic, on_device(): grow_col = jnp.exp(cum_col)  6.49 us
    another operation x10, other arithmetic  5.74 us
    another operation x7, local copies, waits for them, and re-layouts  5.55 us
  transfers between devices with their start and end apart: 16, of which 13 were waited for; matrix products, arithmetic and copies ran while one was open for 3% of the time, Pallas kernels for 17%

profile of v3, /device:TPU:0, one launch (start us, length us, event | category | flops | bytes accessed | tf_op | source)
XLA Modules:
  0.0 215.1 jit_solution(17714012241974380752)
XLA Ops:
  3.1 5.3 %reduce_window_sum.47.col_ref = f32[16,512,1]{2,1,0:T(8,128)} reshape(f32[16,4,128]{2,1,0:T(4,128)S(1)} %copy.58) | data formatting | bytes 65536 | tf_op jit(solution)/shard_map/reduce_window_sum
  8.4 6.5 %fusion.41 = (f32[16,512,1]{2,1,0:T(8,128)}, f32[16,512,1]{2,1,0:T(8,128)}) fusion(f32[16,512,1]{2,1,0:T(8,128)} %reduce_window_sum.47.col_ref, f32[16]{0:T(128)S(1)} %get-tuple-element.193), kind=kLoop, calls=%fused_computation.196 | loop fusion | flops 8192 | bytes 98368 | tf_op jit(solution)/shard_map/exp | solution.py:219
  15.0 12.9 %shard_map.94 = f32[16,128,128]{2,1,0:T(8,128)} custom-call(bf16[512,2048]{1,0:T(8,128)(2,1)} %k_ref.7, bf16[512,2048]{1,0:T(8,128)(2,1)} %v_ref.7, f32[16,512,1]{2,1,0:T(8,128)} %get-tuple-element.183.toend_ref), custom_call_target="tpu_custom_call" | custom-call | flops 268435456 | bytes 4194304 | tf_op jit(solution)/shard_map/pallas_call | solution.py:199
  30.0 2.4 %collective-permute-done = f32[16,136,128]{2,1,0:T(8,128)S(1)} collective-permute-done((f32[16,136,128]{2,1,0:T(8,128)S(1)}, f32[16,136,128]{2,1,0:T(8,128)S(1)}, u32[]{:S(2)}, u32[]{:S(2)}) %collective-permute-start) | collective-permute-done | bytes 1114144 | tf_op jit(solution)/shard_map/ppermute | solution.py:18
  33.3 4.9 %collective-permute-start.1 = (f32[2,128,128]{2,1,0:T(8,128)S(1)}, f32[2,128,128]{2,1,0:T(8,128)S(1)}, u32[]{:S(2)}, u32[]{:S(2)}) collective-permute-start(f32[2,128,128]{2,1,0:T(8,128)S(1)} %bitcast_add_fusion.11), channel_id=1, source_target_pairs={{0,4},{4,8},{8,12},{1,5},{5,9},{9,13},{2,6},{6,10},{10,14},{3,7},{... | collective-permute-start | bytes 393224 | tf_op jit(solution)/shard_map/ppermute | solution.py:56
  41.9 4.4 %collective-permute-start.2 = (f32[2,128,128]{2,1,0:T(8,128)S(1)}, f32[2,128,128]{2,1,0:T(8,128)S(1)}, u32[]{:S(2)}, u32[]{:S(2)}) collective-permute-start(f32[2,128,128]{2,1,0:T(8,128)S(1)} %bitcast_add_fusion.10), channel_id=1, source_target_pairs={{0,4},{4,8},{8,12},{1,5},{5,9},{9,13},{2,6},{6,10},{10,14},{3,7},{... | collective-permute-start | bytes 393224 | tf_op jit(solution)/shard_map/ppermute | solution.py:56
  46.4 2.5 %collective-permute-done.2 = f32[2,128,128]{2,1,0:T(8,128)S(1)} collective-permute-done((f32[2,128,128]{2,1,0:T(8,128)S(1)}, f32[2,128,128]{2,1,0:T(8,128)S(1)}, u32[]{:S(2)}, u32[]{:S(2)}) %collective-permute-start.2) | collective-permute-done | bytes 131104 | tf_op jit(solution)/shard_map/ppermute | solution.py:56
  49.6 4.4 %collective-permute-start.3 = (f32[2,128,128]{2,1,0:T(8,128)S(1)}, f32[2,128,128]{2,1,0:T(8,128)S(1)}, u32[]{:S(2)}, u32[]{:S(2)}) collective-permute-start(f32[2,128,128]{2,1,0:T(8,128)S(1)} %bitcast_add_fusion.9), channel_id=1, source_target_pairs={{0,4},{4,8},{8,12},{1,5},{5,9},{9,13},{2,6},{6,10},{10,14},{3,7},{... | collective-permute-start | bytes 393224 | tf_op jit(solution)/shard_map/ppermute | solution.py:56
  57.2 4.4 %collective-permute-start.4 = (f32[2,128,128]{2,1,0:T(8,128)S(1)}, f32[2,128,128]{2,1,0:T(8,128)S(1)}, u32[]{:S(2)}, u32[]{:S(2)}) collective-permute-start(f32[2,128,128]{2,1,0:T(8,128)S(1)} %bitcast_add_fusion.8), channel_id=1, source_target_pairs={{0,4},{4,8},{8,12},{1,5},{5,9},{9,13},{2,6},{6,10},{10,14},{3,7},{... | collective-permute-start | bytes 393224 | tf_op jit(solution)/shard_map/ppermute | solution.py:56
  61.6 2.5 %collective-permute-done.4 = f32[2,128,128]{2,1,0:T(8,128)S(1)} collective-permute-done((f32[2,128,128]{2,1,0:T(8,128)S(1)}, f32[2,128,128]{2,1,0:T(8,128)S(1)}, u32[]{:S(2)}, u32[]{:S(2)}) %collective-permute-start.4) | collective-permute-done | bytes 131104 | tf_op jit(solution)/shard_map/ppermute | solution.py:56
  64.8 4.4 %collective-permute-start.5 = (f32[2,128,128]{2,1,0:T(8,128)S(1)}, f32[2,128,128]{2,1,0:T(8,128)S(1)}, u32[]{:S(2)}, u32[]{:S(2)}) collective-permute-start(f32[2,128,128]{2,1,0:T(8,128)S(1)} %bitcast_add_fusion.7), channel_id=1, source_target_pairs={{0,4},{4,8},{8,12},{1,5},{5,9},{9,13},{2,6},{6,10},{10,14},{3,7},{... | collective-permute-start | bytes 393224 | tf_op jit(solution)/shard_map/ppermute | solution.py:56
  72.4 4.4 %collective-permute-start.6 = (f32[2,128,128]{2,1,0:T(8,128)S(1)}, f32[2,128,128]{2,1,0:T(8,128)S(1)}, u32[]{:S(2)}, u32[]{:S(2)}) collective-permute-start(f32[2,128,128]{2,1,0:T(8,128)S(1)} %bitcast_add_fusion.6), channel_id=1, source_target_pairs={{0,4},{4,8},{8,12},{1,5},{5,9},{9,13},{2,6},{6,10},{10,14},{3,7},{... | collective-permute-start | bytes 393224 | tf_op jit(solution)/shard_map/ppermute | solution.py:56
  76.8 2.5 %collective-permute-done.6 = f32[2,128,128]{2,1,0:T(8,128)S(1)} collective-permute-done((f32[2,128,128]{2,1,0:T(8,128)S(1)}, f32[2,128,128]{2,1,0:T(8,128)S(1)}, u32[]{:S(2)}, u32[]{:S(2)}) %collective-permute-start.6) | collective-permute-done | bytes 131104 | tf_op jit(solution)/shard_map/ppermute | solution.py:56
  80.1 15.4 %shard_map.93.intra_ref = f32[512,2048]{1,0:T(8,128)} custom-call(bf16[512,2048]{1,0:T(8,128)(2,1)} %q_ref.5, bf16[512,2048]{1,0:T(8,128)(2,1)} %k_ref.7, bf16[512,2048]{1,0:T(8,128)(2,1)} %v_ref.7, f32[16,512,1]{2,1,0:T(8,128)} %reduce_window_sum.47.col_ref, f32[16,1,512]{2,1,0:T(1,128)} %bitcast.231), custom_call_target="tpu_custom_call" | custom-call | flops 2147483648 | bytes 10485760 | tf_op jit(solution)/shard_map/pallas_call | solution.py:199
  96.6 17.0 %shard_map.95 = (bf16[512,2048]{1,0:T(8,128)(2,1)}, f32[16,128,128]{2,1,0:T(8,128)}, f32[16,1,128]{2,1,0:T(1,128)}) custom-call(bf16[512,2048]{1,0:T(8,128)(2,1)} %q_ref.5, bf16[512,2048]{1,0:T(8,128)(2,1)} %g_ref.1, f32[512,2048]{1,0:T(8,128)} %shard_map.93.intra_ref, bf16[16,128,128]{2,1,0:T(8,128)(2,1)} %select_convert_fusion.1.st_ref, ...), custom_call_target="tpu_custom_call" | custom-call | flops 536870912 | bytes 10485760 | tf_op jit(solution)/shard_map/pallas_call | solution.py:199
  115.7 2.5 %collective-permute-done.8 = f32[16,136,128]{2,1,0:T(8,128)} collective-permute-done((f32[16,136,128]{2,1,0:T(8,128)S(1)}, f32[16,136,128]{2,1,0:T(8,128)}, u32[]{:S(2)}, u32[]{:S(2)}) %collective-permute-start.8) | collective-permute-done | bytes 1114144 | tf_op jit(solution)/shard_map/ppermute | solution.py:18
  123.2 6.4 %collective-permute-done.9 = f32[2,128,128]{2,1,0:T(8,128)S(1)} collective-permute-done((f32[2,128,128]{2,1,0:T(8,128)S(1)}, f32[2,128,128]{2,1,0:T(8,128)S(1)}, u32[]{:S(2)}, u32[]{:S(2)}) %collective-permute-start.9) | collective-permute-done | bytes 131104 | tf_op jit(solution)/shard_map/ppermute | solution.py:56
  131.6 5.8 %collective-permute-done.10 = f32[2,128,128]{2,1,0:T(8,128)S(1)} collective-permute-done((f32[2,128,128]{2,1,0:T(8,128)S(1)}, f32[2,128,128]{2,1,0:T(8,128)S(1)}, u32[]{:S(2)}, u32[]{:S(2)}) %collective-permute-start.10) | collective-permute-done | bytes 131104 | tf_op jit(solution)/shard_map/ppermute | solution.py:56
  140.1 4.8 %collective-permute-done.11 = f32[2,128,128]{2,1,0:T(8,128)S(1)} collective-permute-done((f32[2,128,128]{2,1,0:T(8,128)S(1)}, f32[2,128,128]{2,1,0:T(8,128)S(1)}, u32[]{:S(2)}, u32[]{:S(2)}) %collective-permute-start.11) | collective-permute-done | bytes 131104 | tf_op jit(solution)/shard_map/ppermute | solution.py:56
  148.5 3.9 %collective-permute-done.12 = f32[2,128,128]{2,1,0:T(8,128)S(1)} collective-permute-done((f32[2,128,128]{2,1,0:T(8,128)S(1)}, f32[2,128,128]{2,1,0:T(8,128)S(1)}, u32[]{:S(2)}, u32[]{:S(2)}) %collective-permute-start.12) | collective-permute-done | bytes 131104 | tf_op jit(solution)/shard_map/ppermute | solution.py:56
  154.5 14.7 %all-gather = f32[32,1,128]{2,1,0:T(1,128)S(1)} all-gather(f32[8,1,128]{2,1,0:T(1,128)S(1)} %fusion.24), channel_id=2, replica_groups=mesh['groups'=2,'ctx'=4,'head'=2,'dp'=2] {'ctx'}, dimensions={0}, use_global_device_ids=true | all-gather | bytes 20480 | tf_op jit(solution)/shard_map/all_gather | solution.py:97
  171.2 5.5 %collective-permute-done.14 = f32[2,128,128]{2,1,0:T(8,128)S(1)} collective-permute-done((f32[2,128,128]{2,1,0:T(8,128)S(1)}, f32[2,128,128]{2,1,0:T(8,128)S(1)}, u32[]{:S(2)}, u32[]{:S(2)}) %collective-permute-start.14) | collective-permute-done | bytes 131104 | tf_op jit(solution)/shard_map/ppermute | solution.py:56
  177.6 21.6 %shard_map.96 = (bf16[512,2048]{1,0:T(8,128)(2,1)}, f32[512,2048]{1,0:T(8,128)}, f32[512,2048]{1,0:T(8,128)}) custom-call(bf16[512,2048]{1,0:T(8,128)(2,1)} %q_ref.5, bf16[512,2048]{1,0:T(8,128)(2,1)} %k_ref.7, bf16[512,2048]{1,0:T(8,128)(2,1)} %v_ref.7, bf16[512,2048]{1,0:T(8,128)(2,1)} %get-tuple-element.156.og_ref, ...), custom_call_target="tpu_custom_call" | custom-call | flops 5637144576 | bytes 18874368 | tf_op jit(solution)/shard_map/pallas_call | solution.py:199
  201.0 14.1 %shard_map.97 = (bf16[512,2048]{1,0:T(8,128)(2,1)}, bf16[512,2048]{1,0:T(8,128)(2,1)}) custom-call(bf16[512,2048]{1,0:T(8,128)(2,1)} %k_ref.7, bf16[512,2048]{1,0:T(8,128)(2,1)} %v_ref.7, f32[512,2048]{1,0:T(8,128)} %get-tuple-element.158.kg_ref, f32[512,2048]{1,0:T(8,128)} %get-tuple-element.159.vg_ref, bf16[16,128,128]{2,1,0:T(8,128)(2,1)} %select_convert_fusion.gl_ref, ...), custom_call_target="tpu_custom_call" | custom-call | flops 536870912 | bytes 16777216 | tf_op jit(solution)/shard_map/pallas_call | solution.py:199
  (113 shorter events, 41.0 us)
Async XLA Ops:
  0.6 0.8 copy-start
  3.1 5.3 %copy-start.3 = (f32[16,4,128]{2,1,0:T(4,128)}, f32[16,4,128]{2,1,0:T(4,128)S(1)}, u32[]{:S(2)}) copy-start(f32[16,4,128]{2,1,0:T(4,128)S(1)} %copy.58) | copy-start | bytes 98308
  28.0 4.8 %copy-start.1 = (f32[16,128,128]{2,1,0:T(8,128)S(1)}, f32[16,128,128]{2,1,0:T(8,128)}, u32[]{:S(2)}) copy-start(f32[16,128,128]{2,1,0:T(8,128)} %shard_map.94) | copy-start | bytes 3145732
  29.4 2.9 %collective-permute-start = (f32[16,136,128]{2,1,0:T(8,128)S(1)}, f32[16,136,128]{2,1,0:T(8,128)S(1)}, u32[]{:S(2)}, u32[]{:S(2)}) collective-permute-start(f32[16,136,128]{2,1,0:T(8,128)S(1)} %fusion), channel_id=1, source_target_pairs={{0,1},{1,0},{2,3},{3,2},{4,5},{5,4},{6,7},{7,6},{8,9},{9,8},{10,11... | collective-permute-start | bytes 3342344 | tf_op jit(solution)/shard_map/ppermute | solution.py:18
  33.0 5.1 %copy-start.5 = (s32[4]{0:T(128)S(1)}, s32[4]{0:T(128)}, u32[]{:S(2)}) copy-start(s32[4]{0:T(128)} %constant.305.clone.1) | copy-start | bytes 52
  33.3 7.9 %collective-permute-start.1 = (f32[2,128,128]{2,1,0:T(8,128)S(1)}, f32[2,128,128]{2,1,0:T(8,128)S(1)}, u32[]{:S(2)}, u32[]{:S(2)}) collective-permute-start(f32[2,128,128]{2,1,0:T(8,128)S(1)} %bitcast_add_fusion.11), channel_id=1, source_target_pairs={{0,4},{4,8},{8,12},{1,5},{5,9},{9,13},{2,6},{6,10},{10,14},{3,7},{... | collective-permute-start | bytes 393224 | tf_op jit(solution)/shard_map/ppermute | solution.py:56
  41.9 6.9 %collective-permute-start.2 = (f32[2,128,128]{2,1,0:T(8,128)S(1)}, f32[2,128,128]{2,1,0:T(8,128)S(1)}, u32[]{:S(2)}, u32[]{:S(2)}) collective-permute-start(f32[2,128,128]{2,1,0:T(8,128)S(1)} %bitcast_add_fusion.10), channel_id=1, source_target_pairs={{0,4},{4,8},{8,12},{1,5},{5,9},{9,13},{2,6},{6,10},{10,14},{3,7},{... | collective-permute-start | bytes 393224 | tf_op jit(solution)/shard_map/ppermute | solution.py:56
  49.6 6.9 %collective-permute-start.3 = (f32[2,128,128]{2,1,0:T(8,128)S(1)}, f32[2,128,128]{2,1,0:T(8,128)S(1)}, u32[]{:S(2)}, u32[]{:S(2)}) collective-permute-start(f32[2,128,128]{2,1,0:T(8,128)S(1)} %bitcast_add_fusion.9), channel_id=1, source_target_pairs={{0,4},{4,8},{8,12},{1,5},{5,9},{9,13},{2,6},{6,10},{10,14},{3,7},{... | collective-permute-start | bytes 393224 | tf_op jit(solution)/shard_map/ppermute | solution.py:56
  57.2 6.9 %collective-permute-start.4 = (f32[2,128,128]{2,1,0:T(8,128)S(1)}, f32[2,128,128]{2,1,0:T(8,128)S(1)}, u32[]{:S(2)}, u32[]{:S(2)}) collective-permute-start(f32[2,128,128]{2,1,0:T(8,128)S(1)} %bitcast_add_fusion.8), channel_id=1, source_target_pairs={{0,4},{4,8},{8,12},{1,5},{5,9},{9,13},{2,6},{6,10},{10,14},{3,7},{... | collective-permute-start | bytes 393224 | tf_op jit(solution)/shard_map/ppermute | solution.py:56
  64.8 6.9 %collective-permute-start.5 = (f32[2,128,128]{2,1,0:T(8,128)S(1)}, f32[2,128,128]{2,1,0:T(8,128)S(1)}, u32[]{:S(2)}, u32[]{:S(2)}) collective-permute-start(f32[2,128,128]{2,1,0:T(8,128)S(1)} %bitcast_add_fusion.7), channel_id=1, source_target_pairs={{0,4},{4,8},{8,12},{1,5},{5,9},{9,13},{2,6},{6,10},{10,14},{3,7},{... | collective-permute-start | bytes 393224 | tf_op jit(solution)/shard_map/ppermute | solution.py:56
  72.4 6.9 %collective-permute-start.6 = (f32[2,128,128]{2,1,0:T(8,128)S(1)}, f32[2,128,128]{2,1,0:T(8,128)S(1)}, u32[]{:S(2)}, u32[]{:S(2)}) collective-permute-start(f32[2,128,128]{2,1,0:T(8,128)S(1)} %bitcast_add_fusion.6), channel_id=1, source_target_pairs={{0,4},{4,8},{8,12},{1,5},{5,9},{9,13},{2,6},{6,10},{10,14},{3,7},{... | collective-permute-start | bytes 393224 | tf_op jit(solution)/shard_map/ppermute | solution.py:56
  80.0 15.6 %collective-permute-start.7 = (f32[8,128,128]{2,1,0:T(8,128)S(1)}, f32[8,128,128]{2,1,0:T(8,128)S(1)}, u32[]{:S(2)}, u32[]{:S(2)}) collective-permute-start(f32[8,128,128]{2,1,0:T(8,128)S(1)} %bitcast.218), channel_id=1, source_target_pairs={{0,1},{1,0},{2,3},{3,2},{4,5},{5,4},{6,7},{7,6},{8,9},{9,8},{10,11... | collective-permute-start | bytes 1572872 | tf_op jit(solution)/shard_map/ppermute | solution.py:18
  113.6 5.9 %copy-start.2 = (f32[16,128,128]{2,1,0:T(8,128)S(1)}, f32[16,128,128]{2,1,0:T(8,128)}, u32[]{:S(2)}) copy-start(f32[16,128,128]{2,1,0:T(8,128)} %get-tuple-element.160) | copy-start | bytes 3145732
  115.1 3.1 %collective-permute-start.8 = (f32[16,136,128]{2,1,0:T(8,128)S(1)}, f32[16,136,128]{2,1,0:T(8,128)}, u32[]{:S(2)}, u32[]{:S(2)}) collective-permute-start(f32[16,136,128]{2,1,0:T(8,128)S(1)} %fusion.2), channel_id=1, source_target_pairs={{0,1},{1,0},{2,3},{3,2},{4,5},{5,4},{6,7},{7,6},{8,9},{9,8},{10,11... | collective-permute-start | bytes 3342344 | tf_op jit(solution)/shard_map/ppermute | solution.py:18
  121.1 8.4 %collective-permute-start.9 = (f32[2,128,128]{2,1,0:T(8,128)S(1)}, f32[2,128,128]{2,1,0:T(8,128)S(1)}, u32[]{:S(2)}, u32[]{:S(2)}) collective-permute-start(f32[2,128,128]{2,1,0:T(8,128)S(1)} %bitcast_add_fusion.5), channel_id=1, source_target_pairs={{4,0},{8,4},{12,8},{5,1},{9,5},{13,9},{6,2},{10,6},{14,10},{7,3},{... | collective-permute-start | bytes 393224 | tf_op jit(solution)/shard_map/ppermute | solution.py:56
  130.2 7.1 %collective-permute-start.10 = (f32[2,128,128]{2,1,0:T(8,128)S(1)}, f32[2,128,128]{2,1,0:T(8,128)S(1)}, u32[]{:S(2)}, u32[]{:S(2)}) collective-permute-start(f32[2,128,128]{2,1,0:T(8,128)S(1)} %bitcast_add_fusion.4), channel_id=1, source_target_pairs={{4,0},{8,4},{12,8},{5,1},{9,5},{13,9},{6,2},{10,6},{14,10},{7,3},{... | collective-permute-start | bytes 393224 | tf_op jit(solution)/shard_map/ppermute | solution.py:56
  138.1 16.5 %copy-start.4 = (f32[16,1,128]{2,1,0:T(1,128)S(1)}, f32[16,1,128]{2,1,0:T(1,128)}, u32[]{:S(2)}) copy-start(f32[16,1,128]{2,1,0:T(1,128)} %get-tuple-element.161) | copy-start | bytes 24580
  138.1 6.9 %collective-permute-start.11 = (f32[2,128,128]{2,1,0:T(8,128)S(1)}, f32[2,128,128]{2,1,0:T(8,128)S(1)}, u32[]{:S(2)}, u32[]{:S(2)}) collective-permute-start(f32[2,128,128]{2,1,0:T(8,128)S(1)} %bitcast_add_fusion.3), channel_id=1, source_target_pairs={{4,0},{8,4},{12,8},{5,1},{9,5},{13,9},{6,2},{10,6},{14,10},{7,3},{... | collective-permute-start | bytes 393224 | tf_op jit(solution)/shard_map/ppermute | solution.py:56
  145.6 6.9 %collective-permute-start.12 = (f32[2,128,128]{2,1,0:T(8,128)S(1)}, f32[2,128,128]{2,1,0:T(8,128)S(1)}, u32[]{:S(2)}, u32[]{:S(2)}) collective-permute-start(f32[2,128,128]{2,1,0:T(8,128)S(1)} %bitcast_add_fusion.2), channel_id=1, source_target_pairs={{4,0},{8,4},{12,8},{5,1},{9,5},{13,9},{6,2},{10,6},{14,10},{7,3},{... | collective-permute-start | bytes 393224 | tf_op jit(solution)/shard_map/ppermute | solution.py:56
  153.2 16.0 %collective-permute-start.13 = (f32[2,128,128]{2,1,0:T(8,128)S(1)}, f32[2,128,128]{2,1,0:T(8,128)S(1)}, u32[]{:S(2)}, u32[]{:S(2)}) collective-permute-start(f32[2,128,128]{2,1,0:T(8,128)S(1)} %bitcast_add_fusion.1), channel_id=1, source_target_pairs={{4,0},{8,4},{12,8},{5,1},{9,5},{13,9},{6,2},{10,6},{14,10},{7,3},{... | collective-permute-start | bytes 393224 | tf_op jit(solution)/shard_map/ppermute | solution.py:56
  169.9 6.9 %collective-permute-start.14 = (f32[2,128,128]{2,1,0:T(8,128)S(1)}, f32[2,128,128]{2,1,0:T(8,128)S(1)}, u32[]{:S(2)}, u32[]{:S(2)}) collective-permute-start(f32[2,128,128]{2,1,0:T(8,128)S(1)} %bitcast_add_fusion), channel_id=1, source_target_pairs={{4,0},{8,4},{12,8},{5,1},{9,5},{13,9},{6,2},{10,6},{14,10},{7,3},{... | collective-permute-start | bytes 393224 | tf_op jit(solution)/shard_map/ppermute | solution.py:56
  177.5 21.7 %collective-permute-start.15 = (f32[8,136,128]{2,1,0:T(8,128)S(1)}, f32[8,136,128]{2,1,0:T(8,128)S(1)}, u32[]{:S(2)}, u32[]{:S(2)}) collective-permute-start(f32[8,136,128]{2,1,0:T(8,128)S(1)} %maximum_maximum_fusion), channel_id=1, source_target_pairs={{0,1},{1,0},{2,3},{3,2},{4,5},{5,4},{6,7},{7,6},{8,9},{9,8},{10,11... | collective-permute-start | bytes 1671176 | tf_op jit(solution)/shard_map/ppermute | solution.py:18

commit v4 on v3

--- a/solution.py
+++ b/solution.py
@@ -94,11 +94,15 @@
     chip_gain = gain_rows + other[:, DH + 1, :]
     chip_state = first + jnp.exp(fin_first)[:, None, None] * second
     chip_decay = fin_first + fin_second
-    gain_half = jnp.sum(lax.all_gather(halves(chip_gain, c), "ctx"), axis=0)
+    chips = lax.axis_size("ctx")
+    gain_total = chip_gain
+    distance = 1
+    while distance < chips:
+        partners = [(i, i ^ distance) for i in range(chips)]
+        gain_total = gain_total + lax.ppermute(gain_total, "ctx", perm=partners)
+        distance *= 2
     suffix_half = chain_scan(halves(chip_state, c), halves(chip_decay, c), later=True)
-    back = swap_dp(pack_rows(suffix_half, gain_half))
-    suffix = join_halves(suffix_half, back[:, :DH, :], c)
-    gain_total = join_halves(gain_half, back[:, DH, :], c)
+    suffix = join_halves(suffix_half, swap_dp(suffix_half), c)
     core_zero = second + jnp.exp(fin_second)[:, None, None] * suffix
     return jnp.where(c == 0, core_zero, suffix), gain_total.reshape(heads * DH)
 
@@ -132,18 +136,30 @@
     return (_nt(q, k) * decay).astype(jnp.bfloat16)
 
 
-def local_state_kernel(k_ref, v_ref, toend_ref, s_ref):
-    scaled = (k_ref[...].astype(jnp.float32) * toend_ref[0]).astype(jnp.bfloat16)
+def _head_vectors(cum_ref, cumt_ref):
+    h = pl.program_id(0)
+    full = cum_ref[...]
+    lane = lax.broadcasted_iota(jnp.int32, full.shape, 1)
+    col = jnp.sum(jnp.where(lane == h, full, 0.0), axis=1, keepdims=True)
+    row = cumt_ref[pl.ds(h, 1), :]
+    fin = col[col.shape[0] - 1 :, :]
+    return col, row, jnp.exp(col), jnp.exp(fin - col)
+
+
+def local_state_kernel(k_ref, v_ref, cum_ref, cumt_ref, s_ref):
+    _, _, _, toend = _head_vectors(cum_ref, cumt_ref)
+    scaled = (k_ref[...].astype(jnp.float32) * toend).astype(jnp.bfloat16)
     s_ref[0] = _tn(scaled, v_ref[...])
 
 
-def intra_kernel(q_ref, k_ref, v_ref, col_ref, row_ref, out_ref):
-    decay = _decay(col_ref[0], row_ref[0])
+def intra_kernel(q_ref, k_ref, v_ref, cum_ref, cumt_ref, out_ref):
+    col, row, _, _ = _head_vectors(cum_ref, cumt_ref)
+    decay = _decay(col, row)
     out_ref[...] = _nn(_masked(q_ref[...], k_ref[...], decay), v_ref[...])
 
 
-def norm_kernel(q_ref, g_ref, intra_ref, st_ref, grow_ref, gain_ref, og_ref, m_ref, gp_ref):
-    grow = grow_ref[0]
+def norm_kernel(q_ref, g_ref, intra_ref, st_ref, cum_ref, cumt_ref, gain_ref, og_ref, m_ref, gp_ref):
+    _, _, grow, _ = _head_vectors(cum_ref, cumt_ref)
     q = q_ref[...]
     attended = intra_ref[...] + grow * _nn(q, st_ref[0])
     width = attended.shape[-1]
@@ -161,18 +177,19 @@
     m_ref[0] = _tn(q_scaled, out_grad)
 
 
-def grads_kernel(q_ref, k_ref, v_ref, og_ref, col_ref, row_ref, grow_ref, st_ref, qg_ref, kg_ref, vg_ref):
-    decay = _decay(col_ref[0], row_ref[0])
+def grads_kernel(q_ref, k_ref, v_ref, og_ref, cum_ref, cumt_ref, st_ref, qg_ref, kg_ref, vg_ref):
+    col, row, grow, _ = _head_vectors(cum_ref, cumt_ref)
+    decay = _decay(col, row)
     q, k, v, og = q_ref[...], k_ref[...], v_ref[...], og_ref[...]
     masked = _masked(q, k, decay)
     rgrad = (_nt(og, v) * decay).astype(jnp.bfloat16)
-    qg_ref[...] = (_nn(rgrad, k) + grow_ref[0] * _nt(og, st_ref[0])).astype(jnp.bfloat16)
+    qg_ref[...] = (_nn(rgrad, k) + grow * _nt(og, st_ref[0])).astype(jnp.bfloat16)
     kg_ref[...] = _tn(rgrad, q)
     vg_ref[...] = _tn(masked, og)
 
 
-def finish_kernel(k_ref, v_ref, kg_ref, vg_ref, gl_ref, toend_ref, ko_ref, vo_ref):
-    toend = toend_ref[0]
+def finish_kernel(k_ref, v_ref, kg_ref, vg_ref, gl_ref, cum_ref, cumt_ref, ko_ref, vo_ref):
+    _, _, _, toend = _head_vectors(cum_ref, cumt_ref)
     grad_low = gl_ref[0]
     ko_ref[...] = (kg_ref[...] + toend * _nt(v_ref[...], grad_low)).astype(jnp.bfloat16)
     vo_ref[...] = (vg_ref[...] + toend * _nn(k_ref[...], grad_low)).astype(jnp.bfloat16)
@@ -182,10 +199,10 @@
     def spec(kind):
         if kind == "rows":
             return pl.BlockSpec((length, DH), lambda h: (0, h))
-        if kind == "col":
-            return pl.BlockSpec((1, length, 1), lambda h: (h, 0, 0))
-        if kind == "row":
-            return pl.BlockSpec((1, 1, length), lambda h: (h, 0, 0))
+        if kind == "cum":
+            return pl.BlockSpec((length, heads), lambda h: (0, 0))
+        if kind == "cumt":
+            return pl.BlockSpec((heads, length), lambda h: (0, 0))
         if kind == "gain":
             return pl.BlockSpec((1, 1, DH), lambda h: (h, 0, 0))
         return pl.BlockSpec((1, DH, DH), lambda h: (h, 0, 0))
@@ -211,13 +228,13 @@
     heads = log_decay.shape[1]
     f32 = jnp.float32
     bf16 = jnp.bfloat16
-    cumulated = jnp.cumsum(log_decay, axis=0)
-    final_log = cumulated[-1]
-    by_head = cumulated.T
-    cum_col = by_head[:, :, None]
-    cum_row = by_head[:, None, :]
-    grow_col = jnp.exp(cum_col)
-    toend_col = jnp.exp(final_log[:, None, None] - cum_col)
+    t = lax.broadcasted_iota(jnp.int32, (length, length), 0)
+    s = lax.broadcasted_iota(jnp.int32, (length, length), 1)
+    lower = (t >= s).astype(f32)
+    exact = lax.Precision.HIGHEST
+    cum = jnp.dot(lower, log_decay, precision=exact)
+    cum_t = lax.dot_general(log_decay, lower, (((0,), (1,)), ((), ())), precision=exact)
+    final_log = cum[-1]
     gain_rows = norm_gain.reshape(heads, 1, DH)
     q, k, v, g = query_rows, key_rows, value_rows, cotangent
     big = length * length * DH * 2 * heads
@@ -225,29 +242,29 @@
     rows_bytes = length * heads * DH * 2
     (local_state,) = _per_head(
         local_state_kernel,
-        [("rows", k), ("rows", v), ("col", toend_col)],
+        [("rows", k), ("rows", v), ("cum", cum), ("cumt", cum_t)],
         [("square", f32)],
         heads, length, small, 2 * rows_bytes,
     )
     state_in = forward_states(local_state, final_log)
     (intra,) = _per_head(
         intra_kernel,
-        [("rows", q), ("rows", k), ("rows", v), ("col", cum_col), ("row", cum_row)],
+        [("rows", q), ("rows", k), ("rows", v), ("cum", cum), ("cumt", cum_t)],
         [("rows", f32)],
         heads, length, 2 * big, 5 * rows_bytes, heads * length * length,
     )
     state_low = state_in.astype(bf16)
     out_grad, moment, gain_part = _per_head(
         norm_kernel,
-        [("rows", q), ("rows", g), ("rows", intra), ("square", state_low), ("col", grow_col), ("gain", gain_rows)],
+        [("rows", q), ("rows", g), ("rows", intra), ("square", state_low), ("cum", cum), ("cumt", cum_t), ("gain", gain_rows)],
         [("rows", bf16), ("square", f32), ("gain", f32)],
         heads, length, 2 * small, 5 * rows_bytes,
     )
     grad_state, gain_sum = backward_states(moment, final_log, gain_part.reshape(heads * DH))
     query_grad, key_part, value_part = _per_head(
         grads_kernel,
-        [("rows", q), ("rows", k), ("rows", v), ("rows", out_grad), ("col", cum_col), ("row", cum_row),
-         ("col", grow_col), ("square", state_low)],
+        [("rows", q), ("rows", k), ("rows", v), ("rows", out_grad), ("cum", cum), ("cumt", cum_t),
+         ("square", state_low)],
         [("rows", bf16), ("rows", f32), ("rows", f32)],
         heads, length, 5 * big + small, 9 * rows_bytes, heads * length * length,
     )
@@ -255,7 +272,7 @@
     key_grad, value_grad = _per_head(
         finish_kernel,
         [("rows", k), ("rows", v), ("rows", key_part), ("rows", value_part), ("square", grad_low),
-         ("col", toend_col)],
+         ("cum", cum), ("cumt", cum_t)],
         [("rows", bf16), ("rows", bf16)],
         heads, length, 2 * small, 8 * rows_bytes,
     )

time: 218 us -> 195 us (0.89)
  blocking collectives: 14.7 us -> 0 us
  other arithmetic: 29.9 us -> 23.2 us
  local copies, waits for them, and re-layouts: 8.21 us -> 2.81 us
  starting transfers between devices: 35.6 us -> 40.9 us
  Pallas kernels: 81 us -> 76.6 us
  waiting for transfers between devices: 44.4 us -> 47.3 us
    all_gather x1 -> x0, blocking collectives: 14.7 us -> none  [backward_states(): gain_half = jnp.sum(lax.all_gather(halves(chip_gain, c), 'ctx'), axis=0)]
    exp x1 -> x0, other arithmetic: 6.49 us -> none  [on_device(): grow_col = jnp.exp(cum_col)]
    another operation x7 -> x2, local copies, waits for them, and re-layouts: 5.55 us -> 0.07 us
    ppermute x0 -> x2, starting transfers between devices: none -> 5.23 us  [backward_states(): gain_total = gain_total + lax.ppermute(gain_total, 'ctx', perm=partners)]
    pallas_call x5, Pallas kernels: 81 us -> 76.6 us  [_per_head(): pl.pallas_call(kernel, grid=(heads,), in_specs=[spec(kind) for kind, _ in...]
    another operation x10 -> x6, other arithmetic: 5.74 us -> 4.4 us
  transfers between devices with their start and end apart: 16 -> 18, of which waited for: 13 -> 14; matrix products, arithmetic and copies ran while one was open for 3% -> 4% of each run, Pallas kernels for 17% -> 18%
where the time goes in v4:
time: 195 us; the launch traced here: 192 us
  Pallas kernels  76.6 us (39%)
  waiting for transfers between devices  47.3 us (24%)
  starting transfers between devices  40.9 us (21%)
  other arithmetic  23.2 us (12%)
  local copies, waits for them, and re-layouts  2.81 us (1%)
    pallas_call x5, Pallas kernels, _per_head(): pl.pallas_call(kernel, grid=(heads,), in_specs=[spec(kind) for kind, _ in...  76.6 us
    ppermute x12, waiting for transfers between devices, chain_scan(): arrived = lax.ppermute(outgoing, 'ctx', perm=perm)  40.4 us
    ppermute x12, starting transfers between devices, chain_scan(): arrived = lax.ppermute(outgoing, 'ctx', perm=perm)  34.4 us
    scatter x12, other arithmetic, chain_scan(): prefix = prefix.at[slot].set(jnp.where(valid, arrived, prefix[slot]))  7.88 us
    ppermute x2, starting transfers between devices, backward_states(): gain_total = gain_total + lax.ppermute(gain_total, 'ctx', perm=partners)  5.23 us
    ppermute x4, waiting for transfers between devices, swap_dp(): return lax.ppermute(x, 'dp', perm=[(0, 1), (1, 0)])  4.9 us
    another operation x6, other arithmetic  4.4 us
  transfers between devices with their start and end apart: 18, of which 14 were waited for; matrix products, arithmetic and copies ran while one was open for 4% of the time, Pallas kernels for 18%

profile of v4, /device:TPU:0, one launch (start us, length us, event | category | flops | bytes accessed | tf_op | source)
XLA Modules:
  0.0 192.4 jit_solution(11308273164356131536)
XLA Ops:
  3.0 12.6 %shard_map.94 = f32[16,128,128]{2,1,0:T(8,128)} custom-call(bf16[512,2048]{1,0:T(8,128)(2,1)} %k_ref.7, bf16[512,2048]{1,0:T(8,128)(2,1)} %v_ref.7, f32[512,16]{1,0:T(8,128)} %copy.19.cum_ref, f32[16,512]{1,0:T(8,128)} %bitcast.216), custom_call_target="tpu_custom_call" | custom-call | flops 268435456 | bytes 4194304 | tf_op jit(solution)/shard_map/pallas_call | solution.py:216
  17.6 2.4 %collective-permute-done = f32[16,136,128]{2,1,0:T(8,128)S(1)} collective-permute-done((f32[16,136,128]{2,1,0:T(8,128)S(1)}, f32[16,136,128]{2,1,0:T(8,128)S(1)}, u32[]{:S(2)}, u32[]{:S(2)}) %collective-permute-start) | collective-permute-done | bytes 1114144 | tf_op jit(solution)/shard_map/ppermute | solution.py:18
  20.9 4.9 %collective-permute-start.1 = (f32[2,128,128]{2,1,0:T(8,128)S(1)}, f32[2,128,128]{2,1,0:T(8,128)S(1)}, u32[]{:S(2)}, u32[]{:S(2)}) collective-permute-start(f32[2,128,128]{2,1,0:T(8,128)S(1)} %bitcast_add_fusion.11), channel_id=1, source_target_pairs={{0,4},{4,8},{8,12},{1,5},{5,9},{9,13},{2,6},{6,10},{10,14},{3,7},{... | collective-permute-start | bytes 393224 | tf_op jit(solution)/shard_map/ppermute | solution.py:56
  26.5 2.3 %collective-permute-done.1 = f32[2,128,128]{2,1,0:T(8,128)S(1)} collective-permute-done((f32[2,128,128]{2,1,0:T(8,128)S(1)}, f32[2,128,128]{2,1,0:T(8,128)S(1)}, u32[]{:S(2)}, u32[]{:S(2)}) %collective-permute-start.1) | collective-permute-done | bytes 131104 | tf_op jit(solution)/shard_map/ppermute | solution.py:56
  29.6 4.4 %collective-permute-start.2 = (f32[2,128,128]{2,1,0:T(8,128)S(1)}, f32[2,128,128]{2,1,0:T(8,128)S(1)}, u32[]{:S(2)}, u32[]{:S(2)}) collective-permute-start(f32[2,128,128]{2,1,0:T(8,128)S(1)} %bitcast_add_fusion.10), channel_id=1, source_target_pairs={{0,4},{4,8},{8,12},{1,5},{5,9},{9,13},{2,6},{6,10},{10,14},{3,7},{... | collective-permute-start | bytes 393224 | tf_op jit(solution)/shard_map/ppermute | solution.py:56
  34.0 2.5 %collective-permute-done.2 = f32[2,128,128]{2,1,0:T(8,128)S(1)} collective-permute-done((f32[2,128,128]{2,1,0:T(8,128)S(1)}, f32[2,128,128]{2,1,0:T(8,128)S(1)}, u32[]{:S(2)}, u32[]{:S(2)}) %collective-permute-start.2) | collective-permute-done | bytes 131104 | tf_op jit(solution)/shard_map/ppermute | solution.py:56
  37.2 4.4 %collective-permute-start.3 = (f32[2,128,128]{2,1,0:T(8,128)S(1)}, f32[2,128,128]{2,1,0:T(8,128)S(1)}, u32[]{:S(2)}, u32[]{:S(2)}) collective-permute-start(f32[2,128,128]{2,1,0:T(8,128)S(1)} %bitcast_add_fusion.9), channel_id=1, source_target_pairs={{0,4},{4,8},{8,12},{1,5},{5,9},{9,13},{2,6},{6,10},{10,14},{3,7},{... | collective-permute-start | bytes 393224 | tf_op jit(solution)/shard_map/ppermute | solution.py:56
  44.9 4.4 %collective-permute-start.4 = (f32[2,128,128]{2,1,0:T(8,128)S(1)}, f32[2,128,128]{2,1,0:T(8,128)S(1)}, u32[]{:S(2)}, u32[]{:S(2)}) collective-permute-start(f32[2,128,128]{2,1,0:T(8,128)S(1)} %bitcast_add_fusion.8), channel_id=1, source_target_pairs={{0,4},{4,8},{8,12},{1,5},{5,9},{9,13},{2,6},{6,10},{10,14},{3,7},{... | collective-permute-start | bytes 393224 | tf_op jit(solution)/shard_map/ppermute | solution.py:56
  49.3 2.5 %collective-permute-done.4 = f32[2,128,128]{2,1,0:T(8,128)S(1)} collective-permute-done((f32[2,128,128]{2,1,0:T(8,128)S(1)}, f32[2,128,128]{2,1,0:T(8,128)S(1)}, u32[]{:S(2)}, u32[]{:S(2)}) %collective-permute-start.4) | collective-permute-done | bytes 131104 | tf_op jit(solution)/shard_map/ppermute | solution.py:56
  52.5 4.4 %collective-permute-start.5 = (f32[2,128,128]{2,1,0:T(8,128)S(1)}, f32[2,128,128]{2,1,0:T(8,128)S(1)}, u32[]{:S(2)}, u32[]{:S(2)}) collective-permute-start(f32[2,128,128]{2,1,0:T(8,128)S(1)} %bitcast_add_fusion.7), channel_id=1, source_target_pairs={{0,4},{4,8},{8,12},{1,5},{5,9},{9,13},{2,6},{6,10},{10,14},{3,7},{... | collective-permute-start | bytes 393224 | tf_op jit(solution)/shard_map/ppermute | solution.py:56
  60.1 4.4 %collective-permute-start.6 = (f32[2,128,128]{2,1,0:T(8,128)S(1)}, f32[2,128,128]{2,1,0:T(8,128)S(1)}, u32[]{:S(2)}, u32[]{:S(2)}) collective-permute-start(f32[2,128,128]{2,1,0:T(8,128)S(1)} %bitcast_add_fusion.6), channel_id=1, source_target_pairs={{0,4},{4,8},{8,12},{1,5},{5,9},{9,13},{2,6},{6,10},{10,14},{3,7},{... | collective-permute-start | bytes 393224 | tf_op jit(solution)/shard_map/ppermute | solution.py:56
  64.5 2.5 %collective-permute-done.6 = f32[2,128,128]{2,1,0:T(8,128)S(1)} collective-permute-done((f32[2,128,128]{2,1,0:T(8,128)S(1)}, f32[2,128,128]{2,1,0:T(8,128)S(1)}, u32[]{:S(2)}, u32[]{:S(2)}) %collective-permute-start.6) | collective-permute-done | bytes 131104 | tf_op jit(solution)/shard_map/ppermute | solution.py:56
  67.8 15.1 %shard_map.93.intra_ref = f32[512,2048]{1,0:T(8,128)} custom-call(bf16[512,2048]{1,0:T(8,128)(2,1)} %q_ref.5, bf16[512,2048]{1,0:T(8,128)(2,1)} %k_ref.7, bf16[512,2048]{1,0:T(8,128)(2,1)} %v_ref.7, f32[512,16]{1,0:T(8,128)} %copy.19.cum_ref, f32[16,512]{1,0:T(8,128)} %bitcast.217), custom_call_target="tpu_custom_call" | custom-call | flops 2147483648 | bytes 10485760 | tf_op jit(solution)/shard_map/pallas_call | solution.py:216
  84.0 15.3 %shard_map.95 = (bf16[512,2048]{1,0:T(8,128)(2,1)}, f32[16,128,128]{2,1,0:T(8,128)}, f32[16,1,128]{2,1,0:T(1,128)}) custom-call(bf16[512,2048]{1,0:T(8,128)(2,1)} %q_ref.5, bf16[512,2048]{1,0:T(8,128)(2,1)} %g_ref.1, f32[512,2048]{1,0:T(8,128)} %shard_map.93.intra_ref, bf16[16,128,128]{2,1,0:T(8,128)(2,1)} %select_convert_fusion.1.st_ref, ...), custom_call_target="tpu_custom_call" | custom-call | flops 536870912 | bytes 10485760 | tf_op jit(solution)/shard_map/pallas_call | solution.py:216
  101.3 2.5 %collective-permute-done.8 = f32[16,136,128]{2,1,0:T(8,128)} collective-permute-done((f32[16,136,128]{2,1,0:T(8,128)S(1)}, f32[16,136,128]{2,1,0:T(8,128)}, u32[]{:S(2)}, u32[]{:S(2)}) %collective-permute-start.8) | collective-permute-done | bytes 1114144 | tf_op jit(solution)/shard_map/ppermute | solution.py:18
  108.9 6.3 %collective-permute-done.9 = f32[2,128,128]{2,1,0:T(8,128)S(1)} collective-permute-done((f32[2,128,128]{2,1,0:T(8,128)S(1)}, f32[2,128,128]{2,1,0:T(8,128)S(1)}, u32[]{:S(2)}, u32[]{:S(2)}) %collective-permute-start.9) | collective-permute-done | bytes 131104 | tf_op jit(solution)/shard_map/ppermute | solution.py:56
  117.3 5.8 %collective-permute-done.10 = f32[2,128,128]{2,1,0:T(8,128)S(1)} collective-permute-done((f32[2,128,128]{2,1,0:T(8,128)S(1)}, f32[2,128,128]{2,1,0:T(8,128)S(1)}, u32[]{:S(2)}, u32[]{:S(2)}) %collective-permute-start.10) | collective-permute-done | bytes 131104 | tf_op jit(solution)/shard_map/ppermute | solution.py:56
  125.9 4.8 %collective-permute-done.11 = f32[2,128,128]{2,1,0:T(8,128)S(1)} collective-permute-done((f32[2,128,128]{2,1,0:T(8,128)S(1)}, f32[2,128,128]{2,1,0:T(8,128)S(1)}, u32[]{:S(2)}, u32[]{:S(2)}) %collective-permute-start.11) | collective-permute-done | bytes 131104 | tf_op jit(solution)/shard_map/ppermute | solution.py:56
  132.8 5.5 %collective-permute-done.12 = f32[2,128,128]{2,1,0:T(8,128)S(1)} collective-permute-done((f32[2,128,128]{2,1,0:T(8,128)S(1)}, f32[2,128,128]{2,1,0:T(8,128)S(1)}, u32[]{:S(2)}, u32[]{:S(2)}) %collective-permute-start.12) | collective-permute-done | bytes 131104 | tf_op jit(solution)/shard_map/ppermute | solution.py:56
  141.1 4.8 %collective-permute-done.13 = f32[2,128,128]{2,1,0:T(8,128)S(1)} collective-permute-done((f32[2,128,128]{2,1,0:T(8,128)S(1)}, f32[2,128,128]{2,1,0:T(8,128)S(1)}, u32[]{:S(2)}, u32[]{:S(2)}) %collective-permute-start.13) | collective-permute-done | bytes 131104 | tf_op jit(solution)/shard_map/ppermute | solution.py:56
  148.8 2.7 %collective-permute-start.16 = (f32[16,128]{1,0:T(8,128)S(1)}, f32[16,128]{1,0:T(8,128)S(1)}, u32[]{:S(2)}, u32[]{:S(2)}) collective-permute-start(f32[16,128]{1,0:T(8,128)S(1)} %bitcast.223), channel_id=1, source_target_pairs={{0,4},{4,0},{8,12},{12,8},{1,5},{5,1},{9,13},{13,9},{2,6},{6,2},{1... | collective-permute-start | bytes 24584 | tf_op jit(solution)/shard_map/ppermute | solution.py:102
  153.6 2.5 %collective-permute-start.17 = (f32[16,128]{1,0:T(8,128)S(1)}, f32[16,128]{1,0:T(8,128)S(1)}, u32[]{:S(2)}, u32[]{:S(2)}) collective-permute-start(f32[16,128]{1,0:T(8,128)S(1)} %add.229), channel_id=1, source_target_pairs={{0,8},{4,12},{8,0},{12,4},{1,9},{5,13},{9,1},{13,5},{2,10},{6,14},... | collective-permute-start | bytes 24584 | tf_op jit(solution)/shard_map/ppermute | solution.py:102
  156.9 20.2 %shard_map.96 = (bf16[512,2048]{1,0:T(8,128)(2,1)}, f32[512,2048]{1,0:T(8,128)}, f32[512,2048]{1,0:T(8,128)}) custom-call(bf16[512,2048]{1,0:T(8,128)(2,1)} %q_ref.5, bf16[512,2048]{1,0:T(8,128)(2,1)} %k_ref.7, bf16[512,2048]{1,0:T(8,128)(2,1)} %v_ref.7, bf16[512,2048]{1,0:T(8,128)(2,1)} %get-tuple-element.156.og_ref, f32[512,16]{1,0:T(8,128)} %copy.19.cum_ref, ...), custom_call_target="tpu_custom_call" | custom-call | flops 5637144576 | bytes 18874368 | tf_op jit(solution)/shard_map/pallas_call | solution.py:216
  178.9 13.5 %shard_map.97 = (bf16[512,2048]{1,0:T(8,128)(2,1)}, bf16[512,2048]{1,0:T(8,128)(2,1)}) custom-call(bf16[512,2048]{1,0:T(8,128)(2,1)} %k_ref.7, bf16[512,2048]{1,0:T(8,128)(2,1)} %v_ref.7, f32[512,2048]{1,0:T(8,128)} %get-tuple-element.158.kg_ref, f32[512,2048]{1,0:T(8,128)} %get-tuple-element.159.vg_ref, bf16[16,128,128]{2,1,0:T(8,128)(2,1)} %select_convert_fusion.gl_ref, ...), custom_call_target="tpu_custom_call" | custom-call | flops 536870912 | bytes 16777216 | tf_op jit(solution)/shard_map/pallas_call | solution.py:216
  (104 shorter events, 41.0 us)
Async XLA Ops:
  0.6 0.8 copy-start
  1.8 1.2 copy-start.3
  15.6 4.8 %copy-start.1 = (f32[16,128,128]{2,1,0:T(8,128)S(1)}, f32[16,128,128]{2,1,0:T(8,128)}, u32[]{:S(2)}) copy-start(f32[16,128,128]{2,1,0:T(8,128)} %shard_map.94) | copy-start | bytes 3145732
  17.1 2.9 %collective-permute-start = (f32[16,136,128]{2,1,0:T(8,128)S(1)}, f32[16,136,128]{2,1,0:T(8,128)S(1)}, u32[]{:S(2)}, u32[]{:S(2)}) collective-permute-start(f32[16,136,128]{2,1,0:T(8,128)S(1)} %fusion), channel_id=1, source_target_pairs={{0,1},{1,0},{2,3},{3,2},{4,5},{5,4},{6,7},{7,6},{8,9},{9,8},{10,11... | collective-permute-start | bytes 3342344 | tf_op jit(solution)/shard_map/ppermute | solution.py:18
  20.7 5.1 %copy-start.5 = (s32[4]{0:T(128)S(1)}, s32[4]{0:T(128)}, u32[]{:S(2)}) copy-start(s32[4]{0:T(128)} %constant.299.clone.1) | copy-start | bytes 52
  20.9 7.9 %collective-permute-start.1 = (f32[2,128,128]{2,1,0:T(8,128)S(1)}, f32[2,128,128]{2,1,0:T(8,128)S(1)}, u32[]{:S(2)}, u32[]{:S(2)}) collective-permute-start(f32[2,128,128]{2,1,0:T(8,128)S(1)} %bitcast_add_fusion.11), channel_id=1, source_target_pairs={{0,4},{4,8},{8,12},{1,5},{5,9},{9,13},{2,6},{6,10},{10,14},{3,7},{... | collective-permute-start | bytes 393224 | tf_op jit(solution)/shard_map/ppermute | solution.py:56
  29.6 6.9 %collective-permute-start.2 = (f32[2,128,128]{2,1,0:T(8,128)S(1)}, f32[2,128,128]{2,1,0:T(8,128)S(1)}, u32[]{:S(2)}, u32[]{:S(2)}) collective-permute-start(f32[2,128,128]{2,1,0:T(8,128)S(1)} %bitcast_add_fusion.10), channel_id=1, source_target_pairs={{0,4},{4,8},{8,12},{1,5},{5,9},{9,13},{2,6},{6,10},{10,14},{3,7},{... | collective-permute-start | bytes 393224 | tf_op jit(solution)/shard_map/ppermute | solution.py:56
  37.2 6.9 %collective-permute-start.3 = (f32[2,128,128]{2,1,0:T(8,128)S(1)}, f32[2,128,128]{2,1,0:T(8,128)S(1)}, u32[]{:S(2)}, u32[]{:S(2)}) collective-permute-start(f32[2,128,128]{2,1,0:T(8,128)S(1)} %bitcast_add_fusion.9), channel_id=1, source_target_pairs={{0,4},{4,8},{8,12},{1,5},{5,9},{9,13},{2,6},{6,10},{10,14},{3,7},{... | collective-permute-start | bytes 393224 | tf_op jit(solution)/shard_map/ppermute | solution.py:56
  44.9 6.9 %collective-permute-start.4 = (f32[2,128,128]{2,1,0:T(8,128)S(1)}, f32[2,128,128]{2,1,0:T(8,128)S(1)}, u32[]{:S(2)}, u32[]{:S(2)}) collective-permute-start(f32[2,128,128]{2,1,0:T(8,128)S(1)} %bitcast_add_fusion.8), channel_id=1, source_target_pairs={{0,4},{4,8},{8,12},{1,5},{5,9},{9,13},{2,6},{6,10},{10,14},{3,7},{... | collective-permute-start | bytes 393224 | tf_op jit(solution)/shard_map/ppermute | solution.py:56
  52.5 6.9 %collective-permute-start.5 = (f32[2,128,128]{2,1,0:T(8,128)S(1)}, f32[2,128,128]{2,1,0:T(8,128)S(1)}, u32[]{:S(2)}, u32[]{:S(2)}) collective-permute-start(f32[2,128,128]{2,1,0:T(8,128)S(1)} %bitcast_add_fusion.7), channel_id=1, source_target_pairs={{0,4},{4,8},{8,12},{1,5},{5,9},{9,13},{2,6},{6,10},{10,14},{3,7},{... | collective-permute-start | bytes 393224 | tf_op jit(solution)/shard_map/ppermute | solution.py:56
  60.1 6.9 %collective-permute-start.6 = (f32[2,128,128]{2,1,0:T(8,128)S(1)}, f32[2,128,128]{2,1,0:T(8,128)S(1)}, u32[]{:S(2)}, u32[]{:S(2)}) collective-permute-start(f32[2,128,128]{2,1,0:T(8,128)S(1)} %bitcast_add_fusion.6), channel_id=1, source_target_pairs={{0,4},{4,8},{8,12},{1,5},{5,9},{9,13},{2,6},{6,10},{10,14},{3,7},{... | collective-permute-start | bytes 393224 | tf_op jit(solution)/shard_map/ppermute | solution.py:56
  67.6 15.3 %collective-permute-start.7 = (f32[8,128,128]{2,1,0:T(8,128)S(1)}, f32[8,128,128]{2,1,0:T(8,128)S(1)}, u32[]{:S(2)}, u32[]{:S(2)}) collective-permute-start(f32[8,128,128]{2,1,0:T(8,128)S(1)} %bitcast.203), channel_id=1, source_target_pairs={{0,1},{1,0},{2,3},{3,2},{4,5},{5,4},{6,7},{7,6},{8,9},{9,8},{10,11... | collective-permute-start | bytes 1572872 | tf_op jit(solution)/shard_map/ppermute | solution.py:18
  99.3 5.9 %copy-start.2 = (f32[16,128,128]{2,1,0:T(8,128)S(1)}, f32[16,128,128]{2,1,0:T(8,128)}, u32[]{:S(2)}) copy-start(f32[16,128,128]{2,1,0:T(8,128)} %get-tuple-element.160) | copy-start | bytes 3145732
  100.8 3.1 %collective-permute-start.8 = (f32[16,136,128]{2,1,0:T(8,128)S(1)}, f32[16,136,128]{2,1,0:T(8,128)}, u32[]{:S(2)}, u32[]{:S(2)}) collective-permute-start(f32[16,136,128]{2,1,0:T(8,128)S(1)} %fusion.2), channel_id=1, source_target_pairs={{0,1},{1,0},{2,3},{3,2},{4,5},{5,4},{6,7},{7,6},{8,9},{9,8},{10,11... | collective-permute-start | bytes 3342344 | tf_op jit(solution)/shard_map/ppermute | solution.py:18
  106.8 8.4 %collective-permute-start.9 = (f32[2,128,128]{2,1,0:T(8,128)S(1)}, f32[2,128,128]{2,1,0:T(8,128)S(1)}, u32[]{:S(2)}, u32[]{:S(2)}) collective-permute-start(f32[2,128,128]{2,1,0:T(8,128)S(1)} %bitcast_add_fusion.5), channel_id=1, source_target_pairs={{4,0},{8,4},{12,8},{5,1},{9,5},{13,9},{6,2},{10,6},{14,10},{7,3},{... | collective-permute-start | bytes 393224 | tf_op jit(solution)/shard_map/ppermute | solution.py:56
  116.0 7.1 %collective-permute-start.10 = (f32[2,128,128]{2,1,0:T(8,128)S(1)}, f32[2,128,128]{2,1,0:T(8,128)S(1)}, u32[]{:S(2)}, u32[]{:S(2)}) collective-permute-start(f32[2,128,128]{2,1,0:T(8,128)S(1)} %bitcast_add_fusion.4), channel_id=1, source_target_pairs={{4,0},{8,4},{12,8},{5,1},{9,5},{13,9},{6,2},{10,6},{14,10},{7,3},{... | collective-permute-start | bytes 393224 | tf_op jit(solution)/shard_map/ppermute | solution.py:56
  123.8 6.9 %collective-permute-start.11 = (f32[2,128,128]{2,1,0:T(8,128)S(1)}, f32[2,128,128]{2,1,0:T(8,128)S(1)}, u32[]{:S(2)}, u32[]{:S(2)}) collective-permute-start(f32[2,128,128]{2,1,0:T(8,128)S(1)} %bitcast_add_fusion.3), channel_id=1, source_target_pairs={{4,0},{8,4},{12,8},{5,1},{9,5},{13,9},{6,2},{10,6},{14,10},{7,3},{... | collective-permute-start | bytes 393224 | tf_op jit(solution)/shard_map/ppermute | solution.py:56
  131.4 16.6 %copy-start.4 = (f32[16,1,128]{2,1,0:T(1,128)S(1)}, f32[16,1,128]{2,1,0:T(1,128)}, u32[]{:S(2)}) copy-start(f32[16,1,128]{2,1,0:T(1,128)} %get-tuple-element.161) | copy-start | bytes 24580
  131.4 6.9 %collective-permute-start.12 = (f32[2,128,128]{2,1,0:T(8,128)S(1)}, f32[2,128,128]{2,1,0:T(8,128)S(1)}, u32[]{:S(2)}, u32[]{:S(2)}) collective-permute-start(f32[2,128,128]{2,1,0:T(8,128)S(1)} %bitcast_add_fusion.2), channel_id=1, source_target_pairs={{4,0},{8,4},{12,8},{5,1},{9,5},{13,9},{6,2},{10,6},{14,10},{7,3},{... | collective-permute-start | bytes 393224 | tf_op jit(solution)/shard_map/ppermute | solution.py:56
  139.0 6.9 %collective-permute-start.13 = (f32[2,128,128]{2,1,0:T(8,128)S(1)}, f32[2,128,128]{2,1,0:T(8,128)S(1)}, u32[]{:S(2)}, u32[]{:S(2)}) collective-permute-start(f32[2,128,128]{2,1,0:T(8,128)S(1)} %bitcast_add_fusion.1), channel_id=1, source_target_pairs={{4,0},{8,4},{12,8},{5,1},{9,5},{13,9},{6,2},{10,6},{14,10},{7,3},{... | collective-permute-start | bytes 393224 | tf_op jit(solution)/shard_map/ppermute | solution.py:56
  146.7 9.5 %collective-permute-start.14 = (f32[2,128,128]{2,1,0:T(8,128)S(1)}, f32[2,128,128]{2,1,0:T(8,128)S(1)}, u32[]{:S(2)}, u32[]{:S(2)}) collective-permute-start(f32[2,128,128]{2,1,0:T(8,128)S(1)} %bitcast_add_fusion), channel_id=1, source_target_pairs={{4,0},{8,4},{12,8},{5,1},{9,5},{13,9},{6,2},{10,6},{14,10},{7,3},{... | collective-permute-start | bytes 393224 | tf_op jit(solution)/shard_map/ppermute | solution.py:56
  148.8 4.8 %collective-permute-start.16 = (f32[16,128]{1,0:T(8,128)S(1)}, f32[16,128]{1,0:T(8,128)S(1)}, u32[]{:S(2)}, u32[]{:S(2)}) collective-permute-start(f32[16,128]{1,0:T(8,128)S(1)} %bitcast.223), channel_id=1, source_target_pairs={{0,4},{4,0},{8,12},{12,8},{1,5},{5,1},{9,13},{13,9},{2,6},{6,2},{1... | collective-permute-start | bytes 24584 | tf_op jit(solution)/shard_map/ppermute | solution.py:102
  153.6 23.5 %collective-permute-start.17 = (f32[16,128]{1,0:T(8,128)S(1)}, f32[16,128]{1,0:T(8,128)S(1)}, u32[]{:S(2)}, u32[]{:S(2)}) collective-permute-start(f32[16,128]{1,0:T(8,128)S(1)} %add.229), channel_id=1, source_target_pairs={{0,8},{4,12},{8,0},{12,4},{1,9},{5,13},{9,1},{13,5},{2,10},{6,14},... | collective-permute-start | bytes 24584 | tf_op jit(solution)/shard_map/ppermute | solution.py:102
  156.8 20.9 %collective-permute-start.15 = (f32[8,128,128]{2,1,0:T(8,128)S(1)}, f32[8,128,128]{2,1,0:T(8,128)S(1)}, u32[]{:S(2)}, u32[]{:S(2)}) collective-permute-start(f32[8,128,128]{2,1,0:T(8,128)S(1)} %bitcast.202), channel_id=1, source_target_pairs={{0,1},{1,0},{2,3},{3,2},{4,5},{5,4},{6,7},{7,6},{8,9},{9,8},{10,11... | collective-permute-start | bytes 1572872 | tf_op jit(solution)/shard_map/ppermute | solution.py:18

commit v5 on v4

--- a/solution.py
+++ b/solution.py
@@ -9,6 +9,7 @@
 DH = 128
 PAD = 8
 CHUNKS = 4
+TIE_STEP = 1
 
 
 epsilon = 1e-06
@@ -36,7 +37,7 @@
     return jnp.concatenate([first, second], axis=0)
 
 
-def chain_scan(chip_state, chip_decay, later):
+def chain_scan(chip_state, chip_decay, later, cover):
     chips = lax.axis_size("ctx")
     z = lax.axis_index("ctx")
     heads = chip_state.shape[0]
@@ -58,10 +59,12 @@
         valid = (where_to >= 0) & (where_to < count) & (rank >= 1)
         slot = jnp.clip(where_to, 0, count - 1)
         prefix = prefix.at[slot].set(jnp.where(valid, arrived, prefix[slot]))
-    return prefix.reshape(heads, DH, DH)
-
-
-def forward_states(local_state, final_log):
+        if step == TIE_STEP:
+            cover, prefix = lax.optimization_barrier((cover, prefix))
+    return prefix.reshape(heads, DH, DH), cover
+
+
+def forward_states(local_state, final_log, cover):
     c = lax.axis_index("dp")
     message = pack_rows(local_state, final_log)
     other = swap_dp(message)
@@ -73,13 +76,13 @@
     fin_second = jnp.where(c == 0, other_fin, own_fin)
     chip_state = jnp.exp(fin_second)[:, None, None] * first + second
     chip_decay = fin_first + fin_second
-    prefix_half = chain_scan(halves(chip_state, c), halves(chip_decay, c), later=False)
+    prefix_half, cover = chain_scan(halves(chip_state, c), halves(chip_decay, c), False, cover)
     prefix = join_halves(prefix_half, swap_dp(prefix_half), c)
     core_one = jnp.exp(fin_first)[:, None, None] * prefix + first
-    return jnp.where(c == 0, prefix, core_one)
-
-
-def backward_states(moment, final_log, gain_part):
+    return jnp.where(c == 0, prefix, core_one), cover
+
+
+def backward_states(moment, final_log, gain_part, cover):
     c = lax.axis_index("dp")
     heads = moment.shape[0]
     gain_rows = gain_part.reshape(heads, DH)
@@ -101,10 +104,10 @@
         partners = [(i, i ^ distance) for i in range(chips)]
         gain_total = gain_total + lax.ppermute(gain_total, "ctx", perm=partners)
         distance *= 2
-    suffix_half = chain_scan(halves(chip_state, c), halves(chip_decay, c), later=True)
+    suffix_half, cover = chain_scan(halves(chip_state, c), halves(chip_decay, c), True, cover)
     suffix = join_halves(suffix_half, swap_dp(suffix_half), c)
     core_zero = second + jnp.exp(fin_second)[:, None, None] * suffix
-    return jnp.where(c == 0, core_zero, suffix), gain_total.reshape(heads * DH)
+    return jnp.where(c == 0, core_zero, suffix), gain_total.reshape(heads * DH), cover
 
 
 def _dot(a, b, contract):
@@ -246,13 +249,13 @@
         [("square", f32)],
         heads, length, small, 2 * rows_bytes,
     )
-    state_in = forward_states(local_state, final_log)
     (intra,) = _per_head(
         intra_kernel,
         [("rows", q), ("rows", k), ("rows", v), ("cum", cum), ("cumt", cum_t)],
         [("rows", f32)],
         heads, length, 2 * big, 5 * rows_bytes, heads * length * length,
     )
+    state_in, intra = forward_states(local_state, final_log, intra)
     state_low = state_in.astype(bf16)
     out_grad, moment, gain_part = _per_head(
         norm_kernel,
@@ -260,13 +263,15 @@
         [("rows", bf16), ("square", f32), ("gain", f32)],
         heads, length, 2 * small, 5 * rows_bytes,
     )
-    grad_state, gain_sum = backward_states(moment, final_log, gain_part.reshape(heads * DH))
     query_grad, key_part, value_part = _per_head(
         grads_kernel,
         [("rows", q), ("rows", k), ("rows", v), ("rows", out_grad), ("cum", cum), ("cumt", cum_t),
          ("square", state_low)],
         [("rows", bf16), ("rows", f32), ("rows", f32)],
         heads, length, 5 * big + small, 9 * rows_bytes, heads * length * length,
+    )
+    grad_state, gain_sum, (query_grad, key_part, value_part) = backward_states(
+        moment, final_log, gain_part.reshape(heads * DH), (query_grad, key_part, value_part)
     )
     grad_low = grad_state.astype(bf16)
     key_grad, value_grad = _per_head(

time: 195 us -> 195 us (level)
    ppermute x12, waiting for transfers between devices: 40.4 us -> 38 us  [chain_scan(): arrived = lax.ppermute(outgoing, 'ctx', perm=perm)]
    ppermute x4, waiting for transfers between devices: 4.9 us -> 6.94 us  [swap_dp(): return lax.ppermute(x, 'dp', perm=[(0, 1), (1, 0)])]
  transfers between devices with their start and end apart: 18 -> 18, of which waited for: 14 -> 15; matrix products, arithmetic and copies ran while one was open for 4% -> 3% of each run, Pallas kernels for 18% -> 18%
where the time goes in v5:
time: 195 us; the launch traced here: 192 us
  Pallas kernels  76.6 us (39%)
  waiting for transfers between devices  48.3 us (25%)
  starting transfers between devices  39.6 us (20%)
  other arithmetic  23.3 us (12%)
  local copies, waits for them, and re-layouts  2.78 us (1%)
    pallas_call x5, Pallas kernels, _per_head(): pl.pallas_call(kernel, grid=(heads,), in_specs=[spec(kind) for kind, _ in...  76.6 us
    ppermute x12, waiting for transfers between devices, chain_scan(): arrived = lax.ppermute(outgoing, 'ctx', perm=perm)  38 us
    ppermute x12, starting transfers between devices, chain_scan(): arrived = lax.ppermute(outgoing, 'ctx', perm=perm)  33.6 us
    scatter x12, other arithmetic, chain_scan(): prefix = prefix.at[slot].set(jnp.where(valid, arrived, prefix[slot]))  7.99 us
    ppermute x4, waiting for transfers between devices, swap_dp(): return lax.ppermute(x, 'dp', perm=[(0, 1), (1, 0)])  6.94 us
    ppermute x2, starting transfers between devices, backward_states(): gain_total = gain_total + lax.ppermute(gain_total, 'ctx', perm=partners)  5.14 us
    another operation x6, other arithmetic  4.51 us
  transfers between devices with their start and end apart: 18, of which 15 were waited for; matrix products, arithmetic and copies ran while one was open for 3% of the time, Pallas kernels for 18%

profile of v5, /device:TPU:0, one launch (start us, length us, event | category | flops | bytes accessed | tf_op | source)
XLA Modules:
  0.0 192.2 jit_solution(9913326965473022993)
XLA Ops:
  3.0 12.6 %shard_map.94 = f32[16,128,128]{2,1,0:T(8,128)} custom-call(bf16[512,2048]{1,0:T(8,128)(2,1)} %k_ref.7, bf16[512,2048]{1,0:T(8,128)(2,1)} %v_ref.7, f32[512,16]{1,0:T(8,128)} %copy.19.cum_ref, f32[16,512]{1,0:T(8,128)} %bitcast.216), custom_call_target="tpu_custom_call" | custom-call | flops 268435456 | bytes 4194304 | tf_op jit(solution)/shard_map/pallas_call | solution.py:219
  17.6 2.4 %collective-permute-done = f32[16,136,128]{2,1,0:T(8,128)S(1)} collective-permute-done((f32[16,136,128]{2,1,0:T(8,128)S(1)}, f32[16,136,128]{2,1,0:T(8,128)S(1)}, u32[]{:S(2)}, u32[]{:S(2)}) %collective-permute-start) | collective-permute-done | bytes 1114144 | tf_op jit(solution)/shard_map/ppermute | solution.py:19
  20.9 4.9 %collective-permute-start.1 = (f32[2,128,128]{2,1,0:T(8,128)S(1)}, f32[2,128,128]{2,1,0:T(8,128)S(1)}, u32[]{:S(2)}, u32[]{:S(2)}) collective-permute-start(f32[2,128,128]{2,1,0:T(8,128)S(1)} %bitcast_add_fusion.11), channel_id=1, source_target_pairs={{0,4},{4,8},{8,12},{1,5},{5,9},{9,13},{2,6},{6,10},{10,14},{3,7},{... | collective-permute-start | bytes 393224 | tf_op jit(solution)/shard_map/ppermute | solution.py:57
  26.6 2.2 %collective-permute-done.1 = f32[2,128,128]{2,1,0:T(8,128)S(1)} collective-permute-done((f32[2,128,128]{2,1,0:T(8,128)S(1)}, f32[2,128,128]{2,1,0:T(8,128)S(1)}, u32[]{:S(2)}, u32[]{:S(2)}) %collective-permute-start.1) | collective-permute-done | bytes 131104 | tf_op jit(solution)/shard_map/ppermute | solution.py:57
  29.6 4.4 %collective-permute-start.2 = (f32[2,128,128]{2,1,0:T(8,128)S(1)}, f32[2,128,128]{2,1,0:T(8,128)S(1)}, u32[]{:S(2)}, u32[]{:S(2)}) collective-permute-start(f32[2,128,128]{2,1,0:T(8,128)S(1)} %bitcast_add_fusion.10), channel_id=1, source_target_pairs={{0,4},{4,8},{8,12},{1,5},{5,9},{9,13},{2,6},{6,10},{10,14},{3,7},{... | collective-permute-start | bytes 393224 | tf_op jit(solution)/shard_map/ppermute | solution.py:57
  34.0 15.1 %shard_map.93.intra_ref = f32[512,2048]{1,0:T(8,128)} custom-call(bf16[512,2048]{1,0:T(8,128)(2,1)} %q_ref.5, bf16[512,2048]{1,0:T(8,128)(2,1)} %k_ref.7, bf16[512,2048]{1,0:T(8,128)(2,1)} %v_ref.7, f32[512,16]{1,0:T(8,128)} %copy.19.cum_ref, f32[16,512]{1,0:T(8,128)} %bitcast.217), custom_call_target="tpu_custom_call" | custom-call | flops 2147483648 | bytes 10485760 | tf_op jit(solution)/shard_map/pallas_call | solution.py:219
  49.9 3.5 %collective-permute-start.3 = (f32[2,128,128]{2,1,0:T(8,128)S(1)}, f32[2,128,128]{2,1,0:T(8,128)S(1)}, u32[]{:S(2)}, u32[]{:S(2)}) collective-permute-start(f32[2,128,128]{2,1,0:T(8,128)S(1)} %bitcast_add_fusion.9), channel_id=1, source_target_pairs={{0,4},{4,8},{8,12},{1,5},{5,9},{9,13},{2,6},{6,10},{10,14},{3,7},{... | collective-permute-start | bytes 393224 | tf_op jit(solution)/shard_map/ppermute | solution.py:57
  56.7 4.4 %collective-permute-start.4 = (f32[2,128,128]{2,1,0:T(8,128)S(1)}, f32[2,128,128]{2,1,0:T(8,128)S(1)}, u32[]{:S(2)}, u32[]{:S(2)}) collective-permute-start(f32[2,128,128]{2,1,0:T(8,128)S(1)} %bitcast_add_fusion.8), channel_id=1, source_target_pairs={{0,4},{4,8},{8,12},{1,5},{5,9},{9,13},{2,6},{6,10},{10,14},{3,7},{... | collective-permute-start | bytes 393224 | tf_op jit(solution)/shard_map/ppermute | solution.py:57
  61.1 2.5 %collective-permute-done.4 = f32[2,128,128]{2,1,0:T(8,128)S(1)} collective-permute-done((f32[2,128,128]{2,1,0:T(8,128)S(1)}, f32[2,128,128]{2,1,0:T(8,128)S(1)}, u32[]{:S(2)}, u32[]{:S(2)}) %collective-permute-start.4) | collective-permute-done | bytes 131104 | tf_op jit(solution)/shard_map/ppermute | solution.py:57
  64.3 4.4 %collective-permute-start.5 = (f32[2,128,128]{2,1,0:T(8,128)S(1)}, f32[2,128,128]{2,1,0:T(8,128)S(1)}, u32[]{:S(2)}, u32[]{:S(2)}) collective-permute-start(f32[2,128,128]{2,1,0:T(8,128)S(1)} %bitcast_add_fusion.7), channel_id=1, source_target_pairs={{0,4},{4,8},{8,12},{1,5},{5,9},{9,13},{2,6},{6,10},{10,14},{3,7},{... | collective-permute-start | bytes 393224 | tf_op jit(solution)/shard_map/ppermute | solution.py:57
  71.9 4.4 %collective-permute-start.6 = (f32[2,128,128]{2,1,0:T(8,128)S(1)}, f32[2,128,128]{2,1,0:T(8,128)S(1)}, u32[]{:S(2)}, u32[]{:S(2)}) collective-permute-start(f32[2,128,128]{2,1,0:T(8,128)S(1)} %bitcast_add_fusion.6), channel_id=1, source_target_pairs={{0,4},{4,8},{8,12},{1,5},{5,9},{9,13},{2,6},{6,10},{10,14},{3,7},{... | collective-permute-start | bytes 393224 | tf_op jit(solution)/shard_map/ppermute | solution.py:57
  76.3 2.5 %collective-permute-done.6 = f32[2,128,128]{2,1,0:T(8,128)S(1)} collective-permute-done((f32[2,128,128]{2,1,0:T(8,128)S(1)}, f32[2,128,128]{2,1,0:T(8,128)S(1)}, u32[]{:S(2)}, u32[]{:S(2)}) %collective-permute-start.6) | collective-permute-done | bytes 131104 | tf_op jit(solution)/shard_map/ppermute | solution.py:57
  79.6 1.8 collective-permute-done.7
  82.5 15.3 %shard_map.95 = (bf16[512,2048]{1,0:T(8,128)(2,1)}, f32[16,128,128]{2,1,0:T(8,128)}, f32[16,1,128]{2,1,0:T(1,128)}) custom-call(bf16[512,2048]{1,0:T(8,128)(2,1)} %q_ref.5, bf16[512,2048]{1,0:T(8,128)(2,1)} %g_ref.1, f32[512,2048]{1,0:T(8,128)} %shard_map.93.intra_ref, bf16[16,128,128]{2,1,0:T(8,128)(2,1)} %select_convert_fusion.1.st_ref, ...), custom_call_target="tpu_custom_call" | custom-call | flops 536870912 | bytes 10485760 | tf_op jit(solution)/shard_map/pallas_call | solution.py:219
  99.5 2.7 %collective-permute-done.8 = f32[16,136,128]{2,1,0:T(8,128)} collective-permute-done((f32[16,136,128]{2,1,0:T(8,128)S(1)}, f32[16,136,128]{2,1,0:T(8,128)}, u32[]{:S(2)}, u32[]{:S(2)}) %collective-permute-start.8) | collective-permute-done | bytes 1114144 | tf_op jit(solution)/shard_map/ppermute | solution.py:19
  107.3 6.0 %collective-permute-done.9 = f32[2,128,128]{2,1,0:T(8,128)S(1)} collective-permute-done((f32[2,128,128]{2,1,0:T(8,128)S(1)}, f32[2,128,128]{2,1,0:T(8,128)S(1)}, u32[]{:S(2)}, u32[]{:S(2)}) %collective-permute-start.9) | collective-permute-done | bytes 131104 | tf_op jit(solution)/shard_map/ppermute | solution.py:57
  115.4 20.2 %shard_map.96 = (bf16[512,2048]{1,0:T(8,128)(2,1)}, f32[512,2048]{1,0:T(8,128)}, f32[512,2048]{1,0:T(8,128)}) custom-call(bf16[512,2048]{1,0:T(8,128)(2,1)} %q_ref.5, bf16[512,2048]{1,0:T(8,128)(2,1)} %k_ref.7, bf16[512,2048]{1,0:T(8,128)(2,1)} %v_ref.7, bf16[512,2048]{1,0:T(8,128)(2,1)} %get-tuple-element.164.og_ref, f32[512,16]{1,0:T(8,128)} %copy.19.cum_ref, ...), custom_call_target="tpu_custom_call" | custom-call | flops 5637144576 | bytes 18874368 | tf_op jit(solution)/shard_map/pallas_call | solution.py:219
  138.4 5.5 %collective-permute-done.11 = f32[2,128,128]{2,1,0:T(8,128)S(1)} collective-permute-done((f32[2,128,128]{2,1,0:T(8,128)S(1)}, f32[2,128,128]{2,1,0:T(8,128)S(1)}, u32[]{:S(2)}, u32[]{:S(2)}) %collective-permute-start.11) | collective-permute-done | bytes 131104 | tf_op jit(solution)/shard_map/ppermute | solution.py:57
  146.0 5.5 %collective-permute-done.12 = f32[2,128,128]{2,1,0:T(8,128)S(1)} collective-permute-done((f32[2,128,128]{2,1,0:T(8,128)S(1)}, f32[2,128,128]{2,1,0:T(8,128)S(1)}, u32[]{:S(2)}, u32[]{:S(2)}) %collective-permute-start.12) | collective-permute-done | bytes 131104 | tf_op jit(solution)/shard_map/ppermute | solution.py:57
  154.4 4.8 %collective-permute-done.13 = f32[2,128,128]{2,1,0:T(8,128)S(1)} collective-permute-done((f32[2,128,128]{2,1,0:T(8,128)S(1)}, f32[2,128,128]{2,1,0:T(8,128)S(1)}, u32[]{:S(2)}, u32[]{:S(2)}) %collective-permute-start.13) | collective-permute-done | bytes 131104 | tf_op jit(solution)/shard_map/ppermute | solution.py:57
  161.2 5.5 %collective-permute-done.14 = f32[2,128,128]{2,1,0:T(8,128)S(1)} collective-permute-done((f32[2,128,128]{2,1,0:T(8,128)S(1)}, f32[2,128,128]{2,1,0:T(8,128)S(1)}, u32[]{:S(2)}, u32[]{:S(2)}) %collective-permute-start.14) | collective-permute-done | bytes 131104 | tf_op jit(solution)/shard_map/ppermute | solution.py:57
  168.4 2.0 %collective-permute-start.16 = (f32[16,128]{1,0:T(8,128)S(1)}, f32[16,128]{1,0:T(8,128)S(1)}, u32[]{:S(2)}, u32[]{:S(2)}) collective-permute-start(f32[16,128]{1,0:T(8,128)S(1)} %bitcast.223), channel_id=1, source_target_pairs={{0,4},{4,0},{8,12},{12,8},{1,5},{5,1},{9,13},{13,9},{2,6},{6,2},{1... | collective-permute-start | bytes 24584 | tf_op jit(solution)/shard_map/ppermute | solution.py:105
  172.1 3.1 %collective-permute-start.17 = (f32[16,128]{1,0:T(8,128)S(1)}, f32[16,128]{1,0:T(8,128)S(1)}, u32[]{:S(2)}, u32[]{:S(2)}) collective-permute-start(f32[16,128]{1,0:T(8,128)S(1)} %add.229), channel_id=1, source_target_pairs={{0,8},{4,12},{8,0},{12,4},{1,9},{5,13},{9,1},{13,5},{2,10},{6,14},... | collective-permute-start | bytes 24584 | tf_op jit(solution)/shard_map/ppermute | solution.py:105
  178.7 13.5 %shard_map.97 = (bf16[512,2048]{1,0:T(8,128)(2,1)}, bf16[512,2048]{1,0:T(8,128)(2,1)}) custom-call(bf16[512,2048]{1,0:T(8,128)(2,1)} %k_ref.7, bf16[512,2048]{1,0:T(8,128)(2,1)} %v_ref.7, f32[512,2048]{1,0:T(8,128)} %get-tuple-element.171.kg_ref, f32[512,2048]{1,0:T(8,128)} %get-tuple-element.172.vg_ref, bf16[16,128,128]{2,1,0:T(8,128)(2,1)} %select_convert_fusion.gl_ref, ...), custom_call_target="tpu_custom_call" | custom-call | flops 536870912 | bytes 16777216 | tf_op jit(solution)/shard_map/pallas_call | solution.py:219
  (104 shorter events, 42.0 us)
Async XLA Ops:
  0.6 0.8 copy-start
  1.8 1.2 copy-start.3
  15.6 4.8 %copy-start.1 = (f32[16,128,128]{2,1,0:T(8,128)S(1)}, f32[16,128,128]{2,1,0:T(8,128)}, u32[]{:S(2)}) copy-start(f32[16,128,128]{2,1,0:T(8,128)} %shard_map.94) | copy-start | bytes 3145732
  17.1 2.9 %collective-permute-start = (f32[16,136,128]{2,1,0:T(8,128)S(1)}, f32[16,136,128]{2,1,0:T(8,128)S(1)}, u32[]{:S(2)}, u32[]{:S(2)}) collective-permute-start(f32[16,136,128]{2,1,0:T(8,128)S(1)} %fusion), channel_id=1, source_target_pairs={{0,1},{1,0},{2,3},{3,2},{4,5},{5,4},{6,7},{7,6},{8,9},{9,8},{10,11... | collective-permute-start | bytes 3342344 | tf_op jit(solution)/shard_map/ppermute | solution.py:19
  20.6 5.1 %copy-start.5 = (s32[4]{0:T(128)S(1)}, s32[4]{0:T(128)}, u32[]{:S(2)}) copy-start(s32[4]{0:T(128)} %constant.298.clone.1) | copy-start | bytes 52
  20.9 7.9 %collective-permute-start.1 = (f32[2,128,128]{2,1,0:T(8,128)S(1)}, f32[2,128,128]{2,1,0:T(8,128)S(1)}, u32[]{:S(2)}, u32[]{:S(2)}) collective-permute-start(f32[2,128,128]{2,1,0:T(8,128)S(1)} %bitcast_add_fusion.11), channel_id=1, source_target_pairs={{0,4},{4,8},{8,12},{1,5},{5,9},{9,13},{2,6},{6,10},{10,14},{3,7},{... | collective-permute-start | bytes 393224 | tf_op jit(solution)/shard_map/ppermute | solution.py:57
  29.6 19.5 %collective-permute-start.2 = (f32[2,128,128]{2,1,0:T(8,128)S(1)}, f32[2,128,128]{2,1,0:T(8,128)S(1)}, u32[]{:S(2)}, u32[]{:S(2)}) collective-permute-start(f32[2,128,128]{2,1,0:T(8,128)S(1)} %bitcast_add_fusion.10), channel_id=1, source_target_pairs={{0,4},{4,8},{8,12},{1,5},{5,9},{9,13},{2,6},{6,10},{10,14},{3,7},{... | collective-permute-start | bytes 393224 | tf_op jit(solution)/shard_map/ppermute | solution.py:57
  49.9 6.0 %collective-permute-start.3 = (f32[2,128,128]{2,1,0:T(8,128)S(1)}, f32[2,128,128]{2,1,0:T(8,128)S(1)}, u32[]{:S(2)}, u32[]{:S(2)}) collective-permute-start(f32[2,128,128]{2,1,0:T(8,128)S(1)} %bitcast_add_fusion.9), channel_id=1, source_target_pairs={{0,4},{4,8},{8,12},{1,5},{5,9},{9,13},{2,6},{6,10},{10,14},{3,7},{... | collective-permute-start | bytes 393224 | tf_op jit(solution)/shard_map/ppermute | solution.py:57
  56.7 6.9 %collective-permute-start.4 = (f32[2,128,128]{2,1,0:T(8,128)S(1)}, f32[2,128,128]{2,1,0:T(8,128)S(1)}, u32[]{:S(2)}, u32[]{:S(2)}) collective-permute-start(f32[2,128,128]{2,1,0:T(8,128)S(1)} %bitcast_add_fusion.8), channel_id=1, source_target_pairs={{0,4},{4,8},{8,12},{1,5},{5,9},{9,13},{2,6},{6,10},{10,14},{3,7},{... | collective-permute-start | bytes 393224 | tf_op jit(solution)/shard_map/ppermute | solution.py:57
  64.3 6.9 %collective-permute-start.5 = (f32[2,128,128]{2,1,0:T(8,128)S(1)}, f32[2,128,128]{2,1,0:T(8,128)S(1)}, u32[]{:S(2)}, u32[]{:S(2)}) collective-permute-start(f32[2,128,128]{2,1,0:T(8,128)S(1)} %bitcast_add_fusion.7), channel_id=1, source_target_pairs={{0,4},{4,8},{8,12},{1,5},{5,9},{9,13},{2,6},{6,10},{10,14},{3,7},{... | collective-permute-start | bytes 393224 | tf_op jit(solution)/shard_map/ppermute | solution.py:57
  71.9 6.9 %collective-permute-start.6 = (f32[2,128,128]{2,1,0:T(8,128)S(1)}, f32[2,128,128]{2,1,0:T(8,128)S(1)}, u32[]{:S(2)}, u32[]{:S(2)}) collective-permute-start(f32[2,128,128]{2,1,0:T(8,128)S(1)} %bitcast_add_fusion.6), channel_id=1, source_target_pairs={{0,4},{4,8},{8,12},{1,5},{5,9},{9,13},{2,6},{6,10},{10,14},{3,7},{... | collective-permute-start | bytes 393224 | tf_op jit(solution)/shard_map/ppermute | solution.py:57
  79.4 2.0 %collective-permute-start.7 = (f32[8,128,128]{2,1,0:T(8,128)S(1)}, f32[8,128,128]{2,1,0:T(8,128)S(1)}, u32[]{:S(2)}, u32[]{:S(2)}) collective-permute-start(f32[8,128,128]{2,1,0:T(8,128)S(1)} %bitcast.203), channel_id=1, source_target_pairs={{0,1},{1,0},{2,3},{3,2},{4,5},{5,4},{6,7},{7,6},{8,9},{9,8},{10,11... | collective-permute-start | bytes 1572872 | tf_op jit(solution)/shard_map/ppermute | solution.py:19
  97.8 5.7 %copy-start.2 = (f32[16,128,128]{2,1,0:T(8,128)S(1)}, f32[16,128,128]{2,1,0:T(8,128)}, u32[]{:S(2)}) copy-start(f32[16,128,128]{2,1,0:T(8,128)} %get-tuple-element.168) | copy-start | bytes 3145732
  99.2 3.0 %collective-permute-start.8 = (f32[16,136,128]{2,1,0:T(8,128)S(1)}, f32[16,136,128]{2,1,0:T(8,128)}, u32[]{:S(2)}, u32[]{:S(2)}) collective-permute-start(f32[16,136,128]{2,1,0:T(8,128)S(1)} %fusion.2), channel_id=1, source_target_pairs={{0,1},{1,0},{2,3},{3,2},{4,5},{5,4},{6,7},{7,6},{8,9},{9,8},{10,11... | collective-permute-start | bytes 3342344 | tf_op jit(solution)/shard_map/ppermute | solution.py:19
  105.1 8.1 %collective-permute-start.9 = (f32[2,128,128]{2,1,0:T(8,128)S(1)}, f32[2,128,128]{2,1,0:T(8,128)S(1)}, u32[]{:S(2)}, u32[]{:S(2)}) collective-permute-start(f32[2,128,128]{2,1,0:T(8,128)S(1)} %bitcast_add_fusion.5), channel_id=1, source_target_pairs={{4,0},{8,4},{12,8},{5,1},{9,5},{13,9},{6,2},{10,6},{14,10},{7,3},{... | collective-permute-start | bytes 393224 | tf_op jit(solution)/shard_map/ppermute | solution.py:57
  114.1 21.5 %collective-permute-start.10 = (f32[2,128,128]{2,1,0:T(8,128)S(1)}, f32[2,128,128]{2,1,0:T(8,128)S(1)}, u32[]{:S(2)}, u32[]{:S(2)}) collective-permute-start(f32[2,128,128]{2,1,0:T(8,128)S(1)} %bitcast_add_fusion.4), channel_id=1, source_target_pairs={{4,0},{8,4},{12,8},{5,1},{9,5},{13,9},{6,2},{10,6},{14,10},{7,3},{... | collective-permute-start | bytes 393224 | tf_op jit(solution)/shard_map/ppermute | solution.py:57
  136.4 7.6 %collective-permute-start.11 = (f32[2,128,128]{2,1,0:T(8,128)S(1)}, f32[2,128,128]{2,1,0:T(8,128)S(1)}, u32[]{:S(2)}, u32[]{:S(2)}) collective-permute-start(f32[2,128,128]{2,1,0:T(8,128)S(1)} %bitcast_add_fusion.3), channel_id=1, source_target_pairs={{4,0},{8,4},{12,8},{5,1},{9,5},{13,9},{6,2},{10,6},{14,10},{7,3},{... | collective-permute-start | bytes 393224 | tf_op jit(solution)/shard_map/ppermute | solution.py:57
  144.7 6.9 %collective-permute-start.12 = (f32[2,128,128]{2,1,0:T(8,128)S(1)}, f32[2,128,128]{2,1,0:T(8,128)S(1)}, u32[]{:S(2)}, u32[]{:S(2)}) collective-permute-start(f32[2,128,128]{2,1,0:T(8,128)S(1)} %bitcast_add_fusion.2), channel_id=1, source_target_pairs={{4,0},{8,4},{12,8},{5,1},{9,5},{13,9},{6,2},{10,6},{14,10},{7,3},{... | collective-permute-start | bytes 393224 | tf_op jit(solution)/shard_map/ppermute | solution.py:57
  152.2 15.3 %copy-start.4 = (f32[16,1,128]{2,1,0:T(1,128)S(1)}, f32[16,1,128]{2,1,0:T(1,128)}, u32[]{:S(2)}) copy-start(f32[16,1,128]{2,1,0:T(1,128)} %get-tuple-element.169) | copy-start | bytes 24580
  152.3 6.9 %collective-permute-start.13 = (f32[2,128,128]{2,1,0:T(8,128)S(1)}, f32[2,128,128]{2,1,0:T(8,128)S(1)}, u32[]{:S(2)}, u32[]{:S(2)}) collective-permute-start(f32[2,128,128]{2,1,0:T(8,128)S(1)} %bitcast_add_fusion.1), channel_id=1, source_target_pairs={{4,0},{8,4},{12,8},{5,1},{9,5},{13,9},{6,2},{10,6},{14,10},{7,3},{... | collective-permute-start | bytes 393224 | tf_op jit(solution)/shard_map/ppermute | solution.py:57
  159.9 6.9 %collective-permute-start.14 = (f32[2,128,128]{2,1,0:T(8,128)S(1)}, f32[2,128,128]{2,1,0:T(8,128)S(1)}, u32[]{:S(2)}, u32[]{:S(2)}) collective-permute-start(f32[2,128,128]{2,1,0:T(8,128)S(1)} %bitcast_add_fusion), channel_id=1, source_target_pairs={{4,0},{8,4},{12,8},{5,1},{9,5},{13,9},{6,2},{10,6},{14,10},{7,3},{... | collective-permute-start | bytes 393224 | tf_op jit(solution)/shard_map/ppermute | solution.py:57
  167.4 10.0 %collective-permute-start.15 = (f32[8,128,128]{2,1,0:T(8,128)S(1)}, f32[8,128,128]{2,1,0:T(8,128)S(1)}, u32[]{:S(2)}, u32[]{:S(2)}) collective-permute-start(f32[8,128,128]{2,1,0:T(8,128)S(1)} %bitcast.202), channel_id=1, source_target_pairs={{0,1},{1,0},{2,3},{3,2},{4,5},{5,4},{6,7},{7,6},{8,9},{9,8},{10,11... | collective-permute-start | bytes 1572872 | tf_op jit(solution)/shard_map/ppermute | solution.py:19
  168.4 3.7 %collective-permute-start.16 = (f32[16,128]{1,0:T(8,128)S(1)}, f32[16,128]{1,0:T(8,128)S(1)}, u32[]{:S(2)}, u32[]{:S(2)}) collective-permute-start(f32[16,128]{1,0:T(8,128)S(1)} %bitcast.223), channel_id=1, source_target_pairs={{0,4},{4,0},{8,12},{12,8},{1,5},{5,1},{9,13},{13,9},{2,6},{6,2},{1... | collective-permute-start | bytes 24584 | tf_op jit(solution)/shard_map/ppermute | solution.py:105
  172.1 4.7 %collective-permute-start.17 = (f32[16,128]{1,0:T(8,128)S(1)}, f32[16,128]{1,0:T(8,128)S(1)}, u32[]{:S(2)}, u32[]{:S(2)}) collective-permute-start(f32[16,128]{1,0:T(8,128)S(1)} %add.229), channel_id=1, source_target_pairs={{0,8},{4,12},{8,0},{12,4},{1,9},{5,13},{9,1},{13,5},{2,10},{6,14},... | collective-permute-start | bytes 24584 | tf_op jit(solution)/shard_map/ppermute | solution.py:105

commit v6 on v5

--- a/solution.py
+++ b/solution.py
@@ -10,6 +10,7 @@
 PAD = 8
 CHUNKS = 4
 TIE_STEP = 1
+HB = 4
 
 
 epsilon = 1e-06
@@ -139,8 +140,8 @@
     return (_nt(q, k) * decay).astype(jnp.bfloat16)
 
 
-def _head_vectors(cum_ref, cumt_ref):
-    h = pl.program_id(0)
+def _head_vectors(cum_ref, cumt_ref, j):
+    h = pl.program_id(0) * HB + j
     full = cum_ref[...]
     lane = lax.broadcasted_iota(jnp.int32, full.shape, 1)
     col = jnp.sum(jnp.where(lane == h, full, 0.0), axis=1, keepdims=True)
@@ -149,66 +150,80 @@
     return col, row, jnp.exp(col), jnp.exp(fin - col)
 
 
+def _lanes(j):
+    return slice(j * DH, (j + 1) * DH)
+
+
 def local_state_kernel(k_ref, v_ref, cum_ref, cumt_ref, s_ref):
-    _, _, _, toend = _head_vectors(cum_ref, cumt_ref)
-    scaled = (k_ref[...].astype(jnp.float32) * toend).astype(jnp.bfloat16)
-    s_ref[0] = _tn(scaled, v_ref[...])
+    for j in range(HB):
+        cols = _lanes(j)
+        _, _, _, toend = _head_vectors(cum_ref, cumt_ref, j)
+        scaled = (k_ref[:, cols].astype(jnp.float32) * toend).astype(jnp.bfloat16)
+        s_ref[j] = _tn(scaled, v_ref[:, cols])
 
 
 def intra_kernel(q_ref, k_ref, v_ref, cum_ref, cumt_ref, out_ref):
-    col, row, _, _ = _head_vectors(cum_ref, cumt_ref)
-    decay = _decay(col, row)
-    out_ref[...] = _nn(_masked(q_ref[...], k_ref[...], decay), v_ref[...])
+    for j in range(HB):
+        cols = _lanes(j)
+        col, row, _, _ = _head_vectors(cum_ref, cumt_ref, j)
+        decay = _decay(col, row)
+        out_ref[:, cols] = _nn(_masked(q_ref[:, cols], k_ref[:, cols], decay), v_ref[:, cols])
 
 
 def norm_kernel(q_ref, g_ref, intra_ref, st_ref, cum_ref, cumt_ref, gain_ref, og_ref, m_ref, gp_ref):
-    _, _, grow, _ = _head_vectors(cum_ref, cumt_ref)
-    q = q_ref[...]
-    attended = intra_ref[...] + grow * _nn(q, st_ref[0])
-    width = attended.shape[-1]
-    root_mean = jnp.sqrt(jnp.sum(attended * attended, axis=-1, keepdims=True) / width + epsilon)
-    normed = attended / root_mean
-    grad_f = g_ref[...].astype(jnp.float32)
-    scaled = gain_ref[0] * grad_f
-    projected = jnp.sum(scaled * attended, axis=-1, keepdims=True)
-    out_grad = ((scaled - attended * projected / (width * root_mean * root_mean)) / root_mean).astype(
-        jnp.bfloat16
-    )
-    og_ref[...] = out_grad
-    gp_ref[0] = jnp.sum(grad_f * normed, axis=0, keepdims=True)
-    q_scaled = (q.astype(jnp.float32) * grow).astype(jnp.bfloat16)
-    m_ref[0] = _tn(q_scaled, out_grad)
+    for j in range(HB):
+        cols = _lanes(j)
+        _, _, grow, _ = _head_vectors(cum_ref, cumt_ref, j)
+        q = q_ref[:, cols]
+        attended = intra_ref[:, cols] + grow * _nn(q, st_ref[j])
+        width = attended.shape[-1]
+        root_mean = jnp.sqrt(jnp.sum(attended * attended, axis=-1, keepdims=True) / width + epsilon)
+        normed = attended / root_mean
+        grad_f = g_ref[:, cols].astype(jnp.float32)
+        scaled = gain_ref[j] * grad_f
+        projected = jnp.sum(scaled * attended, axis=-1, keepdims=True)
+        out_grad = ((scaled - attended * projected / (width * root_mean * root_mean)) / root_mean).astype(
+            jnp.bfloat16
+        )
+        og_ref[:, cols] = out_grad
+        gp_ref[j] = jnp.sum(grad_f * normed, axis=0, keepdims=True)
+        q_scaled = (q.astype(jnp.float32) * grow).astype(jnp.bfloat16)
+        m_ref[j] = _tn(q_scaled, out_grad)
 
 
 def grads_kernel(q_ref, k_ref, v_ref, og_ref, cum_ref, cumt_ref, st_ref, qg_ref, kg_ref, vg_ref):
-    col, row, grow, _ = _head_vectors(cum_ref, cumt_ref)
-    decay = _decay(col, row)
-    q, k, v, og = q_ref[...], k_ref[...], v_ref[...], og_ref[...]
-    masked = _masked(q, k, decay)
-    rgrad = (_nt(og, v) * decay).astype(jnp.bfloat16)
-    qg_ref[...] = (_nn(rgrad, k) + grow * _nt(og, st_ref[0])).astype(jnp.bfloat16)
-    kg_ref[...] = _tn(rgrad, q)
-    vg_ref[...] = _tn(masked, og)
+    for j in range(HB):
+        cols = _lanes(j)
+        col, row, grow, _ = _head_vectors(cum_ref, cumt_ref, j)
+        decay = _decay(col, row)
+        q, k, v, og = q_ref[:, cols], k_ref[:, cols], v_ref[:, cols], og_ref[:, cols]
+        masked = _masked(q, k, decay)
+        rgrad = (_nt(og, v) * decay).astype(jnp.bfloat16)
+        qg_ref[:, cols] = (_nn(rgrad, k) + grow * _nt(og, st_ref[j])).astype(jnp.bfloat16)
+        kg_ref[:, cols] = _tn(rgrad, q)
+        vg_ref[:, cols] = _tn(masked, og)
 
 
 def finish_kernel(k_ref, v_ref, kg_ref, vg_ref, gl_ref, cum_ref, cumt_ref, ko_ref, vo_ref):
-    _, _, _, toend = _head_vectors(cum_ref, cumt_ref)
-    grad_low = gl_ref[0]
-    ko_ref[...] = (kg_ref[...] + toend * _nt(v_ref[...], grad_low)).astype(jnp.bfloat16)
-    vo_ref[...] = (vg_ref[...] + toend * _nn(k_ref[...], grad_low)).astype(jnp.bfloat16)
+    for j in range(HB):
+        cols = _lanes(j)
+        _, _, _, toend = _head_vectors(cum_ref, cumt_ref, j)
+        grad_low = gl_ref[j]
+        ko_ref[:, cols] = (kg_ref[:, cols] + toend * _nt(v_ref[:, cols], grad_low)).astype(jnp.bfloat16)
+        vo_ref[:, cols] = (vg_ref[:, cols] + toend * _nn(k_ref[:, cols], grad_low)).astype(jnp.bfloat16)
 
 
 def _per_head(kernel, ins, outs, heads, length, flops, nbytes, exps=0):
     def spec(kind):
         if kind == "rows":
-            return pl.BlockSpec((length, DH), lambda h: (0, h))
+            return pl.BlockSpec((length, HB * DH), lambda i: (0, i))
         if kind == "cum":
-            return pl.BlockSpec((length, heads), lambda h: (0, 0))
+            return pl.BlockSpec((length, heads), lambda i: (0, 0))
         if kind == "cumt":
-            return pl.BlockSpec((heads, length), lambda h: (0, 0))
+            return pl.BlockSpec((heads, length), lambda i: (0, 0))
         if kind == "gain":
-            return pl.BlockSpec((1, 1, DH), lambda h: (h, 0, 0))
-        return pl.BlockSpec((1, DH, DH), lambda h: (h, 0, 0))
+            return pl.BlockSpec((HB, 1, DH), lambda i: (i, 0, 0))
+        return pl.BlockSpec((HB, DH, DH), lambda i: (i, 0, 0))
 
     shapes = {
         "rows": (length, heads * DH),
@@ -218,7 +233,7 @@
     out_shape = [jax.ShapeDtypeStruct(shapes[kind], dtype) for kind, dtype in outs]
     return pl.pallas_call(
         kernel,
-        grid=(heads,),
+        grid=(heads // HB,),
         in_specs=[spec(kind) for kind, _ in ins],
         out_specs=[spec(kind) for kind, _ in outs],
         out_shape=out_shape,

time: 195 us -> 166 us (0.85)
  Pallas kernels: 76.6 us -> 49.1 us
    pallas_call x5, Pallas kernels: 76.6 us -> 49.1 us  [_per_head(): pl.pallas_call(kernel, grid=(heads // HB,), in_specs=[spec(kind) for kind...]
  transfers between devices with their start and end apart: 18 -> 18, of which waited for: 15 -> 15; matrix products, arithmetic and copies ran while one was open for 3% -> 4% of each run, Pallas kernels for 18% -> 15%
where the time goes in v6:
time: 166 us; the launch traced here: 165 us
  Pallas kernels  49.1 us (30%)
  waiting for transfers between devices  48.3 us (29%)
  starting transfers between devices  39.6 us (24%)
  other arithmetic  23.3 us (14%)
  local copies, waits for them, and re-layouts  2.78 us (2%)
    pallas_call x5, Pallas kernels, _per_head(): pl.pallas_call(kernel, grid=(heads // HB,), in_specs=[spec(kind) for kind...  49.1 us
    ppermute x12, waiting for transfers between devices, chain_scan(): arrived = lax.ppermute(outgoing, 'ctx', perm=perm)  38 us
    ppermute x12, starting transfers between devices, chain_scan(): arrived = lax.ppermute(outgoing, 'ctx', perm=perm)  33.6 us
    scatter x12, other arithmetic, chain_scan(): prefix = prefix.at[slot].set(jnp.where(valid, arrived, prefix[slot]))  7.99 us
    ppermute x4, waiting for transfers between devices, swap_dp(): return lax.ppermute(x, 'dp', perm=[(0, 1), (1, 0)])  6.95 us
    ppermute x2, starting transfers between devices, backward_states(): gain_total = gain_total + lax.ppermute(gain_total, 'ctx', perm=partners)  5.15 us
    another operation x6, other arithmetic  4.51 us
  transfers between devices with their start and end apart: 18, of which 15 were waited for; matrix products, arithmetic and copies ran while one was open for 4% of the time, Pallas kernels for 15%

profile of v6, /device:TPU:0, one launch (start us, length us, event | category | flops | bytes accessed | tf_op | source)
XLA Modules:
  0.0 164.7 jit_solution(840522819488773046)
XLA Ops:
  3.0 5.8 %shard_map.94 = f32[16,128,128]{2,1,0:T(8,128)} custom-call(bf16[512,2048]{1,0:T(8,128)(2,1)} %k_ref.7, bf16[512,2048]{1,0:T(8,128)(2,1)} %v_ref.7, f32[512,16]{1,0:T(8,128)} %copy.19.cum_ref, f32[16,512]{1,0:T(8,128)} %bitcast.216), custom_call_target="tpu_custom_call" | custom-call | flops 268435456 | bytes 4194304 | tf_op jit(solution)/shard_map/pallas_call | solution.py:234
  10.9 2.4 %collective-permute-done = f32[16,136,128]{2,1,0:T(8,128)S(1)} collective-permute-done((f32[16,136,128]{2,1,0:T(8,128)S(1)}, f32[16,136,128]{2,1,0:T(8,128)S(1)}, u32[]{:S(2)}, u32[]{:S(2)}) %collective-permute-start) | collective-permute-done | bytes 1114144 | tf_op jit(solution)/shard_map/ppermute | solution.py:20
  14.2 4.9 %collective-permute-start.1 = (f32[2,128,128]{2,1,0:T(8,128)S(1)}, f32[2,128,128]{2,1,0:T(8,128)S(1)}, u32[]{:S(2)}, u32[]{:S(2)}) collective-permute-start(f32[2,128,128]{2,1,0:T(8,128)S(1)} %bitcast_add_fusion.11), channel_id=1, source_target_pairs={{0,4},{4,8},{8,12},{1,5},{5,9},{9,13},{2,6},{6,10},{10,14},{3,7},{... | collective-permute-start | bytes 393224 | tf_op jit(solution)/shard_map/ppermute | solution.py:58
  19.8 2.2 %collective-permute-done.1 = f32[2,128,128]{2,1,0:T(8,128)S(1)} collective-permute-done((f32[2,128,128]{2,1,0:T(8,128)S(1)}, f32[2,128,128]{2,1,0:T(8,128)S(1)}, u32[]{:S(2)}, u32[]{:S(2)}) %collective-permute-start.1) | collective-permute-done | bytes 131104 | tf_op jit(solution)/shard_map/ppermute | solution.py:58
  22.9 4.4 %collective-permute-start.2 = (f32[2,128,128]{2,1,0:T(8,128)S(1)}, f32[2,128,128]{2,1,0:T(8,128)S(1)}, u32[]{:S(2)}, u32[]{:S(2)}) collective-permute-start(f32[2,128,128]{2,1,0:T(8,128)S(1)} %bitcast_add_fusion.10), channel_id=1, source_target_pairs={{0,4},{4,8},{8,12},{1,5},{5,9},{9,13},{2,6},{6,10},{10,14},{3,7},{... | collective-permute-start | bytes 393224 | tf_op jit(solution)/shard_map/ppermute | solution.py:58
  27.3 8.6 %shard_map.93.intra_ref = f32[512,2048]{1,0:T(8,128)} custom-call(bf16[512,2048]{1,0:T(8,128)(2,1)} %q_ref.5, bf16[512,2048]{1,0:T(8,128)(2,1)} %k_ref.7, bf16[512,2048]{1,0:T(8,128)(2,1)} %v_ref.7, f32[512,16]{1,0:T(8,128)} %copy.19.cum_ref, f32[16,512]{1,0:T(8,128)} %bitcast.217), custom_call_target="tpu_custom_call" | custom-call | flops 2147483648 | bytes 10485760 | tf_op jit(solution)/shard_map/pallas_call | solution.py:234
  36.6 3.5 %collective-permute-start.3 = (f32[2,128,128]{2,1,0:T(8,128)S(1)}, f32[2,128,128]{2,1,0:T(8,128)S(1)}, u32[]{:S(2)}, u32[]{:S(2)}) collective-permute-start(f32[2,128,128]{2,1,0:T(8,128)S(1)} %bitcast_add_fusion.9), channel_id=1, source_target_pairs={{0,4},{4,8},{8,12},{1,5},{5,9},{9,13},{2,6},{6,10},{10,14},{3,7},{... | collective-permute-start | bytes 393224 | tf_op jit(solution)/shard_map/ppermute | solution.py:58
  43.4 4.4 %collective-permute-start.4 = (f32[2,128,128]{2,1,0:T(8,128)S(1)}, f32[2,128,128]{2,1,0:T(8,128)S(1)}, u32[]{:S(2)}, u32[]{:S(2)}) collective-permute-start(f32[2,128,128]{2,1,0:T(8,128)S(1)} %bitcast_add_fusion.8), channel_id=1, source_target_pairs={{0,4},{4,8},{8,12},{1,5},{5,9},{9,13},{2,6},{6,10},{10,14},{3,7},{... | collective-permute-start | bytes 393224 | tf_op jit(solution)/shard_map/ppermute | solution.py:58
  47.8 2.5 %collective-permute-done.4 = f32[2,128,128]{2,1,0:T(8,128)S(1)} collective-permute-done((f32[2,128,128]{2,1,0:T(8,128)S(1)}, f32[2,128,128]{2,1,0:T(8,128)S(1)}, u32[]{:S(2)}, u32[]{:S(2)}) %collective-permute-start.4) | collective-permute-done | bytes 131104 | tf_op jit(solution)/shard_map/ppermute | solution.py:58
  51.0 4.4 %collective-permute-start.5 = (f32[2,128,128]{2,1,0:T(8,128)S(1)}, f32[2,128,128]{2,1,0:T(8,128)S(1)}, u32[]{:S(2)}, u32[]{:S(2)}) collective-permute-start(f32[2,128,128]{2,1,0:T(8,128)S(1)} %bitcast_add_fusion.7), channel_id=1, source_target_pairs={{0,4},{4,8},{8,12},{1,5},{5,9},{9,13},{2,6},{6,10},{10,14},{3,7},{... | collective-permute-start | bytes 393224 | tf_op jit(solution)/shard_map/ppermute | solution.py:58
  58.6 4.4 %collective-permute-start.6 = (f32[2,128,128]{2,1,0:T(8,128)S(1)}, f32[2,128,128]{2,1,0:T(8,128)S(1)}, u32[]{:S(2)}, u32[]{:S(2)}) collective-permute-start(f32[2,128,128]{2,1,0:T(8,128)S(1)} %bitcast_add_fusion.6), channel_id=1, source_target_pairs={{0,4},{4,8},{8,12},{1,5},{5,9},{9,13},{2,6},{6,10},{10,14},{3,7},{... | collective-permute-start | bytes 393224 | tf_op jit(solution)/shard_map/ppermute | solution.py:58
  63.0 2.5 %collective-permute-done.6 = f32[2,128,128]{2,1,0:T(8,128)S(1)} collective-permute-done((f32[2,128,128]{2,1,0:T(8,128)S(1)}, f32[2,128,128]{2,1,0:T(8,128)S(1)}, u32[]{:S(2)}, u32[]{:S(2)}) %collective-permute-start.6) | collective-permute-done | bytes 131104 | tf_op jit(solution)/shard_map/ppermute | solution.py:58
  66.3 1.8 %collective-permute-done.7 = f32[8,128,128]{2,1,0:T(8,128)S(1)} collective-permute-done((f32[8,128,128]{2,1,0:T(8,128)S(1)}, f32[8,128,128]{2,1,0:T(8,128)S(1)}, u32[]{:S(2)}, u32[]{:S(2)}) %collective-permute-start.7) | collective-permute-done | bytes 524320 | tf_op jit(solution)/shard_map/ppermute | solution.py:20
  69.2 9.4 %shard_map.95 = (bf16[512,2048]{1,0:T(8,128)(2,1)}, f32[16,128,128]{2,1,0:T(8,128)}, f32[16,1,128]{2,1,0:T(1,128)}) custom-call(bf16[512,2048]{1,0:T(8,128)(2,1)} %q_ref.5, bf16[512,2048]{1,0:T(8,128)(2,1)} %g_ref.1, f32[512,2048]{1,0:T(8,128)} %shard_map.93.intra_ref, bf16[16,128,128]{2,1,0:T(8,128)(2,1)} %select_convert_fusion.1.st_ref, ...), custom_call_target="tpu_custom_call" | custom-call | flops 536870912 | bytes 10485760 | tf_op jit(solution)/shard_map/pallas_call | solution.py:234
  80.3 2.8 %collective-permute-done.8 = f32[16,136,128]{2,1,0:T(8,128)} collective-permute-done((f32[16,136,128]{2,1,0:T(8,128)S(1)}, f32[16,136,128]{2,1,0:T(8,128)}, u32[]{:S(2)}, u32[]{:S(2)}) %collective-permute-start.8) | collective-permute-done | bytes 1114144 | tf_op jit(solution)/shard_map/ppermute | solution.py:20
  88.2 6.0 %collective-permute-done.9 = f32[2,128,128]{2,1,0:T(8,128)S(1)} collective-permute-done((f32[2,128,128]{2,1,0:T(8,128)S(1)}, f32[2,128,128]{2,1,0:T(8,128)S(1)}, u32[]{:S(2)}, u32[]{:S(2)}) %collective-permute-start.9) | collective-permute-done | bytes 131104 | tf_op jit(solution)/shard_map/ppermute | solution.py:58
  96.3 16.9 %shard_map.96 = (bf16[512,2048]{1,0:T(8,128)(2,1)}, f32[512,2048]{1,0:T(8,128)}, f32[512,2048]{1,0:T(8,128)}) custom-call(bf16[512,2048]{1,0:T(8,128)(2,1)} %q_ref.5, bf16[512,2048]{1,0:T(8,128)(2,1)} %k_ref.7, bf16[512,2048]{1,0:T(8,128)(2,1)} %v_ref.7, bf16[512,2048]{1,0:T(8,128)(2,1)} %get-tuple-element.164.og_ref, f32[512,16]{1,0:T(8,128)} %copy.19.cum_ref, ...), custom_call_target="tpu_custom_call" | custom-call | flops 5637144576 | bytes 18874368 | tf_op jit(solution)/shard_map/pallas_call | solution.py:234
  116.0 5.5 %collective-permute-done.11 = f32[2,128,128]{2,1,0:T(8,128)S(1)} collective-permute-done((f32[2,128,128]{2,1,0:T(8,128)S(1)}, f32[2,128,128]{2,1,0:T(8,128)S(1)}, u32[]{:S(2)}, u32[]{:S(2)}) %collective-permute-start.11) | collective-permute-done | bytes 131104 | tf_op jit(solution)/shard_map/ppermute | solution.py:58
  123.7 5.5 %collective-permute-done.12 = f32[2,128,128]{2,1,0:T(8,128)S(1)} collective-permute-done((f32[2,128,128]{2,1,0:T(8,128)S(1)}, f32[2,128,128]{2,1,0:T(8,128)S(1)}, u32[]{:S(2)}, u32[]{:S(2)}) %collective-permute-start.12) | collective-permute-done | bytes 131104 | tf_op jit(solution)/shard_map/ppermute | solution.py:58
  132.0 4.8 %collective-permute-done.13 = f32[2,128,128]{2,1,0:T(8,128)S(1)} collective-permute-done((f32[2,128,128]{2,1,0:T(8,128)S(1)}, f32[2,128,128]{2,1,0:T(8,128)S(1)}, u32[]{:S(2)}, u32[]{:S(2)}) %collective-permute-start.13) | collective-permute-done | bytes 131104 | tf_op jit(solution)/shard_map/ppermute | solution.py:58
  138.9 5.5 %collective-permute-done.14 = f32[2,128,128]{2,1,0:T(8,128)S(1)} collective-permute-done((f32[2,128,128]{2,1,0:T(8,128)S(1)}, f32[2,128,128]{2,1,0:T(8,128)S(1)}, u32[]{:S(2)}, u32[]{:S(2)}) %collective-permute-start.14) | collective-permute-done | bytes 131104 | tf_op jit(solution)/shard_map/ppermute | solution.py:58
  146.0 2.0 %collective-permute-start.16 = (f32[16,128]{1,0:T(8,128)S(1)}, f32[16,128]{1,0:T(8,128)S(1)}, u32[]{:S(2)}, u32[]{:S(2)}) collective-permute-start(f32[16,128]{1,0:T(8,128)S(1)} %bitcast.223), channel_id=1, source_target_pairs={{0,4},{4,0},{8,12},{12,8},{1,5},{5,1},{9,13},{13,9},{2,6},{6,2},{1... | collective-permute-start | bytes 24584 | tf_op jit(solution)/shard_map/ppermute | solution.py:106
  149.7 3.1 %collective-permute-start.17 = (f32[16,128]{1,0:T(8,128)S(1)}, f32[16,128]{1,0:T(8,128)S(1)}, u32[]{:S(2)}, u32[]{:S(2)}) collective-permute-start(f32[16,128]{1,0:T(8,128)S(1)} %add.229), channel_id=1, source_target_pairs={{0,8},{4,12},{8,0},{12,4},{1,9},{5,13},{9,1},{13,5},{2,10},{6,14},... | collective-permute-start | bytes 24584 | tf_op jit(solution)/shard_map/ppermute | solution.py:106
  156.3 8.4 %shard_map.97 = (bf16[512,2048]{1,0:T(8,128)(2,1)}, bf16[512,2048]{1,0:T(8,128)(2,1)}) custom-call(bf16[512,2048]{1,0:T(8,128)(2,1)} %k_ref.7, bf16[512,2048]{1,0:T(8,128)(2,1)} %v_ref.7, f32[512,2048]{1,0:T(8,128)} %get-tuple-element.171.kg_ref, f32[512,2048]{1,0:T(8,128)} %get-tuple-element.172.vg_ref, bf16[16,128,128]{2,1,0:T(8,128)(2,1)} %select_convert_fusion.gl_ref, ...), custom_call_target="tpu_custom_call" | custom-call | flops 536870912 | bytes 16777216 | tf_op jit(solution)/shard_map/pallas_call | solution.py:234
  (104 shorter events, 42.0 us)
Async XLA Ops:
  0.6 0.8 copy-start
  1.8 1.2 copy-start.3
  8.9 4.8 %copy-start.1 = (f32[16,128,128]{2,1,0:T(8,128)S(1)}, f32[16,128,128]{2,1,0:T(8,128)}, u32[]{:S(2)}) copy-start(f32[16,128,128]{2,1,0:T(8,128)} %shard_map.94) | copy-start | bytes 3145732
  10.3 2.9 %collective-permute-start = (f32[16,136,128]{2,1,0:T(8,128)S(1)}, f32[16,136,128]{2,1,0:T(8,128)S(1)}, u32[]{:S(2)}, u32[]{:S(2)}) collective-permute-start(f32[16,136,128]{2,1,0:T(8,128)S(1)} %fusion), channel_id=1, source_target_pairs={{0,1},{1,0},{2,3},{3,2},{4,5},{5,4},{6,7},{7,6},{8,9},{9,8},{10,11... | collective-permute-start | bytes 3342344 | tf_op jit(solution)/shard_map/ppermute | solution.py:20
  13.9 5.1 %copy-start.5 = (s32[4]{0:T(128)S(1)}, s32[4]{0:T(128)}, u32[]{:S(2)}) copy-start(s32[4]{0:T(128)} %constant.298.clone.1) | copy-start | bytes 52
  14.2 7.9 %collective-permute-start.1 = (f32[2,128,128]{2,1,0:T(8,128)S(1)}, f32[2,128,128]{2,1,0:T(8,128)S(1)}, u32[]{:S(2)}, u32[]{:S(2)}) collective-permute-start(f32[2,128,128]{2,1,0:T(8,128)S(1)} %bitcast_add_fusion.11), channel_id=1, source_target_pairs={{0,4},{4,8},{8,12},{1,5},{5,9},{9,13},{2,6},{6,10},{10,14},{3,7},{... | collective-permute-start | bytes 393224 | tf_op jit(solution)/shard_map/ppermute | solution.py:58
  22.9 13.0 %collective-permute-start.2 = (f32[2,128,128]{2,1,0:T(8,128)S(1)}, f32[2,128,128]{2,1,0:T(8,128)S(1)}, u32[]{:S(2)}, u32[]{:S(2)}) collective-permute-start(f32[2,128,128]{2,1,0:T(8,128)S(1)} %bitcast_add_fusion.10), channel_id=1, source_target_pairs={{0,4},{4,8},{8,12},{1,5},{5,9},{9,13},{2,6},{6,10},{10,14},{3,7},{... | collective-permute-start | bytes 393224 | tf_op jit(solution)/shard_map/ppermute | solution.py:58
  36.6 6.0 %collective-permute-start.3 = (f32[2,128,128]{2,1,0:T(8,128)S(1)}, f32[2,128,128]{2,1,0:T(8,128)S(1)}, u32[]{:S(2)}, u32[]{:S(2)}) collective-permute-start(f32[2,128,128]{2,1,0:T(8,128)S(1)} %bitcast_add_fusion.9), channel_id=1, source_target_pairs={{0,4},{4,8},{8,12},{1,5},{5,9},{9,13},{2,6},{6,10},{10,14},{3,7},{... | collective-permute-start | bytes 393224 | tf_op jit(solution)/shard_map/ppermute | solution.py:58
  43.4 6.9 %collective-permute-start.4 = (f32[2,128,128]{2,1,0:T(8,128)S(1)}, f32[2,128,128]{2,1,0:T(8,128)S(1)}, u32[]{:S(2)}, u32[]{:S(2)}) collective-permute-start(f32[2,128,128]{2,1,0:T(8,128)S(1)} %bitcast_add_fusion.8), channel_id=1, source_target_pairs={{0,4},{4,8},{8,12},{1,5},{5,9},{9,13},{2,6},{6,10},{10,14},{3,7},{... | collective-permute-start | bytes 393224 | tf_op jit(solution)/shard_map/ppermute | solution.py:58
  51.0 6.9 %collective-permute-start.5 = (f32[2,128,128]{2,1,0:T(8,128)S(1)}, f32[2,128,128]{2,1,0:T(8,128)S(1)}, u32[]{:S(2)}, u32[]{:S(2)}) collective-permute-start(f32[2,128,128]{2,1,0:T(8,128)S(1)} %bitcast_add_fusion.7), channel_id=1, source_target_pairs={{0,4},{4,8},{8,12},{1,5},{5,9},{9,13},{2,6},{6,10},{10,14},{3,7},{... | collective-permute-start | bytes 393224 | tf_op jit(solution)/shard_map/ppermute | solution.py:58
  58.6 6.9 %collective-permute-start.6 = (f32[2,128,128]{2,1,0:T(8,128)S(1)}, f32[2,128,128]{2,1,0:T(8,128)S(1)}, u32[]{:S(2)}, u32[]{:S(2)}) collective-permute-start(f32[2,128,128]{2,1,0:T(8,128)S(1)} %bitcast_add_fusion.6), channel_id=1, source_target_pairs={{0,4},{4,8},{8,12},{1,5},{5,9},{9,13},{2,6},{6,10},{10,14},{3,7},{... | collective-permute-start | bytes 393224 | tf_op jit(solution)/shard_map/ppermute | solution.py:58
  66.2 2.0 %collective-permute-start.7 = (f32[8,128,128]{2,1,0:T(8,128)S(1)}, f32[8,128,128]{2,1,0:T(8,128)S(1)}, u32[]{:S(2)}, u32[]{:S(2)}) collective-permute-start(f32[8,128,128]{2,1,0:T(8,128)S(1)} %bitcast.203), channel_id=1, source_target_pairs={{0,1},{1,0},{2,3},{3,2},{4,5},{5,4},{6,7},{7,6},{8,9},{9,8},{10,11... | collective-permute-start | bytes 1572872 | tf_op jit(solution)/shard_map/ppermute | solution.py:20
  78.6 5.7 %copy-start.2 = (f32[16,128,128]{2,1,0:T(8,128)S(1)}, f32[16,128,128]{2,1,0:T(8,128)}, u32[]{:S(2)}) copy-start(f32[16,128,128]{2,1,0:T(8,128)} %get-tuple-element.168) | copy-start | bytes 3145732
  80.1 3.0 %collective-permute-start.8 = (f32[16,136,128]{2,1,0:T(8,128)S(1)}, f32[16,136,128]{2,1,0:T(8,128)}, u32[]{:S(2)}, u32[]{:S(2)}) collective-permute-start(f32[16,136,128]{2,1,0:T(8,128)S(1)} %fusion.2), channel_id=1, source_target_pairs={{0,1},{1,0},{2,3},{3,2},{4,5},{5,4},{6,7},{7,6},{8,9},{9,8},{10,11... | collective-permute-start | bytes 3342344 | tf_op jit(solution)/shard_map/ppermute | solution.py:20
  86.0 8.1 %collective-permute-start.9 = (f32[2,128,128]{2,1,0:T(8,128)S(1)}, f32[2,128,128]{2,1,0:T(8,128)S(1)}, u32[]{:S(2)}, u32[]{:S(2)}) collective-permute-start(f32[2,128,128]{2,1,0:T(8,128)S(1)} %bitcast_add_fusion.5), channel_id=1, source_target_pairs={{4,0},{8,4},{12,8},{5,1},{9,5},{13,9},{6,2},{10,6},{14,10},{7,3},{... | collective-permute-start | bytes 393224 | tf_op jit(solution)/shard_map/ppermute | solution.py:58
  95.0 18.2 %collective-permute-start.10 = (f32[2,128,128]{2,1,0:T(8,128)S(1)}, f32[2,128,128]{2,1,0:T(8,128)S(1)}, u32[]{:S(2)}, u32[]{:S(2)}) collective-permute-start(f32[2,128,128]{2,1,0:T(8,128)S(1)} %bitcast_add_fusion.4), channel_id=1, source_target_pairs={{4,0},{8,4},{12,8},{5,1},{9,5},{13,9},{6,2},{10,6},{14,10},{7,3},{... | collective-permute-start | bytes 393224 | tf_op jit(solution)/shard_map/ppermute | solution.py:58
  114.0 7.5 %collective-permute-start.11 = (f32[2,128,128]{2,1,0:T(8,128)S(1)}, f32[2,128,128]{2,1,0:T(8,128)S(1)}, u32[]{:S(2)}, u32[]{:S(2)}) collective-permute-start(f32[2,128,128]{2,1,0:T(8,128)S(1)} %bitcast_add_fusion.3), channel_id=1, source_target_pairs={{4,0},{8,4},{12,8},{5,1},{9,5},{13,9},{6,2},{10,6},{14,10},{7,3},{... | collective-permute-start | bytes 393224 | tf_op jit(solution)/shard_map/ppermute | solution.py:58
  122.3 6.9 %collective-permute-start.12 = (f32[2,128,128]{2,1,0:T(8,128)S(1)}, f32[2,128,128]{2,1,0:T(8,128)S(1)}, u32[]{:S(2)}, u32[]{:S(2)}) collective-permute-start(f32[2,128,128]{2,1,0:T(8,128)S(1)} %bitcast_add_fusion.2), channel_id=1, source_target_pairs={{4,0},{8,4},{12,8},{5,1},{9,5},{13,9},{6,2},{10,6},{14,10},{7,3},{... | collective-permute-start | bytes 393224 | tf_op jit(solution)/shard_map/ppermute | solution.py:58
  129.8 15.3 %copy-start.4 = (f32[16,1,128]{2,1,0:T(1,128)S(1)}, f32[16,1,128]{2,1,0:T(1,128)}, u32[]{:S(2)}) copy-start(f32[16,1,128]{2,1,0:T(1,128)} %get-tuple-element.169) | copy-start | bytes 24580
  129.9 6.9 %collective-permute-start.13 = (f32[2,128,128]{2,1,0:T(8,128)S(1)}, f32[2,128,128]{2,1,0:T(8,128)S(1)}, u32[]{:S(2)}, u32[]{:S(2)}) collective-permute-start(f32[2,128,128]{2,1,0:T(8,128)S(1)} %bitcast_add_fusion.1), channel_id=1, source_target_pairs={{4,0},{8,4},{12,8},{5,1},{9,5},{13,9},{6,2},{10,6},{14,10},{7,3},{... | collective-permute-start | bytes 393224 | tf_op jit(solution)/shard_map/ppermute | solution.py:58
  137.5 6.9 %collective-permute-start.14 = (f32[2,128,128]{2,1,0:T(8,128)S(1)}, f32[2,128,128]{2,1,0:T(8,128)S(1)}, u32[]{:S(2)}, u32[]{:S(2)}) collective-permute-start(f32[2,128,128]{2,1,0:T(8,128)S(1)} %bitcast_add_fusion), channel_id=1, source_target_pairs={{4,0},{8,4},{12,8},{5,1},{9,5},{13,9},{6,2},{10,6},{14,10},{7,3},{... | collective-permute-start | bytes 393224 | tf_op jit(solution)/shard_map/ppermute | solution.py:58
  145.1 10.0 %collective-permute-start.15 = (f32[8,128,128]{2,1,0:T(8,128)S(1)}, f32[8,128,128]{2,1,0:T(8,128)S(1)}, u32[]{:S(2)}, u32[]{:S(2)}) collective-permute-start(f32[8,128,128]{2,1,0:T(8,128)S(1)} %bitcast.202), channel_id=1, source_target_pairs={{0,1},{1,0},{2,3},{3,2},{4,5},{5,4},{6,7},{7,6},{8,9},{9,8},{10,11... | collective-permute-start | bytes 1572872 | tf_op jit(solution)/shard_map/ppermute | solution.py:20
  146.0 3.7 %collective-permute-start.16 = (f32[16,128]{1,0:T(8,128)S(1)}, f32[16,128]{1,0:T(8,128)S(1)}, u32[]{:S(2)}, u32[]{:S(2)}) collective-permute-start(f32[16,128]{1,0:T(8,128)S(1)} %bitcast.223), channel_id=1, source_target_pairs={{0,4},{4,0},{8,12},{12,8},{1,5},{5,1},{9,13},{13,9},{2,6},{6,2},{1... | collective-permute-start | bytes 24584 | tf_op jit(solution)/shard_map/ppermute | solution.py:106
  149.7 4.8 %collective-permute-start.17 = (f32[16,128]{1,0:T(8,128)S(1)}, f32[16,128]{1,0:T(8,128)S(1)}, u32[]{:S(2)}, u32[]{:S(2)}) collective-permute-start(f32[16,128]{1,0:T(8,128)S(1)} %add.229), channel_id=1, source_target_pairs={{0,8},{4,12},{8,0},{12,4},{1,9},{5,13},{9,1},{13,5},{2,10},{6,14},... | collective-permute-start | bytes 24584 | tf_op jit(solution)/shard_map/ppermute | solution.py:106

commit v7 on v6

--- a/solution.py
+++ b/solution.py
@@ -10,7 +10,7 @@
 PAD = 8
 CHUNKS = 4
 TIE_STEP = 1
-HB = 4
+HB = 8
 
 
 epsilon = 1e-06

time: 166 us -> 166 us (level)
  transfers between devices with their start and end apart: 18 -> 18, of which waited for: 15 -> 15; matrix products, arithmetic and copies ran while one was open for 4% -> 4% of each run, Pallas kernels for 15% -> 16%
where the time goes in v7:
time: 166 us; the launch traced here: 165 us
  Pallas kernels  49.2 us (30%)
  waiting for transfers between devices  48.3 us (29%)
  starting transfers between devices  39.7 us (24%)
  other arithmetic  23.3 us (14%)
  local copies, waits for them, and re-layouts  2.78 us (2%)
    pallas_call x5, Pallas kernels, _per_head(): pl.pallas_call(kernel, grid=(heads // HB,), in_specs=[spec(kind) for kind...  49.2 us
    ppermute x12, waiting for transfers between devices, chain_scan(): arrived = lax.ppermute(outgoing, 'ctx', perm=perm)  38 us
    ppermute x12, starting transfers between devices, chain_scan(): arrived = lax.ppermute(outgoing, 'ctx', perm=perm)  33.7 us
    scatter x12, other arithmetic, chain_scan(): prefix = prefix.at[slot].set(jnp.where(valid, arrived, prefix[slot]))  7.99 us
    ppermute x4, waiting for transfers between devices, swap_dp(): return lax.ppermute(x, 'dp', perm=[(0, 1), (1, 0)])  6.95 us
    ppermute x2, starting transfers between devices, backward_states(): gain_total = gain_total + lax.ppermute(gain_total, 'ctx', perm=partners)  5.14 us
    another operation x6, other arithmetic  4.51 us
    ppermute x2, waiting for transfers between devices, backward_states(): gain_total = gain_total + lax.ppermute(gain_total, 'ctx', perm=partners)  3.33 us
  transfers between devices with their start and end apart: 18, of which 15 were waited for; matrix products, arithmetic and copies ran while one was open for 4% of the time, Pallas kernels for 16%

profile of v7, /device:TPU:0, one launch (start us, length us, event | category | flops | bytes accessed | tf_op | source)
XLA Modules:
  0.0 165.0 jit_solution(673011013452962205)
XLA Ops:
  3.0 4.7 %shard_map.94 = f32[16,128,128]{2,1,0:T(8,128)} custom-call(bf16[512,2048]{1,0:T(8,128)(2,1)} %k_ref.7, bf16[512,2048]{1,0:T(8,128)(2,1)} %v_ref.7, f32[512,16]{1,0:T(8,128)} %copy.19.cum_ref, f32[16,512]{1,0:T(8,128)} %bitcast.216), custom_call_target="tpu_custom_call" | custom-call | flops 268435456 | bytes 4194304 | tf_op jit(solution)/shard_map/pallas_call | solution.py:234
  9.8 2.4 %collective-permute-done = f32[16,136,128]{2,1,0:T(8,128)S(1)} collective-permute-done((f32[16,136,128]{2,1,0:T(8,128)S(1)}, f32[16,136,128]{2,1,0:T(8,128)S(1)}, u32[]{:S(2)}, u32[]{:S(2)}) %collective-permute-start) | collective-permute-done | bytes 1114144 | tf_op jit(solution)/shard_map/ppermute | solution.py:20
  13.1 4.9 %collective-permute-start.1 = (f32[2,128,128]{2,1,0:T(8,128)S(1)}, f32[2,128,128]{2,1,0:T(8,128)S(1)}, u32[]{:S(2)}, u32[]{:S(2)}) collective-permute-start(f32[2,128,128]{2,1,0:T(8,128)S(1)} %bitcast_add_fusion.11), channel_id=1, source_target_pairs={{0,4},{4,8},{8,12},{1,5},{5,9},{9,13},{2,6},{6,10},{10,14},{3,7},{... | collective-permute-start | bytes 393224 | tf_op jit(solution)/shard_map/ppermute | solution.py:58
  18.8 2.2 %collective-permute-done.1 = f32[2,128,128]{2,1,0:T(8,128)S(1)} collective-permute-done((f32[2,128,128]{2,1,0:T(8,128)S(1)}, f32[2,128,128]{2,1,0:T(8,128)S(1)}, u32[]{:S(2)}, u32[]{:S(2)}) %collective-permute-start.1) | collective-permute-done | bytes 131104 | tf_op jit(solution)/shard_map/ppermute | solution.py:58
  21.8 4.4 %collective-permute-start.2 = (f32[2,128,128]{2,1,0:T(8,128)S(1)}, f32[2,128,128]{2,1,0:T(8,128)S(1)}, u32[]{:S(2)}, u32[]{:S(2)}) collective-permute-start(f32[2,128,128]{2,1,0:T(8,128)S(1)} %bitcast_add_fusion.10), channel_id=1, source_target_pairs={{0,4},{4,8},{8,12},{1,5},{5,9},{9,13},{2,6},{6,10},{10,14},{3,7},{... | collective-permute-start | bytes 393224 | tf_op jit(solution)/shard_map/ppermute | solution.py:58
  26.2 8.5 %shard_map.93.intra_ref = f32[512,2048]{1,0:T(8,128)} custom-call(bf16[512,2048]{1,0:T(8,128)(2,1)} %q_ref.5, bf16[512,2048]{1,0:T(8,128)(2,1)} %k_ref.7, bf16[512,2048]{1,0:T(8,128)(2,1)} %v_ref.7, f32[512,16]{1,0:T(8,128)} %copy.19.cum_ref, f32[16,512]{1,0:T(8,128)} %bitcast.217), custom_call_target="tpu_custom_call" | custom-call | flops 2147483648 | bytes 10485760 | tf_op jit(solution)/shard_map/pallas_call | solution.py:234
  35.5 3.5 %collective-permute-start.3 = (f32[2,128,128]{2,1,0:T(8,128)S(1)}, f32[2,128,128]{2,1,0:T(8,128)S(1)}, u32[]{:S(2)}, u32[]{:S(2)}) collective-permute-start(f32[2,128,128]{2,1,0:T(8,128)S(1)} %bitcast_add_fusion.9), channel_id=1, source_target_pairs={{0,4},{4,8},{8,12},{1,5},{5,9},{9,13},{2,6},{6,10},{10,14},{3,7},{... | collective-permute-start | bytes 393224 | tf_op jit(solution)/shard_map/ppermute | solution.py:58
  42.3 4.4 %collective-permute-start.4 = (f32[2,128,128]{2,1,0:T(8,128)S(1)}, f32[2,128,128]{2,1,0:T(8,128)S(1)}, u32[]{:S(2)}, u32[]{:S(2)}) collective-permute-start(f32[2,128,128]{2,1,0:T(8,128)S(1)} %bitcast_add_fusion.8), channel_id=1, source_target_pairs={{0,4},{4,8},{8,12},{1,5},{5,9},{9,13},{2,6},{6,10},{10,14},{3,7},{... | collective-permute-start | bytes 393224 | tf_op jit(solution)/shard_map/ppermute | solution.py:58
  46.7 2.5 %collective-permute-done.4 = f32[2,128,128]{2,1,0:T(8,128)S(1)} collective-permute-done((f32[2,128,128]{2,1,0:T(8,128)S(1)}, f32[2,128,128]{2,1,0:T(8,128)S(1)}, u32[]{:S(2)}, u32[]{:S(2)}) %collective-permute-start.4) | collective-permute-done | bytes 131104 | tf_op jit(solution)/shard_map/ppermute | solution.py:58
  49.9 4.4 %collective-permute-start.5 = (f32[2,128,128]{2,1,0:T(8,128)S(1)}, f32[2,128,128]{2,1,0:T(8,128)S(1)}, u32[]{:S(2)}, u32[]{:S(2)}) collective-permute-start(f32[2,128,128]{2,1,0:T(8,128)S(1)} %bitcast_add_fusion.7), channel_id=1, source_target_pairs={{0,4},{4,8},{8,12},{1,5},{5,9},{9,13},{2,6},{6,10},{10,14},{3,7},{... | collective-permute-start | bytes 393224 | tf_op jit(solution)/shard_map/ppermute | solution.py:58
  57.5 4.4 %collective-permute-start.6 = (f32[2,128,128]{2,1,0:T(8,128)S(1)}, f32[2,128,128]{2,1,0:T(8,128)S(1)}, u32[]{:S(2)}, u32[]{:S(2)}) collective-permute-start(f32[2,128,128]{2,1,0:T(8,128)S(1)} %bitcast_add_fusion.6), channel_id=1, source_target_pairs={{0,4},{4,8},{8,12},{1,5},{5,9},{9,13},{2,6},{6,10},{10,14},{3,7},{... | collective-permute-start | bytes 393224 | tf_op jit(solution)/shard_map/ppermute | solution.py:58
  61.9 2.5 %collective-permute-done.6 = f32[2,128,128]{2,1,0:T(8,128)S(1)} collective-permute-done((f32[2,128,128]{2,1,0:T(8,128)S(1)}, f32[2,128,128]{2,1,0:T(8,128)S(1)}, u32[]{:S(2)}, u32[]{:S(2)}) %collective-permute-start.6) | collective-permute-done | bytes 131104 | tf_op jit(solution)/shard_map/ppermute | solution.py:58
  65.2 1.8 %collective-permute-done.7 = f32[8,128,128]{2,1,0:T(8,128)S(1)} collective-permute-done((f32[8,128,128]{2,1,0:T(8,128)S(1)}, f32[8,128,128]{2,1,0:T(8,128)S(1)}, u32[]{:S(2)}, u32[]{:S(2)}) %collective-permute-start.7) | collective-permute-done | bytes 524320 | tf_op jit(solution)/shard_map/ppermute | solution.py:20
  68.1 10.0 %shard_map.95 = (bf16[512,2048]{1,0:T(8,128)(2,1)}, f32[16,128,128]{2,1,0:T(8,128)}, f32[16,1,128]{2,1,0:T(1,128)}) custom-call(bf16[512,2048]{1,0:T(8,128)(2,1)} %q_ref.5, bf16[512,2048]{1,0:T(8,128)(2,1)} %g_ref.1, f32[512,2048]{1,0:T(8,128)} %shard_map.93.intra_ref, bf16[16,128,128]{2,1,0:T(8,128)(2,1)} %select_convert_fusion.1.st_ref, ...), custom_call_target="tpu_custom_call" | custom-call | flops 536870912 | bytes 10485760 | tf_op jit(solution)/shard_map/pallas_call | solution.py:234
  79.7 2.8 %collective-permute-done.8 = f32[16,136,128]{2,1,0:T(8,128)} collective-permute-done((f32[16,136,128]{2,1,0:T(8,128)S(1)}, f32[16,136,128]{2,1,0:T(8,128)}, u32[]{:S(2)}, u32[]{:S(2)}) %collective-permute-start.8) | collective-permute-done | bytes 1114144 | tf_op jit(solution)/shard_map/ppermute | solution.py:20
  87.6 6.0 %collective-permute-done.9 = f32[2,128,128]{2,1,0:T(8,128)S(1)} collective-permute-done((f32[2,128,128]{2,1,0:T(8,128)S(1)}, f32[2,128,128]{2,1,0:T(8,128)S(1)}, u32[]{:S(2)}, u32[]{:S(2)}) %collective-permute-start.9) | collective-permute-done | bytes 131104 | tf_op jit(solution)/shard_map/ppermute | solution.py:58
  95.9 17.9 %shard_map.96 = (bf16[512,2048]{1,0:T(8,128)(2,1)}, f32[512,2048]{1,0:T(8,128)}, f32[512,2048]{1,0:T(8,128)}) custom-call(bf16[512,2048]{1,0:T(8,128)(2,1)} %q_ref.5, bf16[512,2048]{1,0:T(8,128)(2,1)} %k_ref.7, bf16[512,2048]{1,0:T(8,128)(2,1)} %v_ref.7, bf16[512,2048]{1,0:T(8,128)(2,1)} %get-tuple-element.164.og_ref, f32[512,16]{1,0:T(8,128)} %copy.19.cum_ref, ...), custom_call_target="tpu_custom_call" | custom-call | flops 5637144576 | bytes 18874368 | tf_op jit(solution)/shard_map/pallas_call | solution.py:234
  116.6 5.5 %collective-permute-done.11 = f32[2,128,128]{2,1,0:T(8,128)S(1)} collective-permute-done((f32[2,128,128]{2,1,0:T(8,128)S(1)}, f32[2,128,128]{2,1,0:T(8,128)S(1)}, u32[]{:S(2)}, u32[]{:S(2)}) %collective-permute-start.11) | collective-permute-done | bytes 131104 | tf_op jit(solution)/shard_map/ppermute | solution.py:58
  124.2 5.5 %collective-permute-done.12 = f32[2,128,128]{2,1,0:T(8,128)S(1)} collective-permute-done((f32[2,128,128]{2,1,0:T(8,128)S(1)}, f32[2,128,128]{2,1,0:T(8,128)S(1)}, u32[]{:S(2)}, u32[]{:S(2)}) %collective-permute-start.12) | collective-permute-done | bytes 131104 | tf_op jit(solution)/shard_map/ppermute | solution.py:58
  132.6 4.8 %collective-permute-done.13 = f32[2,128,128]{2,1,0:T(8,128)S(1)} collective-permute-done((f32[2,128,128]{2,1,0:T(8,128)S(1)}, f32[2,128,128]{2,1,0:T(8,128)S(1)}, u32[]{:S(2)}, u32[]{:S(2)}) %collective-permute-start.13) | collective-permute-done | bytes 131104 | tf_op jit(solution)/shard_map/ppermute | solution.py:58
  139.4 5.5 %collective-permute-done.14 = f32[2,128,128]{2,1,0:T(8,128)S(1)} collective-permute-done((f32[2,128,128]{2,1,0:T(8,128)S(1)}, f32[2,128,128]{2,1,0:T(8,128)S(1)}, u32[]{:S(2)}, u32[]{:S(2)}) %collective-permute-start.14) | collective-permute-done | bytes 131104 | tf_op jit(solution)/shard_map/ppermute | solution.py:58
  146.6 2.0 %collective-permute-start.16 = (f32[16,128]{1,0:T(8,128)S(1)}, f32[16,128]{1,0:T(8,128)S(1)}, u32[]{:S(2)}, u32[]{:S(2)}) collective-permute-start(f32[16,128]{1,0:T(8,128)S(1)} %bitcast.223), channel_id=1, source_target_pairs={{0,4},{4,0},{8,12},{12,8},{1,5},{5,1},{9,13},{13,9},{2,6},{6,2},{1... | collective-permute-start | bytes 24584 | tf_op jit(solution)/shard_map/ppermute | solution.py:106
  150.3 3.1 %collective-permute-start.17 = (f32[16,128]{1,0:T(8,128)S(1)}, f32[16,128]{1,0:T(8,128)S(1)}, u32[]{:S(2)}, u32[]{:S(2)}) collective-permute-start(f32[16,128]{1,0:T(8,128)S(1)} %add.229), channel_id=1, source_target_pairs={{0,8},{4,12},{8,0},{12,4},{1,9},{5,13},{9,1},{13,5},{2,10},{6,14},... | collective-permute-start | bytes 24584 | tf_op jit(solution)/shard_map/ppermute | solution.py:106
  156.8 8.1 %shard_map.97 = (bf16[512,2048]{1,0:T(8,128)(2,1)}, bf16[512,2048]{1,0:T(8,128)(2,1)}) custom-call(bf16[512,2048]{1,0:T(8,128)(2,1)} %k_ref.7, bf16[512,2048]{1,0:T(8,128)(2,1)} %v_ref.7, f32[512,2048]{1,0:T(8,128)} %get-tuple-element.171.kg_ref, f32[512,2048]{1,0:T(8,128)} %get-tuple-element.172.vg_ref, bf16[16,128,128]{2,1,0:T(8,128)(2,1)} %select_convert_fusion.gl_ref, ...), custom_call_target="tpu_custom_call" | custom-call | flops 536870912 | bytes 16777216 | tf_op jit(solution)/shard_map/pallas_call | solution.py:234
  (104 shorter events, 42.2 us)
Async XLA Ops:
  0.6 0.8 copy-start
  1.8 1.2 copy-start.3
  7.8 4.8 %copy-start.1 = (f32[16,128,128]{2,1,0:T(8,128)S(1)}, f32[16,128,128]{2,1,0:T(8,128)}, u32[]{:S(2)}) copy-start(f32[16,128,128]{2,1,0:T(8,128)} %shard_map.94) | copy-start | bytes 3145732
  9.3 2.9 %collective-permute-start = (f32[16,136,128]{2,1,0:T(8,128)S(1)}, f32[16,136,128]{2,1,0:T(8,128)S(1)}, u32[]{:S(2)}, u32[]{:S(2)}) collective-permute-start(f32[16,136,128]{2,1,0:T(8,128)S(1)} %fusion), channel_id=1, source_target_pairs={{0,1},{1,0},{2,3},{3,2},{4,5},{5,4},{6,7},{7,6},{8,9},{9,8},{10,11... | collective-permute-start | bytes 3342344 | tf_op jit(solution)/shard_map/ppermute | solution.py:20
  12.8 5.1 %copy-start.5 = (s32[4]{0:T(128)S(1)}, s32[4]{0:T(128)}, u32[]{:S(2)}) copy-start(s32[4]{0:T(128)} %constant.298.clone.1) | copy-start | bytes 52
  13.1 7.9 %collective-permute-start.1 = (f32[2,128,128]{2,1,0:T(8,128)S(1)}, f32[2,128,128]{2,1,0:T(8,128)S(1)}, u32[]{:S(2)}, u32[]{:S(2)}) collective-permute-start(f32[2,128,128]{2,1,0:T(8,128)S(1)} %bitcast_add_fusion.11), channel_id=1, source_target_pairs={{0,4},{4,8},{8,12},{1,5},{5,9},{9,13},{2,6},{6,10},{10,14},{3,7},{... | collective-permute-start | bytes 393224 | tf_op jit(solution)/shard_map/ppermute | solution.py:58
  21.8 12.9 %collective-permute-start.2 = (f32[2,128,128]{2,1,0:T(8,128)S(1)}, f32[2,128,128]{2,1,0:T(8,128)S(1)}, u32[]{:S(2)}, u32[]{:S(2)}) collective-permute-start(f32[2,128,128]{2,1,0:T(8,128)S(1)} %bitcast_add_fusion.10), channel_id=1, source_target_pairs={{0,4},{4,8},{8,12},{1,5},{5,9},{9,13},{2,6},{6,10},{10,14},{3,7},{... | collective-permute-start | bytes 393224 | tf_op jit(solution)/shard_map/ppermute | solution.py:58
  35.5 6.0 %collective-permute-start.3 = (f32[2,128,128]{2,1,0:T(8,128)S(1)}, f32[2,128,128]{2,1,0:T(8,128)S(1)}, u32[]{:S(2)}, u32[]{:S(2)}) collective-permute-start(f32[2,128,128]{2,1,0:T(8,128)S(1)} %bitcast_add_fusion.9), channel_id=1, source_target_pairs={{0,4},{4,8},{8,12},{1,5},{5,9},{9,13},{2,6},{6,10},{10,14},{3,7},{... | collective-permute-start | bytes 393224 | tf_op jit(solution)/shard_map/ppermute | solution.py:58
  42.3 6.9 %collective-permute-start.4 = (f32[2,128,128]{2,1,0:T(8,128)S(1)}, f32[2,128,128]{2,1,0:T(8,128)S(1)}, u32[]{:S(2)}, u32[]{:S(2)}) collective-permute-start(f32[2,128,128]{2,1,0:T(8,128)S(1)} %bitcast_add_fusion.8), channel_id=1, source_target_pairs={{0,4},{4,8},{8,12},{1,5},{5,9},{9,13},{2,6},{6,10},{10,14},{3,7},{... | collective-permute-start | bytes 393224 | tf_op jit(solution)/shard_map/ppermute | solution.py:58
  49.9 6.9 %collective-permute-start.5 = (f32[2,128,128]{2,1,0:T(8,128)S(1)}, f32[2,128,128]{2,1,0:T(8,128)S(1)}, u32[]{:S(2)}, u32[]{:S(2)}) collective-permute-start(f32[2,128,128]{2,1,0:T(8,128)S(1)} %bitcast_add_fusion.7), channel_id=1, source_target_pairs={{0,4},{4,8},{8,12},{1,5},{5,9},{9,13},{2,6},{6,10},{10,14},{3,7},{... | collective-permute-start | bytes 393224 | tf_op jit(solution)/shard_map/ppermute | solution.py:58
  57.5 6.9 %collective-permute-start.6 = (f32[2,128,128]{2,1,0:T(8,128)S(1)}, f32[2,128,128]{2,1,0:T(8,128)S(1)}, u32[]{:S(2)}, u32[]{:S(2)}) collective-permute-start(f32[2,128,128]{2,1,0:T(8,128)S(1)} %bitcast_add_fusion.6), channel_id=1, source_target_pairs={{0,4},{4,8},{8,12},{1,5},{5,9},{9,13},{2,6},{6,10},{10,14},{3,7},{... | collective-permute-start | bytes 393224 | tf_op jit(solution)/shard_map/ppermute | solution.py:58
  65.0 2.0 %collective-permute-start.7 = (f32[8,128,128]{2,1,0:T(8,128)S(1)}, f32[8,128,128]{2,1,0:T(8,128)S(1)}, u32[]{:S(2)}, u32[]{:S(2)}) collective-permute-start(f32[8,128,128]{2,1,0:T(8,128)S(1)} %bitcast.203), channel_id=1, source_target_pairs={{0,1},{1,0},{2,3},{3,2},{4,5},{5,4},{6,7},{7,6},{8,9},{9,8},{10,11... | collective-permute-start | bytes 1572872 | tf_op jit(solution)/shard_map/ppermute | solution.py:20
  78.1 5.7 %copy-start.2 = (f32[16,128,128]{2,1,0:T(8,128)S(1)}, f32[16,128,128]{2,1,0:T(8,128)}, u32[]{:S(2)}) copy-start(f32[16,128,128]{2,1,0:T(8,128)} %get-tuple-element.168) | copy-start | bytes 3145732
  79.5 3.0 %collective-permute-start.8 = (f32[16,136,128]{2,1,0:T(8,128)S(1)}, f32[16,136,128]{2,1,0:T(8,128)}, u32[]{:S(2)}, u32[]{:S(2)}) collective-permute-start(f32[16,136,128]{2,1,0:T(8,128)S(1)} %fusion.2), channel_id=1, source_target_pairs={{0,1},{1,0},{2,3},{3,2},{4,5},{5,4},{6,7},{7,6},{8,9},{9,8},{10,11... | collective-permute-start | bytes 3342344 | tf_op jit(solution)/shard_map/ppermute | solution.py:20
  85.4 8.1 %collective-permute-start.9 = (f32[2,128,128]{2,1,0:T(8,128)S(1)}, f32[2,128,128]{2,1,0:T(8,128)S(1)}, u32[]{:S(2)}, u32[]{:S(2)}) collective-permute-start(f32[2,128,128]{2,1,0:T(8,128)S(1)} %bitcast_add_fusion.5), channel_id=1, source_target_pairs={{4,0},{8,4},{12,8},{5,1},{9,5},{13,9},{6,2},{10,6},{14,10},{7,3},{... | collective-permute-start | bytes 393224 | tf_op jit(solution)/shard_map/ppermute | solution.py:58
  94.4 19.4 %collective-permute-start.10 = (f32[2,128,128]{2,1,0:T(8,128)S(1)}, f32[2,128,128]{2,1,0:T(8,128)S(1)}, u32[]{:S(2)}, u32[]{:S(2)}) collective-permute-start(f32[2,128,128]{2,1,0:T(8,128)S(1)} %bitcast_add_fusion.4), channel_id=1, source_target_pairs={{4,0},{8,4},{12,8},{5,1},{9,5},{13,9},{6,2},{10,6},{14,10},{7,3},{... | collective-permute-start | bytes 393224 | tf_op jit(solution)/shard_map/ppermute | solution.py:58
  114.5 7.6 %collective-permute-start.11 = (f32[2,128,128]{2,1,0:T(8,128)S(1)}, f32[2,128,128]{2,1,0:T(8,128)S(1)}, u32[]{:S(2)}, u32[]{:S(2)}) collective-permute-start(f32[2,128,128]{2,1,0:T(8,128)S(1)} %bitcast_add_fusion.3), channel_id=1, source_target_pairs={{4,0},{8,4},{12,8},{5,1},{9,5},{13,9},{6,2},{10,6},{14,10},{7,3},{... | collective-permute-start | bytes 393224 | tf_op jit(solution)/shard_map/ppermute | solution.py:58
  122.9 6.9 %collective-permute-start.12 = (f32[2,128,128]{2,1,0:T(8,128)S(1)}, f32[2,128,128]{2,1,0:T(8,128)S(1)}, u32[]{:S(2)}, u32[]{:S(2)}) collective-permute-start(f32[2,128,128]{2,1,0:T(8,128)S(1)} %bitcast_add_fusion.2), channel_id=1, source_target_pairs={{4,0},{8,4},{12,8},{5,1},{9,5},{13,9},{6,2},{10,6},{14,10},{7,3},{... | collective-permute-start | bytes 393224 | tf_op jit(solution)/shard_map/ppermute | solution.py:58
  130.4 15.3 %copy-start.4 = (f32[16,1,128]{2,1,0:T(1,128)S(1)}, f32[16,1,128]{2,1,0:T(1,128)}, u32[]{:S(2)}) copy-start(f32[16,1,128]{2,1,0:T(1,128)} %get-tuple-element.169) | copy-start | bytes 24580
  130.5 6.9 %collective-permute-start.13 = (f32[2,128,128]{2,1,0:T(8,128)S(1)}, f32[2,128,128]{2,1,0:T(8,128)S(1)}, u32[]{:S(2)}, u32[]{:S(2)}) collective-permute-start(f32[2,128,128]{2,1,0:T(8,128)S(1)} %bitcast_add_fusion.1), channel_id=1, source_target_pairs={{4,0},{8,4},{12,8},{5,1},{9,5},{13,9},{6,2},{10,6},{14,10},{7,3},{... | collective-permute-start | bytes 393224 | tf_op jit(solution)/shard_map/ppermute | solution.py:58
  138.1 6.9 %collective-permute-start.14 = (f32[2,128,128]{2,1,0:T(8,128)S(1)}, f32[2,128,128]{2,1,0:T(8,128)S(1)}, u32[]{:S(2)}, u32[]{:S(2)}) collective-permute-start(f32[2,128,128]{2,1,0:T(8,128)S(1)} %bitcast_add_fusion), channel_id=1, source_target_pairs={{4,0},{8,4},{12,8},{5,1},{9,5},{13,9},{6,2},{10,6},{14,10},{7,3},{... | collective-permute-start | bytes 393224 | tf_op jit(solution)/shard_map/ppermute | solution.py:58
  145.6 10.0 %collective-permute-start.15 = (f32[8,128,128]{2,1,0:T(8,128)S(1)}, f32[8,128,128]{2,1,0:T(8,128)S(1)}, u32[]{:S(2)}, u32[]{:S(2)}) collective-permute-start(f32[8,128,128]{2,1,0:T(8,128)S(1)} %bitcast.202), channel_id=1, source_target_pairs={{0,1},{1,0},{2,3},{3,2},{4,5},{5,4},{6,7},{7,6},{8,9},{9,8},{10,11... | collective-permute-start | bytes 1572872 | tf_op jit(solution)/shard_map/ppermute | solution.py:20
  146.6 3.7 %collective-permute-start.16 = (f32[16,128]{1,0:T(8,128)S(1)}, f32[16,128]{1,0:T(8,128)S(1)}, u32[]{:S(2)}, u32[]{:S(2)}) collective-permute-start(f32[16,128]{1,0:T(8,128)S(1)} %bitcast.223), channel_id=1, source_target_pairs={{0,4},{4,0},{8,12},{12,8},{1,5},{5,1},{9,13},{13,9},{2,6},{6,2},{1... | collective-permute-start | bytes 24584 | tf_op jit(solution)/shard_map/ppermute | solution.py:106
  150.3 4.8 %collective-permute-start.17 = (f32[16,128]{1,0:T(8,128)S(1)}, f32[16,128]{1,0:T(8,128)S(1)}, u32[]{:S(2)}, u32[]{:S(2)}) collective-permute-start(f32[16,128]{1,0:T(8,128)S(1)} %add.229), channel_id=1, source_target_pairs={{0,8},{4,12},{8,0},{12,4},{1,9},{5,13},{9,1},{13,5},{2,10},{6,14},... | collective-permute-start | bytes 24584 | tf_op jit(solution)/shard_map/ppermute | solution.py:106

commit v8 on v6

--- a/solution.py
+++ b/solution.py
@@ -1,3 +1,4 @@
+import functools
 import math
 
 import jax
@@ -9,7 +10,6 @@
 DH = 128
 PAD = 8
 CHUNKS = 4
-TIE_STEP = 1
 HB = 4
 
 
@@ -38,7 +38,7 @@
     return jnp.concatenate([first, second], axis=0)
 
 
-def chain_scan(chip_state, chip_decay, later, cover):
+def chain_scan(chip_state, chip_decay, later, pieces_of_cover):
     chips = lax.axis_size("ctx")
     z = lax.axis_index("ctx")
     heads = chip_state.shape[0]
@@ -52,7 +52,9 @@
     else:
         perm = [(i, i + 1) for i in range(chips - 1)]
     prefix = jnp.zeros_like(pieces)
-    for step in range(count + chips - 2):
+    cover = None
+    steps = count + chips - 2
+    for step in range(steps):
         send = jnp.clip(step - rank, 0, count - 1)
         outgoing = factor[send] * prefix[send] + pieces[send]
         arrived = lax.ppermute(outgoing, "ctx", perm=perm)
@@ -60,8 +62,11 @@
         valid = (where_to >= 0) & (where_to < count) & (rank >= 1)
         slot = jnp.clip(where_to, 0, count - 1)
         prefix = prefix.at[slot].set(jnp.where(valid, arrived, prefix[slot]))
-        if step == TIE_STEP:
+        if step < len(pieces_of_cover):
+            cover = pieces_of_cover[step](cover)
             cover, prefix = lax.optimization_barrier((cover, prefix))
+    for piece in pieces_of_cover[steps:]:
+        cover = piece(cover)
     return prefix.reshape(heads, DH, DH), cover
 
 
@@ -140,8 +145,8 @@
     return (_nt(q, k) * decay).astype(jnp.bfloat16)
 
 
-def _head_vectors(cum_ref, cumt_ref, j):
-    h = pl.program_id(0) * HB + j
+def _head_vectors(cum_ref, cumt_ref, j, first=0):
+    h = (pl.program_id(0) + first) * HB + j
     full = cum_ref[...]
     lane = lax.broadcasted_iota(jnp.int32, full.shape, 1)
     col = jnp.sum(jnp.where(lane == h, full, 0.0), axis=1, keepdims=True)
@@ -162,10 +167,10 @@
         s_ref[j] = _tn(scaled, v_ref[:, cols])
 
 
-def intra_kernel(q_ref, k_ref, v_ref, cum_ref, cumt_ref, out_ref):
-    for j in range(HB):
-        cols = _lanes(j)
-        col, row, _, _ = _head_vectors(cum_ref, cumt_ref, j)
+def intra_kernel(first, q_ref, k_ref, v_ref, cum_ref, cumt_ref, out_ref):
+    for j in range(HB):
+        cols = _lanes(j)
+        col, row, _, _ = _head_vectors(cum_ref, cumt_ref, j, first)
         decay = _decay(col, row)
         out_ref[:, cols] = _nn(_masked(q_ref[:, cols], k_ref[:, cols], decay), v_ref[:, cols])
 
@@ -191,10 +196,10 @@
         m_ref[j] = _tn(q_scaled, out_grad)
 
 
-def grads_kernel(q_ref, k_ref, v_ref, og_ref, cum_ref, cumt_ref, st_ref, qg_ref, kg_ref, vg_ref):
-    for j in range(HB):
-        cols = _lanes(j)
-        col, row, grow, _ = _head_vectors(cum_ref, cumt_ref, j)
+def grads_kernel(first, q_ref, k_ref, v_ref, og_ref, cum_ref, cumt_ref, st_ref, qg_ref, kg_ref, vg_ref):
+    for j in range(HB):
+        cols = _lanes(j)
+        col, row, grow, _ = _head_vectors(cum_ref, cumt_ref, j, first)
         decay = _decay(col, row)
         q, k, v, og = q_ref[:, cols], k_ref[:, cols], v_ref[:, cols], og_ref[:, cols]
         masked = _masked(q, k, decay)
@@ -213,17 +218,22 @@
         vo_ref[:, cols] = (vg_ref[:, cols] + toend * _nn(k_ref[:, cols], grad_low)).astype(jnp.bfloat16)
 
 
-def _per_head(kernel, ins, outs, heads, length, flops, nbytes, exps=0):
+def _per_head(kernel, ins, outs, heads, length, flops, nbytes, exps=0, part=None, into=None):
+    groups = heads // HB
+    first, count = (0, groups) if part is None else (part, 1)
+    if part is not None:
+        kernel = functools.partial(kernel, first)
+
     def spec(kind):
         if kind == "rows":
-            return pl.BlockSpec((length, HB * DH), lambda i: (0, i))
+            return pl.BlockSpec((length, HB * DH), lambda i: (0, i + first))
         if kind == "cum":
             return pl.BlockSpec((length, heads), lambda i: (0, 0))
         if kind == "cumt":
             return pl.BlockSpec((heads, length), lambda i: (0, 0))
         if kind == "gain":
-            return pl.BlockSpec((HB, 1, DH), lambda i: (i, 0, 0))
-        return pl.BlockSpec((HB, DH, DH), lambda i: (i, 0, 0))
+            return pl.BlockSpec((HB, 1, DH), lambda i: (i + first, 0, 0))
+        return pl.BlockSpec((HB, DH, DH), lambda i: (i + first, 0, 0))
 
     shapes = {
         "rows": (length, heads * DH),
@@ -231,14 +241,31 @@
         "square": (heads, DH, DH),
     }
     out_shape = [jax.ShapeDtypeStruct(shapes[kind], dtype) for kind, dtype in outs]
+    in_specs = [spec(kind) for kind, _ in ins]
+    operands = [x for _, x in ins]
+    aliases = {}
+    body = kernel
+    if into is not None:
+        given = len(ins)
+        in_specs += [pl.BlockSpec(memory_space=pl.ANY) for _ in into]
+        operands += list(into)
+        aliases = {given + i: i for i in range(len(into))}
+
+        def body(*refs):
+            kernel(*refs[:given], *refs[given + len(into) :])
+
+    share = count / groups
     return pl.pallas_call(
-        kernel,
-        grid=(heads // HB,),
-        in_specs=[spec(kind) for kind, _ in ins],
+        body,
+        grid=(count,),
+        in_specs=in_specs,
         out_specs=[spec(kind) for kind, _ in outs],
         out_shape=out_shape,
-        cost_estimate=pl.CostEstimate(flops=flops, transcendentals=exps, bytes_accessed=nbytes),
-    )(*[x for _, x in ins])
+        input_output_aliases=aliases,
+        cost_estimate=pl.CostEstimate(
+            flops=int(flops * share), transcendentals=int(exps * share), bytes_accessed=int(nbytes * share)
+        ),
+    )(*operands)
 
 
 def on_device(query_rows, key_rows, value_rows, cotangent, log_decay, norm_gain):
@@ -264,13 +291,18 @@
         [("square", f32)],
         heads, length, small, 2 * rows_bytes,
     )
-    (intra,) = _per_head(
-        intra_kernel,
-        [("rows", q), ("rows", k), ("rows", v), ("cum", cum), ("cumt", cum_t)],
-        [("rows", f32)],
-        heads, length, 2 * big, 5 * rows_bytes, heads * length * length,
-    )
-    state_in, intra = forward_states(local_state, final_log, intra)
+    def intra_piece(part, done):
+        return _per_head(
+            intra_kernel,
+            [("rows", q), ("rows", k), ("rows", v), ("cum", cum), ("cumt", cum_t)],
+            [("rows", f32)],
+            heads, length, 2 * big, 5 * rows_bytes, heads * length * length, part=part, into=done,
+        )
+
+    groups = heads // HB
+    state_in, (intra,) = forward_states(
+        local_state, final_log, [functools.partial(intra_piece, p) for p in range(groups)]
+    )
     state_low = state_in.astype(bf16)
     out_grad, moment, gain_part = _per_head(
         norm_kernel,
@@ -278,15 +310,17 @@
         [("rows", bf16), ("square", f32), ("gain", f32)],
         heads, length, 2 * small, 5 * rows_bytes,
     )
-    query_grad, key_part, value_part = _per_head(
-        grads_kernel,
-        [("rows", q), ("rows", k), ("rows", v), ("rows", out_grad), ("cum", cum), ("cumt", cum_t),
-         ("square", state_low)],
-        [("rows", bf16), ("rows", f32), ("rows", f32)],
-        heads, length, 5 * big + small, 9 * rows_bytes, heads * length * length,
-    )
+    def grads_piece(part, done):
+        return _per_head(
+            grads_kernel,
+            [("rows", q), ("rows", k), ("rows", v), ("rows", out_grad), ("cum", cum), ("cumt", cum_t),
+             ("square", state_low)],
+            [("rows", bf16), ("rows", f32), ("rows", f32)],
+            heads, length, 5 * big + small, 9 * rows_bytes, heads * length * length, part=part, into=done,
+        )
+
     grad_state, gain_sum, (query_grad, key_part, value_part) = backward_states(
-        moment, final_log, gain_part.reshape(heads * DH), (query_grad, key_part, value_part)
+        moment, final_log, gain_part.reshape(heads * DH), [functools.partial(grads_piece, p) for p in range(groups)]
     )
     grad_low = grad_state.astype(bf16)
     key_grad, value_grad = _per_head(

time: 166 us -> 155 us (0.934)
  waiting for transfers between devices: 48.3 us -> 26.8 us
  Pallas kernels: 49.1 us -> 64.3 us
  starting transfers between devices: 39.6 us -> 36 us
    ppermute x12, waiting for transfers between devices: 38 us -> 18.5 us  [chain_scan(): arrived = lax.ppermute(outgoing, 'ctx', perm=perm)]
    pallas_call x5 -> x11, Pallas kernels: 49.1 us -> 64.3 us  [_per_head(): pl.pallas_call(body, grid=(count,), in_specs=in_specs, out_specs=[spec(ki...]
    ppermute x12, starting transfers between devices: 33.6 us -> 30.6 us  [chain_scan(): arrived = lax.ppermute(outgoing, 'ctx', perm=perm)]
    ppermute x4, waiting for transfers between devices: 6.95 us -> 4.68 us  [swap_dp(): return lax.ppermute(x, 'dp', perm=[(0, 1), (1, 0)])]
  transfers between devices with their start and end apart: 18 -> 18, of which waited for: 15 -> 13; matrix products, arithmetic and copies ran while one was open for 4% -> 4% of each run, Pallas kernels for 15% -> 26%
where the time goes in v8:
time: 155 us; the launch traced here: 154 us
  Pallas kernels  64.3 us (41%)
  starting transfers between devices  36 us (23%)
  waiting for transfers between devices  26.8 us (17%)
  other arithmetic  22.9 us (15%)
  local copies, waits for them, and re-layouts  2.78 us (2%)
    pallas_call x11, Pallas kernels, _per_head(): pl.pallas_call(body, grid=(count,), in_specs=in_specs, out_specs=[spec(ki...  64.3 us
    ppermute x12, starting transfers between devices, chain_scan(): arrived = lax.ppermute(outgoing, 'ctx', perm=perm)  30.6 us
    ppermute x12, waiting for transfers between devices, chain_scan(): arrived = lax.ppermute(outgoing, 'ctx', perm=perm)  18.5 us
    scatter x12, other arithmetic, chain_scan(): prefix = prefix.at[slot].set(jnp.where(valid, arrived, prefix[slot]))  7.63 us
    ppermute x4, waiting for transfers between devices, swap_dp(): return lax.ppermute(x, 'dp', perm=[(0, 1), (1, 0)])  4.68 us
    ppermute x2, starting transfers between devices, backward_states(): gain_total = gain_total + lax.ppermute(gain_total, 'ctx', perm=partners)  4.59 us
    another operation x6, other arithmetic  4.41 us
    ppermute x2, waiting for transfers between devices, backward_states(): gain_total = gain_total + lax.ppermute(gain_total, 'ctx', perm=partners)  3.68 us
  transfers between devices with their start and end apart: 18, of which 13 were waited for; matrix products, arithmetic and copies ran while one was open for 4% of the time, Pallas kernels for 26%

profile of v8, /device:TPU:0, one launch (start us, length us, event | category | flops | bytes accessed | tf_op | source)
XLA Modules:
  0.0 154.3 jit_solution(7529043533992517808)
XLA Ops:
  3.0 5.8 %shard_map.94 = f32[16,128,128]{2,1,0:T(8,128)} custom-call(bf16[512,2048]{1,0:T(8,128)(2,1)} %k_ref.7, bf16[512,2048]{1,0:T(8,128)(2,1)} %v_ref.7, f32[512,16]{1,0:T(8,128)} %copy.42.cum_ref.refs_3_.refs_4_, f32[16,512]{1,0:T(8,128)} %bitcast.204), custom_call_target="tpu_custom_call" | custom-call | flops 268435456 | bytes 4194304 | tf_op jit(solution)/shard_map/pallas_call | solution.py:258
  14.1 4.9 %collective-permute-start.1 = (f32[2,128,128]{2,1,0:T(8,128)S(1)}, f32[2,128,128]{2,1,0:T(8,128)S(1)}, u32[]{:S(2)}, u32[]{:S(2)}) collective-permute-start(f32[2,128,128]{2,1,0:T(8,128)S(1)} %bitcast_add_fusion.11), channel_id=1, source_target_pairs={{0,4},{4,8},{8,12},{1,5},{5,9},{9,13},{2,6},{6,10},{10,14},{3,7},{... | collective-permute-start | bytes 393224 | tf_op jit(solution)/shard_map/ppermute | solution.py:60
  19.0 3.9 %shard_map.93.refs_5_ = f32[512,2048]{1,0:T(8,128)} custom-call(bf16[512,2048]{1,0:T(8,128)(2,1)} %refs_0_.11, bf16[512,2048]{1,0:T(8,128)(2,1)} %k_ref.7, bf16[512,2048]{1,0:T(8,128)(2,1)} %v_ref.7, f32[512,16]{1,0:T(8,128)} %copy.42.cum_ref.refs_3_.refs_4_, f32[16,512]{1,0:T(8,128)} %bitcast.205), custom_call_target="tpu_custom_call" | custom-call | flops 536870912 | bytes 2621440 | tf_op jit(solution)/shard_map/pallas_call | solution.py:258
  24.4 3.5 %collective-permute-start.2 = (f32[2,128,128]{2,1,0:T(8,128)S(1)}, f32[2,128,128]{2,1,0:T(8,128)S(1)}, u32[]{:S(2)}, u32[]{:S(2)}) collective-permute-start(f32[2,128,128]{2,1,0:T(8,128)S(1)} %bitcast_add_fusion.10), channel_id=1, source_target_pairs={{0,4},{4,8},{8,12},{1,5},{5,9},{9,13},{2,6},{6,10},{10,14},{3,7},{... | collective-permute-start | bytes 393224 | tf_op jit(solution)/shard_map/ppermute | solution.py:60
  27.9 3.9 %shard_map.95.refs_5_ = f32[512,2048]{1,0:T(8,128)} custom-call(bf16[512,2048]{1,0:T(8,128)(2,1)} %refs_0_.11, bf16[512,2048]{1,0:T(8,128)(2,1)} %k_ref.7, bf16[512,2048]{1,0:T(8,128)(2,1)} %v_ref.7, f32[512,16]{1,0:T(8,128)} %copy.42.cum_ref.refs_3_.refs_4_, f32[16,512]{1,0:T(8,128)} %bitcast.206, ...), custom_call_target="tpu_custom_call", output_to_operand_aliasing={{}: (5, {})} | custom-call | flops 536870912 | bytes 2621440 | tf_op jit(solution)/shard_map/pallas_call | solution.py:258
  32.5 3.5 %collective-permute-start.3 = (f32[2,128,128]{2,1,0:T(8,128)S(1)}, f32[2,128,128]{2,1,0:T(8,128)S(1)}, u32[]{:S(2)}, u32[]{:S(2)}) collective-permute-start(f32[2,128,128]{2,1,0:T(8,128)S(1)} %bitcast_add_fusion.9), channel_id=1, source_target_pairs={{0,4},{4,8},{8,12},{1,5},{5,9},{9,13},{2,6},{6,10},{10,14},{3,7},{... | collective-permute-start | bytes 393224 | tf_op jit(solution)/shard_map/ppermute | solution.py:60
  36.0 3.8 %shard_map.96.refs_5_ = f32[512,2048]{1,0:T(8,128)} custom-call(bf16[512,2048]{1,0:T(8,128)(2,1)} %refs_0_.11, bf16[512,2048]{1,0:T(8,128)(2,1)} %k_ref.7, bf16[512,2048]{1,0:T(8,128)(2,1)} %v_ref.7, f32[512,16]{1,0:T(8,128)} %copy.42.cum_ref.refs_3_.refs_4_, f32[16,512]{1,0:T(8,128)} %bitcast.207, ...), custom_call_target="tpu_custom_call", output_to_operand_aliasing={{}: (5, {})} | custom-call | flops 536870912 | bytes 2621440 | tf_op jit(solution)/shard_map/pallas_call | solution.py:258
  40.5 3.2 %collective-permute-start.4 = (f32[2,128,128]{2,1,0:T(8,128)S(1)}, f32[2,128,128]{2,1,0:T(8,128)S(1)}, u32[]{:S(2)}, u32[]{:S(2)}) collective-permute-start(f32[2,128,128]{2,1,0:T(8,128)S(1)} %bitcast_add_fusion.8), channel_id=1, source_target_pairs={{0,4},{4,8},{8,12},{1,5},{5,9},{9,13},{2,6},{6,10},{10,14},{3,7},{... | collective-permute-start | bytes 393224 | tf_op jit(solution)/shard_map/ppermute | solution.py:60
  43.7 3.8 %shard_map.97.intra_ref = f32[512,2048]{1,0:T(8,128)} custom-call(bf16[512,2048]{1,0:T(8,128)(2,1)} %refs_0_.11, bf16[512,2048]{1,0:T(8,128)(2,1)} %k_ref.7, bf16[512,2048]{1,0:T(8,128)(2,1)} %v_ref.7, f32[512,16]{1,0:T(8,128)} %copy.42.cum_ref.refs_3_.refs_4_, f32[16,512]{1,0:T(8,128)} %bitcast.208, ...), custom_call_target="tpu_custom_call", output_to_operand_aliasing={{}: (5, {})} | custom-call | flops 536870912 | bytes 2621440 | tf_op jit(solution)/shard_map/pallas_call | solution.py:258
  48.3 3.0 %collective-permute-start.5 = (f32[2,128,128]{2,1,0:T(8,128)S(1)}, f32[2,128,128]{2,1,0:T(8,128)S(1)}, u32[]{:S(2)}, u32[]{:S(2)}) collective-permute-start(f32[2,128,128]{2,1,0:T(8,128)S(1)} %bitcast_add_fusion.7), channel_id=1, source_target_pairs={{0,4},{4,8},{8,12},{1,5},{5,9},{9,13},{2,6},{6,10},{10,14},{3,7},{... | collective-permute-start | bytes 393224 | tf_op jit(solution)/shard_map/ppermute | solution.py:60
  52.1 1.8 %collective-permute-done.5 = f32[2,128,128]{2,1,0:T(8,128)S(1)} collective-permute-done((f32[2,128,128]{2,1,0:T(8,128)S(1)}, f32[2,128,128]{2,1,0:T(8,128)S(1)}, u32[]{:S(2)}, u32[]{:S(2)}) %collective-permute-start.5) | collective-permute-done | bytes 131104 | tf_op jit(solution)/shard_map/ppermute | solution.py:60
  54.6 4.4 %collective-permute-start.6 = (f32[2,128,128]{2,1,0:T(8,128)S(1)}, f32[2,128,128]{2,1,0:T(8,128)S(1)}, u32[]{:S(2)}, u32[]{:S(2)}) collective-permute-start(f32[2,128,128]{2,1,0:T(8,128)S(1)} %bitcast_add_fusion.6), channel_id=1, source_target_pairs={{0,4},{4,8},{8,12},{1,5},{5,9},{9,13},{2,6},{6,10},{10,14},{3,7},{... | collective-permute-start | bytes 393224 | tf_op jit(solution)/shard_map/ppermute | solution.py:60
  59.0 2.5 %collective-permute-done.6 = f32[2,128,128]{2,1,0:T(8,128)S(1)} collective-permute-done((f32[2,128,128]{2,1,0:T(8,128)S(1)}, f32[2,128,128]{2,1,0:T(8,128)S(1)}, u32[]{:S(2)}, u32[]{:S(2)}) %collective-permute-start.6) | collective-permute-done | bytes 131104 | tf_op jit(solution)/shard_map/ppermute | solution.py:60
  62.3 1.8 %collective-permute-done.7 = f32[8,128,128]{2,1,0:T(8,128)S(1)} collective-permute-done((f32[8,128,128]{2,1,0:T(8,128)S(1)}, f32[8,128,128]{2,1,0:T(8,128)S(1)}, u32[]{:S(2)}, u32[]{:S(2)}) %collective-permute-start.7) | collective-permute-done | bytes 524320 | tf_op jit(solution)/shard_map/ppermute | solution.py:20
  65.2 9.4 %shard_map.98 = (bf16[512,2048]{1,0:T(8,128)(2,1)}, f32[16,128,128]{2,1,0:T(8,128)}, f32[16,1,128]{2,1,0:T(1,128)}) custom-call(bf16[512,2048]{1,0:T(8,128)(2,1)} %refs_0_.11, bf16[512,2048]{1,0:T(8,128)(2,1)} %g_ref.1, f32[512,2048]{1,0:T(8,128)} %shard_map.97.intra_ref, bf16[16,128,128]{2,1,0:T(8,128)(2,1)} %select_convert_fusion.1.st_ref.refs_6_, ...), custom_call_target="tpu_custom_call" | custom-call | flops 536870912 | bytes 10485760 | tf_op jit(solution)/shard_map/pallas_call | solution.py:258
  83.5 6.3 %shard_map.99 = (bf16[512,2048]{1,0:T(8,128)(2,1)}, f32[512,2048]{1,0:T(8,128)}, f32[512,2048]{1,0:T(8,128)}) custom-call(bf16[512,2048]{1,0:T(8,128)(2,1)} %refs_0_.11, bf16[512,2048]{1,0:T(8,128)(2,1)} %k_ref.7, bf16[512,2048]{1,0:T(8,128)(2,1)} %v_ref.7, bf16[512,2048]{1,0:T(8,128)(2,1)} %get-tuple-element.197.og_ref.refs_3_, ...), custom_call_target="tpu_custom_call" | custom-call | flops 1409286144 | bytes 4718592 | tf_op jit(solution)/shard_map/pallas_call | solution.py:258
  92.3 6.3 %shard_map.100 = (bf16[512,2048]{1,0:T(8,128)(2,1)}, f32[512,2048]{1,0:T(8,128)}, f32[512,2048]{1,0:T(8,128)}) custom-call(bf16[512,2048]{1,0:T(8,128)(2,1)} %refs_0_.11, bf16[512,2048]{1,0:T(8,128)(2,1)} %k_ref.7, bf16[512,2048]{1,0:T(8,128)(2,1)} %v_ref.7, ...), custom_call_target="tpu_custom_call", output_to_operand_aliasing={{0}: (7, {}), {1}: (8, {}), {2}: (9, {})} | custom-call | flops 1409286144 | bytes 4718592 | tf_op jit(solution)/shard_map/pallas_call | solution.py:258
  101.5 6.3 %shard_map.101 = (bf16[512,2048]{1,0:T(8,128)(2,1)}, f32[512,2048]{1,0:T(8,128)}, f32[512,2048]{1,0:T(8,128)}) custom-call(bf16[512,2048]{1,0:T(8,128)(2,1)} %refs_0_.11, bf16[512,2048]{1,0:T(8,128)(2,1)} %k_ref.7, bf16[512,2048]{1,0:T(8,128)(2,1)} %v_ref.7, ...), custom_call_target="tpu_custom_call", output_to_operand_aliasing={{0}: (7, {}), {1}: (8, {}), {2}: (9, {})} | custom-call | flops 1409286144 | bytes 4718592 | tf_op jit(solution)/shard_map/pallas_call | solution.py:258
  110.7 6.3 %shard_map.102 = (bf16[512,2048]{1,0:T(8,128)(2,1)}, f32[512,2048]{1,0:T(8,128)}, f32[512,2048]{1,0:T(8,128)}) custom-call(bf16[512,2048]{1,0:T(8,128)(2,1)} %refs_0_.11, bf16[512,2048]{1,0:T(8,128)(2,1)} %k_ref.7, bf16[512,2048]{1,0:T(8,128)(2,1)} %v_ref.7, ...), custom_call_target="tpu_custom_call", output_to_operand_aliasing={{0}: (7, {}), {1}: (8, {}), {2}: (9, {})} | custom-call | flops 1409286144 | bytes 4718592 | tf_op jit(solution)/shard_map/pallas_call | solution.py:258
  120.1 6.4 %collective-permute-done.13 = f32[2,128,128]{2,1,0:T(8,128)S(1)} collective-permute-done((f32[2,128,128]{2,1,0:T(8,128)S(1)}, f32[2,128,128]{2,1,0:T(8,128)S(1)}, u32[]{:S(2)}, u32[]{:S(2)}) %collective-permute-start.13) | collective-permute-done | bytes 131104 | tf_op jit(solution)/shard_map/ppermute | solution.py:60
  128.6 5.6 %collective-permute-done.14 = f32[2,128,128]{2,1,0:T(8,128)S(1)} collective-permute-done((f32[2,128,128]{2,1,0:T(8,128)S(1)}, f32[2,128,128]{2,1,0:T(8,128)S(1)}, u32[]{:S(2)}, u32[]{:S(2)}) %collective-permute-start.14) | collective-permute-done | bytes 131104 | tf_op jit(solution)/shard_map/ppermute | solution.py:60
  137.6 2.0 %collective-permute-done.16 = f32[16,128]{1,0:T(8,128)S(1)} collective-permute-done((f32[16,128]{1,0:T(8,128)S(1)}, f32[16,128]{1,0:T(8,128)S(1)}, u32[]{:S(2)}, u32[]{:S(2)}) %collective-permute-start.16) | collective-permute-done | bytes 8224 | tf_op jit(solution)/shard_map/ppermute | solution.py:111
  139.5 2.8 %collective-permute-start.17 = (f32[16,128]{1,0:T(8,128)S(1)}, f32[16,128]{1,0:T(8,128)S(1)}, u32[]{:S(2)}, u32[]{:S(2)}) collective-permute-start(f32[16,128]{1,0:T(8,128)S(1)} %add.229), channel_id=1, source_target_pairs={{0,8},{4,12},{8,0},{12,4},{1,9},{5,13},{9,1},{13,5},{2,10},{6,14},... | collective-permute-start | bytes 24584 | tf_op jit(solution)/shard_map/ppermute | solution.py:111
  145.9 8.4 %shard_map.103 = (bf16[512,2048]{1,0:T(8,128)(2,1)}, bf16[512,2048]{1,0:T(8,128)(2,1)}) custom-call(bf16[512,2048]{1,0:T(8,128)(2,1)} %k_ref.7, bf16[512,2048]{1,0:T(8,128)(2,1)} %v_ref.7, f32[512,2048]{1,0:T(8,128)} %get-tuple-element.225.kg_ref, f32[512,2048]{1,0:T(8,128)} %get-tuple-element.226.vg_ref, bf16[16,128,128]{2,1,0:T(8,128)(2,1)} %select_convert_fusion.gl_ref, ...), custom_call_target="tpu_custom_call" | custom-call | flops 536870912 | bytes 16777216 | tf_op jit(solution)/shard_map/pallas_call | solution.py:258
  (110 shorter events, 43.6 us)
Async XLA Ops:
  0.6 0.8 copy-start
  1.8 1.2 copy-start.3
  8.8 2.1 %copy-start.5 = (s32[4]{0:T(128)S(1)}, s32[4]{0:T(128)}, u32[]{:S(2)}) copy-start(s32[4]{0:T(128)} %constant.298.clone.1) | copy-start | bytes 52
  8.8 4.9 %copy-start.1 = (f32[16,128,128]{2,1,0:T(8,128)S(1)}, f32[16,128,128]{2,1,0:T(8,128)}, u32[]{:S(2)}) copy-start(f32[16,128,128]{2,1,0:T(8,128)} %shard_map.94) | copy-start | bytes 3145732
  10.3 2.9 %collective-permute-start = (f32[16,136,128]{2,1,0:T(8,128)S(1)}, f32[16,136,128]{2,1,0:T(8,128)S(1)}, u32[]{:S(2)}, u32[]{:S(2)}) collective-permute-start(f32[16,136,128]{2,1,0:T(8,128)S(1)} %fusion), channel_id=1, source_target_pairs={{0,1},{1,0},{2,3},{3,2},{4,5},{5,4},{6,7},{7,6},{8,9},{9,8},{10,11... | collective-permute-start | bytes 3342344 | tf_op jit(solution)/shard_map/ppermute | solution.py:20
  14.1 9.4 %collective-permute-start.1 = (f32[2,128,128]{2,1,0:T(8,128)S(1)}, f32[2,128,128]{2,1,0:T(8,128)S(1)}, u32[]{:S(2)}, u32[]{:S(2)}) collective-permute-start(f32[2,128,128]{2,1,0:T(8,128)S(1)} %bitcast_add_fusion.11), channel_id=1, source_target_pairs={{0,4},{4,8},{8,12},{1,5},{5,9},{9,13},{2,6},{6,10},{10,14},{3,7},{... | collective-permute-start | bytes 393224 | tf_op jit(solution)/shard_map/ppermute | solution.py:60
  24.4 7.4 %collective-permute-start.2 = (f32[2,128,128]{2,1,0:T(8,128)S(1)}, f32[2,128,128]{2,1,0:T(8,128)S(1)}, u32[]{:S(2)}, u32[]{:S(2)}) collective-permute-start(f32[2,128,128]{2,1,0:T(8,128)S(1)} %bitcast_add_fusion.10), channel_id=1, source_target_pairs={{0,4},{4,8},{8,12},{1,5},{5,9},{9,13},{2,6},{6,10},{10,14},{3,7},{... | collective-permute-start | bytes 393224 | tf_op jit(solution)/shard_map/ppermute | solution.py:60
  32.5 7.3 %collective-permute-start.3 = (f32[2,128,128]{2,1,0:T(8,128)S(1)}, f32[2,128,128]{2,1,0:T(8,128)S(1)}, u32[]{:S(2)}, u32[]{:S(2)}) collective-permute-start(f32[2,128,128]{2,1,0:T(8,128)S(1)} %bitcast_add_fusion.9), channel_id=1, source_target_pairs={{0,4},{4,8},{8,12},{1,5},{5,9},{9,13},{2,6},{6,10},{10,14},{3,7},{... | collective-permute-start | bytes 393224 | tf_op jit(solution)/shard_map/ppermute | solution.py:60
  40.5 7.1 %collective-permute-start.4 = (f32[2,128,128]{2,1,0:T(8,128)S(1)}, f32[2,128,128]{2,1,0:T(8,128)S(1)}, u32[]{:S(2)}, u32[]{:S(2)}) collective-permute-start(f32[2,128,128]{2,1,0:T(8,128)S(1)} %bitcast_add_fusion.8), channel_id=1, source_target_pairs={{0,4},{4,8},{8,12},{1,5},{5,9},{9,13},{2,6},{6,10},{10,14},{3,7},{... | collective-permute-start | bytes 393224 | tf_op jit(solution)/shard_map/ppermute | solution.py:60
  48.3 5.5 %collective-permute-start.5 = (f32[2,128,128]{2,1,0:T(8,128)S(1)}, f32[2,128,128]{2,1,0:T(8,128)S(1)}, u32[]{:S(2)}, u32[]{:S(2)}) collective-permute-start(f32[2,128,128]{2,1,0:T(8,128)S(1)} %bitcast_add_fusion.7), channel_id=1, source_target_pairs={{0,4},{4,8},{8,12},{1,5},{5,9},{9,13},{2,6},{6,10},{10,14},{3,7},{... | collective-permute-start | bytes 393224 | tf_op jit(solution)/shard_map/ppermute | solution.py:60
  54.6 6.9 %collective-permute-start.6 = (f32[2,128,128]{2,1,0:T(8,128)S(1)}, f32[2,128,128]{2,1,0:T(8,128)S(1)}, u32[]{:S(2)}, u32[]{:S(2)}) collective-permute-start(f32[2,128,128]{2,1,0:T(8,128)S(1)} %bitcast_add_fusion.6), channel_id=1, source_target_pairs={{0,4},{4,8},{8,12},{1,5},{5,9},{9,13},{2,6},{6,10},{10,14},{3,7},{... | collective-permute-start | bytes 393224 | tf_op jit(solution)/shard_map/ppermute | solution.py:60
  62.1 2.0 %collective-permute-start.7 = (f32[8,128,128]{2,1,0:T(8,128)S(1)}, f32[8,128,128]{2,1,0:T(8,128)S(1)}, u32[]{:S(2)}, u32[]{:S(2)}) collective-permute-start(f32[8,128,128]{2,1,0:T(8,128)S(1)} %bitcast.203), channel_id=1, source_target_pairs={{0,1},{1,0},{2,3},{3,2},{4,5},{5,4},{6,7},{7,6},{8,9},{9,8},{10,11... | collective-permute-start | bytes 1572872 | tf_op jit(solution)/shard_map/ppermute | solution.py:20
  74.6 5.7 %copy-start.2 = (f32[16,128,128]{2,1,0:T(8,128)S(1)}, f32[16,128,128]{2,1,0:T(8,128)}, u32[]{:S(2)}) copy-start(f32[16,128,128]{2,1,0:T(8,128)} %get-tuple-element.201) | copy-start | bytes 3145732
  76.1 3.0 %collective-permute-start.8 = (f32[16,136,128]{2,1,0:T(8,128)S(1)}, f32[16,136,128]{2,1,0:T(8,128)}, u32[]{:S(2)}, u32[]{:S(2)}) collective-permute-start(f32[16,136,128]{2,1,0:T(8,128)S(1)} %fusion.2), channel_id=1, source_target_pairs={{0,1},{1,0},{2,3},{3,2},{4,5},{5,4},{6,7},{7,6},{8,9},{9,8},{10,11... | collective-permute-start | bytes 3342344 | tf_op jit(solution)/shard_map/ppermute | solution.py:20
  82.0 8.1 %collective-permute-start.9 = (f32[2,128,128]{2,1,0:T(8,128)S(1)}, f32[2,128,128]{2,1,0:T(8,128)S(1)}, u32[]{:S(2)}, u32[]{:S(2)}) collective-permute-start(f32[2,128,128]{2,1,0:T(8,128)S(1)} %bitcast_add_fusion.5), channel_id=1, source_target_pairs={{4,0},{8,4},{12,8},{5,1},{9,5},{13,9},{6,2},{10,6},{14,10},{7,3},{... | collective-permute-start | bytes 393224 | tf_op jit(solution)/shard_map/ppermute | solution.py:60
  91.0 8.5 %collective-permute-start.10 = (f32[2,128,128]{2,1,0:T(8,128)S(1)}, f32[2,128,128]{2,1,0:T(8,128)S(1)}, u32[]{:S(2)}, u32[]{:S(2)}) collective-permute-start(f32[2,128,128]{2,1,0:T(8,128)S(1)} %bitcast_add_fusion.4), channel_id=1, source_target_pairs={{4,0},{8,4},{12,8},{5,1},{9,5},{13,9},{6,2},{10,6},{14,10},{7,3},{... | collective-permute-start | bytes 393224 | tf_op jit(solution)/shard_map/ppermute | solution.py:60
  100.2 8.2 %collective-permute-start.11 = (f32[2,128,128]{2,1,0:T(8,128)S(1)}, f32[2,128,128]{2,1,0:T(8,128)S(1)}, u32[]{:S(2)}, u32[]{:S(2)}) collective-permute-start(f32[2,128,128]{2,1,0:T(8,128)S(1)} %bitcast_add_fusion.3), channel_id=1, source_target_pairs={{4,0},{8,4},{12,8},{5,1},{9,5},{13,9},{6,2},{10,6},{14,10},{7,3},{... | collective-permute-start | bytes 393224 | tf_op jit(solution)/shard_map/ppermute | solution.py:60
  109.2 8.2 %collective-permute-start.12 = (f32[2,128,128]{2,1,0:T(8,128)S(1)}, f32[2,128,128]{2,1,0:T(8,128)S(1)}, u32[]{:S(2)}, u32[]{:S(2)}) collective-permute-start(f32[2,128,128]{2,1,0:T(8,128)S(1)} %bitcast_add_fusion.2), channel_id=1, source_target_pairs={{4,0},{8,4},{12,8},{5,1},{9,5},{13,9},{6,2},{10,6},{14,10},{7,3},{... | collective-permute-start | bytes 393224 | tf_op jit(solution)/shard_map/ppermute | solution.py:60
  117.0 18.0 %copy-start.4 = (f32[16,1,128]{2,1,0:T(1,128)S(1)}, f32[16,1,128]{2,1,0:T(1,128)}, u32[]{:S(2)}) copy-start(f32[16,1,128]{2,1,0:T(1,128)} %get-tuple-element.202) | copy-start | bytes 24580
  118.1 8.4 %collective-permute-start.13 = (f32[2,128,128]{2,1,0:T(8,128)S(1)}, f32[2,128,128]{2,1,0:T(8,128)S(1)}, u32[]{:S(2)}, u32[]{:S(2)}) collective-permute-start(f32[2,128,128]{2,1,0:T(8,128)S(1)} %bitcast_add_fusion.1), channel_id=1, source_target_pairs={{4,0},{8,4},{12,8},{5,1},{9,5},{13,9},{6,2},{10,6},{14,10},{7,3},{... | collective-permute-start | bytes 393224 | tf_op jit(solution)/shard_map/ppermute | solution.py:60
  127.3 6.9 %collective-permute-start.14 = (f32[2,128,128]{2,1,0:T(8,128)S(1)}, f32[2,128,128]{2,1,0:T(8,128)S(1)}, u32[]{:S(2)}, u32[]{:S(2)}) collective-permute-start(f32[2,128,128]{2,1,0:T(8,128)S(1)} %bitcast_add_fusion), channel_id=1, source_target_pairs={{4,0},{8,4},{12,8},{5,1},{9,5},{13,9},{6,2},{10,6},{14,10},{7,3},{... | collective-permute-start | bytes 393224 | tf_op jit(solution)/shard_map/ppermute | solution.py:60
  134.9 9.8 %collective-permute-start.15 = (f32[8,128,128]{2,1,0:T(8,128)S(1)}, f32[8,128,128]{2,1,0:T(8,128)S(1)}, u32[]{:S(2)}, u32[]{:S(2)}) collective-permute-start(f32[8,128,128]{2,1,0:T(8,128)S(1)} %bitcast.202), channel_id=1, source_target_pairs={{0,1},{1,0},{2,3},{3,2},{4,5},{5,4},{6,7},{7,6},{8,9},{9,8},{10,11... | collective-permute-start | bytes 1572872 | tf_op jit(solution)/shard_map/ppermute | solution.py:20
  135.8 3.7 %collective-permute-start.16 = (f32[16,128]{1,0:T(8,128)S(1)}, f32[16,128]{1,0:T(8,128)S(1)}, u32[]{:S(2)}, u32[]{:S(2)}) collective-permute-start(f32[16,128]{1,0:T(8,128)S(1)} %bitcast.229), channel_id=1, source_target_pairs={{0,4},{4,0},{8,12},{12,8},{1,5},{5,1},{9,13},{13,9},{2,6},{6,2},{1... | collective-permute-start | bytes 24584 | tf_op jit(solution)/shard_map/ppermute | solution.py:111
  139.5 4.5 %collective-permute-start.17 = (f32[16,128]{1,0:T(8,128)S(1)}, f32[16,128]{1,0:T(8,128)S(1)}, u32[]{:S(2)}, u32[]{:S(2)}) collective-permute-start(f32[16,128]{1,0:T(8,128)S(1)} %add.229), channel_id=1, source_target_pairs={{0,8},{4,12},{8,0},{12,4},{1,9},{5,13},{9,1},{13,5},{2,10},{6,14},... | collective-permute-start | bytes 24584 | tf_op jit(solution)/shard_map/ppermute | solution.py:111

commit v9 on v8

--- a/solution.py
+++ b/solution.py
@@ -38,7 +38,7 @@
     return jnp.concatenate([first, second], axis=0)
 
 
-def chain_scan(chip_state, chip_decay, later, pieces_of_cover):
+def chain_scan(chip_state, chip_decay, later, pieces_of_cover, cover=None):
     chips = lax.axis_size("ctx")
     z = lax.axis_index("ctx")
     heads = chip_state.shape[0]
@@ -52,7 +52,6 @@
     else:
         perm = [(i, i + 1) for i in range(chips - 1)]
     prefix = jnp.zeros_like(pieces)
-    cover = None
     steps = count + chips - 2
     for step in range(steps):
         send = jnp.clip(step - rank, 0, count - 1)
@@ -104,13 +103,22 @@
     chip_state = first + jnp.exp(fin_first)[:, None, None] * second
     chip_decay = fin_first + fin_second
     chips = lax.axis_size("ctx")
-    gain_total = chip_gain
+
+    def grads_step(piece, both):
+        return piece(both[0]), both[1]
+
+    def gain_step(distance, both):
+        partners = [(i, i ^ distance) for i in range(chips)]
+        return both[0], both[1] + lax.ppermute(both[1], "ctx", perm=partners)
+
+    steps = [functools.partial(grads_step, piece) for piece in cover]
     distance = 1
     while distance < chips:
-        partners = [(i, i ^ distance) for i in range(chips)]
-        gain_total = gain_total + lax.ppermute(gain_total, "ctx", perm=partners)
+        steps.append(functools.partial(gain_step, distance))
         distance *= 2
-    suffix_half, cover = chain_scan(halves(chip_state, c), halves(chip_decay, c), True, cover)
+    suffix_half, (cover, gain_total) = chain_scan(
+        halves(chip_state, c), halves(chip_decay, c), True, steps, (None, chip_gain)
+    )
     suffix = join_halves(suffix_half, swap_dp(suffix_half), c)
     core_zero = second + jnp.exp(fin_second)[:, None, None] * suffix
     return jnp.where(c == 0, core_zero, suffix), gain_total.reshape(heads * DH), cover

time: 155 us -> 153 us (0.987)
  waiting for transfers between devices: 26.8 us -> 21.3 us
  starting transfers between devices: 36 us -> 39 us
    ppermute x12, waiting for transfers between devices: 18.5 us -> 11.1 us  [chain_scan(): arrived = lax.ppermute(outgoing, 'ctx', perm=perm)]
    ppermute x2, starting transfers between devices: 4.59 us -> 7.6 us  [gain_step(): return (both[0], both[1] + lax.ppermute(both[1], 'ctx', perm=partners))]
    ppermute x2, waiting for transfers between devices: 3.68 us -> 5.58 us  [gain_step(): return (both[0], both[1] + lax.ppermute(both[1], 'ctx', perm=partners))]
  transfers between devices with their start and end apart: 18 -> 18, of which waited for: 13 -> 9; matrix products, arithmetic and copies ran while one was open for 4% -> 4% of each run, Pallas kernels for 26% -> 27%
where the time goes in v9:
time: 153 us; the launch traced here: 152 us
  Pallas kernels  64.4 us (42%)
  starting transfers between devices  39 us (25%)
  other arithmetic  22.8 us (15%)
  waiting for transfers between devices  21.3 us (14%)
  local copies, waits for them, and re-layouts  2.78 us (2%)
    pallas_call x11, Pallas kernels, _per_head(): pl.pallas_call(body, grid=(count,), in_specs=in_specs, out_specs=[spec(ki...  64.4 us
    ppermute x12, starting transfers between devices, chain_scan(): arrived = lax.ppermute(outgoing, 'ctx', perm=perm)  30.6 us
    ppermute x12, waiting for transfers between devices, chain_scan(): arrived = lax.ppermute(outgoing, 'ctx', perm=perm)  11.1 us
    scatter x12, other arithmetic, chain_scan(): prefix = prefix.at[slot].set(jnp.where(valid, arrived, prefix[slot]))  7.64 us
    ppermute x2, starting transfers between devices, gain_step(): return (both[0], both[1] + lax.ppermute(both[1], 'ctx', perm=partners))  7.6 us
    ppermute x2, waiting for transfers between devices, gain_step(): return (both[0], both[1] + lax.ppermute(both[1], 'ctx', perm=partners))  5.58 us
    ppermute x4, waiting for transfers between devices, swap_dp(): return lax.ppermute(x, 'dp', perm=[(0, 1), (1, 0)])  4.71 us
    another operation x6, other arithmetic  4.41 us
  transfers between devices with their start and end apart: 18, of which 9 were waited for; matrix products, arithmetic and copies ran while one was open for 4% of the time, Pallas kernels for 27%

profile of v9, /device:TPU:0, one launch (start us, length us, event | category | flops | bytes accessed | tf_op | source)
XLA Modules:
  0.0 151.8 jit_solution(1002793320231536798)
XLA Ops:
  3.0 5.8 %shard_map.94 = f32[16,128,128]{2,1,0:T(8,128)} custom-call(bf16[512,2048]{1,0:T(8,128)(2,1)} %k_ref.7, bf16[512,2048]{1,0:T(8,128)(2,1)} %v_ref.7, f32[512,16]{1,0:T(8,128)} %copy.42.cum_ref.refs_3_.refs_4_, f32[16,512]{1,0:T(8,128)} %bitcast.204), custom_call_target="tpu_custom_call" | custom-call | flops 268435456 | bytes 4194304 | tf_op jit(solution)/shard_map/pallas_call | solution.py:266
  14.1 4.9 %collective-permute-start.1 = (f32[2,128,128]{2,1,0:T(8,128)S(1)}, f32[2,128,128]{2,1,0:T(8,128)S(1)}, u32[]{:S(2)}, u32[]{:S(2)}) collective-permute-start(f32[2,128,128]{2,1,0:T(8,128)S(1)} %bitcast_add_fusion.11), channel_id=1, source_target_pairs={{0,4},{4,8},{8,12},{1,5},{5,9},{9,13},{2,6},{6,10},{10,14},{3,7},{... | collective-permute-start | bytes 393224 | tf_op jit(solution)/shard_map/ppermute | solution.py:59
  19.0 3.9 %shard_map.93.refs_5_ = f32[512,2048]{1,0:T(8,128)} custom-call(bf16[512,2048]{1,0:T(8,128)(2,1)} %refs_0_.11, bf16[512,2048]{1,0:T(8,128)(2,1)} %k_ref.7, bf16[512,2048]{1,0:T(8,128)(2,1)} %v_ref.7, f32[512,16]{1,0:T(8,128)} %copy.42.cum_ref.refs_3_.refs_4_, f32[16,512]{1,0:T(8,128)} %bitcast.205), custom_call_target="tpu_custom_call" | custom-call | flops 536870912 | bytes 2621440 | tf_op jit(solution)/shard_map/pallas_call | solution.py:266
  24.4 3.5 %collective-permute-start.2 = (f32[2,128,128]{2,1,0:T(8,128)S(1)}, f32[2,128,128]{2,1,0:T(8,128)S(1)}, u32[]{:S(2)}, u32[]{:S(2)}) collective-permute-start(f32[2,128,128]{2,1,0:T(8,128)S(1)} %bitcast_add_fusion.10), channel_id=1, source_target_pairs={{0,4},{4,8},{8,12},{1,5},{5,9},{9,13},{2,6},{6,10},{10,14},{3,7},{... | collective-permute-start | bytes 393224 | tf_op jit(solution)/shard_map/ppermute | solution.py:59
  27.9 3.9 %shard_map.95.refs_5_ = f32[512,2048]{1,0:T(8,128)} custom-call(bf16[512,2048]{1,0:T(8,128)(2,1)} %refs_0_.11, bf16[512,2048]{1,0:T(8,128)(2,1)} %k_ref.7, bf16[512,2048]{1,0:T(8,128)(2,1)} %v_ref.7, f32[512,16]{1,0:T(8,128)} %copy.42.cum_ref.refs_3_.refs_4_, f32[16,512]{1,0:T(8,128)} %bitcast.206, ...), custom_call_target="tpu_custom_call", output_to_operand_aliasing={{}: (5, {})} | custom-call | flops 536870912 | bytes 2621440 | tf_op jit(solution)/shard_map/pallas_call | solution.py:266
  32.5 3.5 %collective-permute-start.3 = (f32[2,128,128]{2,1,0:T(8,128)S(1)}, f32[2,128,128]{2,1,0:T(8,128)S(1)}, u32[]{:S(2)}, u32[]{:S(2)}) collective-permute-start(f32[2,128,128]{2,1,0:T(8,128)S(1)} %bitcast_add_fusion.9), channel_id=1, source_target_pairs={{0,4},{4,8},{8,12},{1,5},{5,9},{9,13},{2,6},{6,10},{10,14},{3,7},{... | collective-permute-start | bytes 393224 | tf_op jit(solution)/shard_map/ppermute | solution.py:59
  36.0 3.8 %shard_map.96.refs_5_ = f32[512,2048]{1,0:T(8,128)} custom-call(bf16[512,2048]{1,0:T(8,128)(2,1)} %refs_0_.11, bf16[512,2048]{1,0:T(8,128)(2,1)} %k_ref.7, bf16[512,2048]{1,0:T(8,128)(2,1)} %v_ref.7, f32[512,16]{1,0:T(8,128)} %copy.42.cum_ref.refs_3_.refs_4_, f32[16,512]{1,0:T(8,128)} %bitcast.207, ...), custom_call_target="tpu_custom_call", output_to_operand_aliasing={{}: (5, {})} | custom-call | flops 536870912 | bytes 2621440 | tf_op jit(solution)/shard_map/pallas_call | solution.py:266
  40.5 3.2 %collective-permute-start.4 = (f32[2,128,128]{2,1,0:T(8,128)S(1)}, f32[2,128,128]{2,1,0:T(8,128)S(1)}, u32[]{:S(2)}, u32[]{:S(2)}) collective-permute-start(f32[2,128,128]{2,1,0:T(8,128)S(1)} %bitcast_add_fusion.8), channel_id=1, source_target_pairs={{0,4},{4,8},{8,12},{1,5},{5,9},{9,13},{2,6},{6,10},{10,14},{3,7},{... | collective-permute-start | bytes 393224 | tf_op jit(solution)/shard_map/ppermute | solution.py:59
  43.7 3.8 %shard_map.97.intra_ref = f32[512,2048]{1,0:T(8,128)} custom-call(bf16[512,2048]{1,0:T(8,128)(2,1)} %refs_0_.11, bf16[512,2048]{1,0:T(8,128)(2,1)} %k_ref.7, bf16[512,2048]{1,0:T(8,128)(2,1)} %v_ref.7, f32[512,16]{1,0:T(8,128)} %copy.42.cum_ref.refs_3_.refs_4_, f32[16,512]{1,0:T(8,128)} %bitcast.208, ...), custom_call_target="tpu_custom_call", output_to_operand_aliasing={{}: (5, {})} | custom-call | flops 536870912 | bytes 2621440 | tf_op jit(solution)/shard_map/pallas_call | solution.py:266
  48.3 3.0 %collective-permute-start.5 = (f32[2,128,128]{2,1,0:T(8,128)S(1)}, f32[2,128,128]{2,1,0:T(8,128)S(1)}, u32[]{:S(2)}, u32[]{:S(2)}) collective-permute-start(f32[2,128,128]{2,1,0:T(8,128)S(1)} %bitcast_add_fusion.7), channel_id=1, source_target_pairs={{0,4},{4,8},{8,12},{1,5},{5,9},{9,13},{2,6},{6,10},{10,14},{3,7},{... | collective-permute-start | bytes 393224 | tf_op jit(solution)/shard_map/ppermute | solution.py:59
  54.6 4.5 %collective-permute-start.6 = (f32[2,128,128]{2,1,0:T(8,128)S(1)}, f32[2,128,128]{2,1,0:T(8,128)S(1)}, u32[]{:S(2)}, u32[]{:S(2)}) collective-permute-start(f32[2,128,128]{2,1,0:T(8,128)S(1)} %bitcast_add_fusion.6), channel_id=1, source_target_pairs={{0,4},{4,8},{8,12},{1,5},{5,9},{9,13},{2,6},{6,10},{10,14},{3,7},{... | collective-permute-start | bytes 393224 | tf_op jit(solution)/shard_map/ppermute | solution.py:59
  59.2 2.3 %collective-permute-done.6 = f32[2,128,128]{2,1,0:T(8,128)S(1)} collective-permute-done((f32[2,128,128]{2,1,0:T(8,128)S(1)}, f32[2,128,128]{2,1,0:T(8,128)S(1)}, u32[]{:S(2)}, u32[]{:S(2)}) %collective-permute-start.6) | collective-permute-done | bytes 131104 | tf_op jit(solution)/shard_map/ppermute | solution.py:59
  62.3 1.8 %collective-permute-done.7 = f32[8,128,128]{2,1,0:T(8,128)S(1)} collective-permute-done((f32[8,128,128]{2,1,0:T(8,128)S(1)}, f32[8,128,128]{2,1,0:T(8,128)S(1)}, u32[]{:S(2)}, u32[]{:S(2)}) %collective-permute-start.7) | collective-permute-done | bytes 524320 | tf_op jit(solution)/shard_map/ppermute | solution.py:20
  65.2 9.4 %shard_map.98 = (bf16[512,2048]{1,0:T(8,128)(2,1)}, f32[16,128,128]{2,1,0:T(8,128)}, f32[16,1,128]{2,1,0:T(1,128)}) custom-call(bf16[512,2048]{1,0:T(8,128)(2,1)} %refs_0_.11, bf16[512,2048]{1,0:T(8,128)(2,1)} %g_ref.1, f32[512,2048]{1,0:T(8,128)} %shard_map.97.intra_ref, bf16[16,128,128]{2,1,0:T(8,128)(2,1)} %select_convert_fusion.1.st_ref.refs_6_, ...), custom_call_target="tpu_custom_call" | custom-call | flops 536870912 | bytes 10485760 | tf_op jit(solution)/shard_map/pallas_call | solution.py:266
  77.7 6.4 %shard_map.99 = (bf16[512,2048]{1,0:T(8,128)(2,1)}, f32[512,2048]{1,0:T(8,128)}, f32[512,2048]{1,0:T(8,128)}) custom-call(bf16[512,2048]{1,0:T(8,128)(2,1)} %refs_0_.11, bf16[512,2048]{1,0:T(8,128)(2,1)} %k_ref.7, bf16[512,2048]{1,0:T(8,128)(2,1)} %v_ref.7, bf16[512,2048]{1,0:T(8,128)(2,1)} %get-tuple-element.211.og_ref.refs_3_, ...), custom_call_target="tpu_custom_call" | custom-call | flops 1409286144 | bytes 4718592 | tf_op jit(solution)/shard_map/pallas_call | solution.py:266
  89.3 6.2 %collective-permute-done.9 = f32[2,128,128]{2,1,0:T(8,128)S(1)} collective-permute-done((f32[2,128,128]{2,1,0:T(8,128)S(1)}, f32[2,128,128]{2,1,0:T(8,128)S(1)}, u32[]{:S(2)}, u32[]{:S(2)}) %collective-permute-start.9) | collective-permute-done | bytes 131104 | tf_op jit(solution)/shard_map/ppermute | solution.py:59
  97.6 6.3 %shard_map.100 = (bf16[512,2048]{1,0:T(8,128)(2,1)}, f32[512,2048]{1,0:T(8,128)}, f32[512,2048]{1,0:T(8,128)}) custom-call(bf16[512,2048]{1,0:T(8,128)(2,1)} %refs_0_.11, bf16[512,2048]{1,0:T(8,128)(2,1)} %k_ref.7, bf16[512,2048]{1,0:T(8,128)(2,1)} %v_ref.7, ...), custom_call_target="tpu_custom_call", output_to_operand_aliasing={{0}: (7, {}), {1}: (8, {}), {2}: (9, {})} | custom-call | flops 1409286144 | bytes 4718592 | tf_op jit(solution)/shard_map/pallas_call | solution.py:266
  106.2 6.3 %shard_map.101 = (bf16[512,2048]{1,0:T(8,128)(2,1)}, f32[512,2048]{1,0:T(8,128)}, f32[512,2048]{1,0:T(8,128)}) custom-call(bf16[512,2048]{1,0:T(8,128)(2,1)} %refs_0_.11, bf16[512,2048]{1,0:T(8,128)(2,1)} %k_ref.7, bf16[512,2048]{1,0:T(8,128)(2,1)} %v_ref.7, ...), custom_call_target="tpu_custom_call", output_to_operand_aliasing={{0}: (7, {}), {1}: (8, {}), {2}: (9, {})} | custom-call | flops 1409286144 | bytes 4718592 | tf_op jit(solution)/shard_map/pallas_call | solution.py:266
  114.5 6.3 %shard_map.102 = (bf16[512,2048]{1,0:T(8,128)(2,1)}, f32[512,2048]{1,0:T(8,128)}, f32[512,2048]{1,0:T(8,128)}) custom-call(bf16[512,2048]{1,0:T(8,128)(2,1)} %refs_0_.11, bf16[512,2048]{1,0:T(8,128)(2,1)} %k_ref.7, bf16[512,2048]{1,0:T(8,128)(2,1)} %v_ref.7, ...), custom_call_target="tpu_custom_call", output_to_operand_aliasing={{0}: (7, {}), {1}: (8, {}), {2}: (9, {})} | custom-call | flops 1409286144 | bytes 4718592 | tf_op jit(solution)/shard_map/pallas_call | solution.py:266
  124.3 3.8 %collective-permute-start.13 = (f32[16,128]{1,0:T(8,128)S(1)}, f32[16,128]{1,0:T(8,128)S(1)}, u32[]{:S(2)}, u32[]{:S(2)}) collective-permute-start(f32[16,128]{1,0:T(8,128)S(1)} %bitcast.229), channel_id=1, source_target_pairs={{0,4},{4,0},{8,12},{12,8},{1,5},{5,1},{9,13},{13,9},{2,6},{6,2},{1... | collective-permute-start | bytes 24584 | tf_op jit(solution)/shard_map/ppermute | solution.py:112
  128.0 2.6 %collective-permute-done.13 = f32[16,128]{1,0:T(8,128)S(1)} collective-permute-done((f32[16,128]{1,0:T(8,128)S(1)}, f32[16,128]{1,0:T(8,128)S(1)}, u32[]{:S(2)}, u32[]{:S(2)}) %collective-permute-start.13) | collective-permute-done | bytes 8224 | tf_op jit(solution)/shard_map/ppermute | solution.py:112
  132.7 3.8 %collective-permute-start.15 = (f32[16,128]{1,0:T(8,128)S(1)}, f32[16,128]{1,0:T(8,128)S(1)}, u32[]{:S(2)}, u32[]{:S(2)}) collective-permute-start(f32[16,128]{1,0:T(8,128)S(1)} %add.224), channel_id=1, source_target_pairs={{0,8},{4,12},{8,0},{12,4},{1,9},{5,13},{9,1},{13,5},{2,10},{6,14},... | collective-permute-start | bytes 24584 | tf_op jit(solution)/shard_map/ppermute | solution.py:112
  136.6 3.0 %collective-permute-done.15 = f32[16,128]{1,0:T(8,128)S(1)} collective-permute-done((f32[16,128]{1,0:T(8,128)S(1)}, f32[16,128]{1,0:T(8,128)S(1)}, u32[]{:S(2)}, u32[]{:S(2)}) %collective-permute-start.15) | collective-permute-done | bytes 8224 | tf_op jit(solution)/shard_map/ppermute | solution.py:112
  143.4 8.4 %shard_map.103 = (bf16[512,2048]{1,0:T(8,128)(2,1)}, bf16[512,2048]{1,0:T(8,128)(2,1)}) custom-call(bf16[512,2048]{1,0:T(8,128)(2,1)} %k_ref.7, bf16[512,2048]{1,0:T(8,128)(2,1)} %v_ref.7, f32[512,2048]{1,0:T(8,128)} %get-tuple-element.252.kg_ref, f32[512,2048]{1,0:T(8,128)} %get-tuple-element.253.vg_ref, bf16[16,128,128]{2,1,0:T(8,128)(2,1)} %select_convert_fusion.gl_ref, ...), custom_call_target="tpu_custom_call" | custom-call | flops 536870912 | bytes 16777216 | tf_op jit(solution)/shard_map/pallas_call | solution.py:266
  (111 shorter events, 40.2 us)
Async XLA Ops:
  0.6 0.8 copy-start
  1.8 1.2 copy-start.3
  8.8 2.1 %copy-start.5 = (s32[4]{0:T(128)S(1)}, s32[4]{0:T(128)}, u32[]{:S(2)}) copy-start(s32[4]{0:T(128)} %constant.298.clone.1) | copy-start | bytes 52
  8.8 4.9 %copy-start.1 = (f32[16,128,128]{2,1,0:T(8,128)S(1)}, f32[16,128,128]{2,1,0:T(8,128)}, u32[]{:S(2)}) copy-start(f32[16,128,128]{2,1,0:T(8,128)} %shard_map.94) | copy-start | bytes 3145732
  10.3 2.9 %collective-permute-start = (f32[16,136,128]{2,1,0:T(8,128)S(1)}, f32[16,136,128]{2,1,0:T(8,128)S(1)}, u32[]{:S(2)}, u32[]{:S(2)}) collective-permute-start(f32[16,136,128]{2,1,0:T(8,128)S(1)} %fusion), channel_id=1, source_target_pairs={{0,1},{1,0},{2,3},{3,2},{4,5},{5,4},{6,7},{7,6},{8,9},{9,8},{10,11... | collective-permute-start | bytes 3342344 | tf_op jit(solution)/shard_map/ppermute | solution.py:20
  14.1 9.4 %collective-permute-start.1 = (f32[2,128,128]{2,1,0:T(8,128)S(1)}, f32[2,128,128]{2,1,0:T(8,128)S(1)}, u32[]{:S(2)}, u32[]{:S(2)}) collective-permute-start(f32[2,128,128]{2,1,0:T(8,128)S(1)} %bitcast_add_fusion.11), channel_id=1, source_target_pairs={{0,4},{4,8},{8,12},{1,5},{5,9},{9,13},{2,6},{6,10},{10,14},{3,7},{... | collective-permute-start | bytes 393224 | tf_op jit(solution)/shard_map/ppermute | solution.py:59
  24.4 7.4 %collective-permute-start.2 = (f32[2,128,128]{2,1,0:T(8,128)S(1)}, f32[2,128,128]{2,1,0:T(8,128)S(1)}, u32[]{:S(2)}, u32[]{:S(2)}) collective-permute-start(f32[2,128,128]{2,1,0:T(8,128)S(1)} %bitcast_add_fusion.10), channel_id=1, source_target_pairs={{0,4},{4,8},{8,12},{1,5},{5,9},{9,13},{2,6},{6,10},{10,14},{3,7},{... | collective-permute-start | bytes 393224 | tf_op jit(solution)/shard_map/ppermute | solution.py:59
  32.5 7.3 %collective-permute-start.3 = (f32[2,128,128]{2,1,0:T(8,128)S(1)}, f32[2,128,128]{2,1,0:T(8,128)S(1)}, u32[]{:S(2)}, u32[]{:S(2)}) collective-permute-start(f32[2,128,128]{2,1,0:T(8,128)S(1)} %bitcast_add_fusion.9), channel_id=1, source_target_pairs={{0,4},{4,8},{8,12},{1,5},{5,9},{9,13},{2,6},{6,10},{10,14},{3,7},{... | collective-permute-start | bytes 393224 | tf_op jit(solution)/shard_map/ppermute | solution.py:59
  40.5 7.1 %collective-permute-start.4 = (f32[2,128,128]{2,1,0:T(8,128)S(1)}, f32[2,128,128]{2,1,0:T(8,128)S(1)}, u32[]{:S(2)}, u32[]{:S(2)}) collective-permute-start(f32[2,128,128]{2,1,0:T(8,128)S(1)} %bitcast_add_fusion.8), channel_id=1, source_target_pairs={{0,4},{4,8},{8,12},{1,5},{5,9},{9,13},{2,6},{6,10},{10,14},{3,7},{... | collective-permute-start | bytes 393224 | tf_op jit(solution)/shard_map/ppermute | solution.py:59
  48.3 5.5 %collective-permute-start.5 = (f32[2,128,128]{2,1,0:T(8,128)S(1)}, f32[2,128,128]{2,1,0:T(8,128)S(1)}, u32[]{:S(2)}, u32[]{:S(2)}) collective-permute-start(f32[2,128,128]{2,1,0:T(8,128)S(1)} %bitcast_add_fusion.7), channel_id=1, source_target_pairs={{0,4},{4,8},{8,12},{1,5},{5,9},{9,13},{2,6},{6,10},{10,14},{3,7},{... | collective-permute-start | bytes 393224 | tf_op jit(solution)/shard_map/ppermute | solution.py:59
  54.6 6.9 %collective-permute-start.6 = (f32[2,128,128]{2,1,0:T(8,128)S(1)}, f32[2,128,128]{2,1,0:T(8,128)S(1)}, u32[]{:S(2)}, u32[]{:S(2)}) collective-permute-start(f32[2,128,128]{2,1,0:T(8,128)S(1)} %bitcast_add_fusion.6), channel_id=1, source_target_pairs={{0,4},{4,8},{8,12},{1,5},{5,9},{9,13},{2,6},{6,10},{10,14},{3,7},{... | collective-permute-start | bytes 393224 | tf_op jit(solution)/shard_map/ppermute | solution.py:59
  62.1 2.0 %collective-permute-start.7 = (f32[8,128,128]{2,1,0:T(8,128)S(1)}, f32[8,128,128]{2,1,0:T(8,128)S(1)}, u32[]{:S(2)}, u32[]{:S(2)}) collective-permute-start(f32[8,128,128]{2,1,0:T(8,128)S(1)} %bitcast.203), channel_id=1, source_target_pairs={{0,1},{1,0},{2,3},{3,2},{4,5},{5,4},{6,7},{7,6},{8,9},{9,8},{10,11... | collective-permute-start | bytes 1572872 | tf_op jit(solution)/shard_map/ppermute | solution.py:20
  76.0 8.1 %collective-permute-start.8 = (f32[16,136,128]{2,1,0:T(8,128)S(1)}, f32[16,136,128]{2,1,0:T(8,128)}, u32[]{:S(2)}, u32[]{:S(2)}) collective-permute-start(f32[16,136,128]{2,1,0:T(8,128)S(1)} %fusion.2), channel_id=1, source_target_pairs={{0,1},{1,0},{2,3},{3,2},{4,5},{5,4},{6,7},{7,6},{8,9},{9,8},{10,11... | collective-permute-start | bytes 3342344 | tf_op jit(solution)/shard_map/ppermute | solution.py:20
  77.7 7.7 %copy-start.2 = (f32[16,128,128]{2,1,0:T(8,128)S(1)}, f32[16,128,128]{2,1,0:T(8,128)}, u32[]{:S(2)}) copy-start(f32[16,128,128]{2,1,0:T(8,128)} %get-tuple-element.216) | copy-start | bytes 3145732
  86.8 1.6 %copy-start.4 = (f32[16,1,128]{2,1,0:T(1,128)S(1)}, f32[16,1,128]{2,1,0:T(1,128)}, u32[]{:S(2)}) copy-start(f32[16,1,128]{2,1,0:T(1,128)} %get-tuple-element.215) | copy-start | bytes 24580
  87.1 8.4 %collective-permute-start.9 = (f32[2,128,128]{2,1,0:T(8,128)S(1)}, f32[2,128,128]{2,1,0:T(8,128)S(1)}, u32[]{:S(2)}, u32[]{:S(2)}) collective-permute-start(f32[2,128,128]{2,1,0:T(8,128)S(1)} %bitcast_add_fusion.5), channel_id=1, source_target_pairs={{4,0},{8,4},{12,8},{5,1},{9,5},{13,9},{6,2},{10,6},{14,10},{7,3},{... | collective-permute-start | bytes 393224 | tf_op jit(solution)/shard_map/ppermute | solution.py:59
  96.3 7.6 %collective-permute-start.10 = (f32[2,128,128]{2,1,0:T(8,128)S(1)}, f32[2,128,128]{2,1,0:T(8,128)S(1)}, u32[]{:S(2)}, u32[]{:S(2)}) collective-permute-start(f32[2,128,128]{2,1,0:T(8,128)S(1)} %bitcast_add_fusion.4), channel_id=1, source_target_pairs={{4,0},{8,4},{12,8},{5,1},{9,5},{13,9},{6,2},{10,6},{14,10},{7,3},{... | collective-permute-start | bytes 393224 | tf_op jit(solution)/shard_map/ppermute | solution.py:59
  104.7 7.8 %collective-permute-start.11 = (f32[2,128,128]{2,1,0:T(8,128)S(1)}, f32[2,128,128]{2,1,0:T(8,128)S(1)}, u32[]{:S(2)}, u32[]{:S(2)}) collective-permute-start(f32[2,128,128]{2,1,0:T(8,128)S(1)} %bitcast_add_fusion.3), channel_id=1, source_target_pairs={{4,0},{8,4},{12,8},{5,1},{9,5},{13,9},{6,2},{10,6},{14,10},{7,3},{... | collective-permute-start | bytes 393224 | tf_op jit(solution)/shard_map/ppermute | solution.py:59
  113.2 8.4 %collective-permute-start.12 = (f32[2,128,128]{2,1,0:T(8,128)S(1)}, f32[2,128,128]{2,1,0:T(8,128)S(1)}, u32[]{:S(2)}, u32[]{:S(2)}) collective-permute-start(f32[2,128,128]{2,1,0:T(8,128)S(1)} %bitcast_add_fusion.2), channel_id=1, source_target_pairs={{4,0},{8,4},{12,8},{5,1},{9,5},{13,9},{6,2},{10,6},{14,10},{7,3},{... | collective-permute-start | bytes 393224 | tf_op jit(solution)/shard_map/ppermute | solution.py:59
  122.3 8.4 %collective-permute-start.14 = (f32[2,128,128]{2,1,0:T(8,128)S(1)}, f32[2,128,128]{2,1,0:T(8,128)S(1)}, u32[]{:S(2)}, u32[]{:S(2)}) collective-permute-start(f32[2,128,128]{2,1,0:T(8,128)S(1)} %bitcast_add_fusion.1), channel_id=1, source_target_pairs={{4,0},{8,4},{12,8},{5,1},{9,5},{13,9},{6,2},{10,6},{14,10},{7,3},{... | collective-permute-start | bytes 393224 | tf_op jit(solution)/shard_map/ppermute | solution.py:59
  124.3 6.4 %collective-permute-start.13 = (f32[16,128]{1,0:T(8,128)S(1)}, f32[16,128]{1,0:T(8,128)S(1)}, u32[]{:S(2)}, u32[]{:S(2)}) collective-permute-start(f32[16,128]{1,0:T(8,128)S(1)} %bitcast.229), channel_id=1, source_target_pairs={{0,4},{4,0},{8,12},{12,8},{1,5},{5,1},{9,13},{13,9},{2,6},{6,2},{1... | collective-permute-start | bytes 24584 | tf_op jit(solution)/shard_map/ppermute | solution.py:112
  131.4 8.1 %collective-permute-start.16 = (f32[2,128,128]{2,1,0:T(8,128)S(1)}, f32[2,128,128]{2,1,0:T(8,128)S(1)}, u32[]{:S(2)}, u32[]{:S(2)}) collective-permute-start(f32[2,128,128]{2,1,0:T(8,128)S(1)} %bitcast_add_fusion), channel_id=1, source_target_pairs={{4,0},{8,4},{12,8},{5,1},{9,5},{13,9},{6,2},{10,6},{14,10},{7,3},{... | collective-permute-start | bytes 393224 | tf_op jit(solution)/shard_map/ppermute | solution.py:59
  132.7 6.8 %collective-permute-start.15 = (f32[16,128]{1,0:T(8,128)S(1)}, f32[16,128]{1,0:T(8,128)S(1)}, u32[]{:S(2)}, u32[]{:S(2)}) collective-permute-start(f32[16,128]{1,0:T(8,128)S(1)} %add.224), channel_id=1, source_target_pairs={{0,8},{4,12},{8,0},{12,4},{1,9},{5,13},{9,1},{13,5},{2,10},{6,14},... | collective-permute-start | bytes 24584 | tf_op jit(solution)/shard_map/ppermute | solution.py:112
  140.2 2.0 %collective-permute-start.17 = (f32[8,128,128]{2,1,0:T(8,128)S(1)}, f32[8,128,128]{2,1,0:T(8,128)S(1)}, u32[]{:S(2)}, u32[]{:S(2)}) collective-permute-start(f32[8,128,128]{2,1,0:T(8,128)S(1)} %bitcast.202), channel_id=1, source_target_pairs={{0,1},{1,0},{2,3},{3,2},{4,5},{5,4},{6,7},{7,6},{8,9},{9,8},{10,11... | collective-permute-start | bytes 1572872 | tf_op jit(solution)/shard_map/ppermute | solution.py:20

commit v10 on v9

--- a/solution.py
+++ b/solution.py
@@ -56,16 +56,17 @@
     for step in range(steps):
         send = jnp.clip(step - rank, 0, count - 1)
         outgoing = factor[send] * prefix[send] + pieces[send]
+        if step < len(pieces_of_cover):
+            cover = pieces_of_cover[step](cover, outgoing)
         arrived = lax.ppermute(outgoing, "ctx", perm=perm)
         where_to = step - rank + 1
         valid = (where_to >= 0) & (where_to < count) & (rank >= 1)
         slot = jnp.clip(where_to, 0, count - 1)
         prefix = prefix.at[slot].set(jnp.where(valid, arrived, prefix[slot]))
         if step < len(pieces_of_cover):
-            cover = pieces_of_cover[step](cover)
             cover, prefix = lax.optimization_barrier((cover, prefix))
     for piece in pieces_of_cover[steps:]:
-        cover = piece(cover)
+        cover = piece(cover, prefix)
     return prefix.reshape(heads, DH, DH), cover
 
 
@@ -104,10 +105,10 @@
     chip_decay = fin_first + fin_second
     chips = lax.axis_size("ctx")
 
-    def grads_step(piece, both):
-        return piece(both[0]), both[1]
-
-    def gain_step(distance, both):
+    def grads_step(piece, both, anchor):
+        return piece(both[0], anchor), both[1]
+
+    def gain_step(distance, both, anchor):
         partners = [(i, i ^ distance) for i in range(chips)]
         return both[0], both[1] + lax.ppermute(both[1], "ctx", perm=partners)
 
@@ -299,10 +300,11 @@
         [("square", f32)],
         heads, length, small, 2 * rows_bytes,
     )
-    def intra_piece(part, done):
+    def intra_piece(part, done, anchor):
+        q_tied, _ = lax.optimization_barrier((q, anchor))
         return _per_head(
             intra_kernel,
-            [("rows", q), ("rows", k), ("rows", v), ("cum", cum), ("cumt", cum_t)],
+            [("rows", q_tied), ("rows", k), ("rows", v), ("cum", cum), ("cumt", cum_t)],
             [("rows", f32)],
             heads, length, 2 * big, 5 * rows_bytes, heads * length * length, part=part, into=done,
         )
@@ -318,10 +320,11 @@
         [("rows", bf16), ("square", f32), ("gain", f32)],
         heads, length, 2 * small, 5 * rows_bytes,
     )
-    def grads_piece(part, done):
+    def grads_piece(part, done, anchor):
+        og_tied, _ = lax.optimization_barrier((out_grad, anchor))
         return _per_head(
             grads_kernel,
-            [("rows", q), ("rows", k), ("rows", v), ("rows", out_grad), ("cum", cum), ("cumt", cum_t),
+            [("rows", q), ("rows", k), ("rows", v), ("rows", og_tied), ("cum", cum), ("cumt", cum_t),
              ("square", state_low)],
             [("rows", bf16), ("rows", f32), ("rows", f32)],
             heads, length, 5 * big + small, 9 * rows_bytes, heads * length * length, part=part, into=done,

time: 153 us -> 150 us (0.980)
  waiting for transfers between devices: 21.3 us -> 18.6 us
    ppermute x12, waiting for transfers between devices: 11.1 us -> 6.48 us  [chain_scan(): arrived = lax.ppermute(outgoing, 'ctx', perm=perm)]
  transfers between devices with their start and end apart: 18 -> 18, of which waited for: 9 -> 11; matrix products, arithmetic and copies ran while one was open for 4% -> 4% of each run, Pallas kernels for 27% -> 27%
where the time goes in v10:
time: 150 us; the launch traced here: 149 us
  Pallas kernels  64.3 us (43%)
  starting transfers between devices  38.5 us (26%)
  other arithmetic  23.2 us (15%)
  waiting for transfers between devices  18.6 us (12%)
  local copies, waits for them, and re-layouts  2.79 us (2%)
    pallas_call x11, Pallas kernels, _per_head(): pl.pallas_call(body, grid=(count,), in_specs=in_specs, out_specs=[spec(ki...  64.3 us
    ppermute x12, starting transfers between devices, chain_scan(): arrived = lax.ppermute(outgoing, 'ctx', perm=perm)  30.6 us
    scatter x12, other arithmetic, chain_scan(): prefix = prefix.at[slot].set(jnp.where(valid, arrived, prefix[slot]))  7.77 us
    ppermute x2, starting transfers between devices, gain_step(): return (both[0], both[1] + lax.ppermute(both[1], 'ctx', perm=partners))  7.06 us
    ppermute x12, waiting for transfers between devices, chain_scan(): arrived = lax.ppermute(outgoing, 'ctx', perm=perm)  6.48 us
    ppermute x2, waiting for transfers between devices, gain_step(): return (both[0], both[1] + lax.ppermute(both[1], 'ctx', perm=partners))  6.23 us
    ppermute x4, waiting for transfers between devices, swap_dp(): return lax.ppermute(x, 'dp', perm=[(0, 1), (1, 0)])  5.88 us
    another operation x6, other arithmetic  4.5 us
  transfers between devices with their start and end apart: 18, of which 11 were waited for; matrix products, arithmetic and copies ran while one was open for 4% of the time, Pallas kernels for 27%

profile of v10, /device:TPU:0, one launch (start us, length us, event | category | flops | bytes accessed | tf_op | source)
XLA Modules:
  0.0 148.8 jit_solution(3094251204266739083)
XLA Ops:
  3.0 5.8 %shard_map.93 = f32[16,128,128]{2,1,0:T(8,128)} custom-call(bf16[512,2048]{1,0:T(8,128)(2,1)} %k_ref.7, bf16[512,2048]{1,0:T(8,128)(2,1)} %v_ref.7, f32[512,16]{1,0:T(8,128)} %copy.37.cum_ref.refs_3_.refs_4_, f32[16,512]{1,0:T(8,128)} %bitcast.204), custom_call_target="tpu_custom_call" | custom-call | flops 268435456 | bytes 4194304 | tf_op jit(solution)/shard_map/pallas_call | solution.py:267
  14.2 4.9 %collective-permute-start.1 = (f32[2,128,128]{2,1,0:T(8,128)S(1)}, f32[2,128,128]{2,1,0:T(8,128)S(1)}, u32[]{:S(2)}, u32[]{:S(2)}) collective-permute-start(f32[2,128,128]{2,1,0:T(8,128)S(1)} %bitcast_add_fusion.11), channel_id=1, source_target_pairs={{0,4},{4,8},{8,12},{1,5},{5,9},{9,13},{2,6},{6,10},{10,14},{3,7},{... | collective-permute-start | bytes 393224 | tf_op jit(solution)/shard_map/ppermute | solution.py:61
  19.7 3.8 %shard_map.94.refs_5_ = f32[512,2048]{1,0:T(8,128)} custom-call(bf16[512,2048]{1,0:T(8,128)(2,1)} %refs_0_.8, bf16[512,2048]{1,0:T(8,128)(2,1)} %k_ref.7, bf16[512,2048]{1,0:T(8,128)(2,1)} %v_ref.7, f32[512,16]{1,0:T(8,128)} %copy.37.cum_ref.refs_3_.refs_4_, f32[16,512]{1,0:T(8,128)} %bitcast.205), custom_call_target="tpu_custom_call" | custom-call | flops 536870912 | bytes 2621440 | tf_op jit(solution)/shard_map/pallas_call | solution.py:267
  24.4 3.5 %collective-permute-start.2 = (f32[2,128,128]{2,1,0:T(8,128)S(1)}, f32[2,128,128]{2,1,0:T(8,128)S(1)}, u32[]{:S(2)}, u32[]{:S(2)}) collective-permute-start(f32[2,128,128]{2,1,0:T(8,128)S(1)} %bitcast_add_fusion.10), channel_id=1, source_target_pairs={{0,4},{4,8},{8,12},{1,5},{5,9},{9,13},{2,6},{6,10},{10,14},{3,7},{... | collective-permute-start | bytes 393224 | tf_op jit(solution)/shard_map/ppermute | solution.py:61
  27.9 3.9 %shard_map.95.refs_5_ = f32[512,2048]{1,0:T(8,128)} custom-call(bf16[512,2048]{1,0:T(8,128)(2,1)} %refs_0_.8, bf16[512,2048]{1,0:T(8,128)(2,1)} %k_ref.7, bf16[512,2048]{1,0:T(8,128)(2,1)} %v_ref.7, f32[512,16]{1,0:T(8,128)} %copy.37.cum_ref.refs_3_.refs_4_, f32[16,512]{1,0:T(8,128)} %bitcast.206, ...), custom_call_target="tpu_custom_call", output_to_operand_aliasing={{}: (5, {})} | custom-call | flops 536870912 | bytes 2621440 | tf_op jit(solution)/shard_map/pallas_call | solution.py:267
  32.5 3.5 %collective-permute-start.3 = (f32[2,128,128]{2,1,0:T(8,128)S(1)}, f32[2,128,128]{2,1,0:T(8,128)S(1)}, u32[]{:S(2)}, u32[]{:S(2)}) collective-permute-start(f32[2,128,128]{2,1,0:T(8,128)S(1)} %bitcast_add_fusion.9), channel_id=1, source_target_pairs={{0,4},{4,8},{8,12},{1,5},{5,9},{9,13},{2,6},{6,10},{10,14},{3,7},{... | collective-permute-start | bytes 393224 | tf_op jit(solution)/shard_map/ppermute | solution.py:61
  36.0 3.8 %shard_map.96.refs_5_ = f32[512,2048]{1,0:T(8,128)} custom-call(bf16[512,2048]{1,0:T(8,128)(2,1)} %refs_0_.8, bf16[512,2048]{1,0:T(8,128)(2,1)} %k_ref.7, bf16[512,2048]{1,0:T(8,128)(2,1)} %v_ref.7, f32[512,16]{1,0:T(8,128)} %copy.37.cum_ref.refs_3_.refs_4_, f32[16,512]{1,0:T(8,128)} %bitcast.207, ...), custom_call_target="tpu_custom_call", output_to_operand_aliasing={{}: (5, {})} | custom-call | flops 536870912 | bytes 2621440 | tf_op jit(solution)/shard_map/pallas_call | solution.py:267
  40.5 3.2 %collective-permute-start.4 = (f32[2,128,128]{2,1,0:T(8,128)S(1)}, f32[2,128,128]{2,1,0:T(8,128)S(1)}, u32[]{:S(2)}, u32[]{:S(2)}) collective-permute-start(f32[2,128,128]{2,1,0:T(8,128)S(1)} %bitcast_add_fusion.8), channel_id=1, source_target_pairs={{0,4},{4,8},{8,12},{1,5},{5,9},{9,13},{2,6},{6,10},{10,14},{3,7},{... | collective-permute-start | bytes 393224 | tf_op jit(solution)/shard_map/ppermute | solution.py:61
  43.8 3.8 %shard_map.97.intra_ref = f32[512,2048]{1,0:T(8,128)} custom-call(bf16[512,2048]{1,0:T(8,128)(2,1)} %refs_0_.8, bf16[512,2048]{1,0:T(8,128)(2,1)} %k_ref.7, bf16[512,2048]{1,0:T(8,128)(2,1)} %v_ref.7, f32[512,16]{1,0:T(8,128)} %copy.37.cum_ref.refs_3_.refs_4_, f32[16,512]{1,0:T(8,128)} %bitcast.208, ...), custom_call_target="tpu_custom_call", output_to_operand_aliasing={{}: (5, {})} | custom-call | flops 536870912 | bytes 2621440 | tf_op jit(solution)/shard_map/pallas_call | solution.py:267
  48.4 3.0 %collective-permute-start.5 = (f32[2,128,128]{2,1,0:T(8,128)S(1)}, f32[2,128,128]{2,1,0:T(8,128)S(1)}, u32[]{:S(2)}, u32[]{:S(2)}) collective-permute-start(f32[2,128,128]{2,1,0:T(8,128)S(1)} %bitcast_add_fusion.7), channel_id=1, source_target_pairs={{0,4},{4,8},{8,12},{1,5},{5,9},{9,13},{2,6},{6,10},{10,14},{3,7},{... | collective-permute-start | bytes 393224 | tf_op jit(solution)/shard_map/ppermute | solution.py:61
  52.1 1.8 %collective-permute-done.5 = f32[2,128,128]{2,1,0:T(8,128)S(1)} collective-permute-done((f32[2,128,128]{2,1,0:T(8,128)S(1)}, f32[2,128,128]{2,1,0:T(8,128)S(1)}, u32[]{:S(2)}, u32[]{:S(2)}) %collective-permute-start.5) | collective-permute-done | bytes 131104 | tf_op jit(solution)/shard_map/ppermute | solution.py:61
  54.6 4.4 %collective-permute-start.6 = (f32[2,128,128]{2,1,0:T(8,128)S(1)}, f32[2,128,128]{2,1,0:T(8,128)S(1)}, u32[]{:S(2)}, u32[]{:S(2)}) collective-permute-start(f32[2,128,128]{2,1,0:T(8,128)S(1)} %bitcast_add_fusion.6), channel_id=1, source_target_pairs={{0,4},{4,8},{8,12},{1,5},{5,9},{9,13},{2,6},{6,10},{10,14},{3,7},{... | collective-permute-start | bytes 393224 | tf_op jit(solution)/shard_map/ppermute | solution.py:61
  59.0 2.5 %collective-permute-done.6 = f32[2,128,128]{2,1,0:T(8,128)S(1)} collective-permute-done((f32[2,128,128]{2,1,0:T(8,128)S(1)}, f32[2,128,128]{2,1,0:T(8,128)S(1)}, u32[]{:S(2)}, u32[]{:S(2)}) %collective-permute-start.6) | collective-permute-done | bytes 131104 | tf_op jit(solution)/shard_map/ppermute | solution.py:61
  62.3 1.8 %collective-permute-done.7 = f32[8,128,128]{2,1,0:T(8,128)S(1)} collective-permute-done((f32[8,128,128]{2,1,0:T(8,128)S(1)}, f32[8,128,128]{2,1,0:T(8,128)S(1)}, u32[]{:S(2)}, u32[]{:S(2)}) %collective-permute-start.7) | collective-permute-done | bytes 524320 | tf_op jit(solution)/shard_map/ppermute | solution.py:20
  65.3 9.4 %shard_map.98 = (bf16[512,2048]{1,0:T(8,128)(2,1)}, f32[16,128,128]{2,1,0:T(8,128)}, f32[16,1,128]{2,1,0:T(1,128)}) custom-call(bf16[512,2048]{1,0:T(8,128)(2,1)} %refs_0_.8, bf16[512,2048]{1,0:T(8,128)(2,1)} %g_ref.1, f32[512,2048]{1,0:T(8,128)} %shard_map.97.intra_ref, bf16[16,128,128]{2,1,0:T(8,128)(2,1)} %select_convert_fusion.1.st_ref.refs_6_, ...), custom_call_target="tpu_custom_call" | custom-call | flops 536870912 | bytes 10485760 | tf_op jit(solution)/shard_map/pallas_call | solution.py:267
  84.4 6.3 %shard_map.99 = (bf16[512,2048]{1,0:T(8,128)(2,1)}, f32[512,2048]{1,0:T(8,128)}, f32[512,2048]{1,0:T(8,128)}) custom-call(bf16[512,2048]{1,0:T(8,128)(2,1)} %refs_0_.8, bf16[512,2048]{1,0:T(8,128)(2,1)} %k_ref.7, bf16[512,2048]{1,0:T(8,128)(2,1)} %v_ref.7, bf16[512,2048]{1,0:T(8,128)(2,1)} %get-tuple-element.249.og_ref.refs_3_, ...), custom_call_target="tpu_custom_call" | custom-call | flops 1409286144 | bytes 4718592 | tf_op jit(solution)/shard_map/pallas_call | solution.py:267
  92.9 6.3 %shard_map.100 = (bf16[512,2048]{1,0:T(8,128)(2,1)}, f32[512,2048]{1,0:T(8,128)}, f32[512,2048]{1,0:T(8,128)}) custom-call(bf16[512,2048]{1,0:T(8,128)(2,1)} %refs_0_.8, bf16[512,2048]{1,0:T(8,128)(2,1)} %k_ref.7, bf16[512,2048]{1,0:T(8,128)(2,1)} %v_ref.7, ...), custom_call_target="tpu_custom_call", output_to_operand_aliasing={{0}: (7, {}), {1}: (8, {}), {2}: (9, {})} | custom-call | flops 1409286144 | bytes 4718592 | tf_op jit(solution)/shard_map/pallas_call | solution.py:267
  102.4 6.3 %shard_map.101 = (bf16[512,2048]{1,0:T(8,128)(2,1)}, f32[512,2048]{1,0:T(8,128)}, f32[512,2048]{1,0:T(8,128)}) custom-call(bf16[512,2048]{1,0:T(8,128)(2,1)} %refs_0_.8, bf16[512,2048]{1,0:T(8,128)(2,1)} %k_ref.7, bf16[512,2048]{1,0:T(8,128)(2,1)} %v_ref.7, ...), custom_call_target="tpu_custom_call", output_to_operand_aliasing={{0}: (7, {}), {1}: (8, {}), {2}: (9, {})} | custom-call | flops 1409286144 | bytes 4718592 | tf_op jit(solution)/shard_map/pallas_call | solution.py:267
  111.7 6.3 %shard_map.102 = (bf16[512,2048]{1,0:T(8,128)(2,1)}, f32[512,2048]{1,0:T(8,128)}, f32[512,2048]{1,0:T(8,128)}) custom-call(bf16[512,2048]{1,0:T(8,128)(2,1)} %refs_0_.8, bf16[512,2048]{1,0:T(8,128)(2,1)} %k_ref.7, bf16[512,2048]{1,0:T(8,128)(2,1)} %v_ref.7, ...), custom_call_target="tpu_custom_call", output_to_operand_aliasing={{0}: (7, {}), {1}: (8, {}), {2}: (9, {})} | custom-call | flops 1409286144 | bytes 4718592 | tf_op jit(solution)/shard_map/pallas_call | solution.py:267
  121.2 3.4 %collective-permute-start.13 = (f32[16,128]{1,0:T(8,128)S(1)}, f32[16,128]{1,0:T(8,128)S(1)}, u32[]{:S(2)}, u32[]{:S(2)}) collective-permute-start(f32[16,128]{1,0:T(8,128)S(1)} %bitcast.229), channel_id=1, source_target_pairs={{0,4},{4,0},{8,12},{12,8},{1,5},{5,1},{9,13},{13,9},{2,6},{6,2},{1... | collective-permute-start | bytes 24584 | tf_op jit(solution)/shard_map/ppermute | solution.py:113
  124.6 3.2 %collective-permute-done.13 = f32[16,128]{1,0:T(8,128)S(1)} collective-permute-done((f32[16,128]{1,0:T(8,128)S(1)}, f32[16,128]{1,0:T(8,128)S(1)}, u32[]{:S(2)}, u32[]{:S(2)}) %collective-permute-start.13) | collective-permute-done | bytes 8224 | tf_op jit(solution)/shard_map/ppermute | solution.py:113
  129.8 3.7 %collective-permute-start.15 = (f32[16,128]{1,0:T(8,128)S(1)}, f32[16,128]{1,0:T(8,128)S(1)}, u32[]{:S(2)}, u32[]{:S(2)}) collective-permute-start(f32[16,128]{1,0:T(8,128)S(1)} %add.209), channel_id=1, source_target_pairs={{0,8},{4,12},{8,0},{12,4},{1,9},{5,13},{9,1},{13,5},{2,10},{6,14},... | collective-permute-start | bytes 24584 | tf_op jit(solution)/shard_map/ppermute | solution.py:113
  133.6 3.0 %collective-permute-done.15 = f32[16,128]{1,0:T(8,128)S(1)} collective-permute-done((f32[16,128]{1,0:T(8,128)S(1)}, f32[16,128]{1,0:T(8,128)S(1)}, u32[]{:S(2)}, u32[]{:S(2)}) %collective-permute-start.15) | collective-permute-done | bytes 8224 | tf_op jit(solution)/shard_map/ppermute | solution.py:113
  140.4 8.4 %shard_map.103 = (bf16[512,2048]{1,0:T(8,128)(2,1)}, bf16[512,2048]{1,0:T(8,128)(2,1)}) custom-call(bf16[512,2048]{1,0:T(8,128)(2,1)} %k_ref.7, bf16[512,2048]{1,0:T(8,128)(2,1)} %v_ref.7, f32[512,2048]{1,0:T(8,128)} %get-tuple-element.268.kg_ref, f32[512,2048]{1,0:T(8,128)} %get-tuple-element.269.vg_ref, bf16[16,128,128]{2,1,0:T(8,128)(2,1)} %select_convert_fusion.gl_ref, ...), custom_call_target="tpu_custom_call" | custom-call | flops 536870912 | bytes 16777216 | tf_op jit(solution)/shard_map/pallas_call | solution.py:267
  (111 shorter events, 41.7 us)
Async XLA Ops:
  0.6 0.8 copy-start
  1.8 1.2 copy-start.3
  8.8 2.1 %copy-start.5 = (s32[4]{0:T(128)S(1)}, s32[4]{0:T(128)}, u32[]{:S(2)}) copy-start(s32[4]{0:T(128)} %constant.302.clone.1) | copy-start | bytes 52
  8.8 4.9 %copy-start.1 = (f32[16,128,128]{2,1,0:T(8,128)S(1)}, f32[16,128,128]{2,1,0:T(8,128)}, u32[]{:S(2)}) copy-start(f32[16,128,128]{2,1,0:T(8,128)} %shard_map.93) | copy-start | bytes 3145732
  10.3 2.9 %collective-permute-start = (f32[16,136,128]{2,1,0:T(8,128)S(1)}, f32[16,136,128]{2,1,0:T(8,128)S(1)}, u32[]{:S(2)}, u32[]{:S(2)}) collective-permute-start(f32[16,136,128]{2,1,0:T(8,128)S(1)} %fusion), channel_id=1, source_target_pairs={{0,1},{1,0},{2,3},{3,2},{4,5},{5,4},{6,7},{7,6},{8,9},{9,8},{10,11... | collective-permute-start | bytes 3342344 | tf_op jit(solution)/shard_map/ppermute | solution.py:20
  14.2 9.4 %collective-permute-start.1 = (f32[2,128,128]{2,1,0:T(8,128)S(1)}, f32[2,128,128]{2,1,0:T(8,128)S(1)}, u32[]{:S(2)}, u32[]{:S(2)}) collective-permute-start(f32[2,128,128]{2,1,0:T(8,128)S(1)} %bitcast_add_fusion.11), channel_id=1, source_target_pairs={{0,4},{4,8},{8,12},{1,5},{5,9},{9,13},{2,6},{6,10},{10,14},{3,7},{... | collective-permute-start | bytes 393224 | tf_op jit(solution)/shard_map/ppermute | solution.py:61
  24.4 7.4 %collective-permute-start.2 = (f32[2,128,128]{2,1,0:T(8,128)S(1)}, f32[2,128,128]{2,1,0:T(8,128)S(1)}, u32[]{:S(2)}, u32[]{:S(2)}) collective-permute-start(f32[2,128,128]{2,1,0:T(8,128)S(1)} %bitcast_add_fusion.10), channel_id=1, source_target_pairs={{0,4},{4,8},{8,12},{1,5},{5,9},{9,13},{2,6},{6,10},{10,14},{3,7},{... | collective-permute-start | bytes 393224 | tf_op jit(solution)/shard_map/ppermute | solution.py:61
  32.5 7.3 %collective-permute-start.3 = (f32[2,128,128]{2,1,0:T(8,128)S(1)}, f32[2,128,128]{2,1,0:T(8,128)S(1)}, u32[]{:S(2)}, u32[]{:S(2)}) collective-permute-start(f32[2,128,128]{2,1,0:T(8,128)S(1)} %bitcast_add_fusion.9), channel_id=1, source_target_pairs={{0,4},{4,8},{8,12},{1,5},{5,9},{9,13},{2,6},{6,10},{10,14},{3,7},{... | collective-permute-start | bytes 393224 | tf_op jit(solution)/shard_map/ppermute | solution.py:61
  40.5 7.1 %collective-permute-start.4 = (f32[2,128,128]{2,1,0:T(8,128)S(1)}, f32[2,128,128]{2,1,0:T(8,128)S(1)}, u32[]{:S(2)}, u32[]{:S(2)}) collective-permute-start(f32[2,128,128]{2,1,0:T(8,128)S(1)} %bitcast_add_fusion.8), channel_id=1, source_target_pairs={{0,4},{4,8},{8,12},{1,5},{5,9},{9,13},{2,6},{6,10},{10,14},{3,7},{... | collective-permute-start | bytes 393224 | tf_op jit(solution)/shard_map/ppermute | solution.py:61
  48.4 5.5 %collective-permute-start.5 = (f32[2,128,128]{2,1,0:T(8,128)S(1)}, f32[2,128,128]{2,1,0:T(8,128)S(1)}, u32[]{:S(2)}, u32[]{:S(2)}) collective-permute-start(f32[2,128,128]{2,1,0:T(8,128)S(1)} %bitcast_add_fusion.7), channel_id=1, source_target_pairs={{0,4},{4,8},{8,12},{1,5},{5,9},{9,13},{2,6},{6,10},{10,14},{3,7},{... | collective-permute-start | bytes 393224 | tf_op jit(solution)/shard_map/ppermute | solution.py:61
  54.6 6.9 %collective-permute-start.6 = (f32[2,128,128]{2,1,0:T(8,128)S(1)}, f32[2,128,128]{2,1,0:T(8,128)S(1)}, u32[]{:S(2)}, u32[]{:S(2)}) collective-permute-start(f32[2,128,128]{2,1,0:T(8,128)S(1)} %bitcast_add_fusion.6), channel_id=1, source_target_pairs={{0,4},{4,8},{8,12},{1,5},{5,9},{9,13},{2,6},{6,10},{10,14},{3,7},{... | collective-permute-start | bytes 393224 | tf_op jit(solution)/shard_map/ppermute | solution.py:61
  62.2 2.0 %collective-permute-start.7 = (f32[8,128,128]{2,1,0:T(8,128)S(1)}, f32[8,128,128]{2,1,0:T(8,128)S(1)}, u32[]{:S(2)}, u32[]{:S(2)}) collective-permute-start(f32[8,128,128]{2,1,0:T(8,128)S(1)} %bitcast.203), channel_id=1, source_target_pairs={{0,1},{1,0},{2,3},{3,2},{4,5},{5,4},{6,7},{7,6},{8,9},{9,8},{10,11... | collective-permute-start | bytes 1572872 | tf_op jit(solution)/shard_map/ppermute | solution.py:20
  74.7 5.7 %copy-start.2 = (f32[16,128,128]{2,1,0:T(8,128)S(1)}, f32[16,128,128]{2,1,0:T(8,128)}, u32[]{:S(2)}) copy-start(f32[16,128,128]{2,1,0:T(8,128)} %get-tuple-element.224) | copy-start | bytes 3145732
  76.2 3.0 %collective-permute-start.8 = (f32[16,136,128]{2,1,0:T(8,128)S(1)}, f32[16,136,128]{2,1,0:T(8,128)}, u32[]{:S(2)}, u32[]{:S(2)}) collective-permute-start(f32[16,136,128]{2,1,0:T(8,128)S(1)} %fusion.2), channel_id=1, source_target_pairs={{0,1},{1,0},{2,3},{3,2},{4,5},{5,4},{6,7},{7,6},{8,9},{9,8},{10,11... | collective-permute-start | bytes 3342344 | tf_op jit(solution)/shard_map/ppermute | solution.py:20
  81.8 1.7 %copy-start.4 = (f32[16,1,128]{2,1,0:T(1,128)S(1)}, f32[16,1,128]{2,1,0:T(1,128)}, u32[]{:S(2)}) copy-start(f32[16,1,128]{2,1,0:T(1,128)} %get-tuple-element.225) | copy-start | bytes 24580
  82.1 8.7 %collective-permute-start.9 = (f32[2,128,128]{2,1,0:T(8,128)S(1)}, f32[2,128,128]{2,1,0:T(8,128)S(1)}, u32[]{:S(2)}, u32[]{:S(2)}) collective-permute-start(f32[2,128,128]{2,1,0:T(8,128)S(1)} %bitcast_add_fusion.5), channel_id=1, source_target_pairs={{4,0},{8,4},{12,8},{5,1},{9,5},{13,9},{6,2},{10,6},{14,10},{7,3},{... | collective-permute-start | bytes 393224 | tf_op jit(solution)/shard_map/ppermute | solution.py:61
  91.6 8.8 %collective-permute-start.10 = (f32[2,128,128]{2,1,0:T(8,128)S(1)}, f32[2,128,128]{2,1,0:T(8,128)S(1)}, u32[]{:S(2)}, u32[]{:S(2)}) collective-permute-start(f32[2,128,128]{2,1,0:T(8,128)S(1)} %bitcast_add_fusion.4), channel_id=1, source_target_pairs={{4,0},{8,4},{12,8},{5,1},{9,5},{13,9},{6,2},{10,6},{14,10},{7,3},{... | collective-permute-start | bytes 393224 | tf_op jit(solution)/shard_map/ppermute | solution.py:61
  101.1 8.2 %collective-permute-start.11 = (f32[2,128,128]{2,1,0:T(8,128)S(1)}, f32[2,128,128]{2,1,0:T(8,128)S(1)}, u32[]{:S(2)}, u32[]{:S(2)}) collective-permute-start(f32[2,128,128]{2,1,0:T(8,128)S(1)} %bitcast_add_fusion.3), channel_id=1, source_target_pairs={{4,0},{8,4},{12,8},{5,1},{9,5},{13,9},{6,2},{10,6},{14,10},{7,3},{... | collective-permute-start | bytes 393224 | tf_op jit(solution)/shard_map/ppermute | solution.py:61
  110.2 8.2 %collective-permute-start.12 = (f32[2,128,128]{2,1,0:T(8,128)S(1)}, f32[2,128,128]{2,1,0:T(8,128)S(1)}, u32[]{:S(2)}, u32[]{:S(2)}) collective-permute-start(f32[2,128,128]{2,1,0:T(8,128)S(1)} %bitcast_add_fusion.2), channel_id=1, source_target_pairs={{4,0},{8,4},{12,8},{5,1},{9,5},{13,9},{6,2},{10,6},{14,10},{7,3},{... | collective-permute-start | bytes 393224 | tf_op jit(solution)/shard_map/ppermute | solution.py:61
  119.2 8.6 %collective-permute-start.14 = (f32[2,128,128]{2,1,0:T(8,128)S(1)}, f32[2,128,128]{2,1,0:T(8,128)S(1)}, u32[]{:S(2)}, u32[]{:S(2)}) collective-permute-start(f32[2,128,128]{2,1,0:T(8,128)S(1)} %bitcast_add_fusion.1), channel_id=1, source_target_pairs={{4,0},{8,4},{12,8},{5,1},{9,5},{13,9},{6,2},{10,6},{14,10},{7,3},{... | collective-permute-start | bytes 393224 | tf_op jit(solution)/shard_map/ppermute | solution.py:61
  121.2 6.6 %collective-permute-start.13 = (f32[16,128]{1,0:T(8,128)S(1)}, f32[16,128]{1,0:T(8,128)S(1)}, u32[]{:S(2)}, u32[]{:S(2)}) collective-permute-start(f32[16,128]{1,0:T(8,128)S(1)} %bitcast.229), channel_id=1, source_target_pairs={{0,4},{4,0},{8,12},{12,8},{1,5},{5,1},{9,13},{13,9},{2,6},{6,2},{1... | collective-permute-start | bytes 24584 | tf_op jit(solution)/shard_map/ppermute | solution.py:113
  128.5 8.0 %collective-permute-start.16 = (f32[2,128,128]{2,1,0:T(8,128)S(1)}, f32[2,128,128]{2,1,0:T(8,128)S(1)}, u32[]{:S(2)}, u32[]{:S(2)}) collective-permute-start(f32[2,128,128]{2,1,0:T(8,128)S(1)} %bitcast_add_fusion), channel_id=1, source_target_pairs={{4,0},{8,4},{12,8},{5,1},{9,5},{13,9},{6,2},{10,6},{14,10},{7,3},{... | collective-permute-start | bytes 393224 | tf_op jit(solution)/shard_map/ppermute | solution.py:61
  129.8 6.7 %collective-permute-start.15 = (f32[16,128]{1,0:T(8,128)S(1)}, f32[16,128]{1,0:T(8,128)S(1)}, u32[]{:S(2)}, u32[]{:S(2)}) collective-permute-start(f32[16,128]{1,0:T(8,128)S(1)} %add.209), channel_id=1, source_target_pairs={{0,8},{4,12},{8,0},{12,4},{1,9},{5,13},{9,1},{13,5},{2,10},{6,14},... | collective-permute-start | bytes 24584 | tf_op jit(solution)/shard_map/ppermute | solution.py:113
  137.2 2.0 %collective-permute-start.17 = (f32[8,128,128]{2,1,0:T(8,128)S(1)}, f32[8,128,128]{2,1,0:T(8,128)S(1)}, u32[]{:S(2)}, u32[]{:S(2)}) collective-permute-start(f32[8,128,128]{2,1,0:T(8,128)S(1)} %bitcast.202), channel_id=1, source_target_pairs={{0,1},{1,0},{2,3},{3,2},{4,5},{5,4},{6,7},{7,6},{8,9},{9,8},{10,11... | collective-permute-start | bytes 1572872 | tf_op jit(solution)/shard_map/ppermute | solution.py:20

commit v11 on v10

--- a/solution.py
+++ b/solution.py
@@ -11,6 +11,7 @@
 PAD = 8
 CHUNKS = 4
 HB = 4
+PIECE_STEPS = 2
 
 
 epsilon = 1e-06
@@ -154,8 +155,8 @@
     return (_nt(q, k) * decay).astype(jnp.bfloat16)
 
 
-def _head_vectors(cum_ref, cumt_ref, j, first=0):
-    h = (pl.program_id(0) + first) * HB + j
+def _head_vectors(cum_ref, cumt_ref, j, first=0, hb=None):
+    h = (pl.program_id(0) + first) * (HB if hb is None else hb) + j
     full = cum_ref[...]
     lane = lax.broadcasted_iota(jnp.int32, full.shape, 1)
     col = jnp.sum(jnp.where(lane == h, full, 0.0), axis=1, keepdims=True)
@@ -176,10 +177,10 @@
         s_ref[j] = _tn(scaled, v_ref[:, cols])
 
 
-def intra_kernel(first, q_ref, k_ref, v_ref, cum_ref, cumt_ref, out_ref):
-    for j in range(HB):
-        cols = _lanes(j)
-        col, row, _, _ = _head_vectors(cum_ref, cumt_ref, j, first)
+def intra_kernel(first, hb, q_ref, k_ref, v_ref, cum_ref, cumt_ref, out_ref):
+    for j in range(hb):
+        cols = _lanes(j)
+        col, row, _, _ = _head_vectors(cum_ref, cumt_ref, j, first, hb)
         decay = _decay(col, row)
         out_ref[:, cols] = _nn(_masked(q_ref[:, cols], k_ref[:, cols], decay), v_ref[:, cols])
 
@@ -205,10 +206,10 @@
         m_ref[j] = _tn(q_scaled, out_grad)
 
 
-def grads_kernel(first, q_ref, k_ref, v_ref, og_ref, cum_ref, cumt_ref, st_ref, qg_ref, kg_ref, vg_ref):
-    for j in range(HB):
-        cols = _lanes(j)
-        col, row, grow, _ = _head_vectors(cum_ref, cumt_ref, j, first)
+def grads_kernel(first, hb, q_ref, k_ref, v_ref, og_ref, cum_ref, cumt_ref, st_ref, qg_ref, kg_ref, vg_ref):
+    for j in range(hb):
+        cols = _lanes(j)
+        col, row, grow, _ = _head_vectors(cum_ref, cumt_ref, j, first, hb)
         decay = _decay(col, row)
         q, k, v, og = q_ref[:, cols], k_ref[:, cols], v_ref[:, cols], og_ref[:, cols]
         masked = _masked(q, k, decay)
@@ -228,21 +229,22 @@
 
 
 def _per_head(kernel, ins, outs, heads, length, flops, nbytes, exps=0, part=None, into=None):
-    groups = heads // HB
-    first, count = (0, groups) if part is None else (part, 1)
+    hb = HB if part is None else HB // PIECE_STEPS
+    groups = heads // hb
+    first, count = (0, groups) if part is None else (part * PIECE_STEPS, PIECE_STEPS)
     if part is not None:
-        kernel = functools.partial(kernel, first)
+        kernel = functools.partial(kernel, first, hb)
 
     def spec(kind):
         if kind == "rows":
-            return pl.BlockSpec((length, HB * DH), lambda i: (0, i + first))
+            return pl.BlockSpec((length, hb * DH), lambda i: (0, i + first))
         if kind == "cum":
             return pl.BlockSpec((length, heads), lambda i: (0, 0))
         if kind == "cumt":
             return pl.BlockSpec((heads, length), lambda i: (0, 0))
         if kind == "gain":
-            return pl.BlockSpec((HB, 1, DH), lambda i: (i + first, 0, 0))
-        return pl.BlockSpec((HB, DH, DH), lambda i: (i + first, 0, 0))
+            return pl.BlockSpec((hb, 1, DH), lambda i: (i + first, 0, 0))
+        return pl.BlockSpec((hb, DH, DH), lambda i: (i + first, 0, 0))
 
     shapes = {
         "rows": (length, heads * DH),

time: 150 us -> 150 us (level)
  no operation moved by 1% of the time
where the time goes in v11:
time: 150 us; the launch traced here: 148 us
  Pallas kernels  64.1 us (43%)
  starting transfers between devices  38.1 us (25%)
  other arithmetic  23.2 us (15%)
  waiting for transfers between devices  18.8 us (13%)
  local copies, waits for them, and re-layouts  2.79 us (2%)
    pallas_call x11, Pallas kernels, _per_head(): pl.pallas_call(body, grid=(count,), in_specs=in_specs, out_specs=[spec(ki...  64.1 us
    ppermute x12, starting transfers between devices, chain_scan(): arrived = lax.ppermute(outgoing, 'ctx', perm=perm)  30.4 us
    scatter x12, other arithmetic, chain_scan(): prefix = prefix.at[slot].set(jnp.where(valid, arrived, prefix[slot]))  7.77 us
    ppermute x2, starting transfers between devices, gain_step(): return (both[0], both[1] + lax.ppermute(both[1], 'ctx', perm=partners))  6.85 us
    ppermute x12, waiting for transfers between devices, chain_scan(): arrived = lax.ppermute(outgoing, 'ctx', perm=perm)  6.71 us
    ppermute x2, waiting for transfers between devices, gain_step(): return (both[0], both[1] + lax.ppermute(both[1], 'ctx', perm=partners))  6.23 us
    ppermute x4, waiting for transfers between devices, swap_dp(): return lax.ppermute(x, 'dp', perm=[(0, 1), (1, 0)])  5.88 us
    another operation x6, other arithmetic  4.5 us
  transfers between devices with their start and end apart: 18, of which 11 were waited for; matrix products, arithmetic and copies ran while one was open for 4% of the time, Pallas kernels for 27%

profile of v11, /device:TPU:0, one launch (start us, length us, event | category | flops | bytes accessed | tf_op | source)
XLA Modules:
  0.0 148.5 jit_solution(7845412681458403281)
XLA Ops:
  3.0 5.8 %shard_map.93 = f32[16,128,128]{2,1,0:T(8,128)} custom-call(bf16[512,2048]{1,0:T(8,128)(2,1)} %k_ref.7, bf16[512,2048]{1,0:T(8,128)(2,1)} %v_ref.7, f32[512,16]{1,0:T(8,128)} %copy.37.cum_ref.refs_3_.refs_4_, f32[16,512]{1,0:T(8,128)} %bitcast.204), custom_call_target="tpu_custom_call" | custom-call | flops 268435456 | bytes 4194304 | tf_op jit(solution)/shard_map/pallas_call | solution.py:269
  14.2 4.9 %collective-permute-start.1 = (f32[2,128,128]{2,1,0:T(8,128)S(1)}, f32[2,128,128]{2,1,0:T(8,128)S(1)}, u32[]{:S(2)}, u32[]{:S(2)}) collective-permute-start(f32[2,128,128]{2,1,0:T(8,128)S(1)} %bitcast_add_fusion.11), channel_id=1, source_target_pairs={{0,4},{4,8},{8,12},{1,5},{5,9},{9,13},{2,6},{6,10},{10,14},{3,7},{... | collective-permute-start | bytes 393224 | tf_op jit(solution)/shard_map/ppermute | solution.py:62
  19.7 3.8 %shard_map.94.refs_5_ = f32[512,2048]{1,0:T(8,128)} custom-call(bf16[512,2048]{1,0:T(8,128)(2,1)} %refs_0_.8, bf16[512,2048]{1,0:T(8,128)(2,1)} %k_ref.7, bf16[512,2048]{1,0:T(8,128)(2,1)} %v_ref.7, f32[512,16]{1,0:T(8,128)} %copy.37.cum_ref.refs_3_.refs_4_, f32[16,512]{1,0:T(8,128)} %bitcast.205), custom_call_target="tpu_custom_call" | custom-call | flops 536870912 | bytes 2621440 | tf_op jit(solution)/shard_map/pallas_call | solution.py:269
  24.3 3.5 %collective-permute-start.2 = (f32[2,128,128]{2,1,0:T(8,128)S(1)}, f32[2,128,128]{2,1,0:T(8,128)S(1)}, u32[]{:S(2)}, u32[]{:S(2)}) collective-permute-start(f32[2,128,128]{2,1,0:T(8,128)S(1)} %bitcast_add_fusion.10), channel_id=1, source_target_pairs={{0,4},{4,8},{8,12},{1,5},{5,9},{9,13},{2,6},{6,10},{10,14},{3,7},{... | collective-permute-start | bytes 393224 | tf_op jit(solution)/shard_map/ppermute | solution.py:62
  27.8 3.9 %shard_map.95.refs_5_ = f32[512,2048]{1,0:T(8,128)} custom-call(bf16[512,2048]{1,0:T(8,128)(2,1)} %refs_0_.8, bf16[512,2048]{1,0:T(8,128)(2,1)} %k_ref.7, bf16[512,2048]{1,0:T(8,128)(2,1)} %v_ref.7, f32[512,16]{1,0:T(8,128)} %copy.37.cum_ref.refs_3_.refs_4_, f32[16,512]{1,0:T(8,128)} %bitcast.206, ...), custom_call_target="tpu_custom_call", output_to_operand_aliasing={{}: (5, {})} | custom-call | flops 536870912 | bytes 2621440 | tf_op jit(solution)/shard_map/pallas_call | solution.py:269
  32.4 3.5 %collective-permute-start.3 = (f32[2,128,128]{2,1,0:T(8,128)S(1)}, f32[2,128,128]{2,1,0:T(8,128)S(1)}, u32[]{:S(2)}, u32[]{:S(2)}) collective-permute-start(f32[2,128,128]{2,1,0:T(8,128)S(1)} %bitcast_add_fusion.9), channel_id=1, source_target_pairs={{0,4},{4,8},{8,12},{1,5},{5,9},{9,13},{2,6},{6,10},{10,14},{3,7},{... | collective-permute-start | bytes 393224 | tf_op jit(solution)/shard_map/ppermute | solution.py:62
  35.9 3.8 %shard_map.96.refs_5_ = f32[512,2048]{1,0:T(8,128)} custom-call(bf16[512,2048]{1,0:T(8,128)(2,1)} %refs_0_.8, bf16[512,2048]{1,0:T(8,128)(2,1)} %k_ref.7, bf16[512,2048]{1,0:T(8,128)(2,1)} %v_ref.7, f32[512,16]{1,0:T(8,128)} %copy.37.cum_ref.refs_3_.refs_4_, f32[16,512]{1,0:T(8,128)} %bitcast.207, ...), custom_call_target="tpu_custom_call", output_to_operand_aliasing={{}: (5, {})} | custom-call | flops 536870912 | bytes 2621440 | tf_op jit(solution)/shard_map/pallas_call | solution.py:269
  40.4 3.2 %collective-permute-start.4 = (f32[2,128,128]{2,1,0:T(8,128)S(1)}, f32[2,128,128]{2,1,0:T(8,128)S(1)}, u32[]{:S(2)}, u32[]{:S(2)}) collective-permute-start(f32[2,128,128]{2,1,0:T(8,128)S(1)} %bitcast_add_fusion.8), channel_id=1, source_target_pairs={{0,4},{4,8},{8,12},{1,5},{5,9},{9,13},{2,6},{6,10},{10,14},{3,7},{... | collective-permute-start | bytes 393224 | tf_op jit(solution)/shard_map/ppermute | solution.py:62
  43.7 3.8 %shard_map.97.intra_ref = f32[512,2048]{1,0:T(8,128)} custom-call(bf16[512,2048]{1,0:T(8,128)(2,1)} %refs_0_.8, bf16[512,2048]{1,0:T(8,128)(2,1)} %k_ref.7, bf16[512,2048]{1,0:T(8,128)(2,1)} %v_ref.7, f32[512,16]{1,0:T(8,128)} %copy.37.cum_ref.refs_3_.refs_4_, f32[16,512]{1,0:T(8,128)} %bitcast.208, ...), custom_call_target="tpu_custom_call", output_to_operand_aliasing={{}: (5, {})} | custom-call | flops 536870912 | bytes 2621440 | tf_op jit(solution)/shard_map/pallas_call | solution.py:269
  48.3 3.0 %collective-permute-start.5 = (f32[2,128,128]{2,1,0:T(8,128)S(1)}, f32[2,128,128]{2,1,0:T(8,128)S(1)}, u32[]{:S(2)}, u32[]{:S(2)}) collective-permute-start(f32[2,128,128]{2,1,0:T(8,128)S(1)} %bitcast_add_fusion.7), channel_id=1, source_target_pairs={{0,4},{4,8},{8,12},{1,5},{5,9},{9,13},{2,6},{6,10},{10,14},{3,7},{... | collective-permute-start | bytes 393224 | tf_op jit(solution)/shard_map/ppermute | solution.py:62
  52.0 1.8 %collective-permute-done.5 = f32[2,128,128]{2,1,0:T(8,128)S(1)} collective-permute-done((f32[2,128,128]{2,1,0:T(8,128)S(1)}, f32[2,128,128]{2,1,0:T(8,128)S(1)}, u32[]{:S(2)}, u32[]{:S(2)}) %collective-permute-start.5) | collective-permute-done | bytes 131104 | tf_op jit(solution)/shard_map/ppermute | solution.py:62
  54.5 4.4 %collective-permute-start.6 = (f32[2,128,128]{2,1,0:T(8,128)S(1)}, f32[2,128,128]{2,1,0:T(8,128)S(1)}, u32[]{:S(2)}, u32[]{:S(2)}) collective-permute-start(f32[2,128,128]{2,1,0:T(8,128)S(1)} %bitcast_add_fusion.6), channel_id=1, source_target_pairs={{0,4},{4,8},{8,12},{1,5},{5,9},{9,13},{2,6},{6,10},{10,14},{3,7},{... | collective-permute-start | bytes 393224 | tf_op jit(solution)/shard_map/ppermute | solution.py:62
  58.9 2.5 %collective-permute-done.6 = f32[2,128,128]{2,1,0:T(8,128)S(1)} collective-permute-done((f32[2,128,128]{2,1,0:T(8,128)S(1)}, f32[2,128,128]{2,1,0:T(8,128)S(1)}, u32[]{:S(2)}, u32[]{:S(2)}) %collective-permute-start.6) | collective-permute-done | bytes 131104 | tf_op jit(solution)/shard_map/ppermute | solution.py:62
  62.2 1.8 %collective-permute-done.7 = f32[8,128,128]{2,1,0:T(8,128)S(1)} collective-permute-done((f32[8,128,128]{2,1,0:T(8,128)S(1)}, f32[8,128,128]{2,1,0:T(8,128)S(1)}, u32[]{:S(2)}, u32[]{:S(2)}) %collective-permute-start.7) | collective-permute-done | bytes 524320 | tf_op jit(solution)/shard_map/ppermute | solution.py:21
  65.2 9.4 %shard_map.98 = (bf16[512,2048]{1,0:T(8,128)(2,1)}, f32[16,128,128]{2,1,0:T(8,128)}, f32[16,1,128]{2,1,0:T(1,128)}) custom-call(bf16[512,2048]{1,0:T(8,128)(2,1)} %refs_0_.8, bf16[512,2048]{1,0:T(8,128)(2,1)} %g_ref.1, f32[512,2048]{1,0:T(8,128)} %shard_map.97.intra_ref, bf16[16,128,128]{2,1,0:T(8,128)(2,1)} %select_convert_fusion.1.st_ref.refs_6_, ...), custom_call_target="tpu_custom_call" | custom-call | flops 536870912 | bytes 10485760 | tf_op jit(solution)/shard_map/pallas_call | solution.py:269
  84.2 6.3 %shard_map.99 = (bf16[512,2048]{1,0:T(8,128)(2,1)}, f32[512,2048]{1,0:T(8,128)}, f32[512,2048]{1,0:T(8,128)}) custom-call(bf16[512,2048]{1,0:T(8,128)(2,1)} %refs_0_.8, bf16[512,2048]{1,0:T(8,128)(2,1)} %k_ref.7, bf16[512,2048]{1,0:T(8,128)(2,1)} %v_ref.7, bf16[512,2048]{1,0:T(8,128)(2,1)} %get-tuple-element.249.og_ref.refs_3_, ...), custom_call_target="tpu_custom_call" | custom-call | flops 1409286144 | bytes 4718592 | tf_op jit(solution)/shard_map/pallas_call | solution.py:269
  92.8 6.3 %shard_map.100 = (bf16[512,2048]{1,0:T(8,128)(2,1)}, f32[512,2048]{1,0:T(8,128)}, f32[512,2048]{1,0:T(8,128)}) custom-call(bf16[512,2048]{1,0:T(8,128)(2,1)} %refs_0_.8, bf16[512,2048]{1,0:T(8,128)(2,1)} %k_ref.7, bf16[512,2048]{1,0:T(8,128)(2,1)} %v_ref.7, ...), custom_call_target="tpu_custom_call", output_to_operand_aliasing={{0}: (7, {}), {1}: (8, {}), {2}: (9, {})} | custom-call | flops 1409286144 | bytes 4718592 | tf_op jit(solution)/shard_map/pallas_call | solution.py:269
  102.1 6.3 %shard_map.101 = (bf16[512,2048]{1,0:T(8,128)(2,1)}, f32[512,2048]{1,0:T(8,128)}, f32[512,2048]{1,0:T(8,128)}) custom-call(bf16[512,2048]{1,0:T(8,128)(2,1)} %refs_0_.8, bf16[512,2048]{1,0:T(8,128)(2,1)} %k_ref.7, bf16[512,2048]{1,0:T(8,128)(2,1)} %v_ref.7, ...), custom_call_target="tpu_custom_call", output_to_operand_aliasing={{0}: (7, {}), {1}: (8, {}), {2}: (9, {})} | custom-call | flops 1409286144 | bytes 4718592 | tf_op jit(solution)/shard_map/pallas_call | solution.py:269
  111.3 6.3 %shard_map.102 = (bf16[512,2048]{1,0:T(8,128)(2,1)}, f32[512,2048]{1,0:T(8,128)}, f32[512,2048]{1,0:T(8,128)}) custom-call(bf16[512,2048]{1,0:T(8,128)(2,1)} %refs_0_.8, bf16[512,2048]{1,0:T(8,128)(2,1)} %k_ref.7, bf16[512,2048]{1,0:T(8,128)(2,1)} %v_ref.7, ...), custom_call_target="tpu_custom_call", output_to_operand_aliasing={{0}: (7, {}), {1}: (8, {}), {2}: (9, {})} | custom-call | flops 1409286144 | bytes 4718592 | tf_op jit(solution)/shard_map/pallas_call | solution.py:269
  121.0 3.1 %collective-permute-start.13 = (f32[16,128]{1,0:T(8,128)S(1)}, f32[16,128]{1,0:T(8,128)S(1)}, u32[]{:S(2)}, u32[]{:S(2)}) collective-permute-start(f32[16,128]{1,0:T(8,128)S(1)} %bitcast.229), channel_id=1, source_target_pairs={{0,4},{4,0},{8,12},{12,8},{1,5},{5,1},{9,13},{13,9},{2,6},{6,2},{1... | collective-permute-start | bytes 24584 | tf_op jit(solution)/shard_map/ppermute | solution.py:114
  124.2 3.2 %collective-permute-done.13 = f32[16,128]{1,0:T(8,128)S(1)} collective-permute-done((f32[16,128]{1,0:T(8,128)S(1)}, f32[16,128]{1,0:T(8,128)S(1)}, u32[]{:S(2)}, u32[]{:S(2)}) %collective-permute-start.13) | collective-permute-done | bytes 8224 | tf_op jit(solution)/shard_map/ppermute | solution.py:114
  129.5 3.7 %collective-permute-start.15 = (f32[16,128]{1,0:T(8,128)S(1)}, f32[16,128]{1,0:T(8,128)S(1)}, u32[]{:S(2)}, u32[]{:S(2)}) collective-permute-start(f32[16,128]{1,0:T(8,128)S(1)} %add.209), channel_id=1, source_target_pairs={{0,8},{4,12},{8,0},{12,4},{1,9},{5,13},{9,1},{13,5},{2,10},{6,14},... | collective-permute-start | bytes 24584 | tf_op jit(solution)/shard_map/ppermute | solution.py:114
  133.2 3.0 %collective-permute-done.15 = f32[16,128]{1,0:T(8,128)S(1)} collective-permute-done((f32[16,128]{1,0:T(8,128)S(1)}, f32[16,128]{1,0:T(8,128)S(1)}, u32[]{:S(2)}, u32[]{:S(2)}) %collective-permute-start.15) | collective-permute-done | bytes 8224 | tf_op jit(solution)/shard_map/ppermute | solution.py:114
  140.0 8.4 %shard_map.103 = (bf16[512,2048]{1,0:T(8,128)(2,1)}, bf16[512,2048]{1,0:T(8,128)(2,1)}) custom-call(bf16[512,2048]{1,0:T(8,128)(2,1)} %k_ref.7, bf16[512,2048]{1,0:T(8,128)(2,1)} %v_ref.7, f32[512,2048]{1,0:T(8,128)} %get-tuple-element.268.kg_ref, f32[512,2048]{1,0:T(8,128)} %get-tuple-element.269.vg_ref, bf16[16,128,128]{2,1,0:T(8,128)(2,1)} %select_convert_fusion.gl_ref, ...), custom_call_target="tpu_custom_call" | custom-call | flops 536870912 | bytes 16777216 | tf_op jit(solution)/shard_map/pallas_call | solution.py:269
  (111 shorter events, 41.7 us)
Async XLA Ops:
  0.6 0.8 copy-start
  1.8 1.2 copy-start.3
  8.8 2.1 %copy-start.5 = (s32[4]{0:T(128)S(1)}, s32[4]{0:T(128)}, u32[]{:S(2)}) copy-start(s32[4]{0:T(128)} %constant.302.clone.1) | copy-start | bytes 52
  8.8 4.9 %copy-start.1 = (f32[16,128,128]{2,1,0:T(8,128)S(1)}, f32[16,128,128]{2,1,0:T(8,128)}, u32[]{:S(2)}) copy-start(f32[16,128,128]{2,1,0:T(8,128)} %shard_map.93) | copy-start | bytes 3145732
  10.3 2.9 %collective-permute-start = (f32[16,136,128]{2,1,0:T(8,128)S(1)}, f32[16,136,128]{2,1,0:T(8,128)S(1)}, u32[]{:S(2)}, u32[]{:S(2)}) collective-permute-start(f32[16,136,128]{2,1,0:T(8,128)S(1)} %fusion), channel_id=1, source_target_pairs={{0,1},{1,0},{2,3},{3,2},{4,5},{5,4},{6,7},{7,6},{8,9},{9,8},{10,11... | collective-permute-start | bytes 3342344 | tf_op jit(solution)/shard_map/ppermute | solution.py:21
  14.2 9.4 %collective-permute-start.1 = (f32[2,128,128]{2,1,0:T(8,128)S(1)}, f32[2,128,128]{2,1,0:T(8,128)S(1)}, u32[]{:S(2)}, u32[]{:S(2)}) collective-permute-start(f32[2,128,128]{2,1,0:T(8,128)S(1)} %bitcast_add_fusion.11), channel_id=1, source_target_pairs={{0,4},{4,8},{8,12},{1,5},{5,9},{9,13},{2,6},{6,10},{10,14},{3,7},{... | collective-permute-start | bytes 393224 | tf_op jit(solution)/shard_map/ppermute | solution.py:62
  24.3 7.4 %collective-permute-start.2 = (f32[2,128,128]{2,1,0:T(8,128)S(1)}, f32[2,128,128]{2,1,0:T(8,128)S(1)}, u32[]{:S(2)}, u32[]{:S(2)}) collective-permute-start(f32[2,128,128]{2,1,0:T(8,128)S(1)} %bitcast_add_fusion.10), channel_id=1, source_target_pairs={{0,4},{4,8},{8,12},{1,5},{5,9},{9,13},{2,6},{6,10},{10,14},{3,7},{... | collective-permute-start | bytes 393224 | tf_op jit(solution)/shard_map/ppermute | solution.py:62
  32.4 7.3 %collective-permute-start.3 = (f32[2,128,128]{2,1,0:T(8,128)S(1)}, f32[2,128,128]{2,1,0:T(8,128)S(1)}, u32[]{:S(2)}, u32[]{:S(2)}) collective-permute-start(f32[2,128,128]{2,1,0:T(8,128)S(1)} %bitcast_add_fusion.9), channel_id=1, source_target_pairs={{0,4},{4,8},{8,12},{1,5},{5,9},{9,13},{2,6},{6,10},{10,14},{3,7},{... | collective-permute-start | bytes 393224 | tf_op jit(solution)/shard_map/ppermute | solution.py:62
  40.4 7.1 %collective-permute-start.4 = (f32[2,128,128]{2,1,0:T(8,128)S(1)}, f32[2,128,128]{2,1,0:T(8,128)S(1)}, u32[]{:S(2)}, u32[]{:S(2)}) collective-permute-start(f32[2,128,128]{2,1,0:T(8,128)S(1)} %bitcast_add_fusion.8), channel_id=1, source_target_pairs={{0,4},{4,8},{8,12},{1,5},{5,9},{9,13},{2,6},{6,10},{10,14},{3,7},{... | collective-permute-start | bytes 393224 | tf_op jit(solution)/shard_map/ppermute | solution.py:62
  48.3 5.5 %collective-permute-start.5 = (f32[2,128,128]{2,1,0:T(8,128)S(1)}, f32[2,128,128]{2,1,0:T(8,128)S(1)}, u32[]{:S(2)}, u32[]{:S(2)}) collective-permute-start(f32[2,128,128]{2,1,0:T(8,128)S(1)} %bitcast_add_fusion.7), channel_id=1, source_target_pairs={{0,4},{4,8},{8,12},{1,5},{5,9},{9,13},{2,6},{6,10},{10,14},{3,7},{... | collective-permute-start | bytes 393224 | tf_op jit(solution)/shard_map/ppermute | solution.py:62
  54.5 6.9 %collective-permute-start.6 = (f32[2,128,128]{2,1,0:T(8,128)S(1)}, f32[2,128,128]{2,1,0:T(8,128)S(1)}, u32[]{:S(2)}, u32[]{:S(2)}) collective-permute-start(f32[2,128,128]{2,1,0:T(8,128)S(1)} %bitcast_add_fusion.6), channel_id=1, source_target_pairs={{0,4},{4,8},{8,12},{1,5},{5,9},{9,13},{2,6},{6,10},{10,14},{3,7},{... | collective-permute-start | bytes 393224 | tf_op jit(solution)/shard_map/ppermute | solution.py:62
  62.1 2.0 %collective-permute-start.7 = (f32[8,128,128]{2,1,0:T(8,128)S(1)}, f32[8,128,128]{2,1,0:T(8,128)S(1)}, u32[]{:S(2)}, u32[]{:S(2)}) collective-permute-start(f32[8,128,128]{2,1,0:T(8,128)S(1)} %bitcast.203), channel_id=1, source_target_pairs={{0,1},{1,0},{2,3},{3,2},{4,5},{5,4},{6,7},{7,6},{8,9},{9,8},{10,11... | collective-permute-start | bytes 1572872 | tf_op jit(solution)/shard_map/ppermute | solution.py:21
  74.6 5.7 %copy-start.2 = (f32[16,128,128]{2,1,0:T(8,128)S(1)}, f32[16,128,128]{2,1,0:T(8,128)}, u32[]{:S(2)}) copy-start(f32[16,128,128]{2,1,0:T(8,128)} %get-tuple-element.224) | copy-start | bytes 3145732
  76.1 3.0 %collective-permute-start.8 = (f32[16,136,128]{2,1,0:T(8,128)S(1)}, f32[16,136,128]{2,1,0:T(8,128)}, u32[]{:S(2)}, u32[]{:S(2)}) collective-permute-start(f32[16,136,128]{2,1,0:T(8,128)S(1)} %fusion.2), channel_id=1, source_target_pairs={{0,1},{1,0},{2,3},{3,2},{4,5},{5,4},{6,7},{7,6},{8,9},{9,8},{10,11... | collective-permute-start | bytes 3342344 | tf_op jit(solution)/shard_map/ppermute | solution.py:21
  81.8 1.6 %copy-start.4 = (f32[16,1,128]{2,1,0:T(1,128)S(1)}, f32[16,1,128]{2,1,0:T(1,128)}, u32[]{:S(2)}) copy-start(f32[16,1,128]{2,1,0:T(1,128)} %get-tuple-element.225) | copy-start | bytes 24580
  82.0 8.4 %collective-permute-start.9 = (f32[2,128,128]{2,1,0:T(8,128)S(1)}, f32[2,128,128]{2,1,0:T(8,128)S(1)}, u32[]{:S(2)}, u32[]{:S(2)}) collective-permute-start(f32[2,128,128]{2,1,0:T(8,128)S(1)} %bitcast_add_fusion.5), channel_id=1, source_target_pairs={{4,0},{8,4},{12,8},{5,1},{9,5},{13,9},{6,2},{10,6},{14,10},{7,3},{... | collective-permute-start | bytes 393224 | tf_op jit(solution)/shard_map/ppermute | solution.py:62
  91.3 8.8 %collective-permute-start.10 = (f32[2,128,128]{2,1,0:T(8,128)S(1)}, f32[2,128,128]{2,1,0:T(8,128)S(1)}, u32[]{:S(2)}, u32[]{:S(2)}) collective-permute-start(f32[2,128,128]{2,1,0:T(8,128)S(1)} %bitcast_add_fusion.4), channel_id=1, source_target_pairs={{4,0},{8,4},{12,8},{5,1},{9,5},{13,9},{6,2},{10,6},{14,10},{7,3},{... | collective-permute-start | bytes 393224 | tf_op jit(solution)/shard_map/ppermute | solution.py:62
  100.8 8.4 %collective-permute-start.11 = (f32[2,128,128]{2,1,0:T(8,128)S(1)}, f32[2,128,128]{2,1,0:T(8,128)S(1)}, u32[]{:S(2)}, u32[]{:S(2)}) collective-permute-start(f32[2,128,128]{2,1,0:T(8,128)S(1)} %bitcast_add_fusion.3), channel_id=1, source_target_pairs={{4,0},{8,4},{12,8},{5,1},{9,5},{13,9},{6,2},{10,6},{14,10},{7,3},{... | collective-permute-start | bytes 393224 | tf_op jit(solution)/shard_map/ppermute | solution.py:62
  110.0 8.2 %collective-permute-start.12 = (f32[2,128,128]{2,1,0:T(8,128)S(1)}, f32[2,128,128]{2,1,0:T(8,128)S(1)}, u32[]{:S(2)}, u32[]{:S(2)}) collective-permute-start(f32[2,128,128]{2,1,0:T(8,128)S(1)} %bitcast_add_fusion.2), channel_id=1, source_target_pairs={{4,0},{8,4},{12,8},{5,1},{9,5},{13,9},{6,2},{10,6},{14,10},{7,3},{... | collective-permute-start | bytes 393224 | tf_op jit(solution)/shard_map/ppermute | solution.py:62
  119.0 8.4 %collective-permute-start.14 = (f32[2,128,128]{2,1,0:T(8,128)S(1)}, f32[2,128,128]{2,1,0:T(8,128)S(1)}, u32[]{:S(2)}, u32[]{:S(2)}) collective-permute-start(f32[2,128,128]{2,1,0:T(8,128)S(1)} %bitcast_add_fusion.1), channel_id=1, source_target_pairs={{4,0},{8,4},{12,8},{5,1},{9,5},{13,9},{6,2},{10,6},{14,10},{7,3},{... | collective-permute-start | bytes 393224 | tf_op jit(solution)/shard_map/ppermute | solution.py:62
  121.0 6.4 %collective-permute-start.13 = (f32[16,128]{1,0:T(8,128)S(1)}, f32[16,128]{1,0:T(8,128)S(1)}, u32[]{:S(2)}, u32[]{:S(2)}) collective-permute-start(f32[16,128]{1,0:T(8,128)S(1)} %bitcast.229), channel_id=1, source_target_pairs={{0,4},{4,0},{8,12},{12,8},{1,5},{5,1},{9,13},{13,9},{2,6},{6,2},{1... | collective-permute-start | bytes 24584 | tf_op jit(solution)/shard_map/ppermute | solution.py:114
  128.1 8.0 %collective-permute-start.16 = (f32[2,128,128]{2,1,0:T(8,128)S(1)}, f32[2,128,128]{2,1,0:T(8,128)S(1)}, u32[]{:S(2)}, u32[]{:S(2)}) collective-permute-start(f32[2,128,128]{2,1,0:T(8,128)S(1)} %bitcast_add_fusion), channel_id=1, source_target_pairs={{4,0},{8,4},{12,8},{5,1},{9,5},{13,9},{6,2},{10,6},{14,10},{7,3},{... | collective-permute-start | bytes 393224 | tf_op jit(solution)/shard_map/ppermute | solution.py:62
  129.5 6.7 %collective-permute-start.15 = (f32[16,128]{1,0:T(8,128)S(1)}, f32[16,128]{1,0:T(8,128)S(1)}, u32[]{:S(2)}, u32[]{:S(2)}) collective-permute-start(f32[16,128]{1,0:T(8,128)S(1)} %add.209), channel_id=1, source_target_pairs={{0,8},{4,12},{8,0},{12,4},{1,9},{5,13},{9,1},{13,5},{2,10},{6,14},... | collective-permute-start | bytes 24584 | tf_op jit(solution)/shard_map/ppermute | solution.py:114
  136.9 2.0 %collective-permute-start.17 = (f32[8,128,128]{2,1,0:T(8,128)S(1)}, f32[8,128,128]{2,1,0:T(8,128)S(1)}, u32[]{:S(2)}, u32[]{:S(2)}) collective-permute-start(f32[8,128,128]{2,1,0:T(8,128)S(1)} %bitcast.202), channel_id=1, source_target_pairs={{0,1},{1,0},{2,3},{3,2},{4,5},{5,4},{6,7},{7,6},{8,9},{9,8},{10,11... | collective-permute-start | bytes 1572872 | tf_op jit(solution)/shard_map/ppermute | solution.py:21

commit v12 on v11

--- a/solution.py
+++ b/solution.py
@@ -177,12 +177,30 @@
         s_ref[j] = _tn(scaled, v_ref[:, cols])
 
 
+def _tile_decays(col, row):
+    size = col.shape[0] // 2
+    tiles = {}
+    for i in range(2):
+        for j in range(i + 1):
+            c = col[i * size : (i + 1) * size]
+            r = row[:, j * size : (j + 1) * size]
+            tiles[i, j] = _decay(c, r) if i == j else jnp.exp(c - r)
+    return tiles, size
+
+
 def intra_kernel(first, hb, q_ref, k_ref, v_ref, cum_ref, cumt_ref, out_ref):
     for j in range(hb):
         cols = _lanes(j)
         col, row, _, _ = _head_vectors(cum_ref, cumt_ref, j, first, hb)
-        decay = _decay(col, row)
-        out_ref[:, cols] = _nn(_masked(q_ref[:, cols], k_ref[:, cols], decay), v_ref[:, cols])
+        tiles, size = _tile_decays(col, row)
+        q, k, v = q_ref[:, cols], k_ref[:, cols], v_ref[:, cols]
+        for a in range(2):
+            qa = q[a * size : (a + 1) * size]
+            total = None
+            for b in range(a + 1):
+                part = _nn(_masked(qa, k[b * size : (b + 1) * size], tiles[a, b]), v[b * size : (b + 1) * size])
+                total = part if total is None else total + part
+            out_ref[a * size : (a + 1) * size, cols] = total
 
 
 def norm_kernel(q_ref, g_ref, intra_ref, st_ref, cum_ref, cumt_ref, gain_ref, og_ref, m_ref, gp_ref):
@@ -210,13 +228,29 @@
     for j in range(hb):
         cols = _lanes(j)
         col, row, grow, _ = _head_vectors(cum_ref, cumt_ref, j, first, hb)
-        decay = _decay(col, row)
+        tiles, size = _tile_decays(col, row)
         q, k, v, og = q_ref[:, cols], k_ref[:, cols], v_ref[:, cols], og_ref[:, cols]
-        masked = _masked(q, k, decay)
-        rgrad = (_nt(og, v) * decay).astype(jnp.bfloat16)
-        qg_ref[:, cols] = (_nn(rgrad, k) + grow * _nt(og, st_ref[j])).astype(jnp.bfloat16)
-        kg_ref[:, cols] = _tn(rgrad, q)
-        vg_ref[:, cols] = _tn(masked, og)
+        part = lambda x, i: x[i * size : (i + 1) * size]
+        qg = [None, None]
+        kg = [None, None]
+        vg = [None, None]
+
+        def add(acc, i, value):
+            acc[i] = value if acc[i] is None else acc[i] + value
+
+        for a in range(2):
+            for b in range(a + 1):
+                masked = _masked(part(q, a), part(k, b), tiles[a, b])
+                rgrad = (_nt(part(og, a), part(v, b)) * tiles[a, b]).astype(jnp.bfloat16)
+                add(qg, a, _nn(rgrad, part(k, b)))
+                add(kg, b, _tn(rgrad, part(q, a)))
+                add(vg, b, _tn(masked, part(og, a)))
+        state_part = grow * _nt(og, st_ref[j])
+        for a in range(2):
+            rows = slice(a * size, (a + 1) * size)
+            qg_ref[rows, cols] = (qg[a] + state_part[rows]).astype(jnp.bfloat16)
+            kg_ref[rows, cols] = kg[a]
+            vg_ref[rows, cols] = vg[a]
 
 
 def finish_kernel(k_ref, v_ref, kg_ref, vg_ref, gl_ref, cum_ref, cumt_ref, ko_ref, vo_ref):

time: 150 us -> 149 us (level)
  no operation moved by 1% of the time
where the time goes in v12:
time: 149 us; the launch traced here: 148 us
  Pallas kernels  64.2 us (43%)
  starting transfers between devices  37.7 us (25%)
  other arithmetic  23.2 us (16%)
  waiting for transfers between devices  18.9 us (13%)
  local copies, waits for them, and re-layouts  2.79 us (2%)
    pallas_call x11, Pallas kernels, _per_head(): pl.pallas_call(body, grid=(count,), in_specs=in_specs, out_specs=[spec(ki...  64.2 us
    ppermute x12, starting transfers between devices, chain_scan(): arrived = lax.ppermute(outgoing, 'ctx', perm=perm)  30.1 us
    scatter x12, other arithmetic, chain_scan(): prefix = prefix.at[slot].set(jnp.where(valid, arrived, prefix[slot]))  7.77 us
    ppermute x12, waiting for transfers between devices, chain_scan(): arrived = lax.ppermute(outgoing, 'ctx', perm=perm)  6.81 us
    ppermute x2, starting transfers between devices, gain_step(): return (both[0], both[1] + lax.ppermute(both[1], 'ctx', perm=partners))  6.75 us
    ppermute x2, waiting for transfers between devices, gain_step(): return (both[0], both[1] + lax.ppermute(both[1], 'ctx', perm=partners))  6.22 us
    ppermute x4, waiting for transfers between devices, swap_dp(): return lax.ppermute(x, 'dp', perm=[(0, 1), (1, 0)])  5.88 us
    another operation x6, other arithmetic  4.5 us
  transfers between devices with their start and end apart: 18, of which 11 were waited for; matrix products, arithmetic and copies ran while one was open for 4% of the time, Pallas kernels for 27%

profile of v12, /device:TPU:0, one launch (start us, length us, event | category | flops | bytes accessed | tf_op | source)
XLA Modules:
  0.0 148.3 jit_solution(5753975146410591886)
XLA Ops:
  3.0 5.8 %shard_map.93 = f32[16,128,128]{2,1,0:T(8,128)} custom-call(bf16[512,2048]{1,0:T(8,128)(2,1)} %k_ref.7, bf16[512,2048]{1,0:T(8,128)(2,1)} %v_ref.7, f32[512,16]{1,0:T(8,128)} %copy.37.cum_ref.refs_3_.refs_4_, f32[16,512]{1,0:T(8,128)} %bitcast.204), custom_call_target="tpu_custom_call" | custom-call | flops 268435456 | bytes 4194304 | tf_op jit(solution)/shard_map/pallas_call | solution.py:303
  14.2 4.9 %collective-permute-start.1 = (f32[2,128,128]{2,1,0:T(8,128)S(1)}, f32[2,128,128]{2,1,0:T(8,128)S(1)}, u32[]{:S(2)}, u32[]{:S(2)}) collective-permute-start(f32[2,128,128]{2,1,0:T(8,128)S(1)} %bitcast_add_fusion.11), channel_id=1, source_target_pairs={{0,4},{4,8},{8,12},{1,5},{5,9},{9,13},{2,6},{6,10},{10,14},{3,7},{... | collective-permute-start | bytes 393224 | tf_op jit(solution)/shard_map/ppermute | solution.py:62
  19.7 3.9 %shard_map.94.refs_5_ = f32[512,2048]{1,0:T(8,128)} custom-call(bf16[512,2048]{1,0:T(8,128)(2,1)} %refs_0_.8, bf16[512,2048]{1,0:T(8,128)(2,1)} %k_ref.7, bf16[512,2048]{1,0:T(8,128)(2,1)} %v_ref.7, f32[512,16]{1,0:T(8,128)} %copy.37.cum_ref.refs_3_.refs_4_, f32[16,512]{1,0:T(8,128)} %bitcast.205), custom_call_target="tpu_custom_call" | custom-call | flops 536870912 | bytes 2621440 | tf_op jit(solution)/shard_map/pallas_call | solution.py:303
  24.5 3.5 %collective-permute-start.2 = (f32[2,128,128]{2,1,0:T(8,128)S(1)}, f32[2,128,128]{2,1,0:T(8,128)S(1)}, u32[]{:S(2)}, u32[]{:S(2)}) collective-permute-start(f32[2,128,128]{2,1,0:T(8,128)S(1)} %bitcast_add_fusion.10), channel_id=1, source_target_pairs={{0,4},{4,8},{8,12},{1,5},{5,9},{9,13},{2,6},{6,10},{10,14},{3,7},{... | collective-permute-start | bytes 393224 | tf_op jit(solution)/shard_map/ppermute | solution.py:62
  28.0 4.0 %shard_map.95.refs_5_ = f32[512,2048]{1,0:T(8,128)} custom-call(bf16[512,2048]{1,0:T(8,128)(2,1)} %refs_0_.8, bf16[512,2048]{1,0:T(8,128)(2,1)} %k_ref.7, bf16[512,2048]{1,0:T(8,128)(2,1)} %v_ref.7, f32[512,16]{1,0:T(8,128)} %copy.37.cum_ref.refs_3_.refs_4_, f32[16,512]{1,0:T(8,128)} %bitcast.206, ...), custom_call_target="tpu_custom_call", output_to_operand_aliasing={{}: (5, {})} | custom-call | flops 536870912 | bytes 2621440 | tf_op jit(solution)/shard_map/pallas_call | solution.py:303
  32.7 3.5 %collective-permute-start.3 = (f32[2,128,128]{2,1,0:T(8,128)S(1)}, f32[2,128,128]{2,1,0:T(8,128)S(1)}, u32[]{:S(2)}, u32[]{:S(2)}) collective-permute-start(f32[2,128,128]{2,1,0:T(8,128)S(1)} %bitcast_add_fusion.9), channel_id=1, source_target_pairs={{0,4},{4,8},{8,12},{1,5},{5,9},{9,13},{2,6},{6,10},{10,14},{3,7},{... | collective-permute-start | bytes 393224 | tf_op jit(solution)/shard_map/ppermute | solution.py:62
  36.1 3.9 %shard_map.96.refs_5_ = f32[512,2048]{1,0:T(8,128)} custom-call(bf16[512,2048]{1,0:T(8,128)(2,1)} %refs_0_.8, bf16[512,2048]{1,0:T(8,128)(2,1)} %k_ref.7, bf16[512,2048]{1,0:T(8,128)(2,1)} %v_ref.7, f32[512,16]{1,0:T(8,128)} %copy.37.cum_ref.refs_3_.refs_4_, f32[16,512]{1,0:T(8,128)} %bitcast.207, ...), custom_call_target="tpu_custom_call", output_to_operand_aliasing={{}: (5, {})} | custom-call | flops 536870912 | bytes 2621440 | tf_op jit(solution)/shard_map/pallas_call | solution.py:303
  40.8 3.1 %collective-permute-start.4 = (f32[2,128,128]{2,1,0:T(8,128)S(1)}, f32[2,128,128]{2,1,0:T(8,128)S(1)}, u32[]{:S(2)}, u32[]{:S(2)}) collective-permute-start(f32[2,128,128]{2,1,0:T(8,128)S(1)} %bitcast_add_fusion.8), channel_id=1, source_target_pairs={{0,4},{4,8},{8,12},{1,5},{5,9},{9,13},{2,6},{6,10},{10,14},{3,7},{... | collective-permute-start | bytes 393224 | tf_op jit(solution)/shard_map/ppermute | solution.py:62
  43.9 4.0 %shard_map.97.intra_ref = f32[512,2048]{1,0:T(8,128)} custom-call(bf16[512,2048]{1,0:T(8,128)(2,1)} %refs_0_.8, bf16[512,2048]{1,0:T(8,128)(2,1)} %k_ref.7, bf16[512,2048]{1,0:T(8,128)(2,1)} %v_ref.7, f32[512,16]{1,0:T(8,128)} %copy.37.cum_ref.refs_3_.refs_4_, f32[16,512]{1,0:T(8,128)} %bitcast.208, ...), custom_call_target="tpu_custom_call", output_to_operand_aliasing={{}: (5, {})} | custom-call | flops 536870912 | bytes 2621440 | tf_op jit(solution)/shard_map/pallas_call | solution.py:303
  48.7 2.9 %collective-permute-start.5 = (f32[2,128,128]{2,1,0:T(8,128)S(1)}, f32[2,128,128]{2,1,0:T(8,128)S(1)}, u32[]{:S(2)}, u32[]{:S(2)}) collective-permute-start(f32[2,128,128]{2,1,0:T(8,128)S(1)} %bitcast_add_fusion.7), channel_id=1, source_target_pairs={{0,4},{4,8},{8,12},{1,5},{5,9},{9,13},{2,6},{6,10},{10,14},{3,7},{... | collective-permute-start | bytes 393224 | tf_op jit(solution)/shard_map/ppermute | solution.py:62
  52.3 1.8 %collective-permute-done.5 = f32[2,128,128]{2,1,0:T(8,128)S(1)} collective-permute-done((f32[2,128,128]{2,1,0:T(8,128)S(1)}, f32[2,128,128]{2,1,0:T(8,128)S(1)}, u32[]{:S(2)}, u32[]{:S(2)}) %collective-permute-start.5) | collective-permute-done | bytes 131104 | tf_op jit(solution)/shard_map/ppermute | solution.py:62
  54.8 4.4 %collective-permute-start.6 = (f32[2,128,128]{2,1,0:T(8,128)S(1)}, f32[2,128,128]{2,1,0:T(8,128)S(1)}, u32[]{:S(2)}, u32[]{:S(2)}) collective-permute-start(f32[2,128,128]{2,1,0:T(8,128)S(1)} %bitcast_add_fusion.6), channel_id=1, source_target_pairs={{0,4},{4,8},{8,12},{1,5},{5,9},{9,13},{2,6},{6,10},{10,14},{3,7},{... | collective-permute-start | bytes 393224 | tf_op jit(solution)/shard_map/ppermute | solution.py:62
  59.2 2.5 %collective-permute-done.6 = f32[2,128,128]{2,1,0:T(8,128)S(1)} collective-permute-done((f32[2,128,128]{2,1,0:T(8,128)S(1)}, f32[2,128,128]{2,1,0:T(8,128)S(1)}, u32[]{:S(2)}, u32[]{:S(2)}) %collective-permute-start.6) | collective-permute-done | bytes 131104 | tf_op jit(solution)/shard_map/ppermute | solution.py:62
  62.5 1.8 %collective-permute-done.7 = f32[8,128,128]{2,1,0:T(8,128)S(1)} collective-permute-done((f32[8,128,128]{2,1,0:T(8,128)S(1)}, f32[8,128,128]{2,1,0:T(8,128)S(1)}, u32[]{:S(2)}, u32[]{:S(2)}) %collective-permute-start.7) | collective-permute-done | bytes 524320 | tf_op jit(solution)/shard_map/ppermute | solution.py:21
  65.5 9.4 %shard_map.98 = (bf16[512,2048]{1,0:T(8,128)(2,1)}, f32[16,128,128]{2,1,0:T(8,128)}, f32[16,1,128]{2,1,0:T(1,128)}) custom-call(bf16[512,2048]{1,0:T(8,128)(2,1)} %refs_0_.8, bf16[512,2048]{1,0:T(8,128)(2,1)} %g_ref.1, f32[512,2048]{1,0:T(8,128)} %shard_map.97.intra_ref, bf16[16,128,128]{2,1,0:T(8,128)(2,1)} %select_convert_fusion.1.st_ref.refs_6_, ...), custom_call_target="tpu_custom_call" | custom-call | flops 536870912 | bytes 10485760 | tf_op jit(solution)/shard_map/pallas_call | solution.py:303
  84.5 6.2 %shard_map.99 = (bf16[512,2048]{1,0:T(8,128)(2,1)}, f32[512,2048]{1,0:T(8,128)}, f32[512,2048]{1,0:T(8,128)}) custom-call(bf16[512,2048]{1,0:T(8,128)(2,1)} %refs_0_.8, bf16[512,2048]{1,0:T(8,128)(2,1)} %k_ref.7, bf16[512,2048]{1,0:T(8,128)(2,1)} %v_ref.7, bf16[512,2048]{1,0:T(8,128)(2,1)} %get-tuple-element.249.og_ref.refs_3_, ...), custom_call_target="tpu_custom_call" | custom-call | flops 1409286144 | bytes 4718592 | tf_op jit(solution)/shard_map/pallas_call | solution.py:303
  93.0 6.2 %shard_map.100 = (bf16[512,2048]{1,0:T(8,128)(2,1)}, f32[512,2048]{1,0:T(8,128)}, f32[512,2048]{1,0:T(8,128)}) custom-call(bf16[512,2048]{1,0:T(8,128)(2,1)} %refs_0_.8, bf16[512,2048]{1,0:T(8,128)(2,1)} %k_ref.7, bf16[512,2048]{1,0:T(8,128)(2,1)} %v_ref.7, ...), custom_call_target="tpu_custom_call", output_to_operand_aliasing={{0}: (7, {}), {1}: (8, {}), {2}: (9, {})} | custom-call | flops 1409286144 | bytes 4718592 | tf_op jit(solution)/shard_map/pallas_call | solution.py:303
  102.3 6.2 %shard_map.101 = (bf16[512,2048]{1,0:T(8,128)(2,1)}, f32[512,2048]{1,0:T(8,128)}, f32[512,2048]{1,0:T(8,128)}) custom-call(bf16[512,2048]{1,0:T(8,128)(2,1)} %refs_0_.8, bf16[512,2048]{1,0:T(8,128)(2,1)} %k_ref.7, bf16[512,2048]{1,0:T(8,128)(2,1)} %v_ref.7, ...), custom_call_target="tpu_custom_call", output_to_operand_aliasing={{0}: (7, {}), {1}: (8, {}), {2}: (9, {})} | custom-call | flops 1409286144 | bytes 4718592 | tf_op jit(solution)/shard_map/pallas_call | solution.py:303
  111.4 6.2 %shard_map.102 = (bf16[512,2048]{1,0:T(8,128)(2,1)}, f32[512,2048]{1,0:T(8,128)}, f32[512,2048]{1,0:T(8,128)}) custom-call(bf16[512,2048]{1,0:T(8,128)(2,1)} %refs_0_.8, bf16[512,2048]{1,0:T(8,128)(2,1)} %k_ref.7, bf16[512,2048]{1,0:T(8,128)(2,1)} %v_ref.7, ...), custom_call_target="tpu_custom_call", output_to_operand_aliasing={{0}: (7, {}), {1}: (8, {}), {2}: (9, {})} | custom-call | flops 1409286144 | bytes 4718592 | tf_op jit(solution)/shard_map/pallas_call | solution.py:303
  121.0 3.0 %collective-permute-start.13 = (f32[16,128]{1,0:T(8,128)S(1)}, f32[16,128]{1,0:T(8,128)S(1)}, u32[]{:S(2)}, u32[]{:S(2)}) collective-permute-start(f32[16,128]{1,0:T(8,128)S(1)} %bitcast.229), channel_id=1, source_target_pairs={{0,4},{4,0},{8,12},{12,8},{1,5},{5,1},{9,13},{13,9},{2,6},{6,2},{1... | collective-permute-start | bytes 24584 | tf_op jit(solution)/shard_map/ppermute | solution.py:114
  124.1 3.2 %collective-permute-done.13 = f32[16,128]{1,0:T(8,128)S(1)} collective-permute-done((f32[16,128]{1,0:T(8,128)S(1)}, f32[16,128]{1,0:T(8,128)S(1)}, u32[]{:S(2)}, u32[]{:S(2)}) %collective-permute-start.13) | collective-permute-done | bytes 8224 | tf_op jit(solution)/shard_map/ppermute | solution.py:114
  129.4 3.7 %collective-permute-start.15 = (f32[16,128]{1,0:T(8,128)S(1)}, f32[16,128]{1,0:T(8,128)S(1)}, u32[]{:S(2)}, u32[]{:S(2)}) collective-permute-start(f32[16,128]{1,0:T(8,128)S(1)} %add.209), channel_id=1, source_target_pairs={{0,8},{4,12},{8,0},{12,4},{1,9},{5,13},{9,1},{13,5},{2,10},{6,14},... | collective-permute-start | bytes 24584 | tf_op jit(solution)/shard_map/ppermute | solution.py:114
  133.1 3.0 %collective-permute-done.15 = f32[16,128]{1,0:T(8,128)S(1)} collective-permute-done((f32[16,128]{1,0:T(8,128)S(1)}, f32[16,128]{1,0:T(8,128)S(1)}, u32[]{:S(2)}, u32[]{:S(2)}) %collective-permute-start.15) | collective-permute-done | bytes 8224 | tf_op jit(solution)/shard_map/ppermute | solution.py:114
  139.9 8.4 %shard_map.103 = (bf16[512,2048]{1,0:T(8,128)(2,1)}, bf16[512,2048]{1,0:T(8,128)(2,1)}) custom-call(bf16[512,2048]{1,0:T(8,128)(2,1)} %k_ref.7, bf16[512,2048]{1,0:T(8,128)(2,1)} %v_ref.7, f32[512,2048]{1,0:T(8,128)} %get-tuple-element.268.kg_ref, f32[512,2048]{1,0:T(8,128)} %get-tuple-element.269.vg_ref, bf16[16,128,128]{2,1,0:T(8,128)(2,1)} %select_convert_fusion.gl_ref, ...), custom_call_target="tpu_custom_call" | custom-call | flops 536870912 | bytes 16777216 | tf_op jit(solution)/shard_map/pallas_call | solution.py:303
  (111 shorter events, 41.8 us)
Async XLA Ops:
  0.6 0.8 copy-start
  1.8 1.2 copy-start.3
  8.8 2.1 %copy-start.5 = (s32[4]{0:T(128)S(1)}, s32[4]{0:T(128)}, u32[]{:S(2)}) copy-start(s32[4]{0:T(128)} %constant.302.clone.1) | copy-start | bytes 52
  8.8 4.9 %copy-start.1 = (f32[16,128,128]{2,1,0:T(8,128)S(1)}, f32[16,128,128]{2,1,0:T(8,128)}, u32[]{:S(2)}) copy-start(f32[16,128,128]{2,1,0:T(8,128)} %shard_map.93) | copy-start | bytes 3145732
  10.3 2.9 %collective-permute-start = (f32[16,136,128]{2,1,0:T(8,128)S(1)}, f32[16,136,128]{2,1,0:T(8,128)S(1)}, u32[]{:S(2)}, u32[]{:S(2)}) collective-permute-start(f32[16,136,128]{2,1,0:T(8,128)S(1)} %fusion), channel_id=1, source_target_pairs={{0,1},{1,0},{2,3},{3,2},{4,5},{5,4},{6,7},{7,6},{8,9},{9,8},{10,11... | collective-permute-start | bytes 3342344 | tf_op jit(solution)/shard_map/ppermute | solution.py:21
  14.2 9.5 %collective-permute-start.1 = (f32[2,128,128]{2,1,0:T(8,128)S(1)}, f32[2,128,128]{2,1,0:T(8,128)S(1)}, u32[]{:S(2)}, u32[]{:S(2)}) collective-permute-start(f32[2,128,128]{2,1,0:T(8,128)S(1)} %bitcast_add_fusion.11), channel_id=1, source_target_pairs={{0,4},{4,8},{8,12},{1,5},{5,9},{9,13},{2,6},{6,10},{10,14},{3,7},{... | collective-permute-start | bytes 393224 | tf_op jit(solution)/shard_map/ppermute | solution.py:62
  24.5 7.5 %collective-permute-start.2 = (f32[2,128,128]{2,1,0:T(8,128)S(1)}, f32[2,128,128]{2,1,0:T(8,128)S(1)}, u32[]{:S(2)}, u32[]{:S(2)}) collective-permute-start(f32[2,128,128]{2,1,0:T(8,128)S(1)} %bitcast_add_fusion.10), channel_id=1, source_target_pairs={{0,4},{4,8},{8,12},{1,5},{5,9},{9,13},{2,6},{6,10},{10,14},{3,7},{... | collective-permute-start | bytes 393224 | tf_op jit(solution)/shard_map/ppermute | solution.py:62
  32.7 7.5 %collective-permute-start.3 = (f32[2,128,128]{2,1,0:T(8,128)S(1)}, f32[2,128,128]{2,1,0:T(8,128)S(1)}, u32[]{:S(2)}, u32[]{:S(2)}) collective-permute-start(f32[2,128,128]{2,1,0:T(8,128)S(1)} %bitcast_add_fusion.9), channel_id=1, source_target_pairs={{0,4},{4,8},{8,12},{1,5},{5,9},{9,13},{2,6},{6,10},{10,14},{3,7},{... | collective-permute-start | bytes 393224 | tf_op jit(solution)/shard_map/ppermute | solution.py:62
  40.8 7.1 %collective-permute-start.4 = (f32[2,128,128]{2,1,0:T(8,128)S(1)}, f32[2,128,128]{2,1,0:T(8,128)S(1)}, u32[]{:S(2)}, u32[]{:S(2)}) collective-permute-start(f32[2,128,128]{2,1,0:T(8,128)S(1)} %bitcast_add_fusion.8), channel_id=1, source_target_pairs={{0,4},{4,8},{8,12},{1,5},{5,9},{9,13},{2,6},{6,10},{10,14},{3,7},{... | collective-permute-start | bytes 393224 | tf_op jit(solution)/shard_map/ppermute | solution.py:62
  48.7 5.4 %collective-permute-start.5 = (f32[2,128,128]{2,1,0:T(8,128)S(1)}, f32[2,128,128]{2,1,0:T(8,128)S(1)}, u32[]{:S(2)}, u32[]{:S(2)}) collective-permute-start(f32[2,128,128]{2,1,0:T(8,128)S(1)} %bitcast_add_fusion.7), channel_id=1, source_target_pairs={{0,4},{4,8},{8,12},{1,5},{5,9},{9,13},{2,6},{6,10},{10,14},{3,7},{... | collective-permute-start | bytes 393224 | tf_op jit(solution)/shard_map/ppermute | solution.py:62
  54.8 6.9 %collective-permute-start.6 = (f32[2,128,128]{2,1,0:T(8,128)S(1)}, f32[2,128,128]{2,1,0:T(8,128)S(1)}, u32[]{:S(2)}, u32[]{:S(2)}) collective-permute-start(f32[2,128,128]{2,1,0:T(8,128)S(1)} %bitcast_add_fusion.6), channel_id=1, source_target_pairs={{0,4},{4,8},{8,12},{1,5},{5,9},{9,13},{2,6},{6,10},{10,14},{3,7},{... | collective-permute-start | bytes 393224 | tf_op jit(solution)/shard_map/ppermute | solution.py:62
  62.3 2.0 %collective-permute-start.7 = (f32[8,128,128]{2,1,0:T(8,128)S(1)}, f32[8,128,128]{2,1,0:T(8,128)S(1)}, u32[]{:S(2)}, u32[]{:S(2)}) collective-permute-start(f32[8,128,128]{2,1,0:T(8,128)S(1)} %bitcast.203), channel_id=1, source_target_pairs={{0,1},{1,0},{2,3},{3,2},{4,5},{5,4},{6,7},{7,6},{8,9},{9,8},{10,11... | collective-permute-start | bytes 1572872 | tf_op jit(solution)/shard_map/ppermute | solution.py:21
  74.9 5.7 %copy-start.2 = (f32[16,128,128]{2,1,0:T(8,128)S(1)}, f32[16,128,128]{2,1,0:T(8,128)}, u32[]{:S(2)}) copy-start(f32[16,128,128]{2,1,0:T(8,128)} %get-tuple-element.224) | copy-start | bytes 3145732
  76.4 3.0 %collective-permute-start.8 = (f32[16,136,128]{2,1,0:T(8,128)S(1)}, f32[16,136,128]{2,1,0:T(8,128)}, u32[]{:S(2)}, u32[]{:S(2)}) collective-permute-start(f32[16,136,128]{2,1,0:T(8,128)S(1)} %fusion.2), channel_id=1, source_target_pairs={{0,1},{1,0},{2,3},{3,2},{4,5},{5,4},{6,7},{7,6},{8,9},{9,8},{10,11... | collective-permute-start | bytes 3342344 | tf_op jit(solution)/shard_map/ppermute | solution.py:21
  82.0 1.6 %copy-start.4 = (f32[16,1,128]{2,1,0:T(1,128)S(1)}, f32[16,1,128]{2,1,0:T(1,128)}, u32[]{:S(2)}) copy-start(f32[16,1,128]{2,1,0:T(1,128)} %get-tuple-element.225) | copy-start | bytes 24580
  82.3 8.3 %collective-permute-start.9 = (f32[2,128,128]{2,1,0:T(8,128)S(1)}, f32[2,128,128]{2,1,0:T(8,128)S(1)}, u32[]{:S(2)}, u32[]{:S(2)}) collective-permute-start(f32[2,128,128]{2,1,0:T(8,128)S(1)} %bitcast_add_fusion.5), channel_id=1, source_target_pairs={{4,0},{8,4},{12,8},{5,1},{9,5},{13,9},{6,2},{10,6},{14,10},{7,3},{... | collective-permute-start | bytes 393224 | tf_op jit(solution)/shard_map/ppermute | solution.py:62
  91.5 8.8 %collective-permute-start.10 = (f32[2,128,128]{2,1,0:T(8,128)S(1)}, f32[2,128,128]{2,1,0:T(8,128)S(1)}, u32[]{:S(2)}, u32[]{:S(2)}) collective-permute-start(f32[2,128,128]{2,1,0:T(8,128)S(1)} %bitcast_add_fusion.4), channel_id=1, source_target_pairs={{4,0},{8,4},{12,8},{5,1},{9,5},{13,9},{6,2},{10,6},{14,10},{7,3},{... | collective-permute-start | bytes 393224 | tf_op jit(solution)/shard_map/ppermute | solution.py:62
  101.0 8.3 %collective-permute-start.11 = (f32[2,128,128]{2,1,0:T(8,128)S(1)}, f32[2,128,128]{2,1,0:T(8,128)S(1)}, u32[]{:S(2)}, u32[]{:S(2)}) collective-permute-start(f32[2,128,128]{2,1,0:T(8,128)S(1)} %bitcast_add_fusion.3), channel_id=1, source_target_pairs={{4,0},{8,4},{12,8},{5,1},{9,5},{13,9},{6,2},{10,6},{14,10},{7,3},{... | collective-permute-start | bytes 393224 | tf_op jit(solution)/shard_map/ppermute | solution.py:62
  110.1 8.1 %collective-permute-start.12 = (f32[2,128,128]{2,1,0:T(8,128)S(1)}, f32[2,128,128]{2,1,0:T(8,128)S(1)}, u32[]{:S(2)}, u32[]{:S(2)}) collective-permute-start(f32[2,128,128]{2,1,0:T(8,128)S(1)} %bitcast_add_fusion.2), channel_id=1, source_target_pairs={{4,0},{8,4},{12,8},{5,1},{9,5},{13,9},{6,2},{10,6},{14,10},{7,3},{... | collective-permute-start | bytes 393224 | tf_op jit(solution)/shard_map/ppermute | solution.py:62
  119.0 8.3 %collective-permute-start.14 = (f32[2,128,128]{2,1,0:T(8,128)S(1)}, f32[2,128,128]{2,1,0:T(8,128)S(1)}, u32[]{:S(2)}, u32[]{:S(2)}) collective-permute-start(f32[2,128,128]{2,1,0:T(8,128)S(1)} %bitcast_add_fusion.1), channel_id=1, source_target_pairs={{4,0},{8,4},{12,8},{5,1},{9,5},{13,9},{6,2},{10,6},{14,10},{7,3},{... | collective-permute-start | bytes 393224 | tf_op jit(solution)/shard_map/ppermute | solution.py:62
  121.0 6.3 %collective-permute-start.13 = (f32[16,128]{1,0:T(8,128)S(1)}, f32[16,128]{1,0:T(8,128)S(1)}, u32[]{:S(2)}, u32[]{:S(2)}) collective-permute-start(f32[16,128]{1,0:T(8,128)S(1)} %bitcast.229), channel_id=1, source_target_pairs={{0,4},{4,0},{8,12},{12,8},{1,5},{5,1},{9,13},{13,9},{2,6},{6,2},{1... | collective-permute-start | bytes 24584 | tf_op jit(solution)/shard_map/ppermute | solution.py:114
  128.0 8.0 %collective-permute-start.16 = (f32[2,128,128]{2,1,0:T(8,128)S(1)}, f32[2,128,128]{2,1,0:T(8,128)S(1)}, u32[]{:S(2)}, u32[]{:S(2)}) collective-permute-start(f32[2,128,128]{2,1,0:T(8,128)S(1)} %bitcast_add_fusion), channel_id=1, source_target_pairs={{4,0},{8,4},{12,8},{5,1},{9,5},{13,9},{6,2},{10,6},{14,10},{7,3},{... | collective-permute-start | bytes 393224 | tf_op jit(solution)/shard_map/ppermute | solution.py:62
  129.4 6.7 %collective-permute-start.15 = (f32[16,128]{1,0:T(8,128)S(1)}, f32[16,128]{1,0:T(8,128)S(1)}, u32[]{:S(2)}, u32[]{:S(2)}) collective-permute-start(f32[16,128]{1,0:T(8,128)S(1)} %add.209), channel_id=1, source_target_pairs={{0,8},{4,12},{8,0},{12,4},{1,9},{5,13},{9,1},{13,5},{2,10},{6,14},... | collective-permute-start | bytes 24584 | tf_op jit(solution)/shard_map/ppermute | solution.py:114
  136.7 2.0 %collective-permute-start.17 = (f32[8,128,128]{2,1,0:T(8,128)S(1)}, f32[8,128,128]{2,1,0:T(8,128)S(1)}, u32[]{:S(2)}, u32[]{:S(2)}) collective-permute-start(f32[8,128,128]{2,1,0:T(8,128)S(1)} %bitcast.202), channel_id=1, source_target_pairs={{0,1},{1,0},{2,3},{3,2},{4,5},{5,4},{6,7},{7,6},{8,9},{9,8},{10,11... | collective-permute-start | bytes 1572872 | tf_op jit(solution)/shard_map/ppermute | solution.py:21

commit v13 on v12

--- a/solution.py
+++ b/solution.py
@@ -9,7 +9,7 @@
 
 DH = 128
 PAD = 8
-CHUNKS = 4
+CHUNKS = 2
 HB = 4
 PIECE_STEPS = 2
 
@@ -109,15 +109,24 @@
     def grads_step(piece, both, anchor):
         return piece(both[0], anchor), both[1]
 
+    def both_steps(first, second, both, anchor):
+        return second(first(both, anchor), anchor)
+
     def gain_step(distance, both, anchor):
         partners = [(i, i ^ distance) for i in range(chips)]
         return both[0], both[1] + lax.ppermute(both[1], "ctx", perm=partners)
 
-    steps = [functools.partial(grads_step, piece) for piece in cover]
+    rounds = []
     distance = 1
     while distance < chips:
-        steps.append(functools.partial(gain_step, distance))
+        rounds.append(functools.partial(gain_step, distance))
         distance *= 2
+    steps = [functools.partial(grads_step, piece) for piece in cover]
+    for index, gain_round in enumerate(rounds):
+        if index < len(steps):
+            steps[index] = functools.partial(both_steps, steps[index], gain_round)
+        else:
+            steps.append(gain_round)
     suffix_half, (cover, gain_total) = chain_scan(
         halves(chip_state, c), halves(chip_decay, c), True, steps, (None, chip_gain)
     )

time: 149 us -> 131 us (0.88)
  starting transfers between devices: 37.7 us -> 30.4 us
  waiting for transfers between devices: 18.9 us -> 12.1 us
  other arithmetic: 23.2 us -> 18.8 us
    ppermute x12 -> x8, starting transfers between devices: 30.1 us -> 22.8 us  [chain_scan(): arrived = lax.ppermute(outgoing, 'ctx', perm=perm)]
    ppermute x2, waiting for transfers between devices: 6.22 us -> 0.01 us  [gain_step(): return (both[0], both[1] + lax.ppermute(both[1], 'ctx', perm=partners))]
    scatter x12 -> x8, other arithmetic: 7.77 us -> 5.25 us  [chain_scan(): prefix = prefix.at[slot].set(jnp.where(valid, arrived, prefix[slot]))]
    ppermute x12 -> x8, waiting for transfers between devices: 6.81 us -> 4.66 us  [chain_scan(): arrived = lax.ppermute(outgoing, 'ctx', perm=perm)]
    ppermute x4, waiting for transfers between devices: 5.88 us -> 7.45 us  [swap_dp(): return lax.ppermute(x, 'dp', perm=[(0, 1), (1, 0)])]
    another operation x6 -> x4, other arithmetic: 4.5 us -> 2.95 us
  transfers between devices with their start and end apart: 18 -> 14, of which waited for: 11 -> 8; matrix products, arithmetic and copies ran while one was open for 4% -> 4% of each run, Pallas kernels for 27% -> 31%
where the time goes in v13:
time: 131 us; the launch traced here: 130 us
  Pallas kernels  64.2 us (49%)
  starting transfers between devices  30.4 us (23%)
  other arithmetic  18.8 us (14%)
  waiting for transfers between devices  12.1 us (9%)
  local copies, waits for them, and re-layouts  2.78 us (2%)
    pallas_call x11, Pallas kernels, _per_head(): pl.pallas_call(body, grid=(count,), in_specs=in_specs, out_specs=[spec(ki...  64.2 us
    ppermute x8, starting transfers between devices, chain_scan(): arrived = lax.ppermute(outgoing, 'ctx', perm=perm)  22.8 us
    ppermute x4, waiting for transfers between devices, swap_dp(): return lax.ppermute(x, 'dp', perm=[(0, 1), (1, 0)])  7.45 us
    ppermute x2, starting transfers between devices, gain_step(): return (both[0], both[1] + lax.ppermute(both[1], 'ctx', perm=partners))  6.76 us
    scatter x8, other arithmetic, chain_scan(): prefix = prefix.at[slot].set(jnp.where(valid, arrived, prefix[slot]))  5.25 us
    ppermute x8, waiting for transfers between devices, chain_scan(): arrived = lax.ppermute(outgoing, 'ctx', perm=perm)  4.66 us
    another operation x4, other arithmetic  2.95 us
    concatenate x2, other arithmetic, pack_rows(): return jnp.concatenate([core] + pad + [fill], axis=1)  2.92 us
  transfers between devices with their start and end apart: 14, of which 8 were waited for; matrix products, arithmetic and copies ran while one was open for 4% of the time, Pallas kernels for 31%

profile of v13, /device:TPU:0, one launch (start us, length us, event | category | flops | bytes accessed | tf_op | source)
XLA Modules:
  0.0 129.9 jit_solution(3220113408100330884)
XLA Ops:
  3.0 5.8 %shard_map.93 = f32[16,128,128]{2,1,0:T(8,128)} custom-call(bf16[512,2048]{1,0:T(8,128)(2,1)} %k_ref.7, bf16[512,2048]{1,0:T(8,128)(2,1)} %v_ref.7, f32[512,16]{1,0:T(8,128)} %copy.37.cum_ref.refs_3_.refs_4_, f32[16,512]{1,0:T(8,128)} %bitcast.136), custom_call_target="tpu_custom_call" | custom-call | flops 268435456 | bytes 4194304 | tf_op jit(solution)/shard_map/pallas_call | solution.py:312
  8.9 1.4 %fusion = f32[16,136,128]{2,1,0:T(8,128)S(1)} fusion(f32[16,1,128]{2,1,0:T(1,128)S(1)} %broadcast_in_dim.6, f32[16,128,128]{2,1,0:T(8,128)} %shard_map.93, f32[136]{0:T(256)S(1)} %pad.58.clone), kind=kLoop, calls=%fused_computation.2 | loop fusion | flops 557056 | bytes 2171424 | tf_op jit(solution)/shard_map/concatenate | solution.py:28
  10.9 2.4 %collective-permute-done = f32[16,136,128]{2,1,0:T(8,128)S(1)} collective-permute-done((f32[16,136,128]{2,1,0:T(8,128)S(1)}, f32[16,136,128]{2,1,0:T(8,128)S(1)}, u32[]{:S(2)}, u32[]{:S(2)}) %collective-permute-start) | collective-permute-done | bytes 1114144 | tf_op jit(solution)/shard_map/ppermute | solution.py:21
  14.2 4.9 %collective-permute-start.1 = (f32[4,128,128]{2,1,0:T(8,128)S(1)}, f32[4,128,128]{2,1,0:T(8,128)S(1)}, u32[]{:S(2)}, u32[]{:S(2)}) collective-permute-start(f32[4,128,128]{2,1,0:T(8,128)S(1)} %bitcast_add_fusion.7), channel_id=1, source_target_pairs={{0,4},{4,8},{8,12},{1,5},{5,9},{9,13},{2,6},{6,10},{10,14},{3,7},{... | collective-permute-start | bytes 786440 | tf_op jit(solution)/shard_map/ppermute | solution.py:62
  19.8 3.9 %shard_map.94.refs_5_ = f32[512,2048]{1,0:T(8,128)} custom-call(bf16[512,2048]{1,0:T(8,128)(2,1)} %refs_0_.8, bf16[512,2048]{1,0:T(8,128)(2,1)} %k_ref.7, bf16[512,2048]{1,0:T(8,128)(2,1)} %v_ref.7, f32[512,16]{1,0:T(8,128)} %copy.37.cum_ref.refs_3_.refs_4_, f32[16,512]{1,0:T(8,128)} %bitcast.137), custom_call_target="tpu_custom_call" | custom-call | flops 536870912 | bytes 2621440 | tf_op jit(solution)/shard_map/pallas_call | solution.py:312
  25.7 4.4 %collective-permute-start.2 = (f32[4,128,128]{2,1,0:T(8,128)S(1)}, f32[4,128,128]{2,1,0:T(8,128)S(1)}, u32[]{:S(2)}, u32[]{:S(2)}) collective-permute-start(f32[4,128,128]{2,1,0:T(8,128)S(1)} %bitcast_add_fusion.6), channel_id=1, source_target_pairs={{0,4},{4,8},{8,12},{1,5},{5,9},{9,13},{2,6},{6,10},{10,14},{3,7},{... | collective-permute-start | bytes 786440 | tf_op jit(solution)/shard_map/ppermute | solution.py:62
  30.1 4.0 %shard_map.95.refs_5_ = f32[512,2048]{1,0:T(8,128)} custom-call(bf16[512,2048]{1,0:T(8,128)(2,1)} %refs_0_.8, bf16[512,2048]{1,0:T(8,128)(2,1)} %k_ref.7, bf16[512,2048]{1,0:T(8,128)(2,1)} %v_ref.7, f32[512,16]{1,0:T(8,128)} %copy.37.cum_ref.refs_3_.refs_4_, f32[16,512]{1,0:T(8,128)} %bitcast.138, ...), custom_call_target="tpu_custom_call", output_to_operand_aliasing={{}: (5, {})} | custom-call | flops 536870912 | bytes 2621440 | tf_op jit(solution)/shard_map/pallas_call | solution.py:312
  35.8 4.4 %collective-permute-start.3 = (f32[4,128,128]{2,1,0:T(8,128)S(1)}, f32[4,128,128]{2,1,0:T(8,128)S(1)}, u32[]{:S(2)}, u32[]{:S(2)}) collective-permute-start(f32[4,128,128]{2,1,0:T(8,128)S(1)} %bitcast_add_fusion.5), channel_id=1, source_target_pairs={{0,4},{4,8},{8,12},{1,5},{5,9},{9,13},{2,6},{6,10},{10,14},{3,7},{... | collective-permute-start | bytes 786440 | tf_op jit(solution)/shard_map/ppermute | solution.py:62
  41.0 3.9 %shard_map.96.refs_5_ = f32[512,2048]{1,0:T(8,128)} custom-call(bf16[512,2048]{1,0:T(8,128)(2,1)} %refs_0_.8, bf16[512,2048]{1,0:T(8,128)(2,1)} %k_ref.7, bf16[512,2048]{1,0:T(8,128)(2,1)} %v_ref.7, f32[512,16]{1,0:T(8,128)} %copy.37.cum_ref.refs_3_.refs_4_, f32[16,512]{1,0:T(8,128)} %bitcast.139, ...), custom_call_target="tpu_custom_call", output_to_operand_aliasing={{}: (5, {})} | custom-call | flops 536870912 | bytes 2621440 | tf_op jit(solution)/shard_map/pallas_call | solution.py:312
  45.7 3.8 %collective-permute-start.4 = (f32[4,128,128]{2,1,0:T(8,128)S(1)}, f32[4,128,128]{2,1,0:T(8,128)S(1)}, u32[]{:S(2)}, u32[]{:S(2)}) collective-permute-start(f32[4,128,128]{2,1,0:T(8,128)S(1)} %bitcast_add_fusion.4), channel_id=1, source_target_pairs={{0,4},{4,8},{8,12},{1,5},{5,9},{9,13},{2,6},{6,10},{10,14},{3,7},{... | collective-permute-start | bytes 786440 | tf_op jit(solution)/shard_map/ppermute | solution.py:62
  49.5 4.0 %shard_map.97.intra_ref = f32[512,2048]{1,0:T(8,128)} custom-call(bf16[512,2048]{1,0:T(8,128)(2,1)} %refs_0_.8, bf16[512,2048]{1,0:T(8,128)(2,1)} %k_ref.7, bf16[512,2048]{1,0:T(8,128)(2,1)} %v_ref.7, f32[512,16]{1,0:T(8,128)} %copy.37.cum_ref.refs_3_.refs_4_, f32[16,512]{1,0:T(8,128)} %bitcast.140, ...), custom_call_target="tpu_custom_call", output_to_operand_aliasing={{}: (5, {})} | custom-call | flops 536870912 | bytes 2621440 | tf_op jit(solution)/shard_map/pallas_call | solution.py:312
  54.4 1.8 %collective-permute-done.5 = f32[8,128,128]{2,1,0:T(8,128)S(1)} collective-permute-done((f32[8,128,128]{2,1,0:T(8,128)S(1)}, f32[8,128,128]{2,1,0:T(8,128)S(1)}, u32[]{:S(2)}, u32[]{:S(2)}) %collective-permute-start.5) | collective-permute-done | bytes 524320 | tf_op jit(solution)/shard_map/ppermute | solution.py:21
  57.4 9.4 %shard_map.98 = (bf16[512,2048]{1,0:T(8,128)(2,1)}, f32[16,128,128]{2,1,0:T(8,128)}, f32[16,1,128]{2,1,0:T(1,128)}) custom-call(bf16[512,2048]{1,0:T(8,128)(2,1)} %refs_0_.8, bf16[512,2048]{1,0:T(8,128)(2,1)} %g_ref.1, f32[512,2048]{1,0:T(8,128)} %shard_map.97.intra_ref, bf16[16,128,128]{2,1,0:T(8,128)(2,1)} %select_convert_fusion.1.st_ref.refs_6_, ...), custom_call_target="tpu_custom_call" | custom-call | flops 536870912 | bytes 10485760 | tf_op jit(solution)/shard_map/pallas_call | solution.py:312
  66.8 1.5 %fusion.2 = f32[16,136,128]{2,1,0:T(8,128)S(1)} fusion(f32[16,1,128]{2,1,0:T(1,128)S(1)} %broadcast_in_dim.6, f32[16,1,128]{2,1,0:T(1,128)} %get-tuple-element.167, f32[16,128,128]{2,1,0:T(8,128)} %get-tuple-element.166, f32[136]{0:T(256)S(1)} %pad.37.clone), kind=kLoop, calls=%fused_computation.4 | loop fusion | flops 835584 | bytes 2179616 | tf_op jit(solution)/shard_map/concatenate | solution.py:28
  69.2 2.0 %collective-permute-done.6 = f32[16,136,128]{2,1,0:T(8,128)} collective-permute-done((f32[16,136,128]{2,1,0:T(8,128)S(1)}, f32[16,136,128]{2,1,0:T(8,128)}, u32[]{:S(2)}, u32[]{:S(2)}) %collective-permute-start.6) | collective-permute-done | bytes 1114144 | tf_op jit(solution)/shard_map/ppermute | solution.py:21
  72.5 1.4 %fusion.32 = (f32[16,128,128]{2,1,0:T(8,128)S(1)}, f32[16,128,128]{2,1,0:T(8,128)S(1)}) fusion(f32[16,136,128]{2,1,0:T(8,128)} %collective-permute-done.6, f32[16,128,128]{2,1,0:T(8,128)S(1)} %copy-done.2, pred[]{:T(512)S(6)} %eq.2), kind=kLoop, calls=%fused_computation.138 | loop fusion | flops 262144 | bytes 4194305 | tf_op jit(solution)/shard_map/slice | solution.py:98
  76.3 3.0 %collective-permute-start.7 = (f32[16,128]{1,0:T(8,128)S(1)}, f32[16,128]{1,0:T(8,128)S(1)}, u32[]{:S(2)}, u32[]{:S(2)}) collective-permute-start(f32[16,128]{1,0:T(8,128)S(1)} %bitcast.157), channel_id=1, source_target_pairs={{0,4},{4,0},{8,12},{12,8},{1,5},{5,1},{9,13},{13,9},{2,6},{6,2},{1... | collective-permute-start | bytes 24584 | tf_op jit(solution)/shard_map/ppermute | solution.py:117
  79.4 6.2 %shard_map.99 = (bf16[512,2048]{1,0:T(8,128)(2,1)}, f32[512,2048]{1,0:T(8,128)}, f32[512,2048]{1,0:T(8,128)}) custom-call(bf16[512,2048]{1,0:T(8,128)(2,1)} %refs_0_.8, bf16[512,2048]{1,0:T(8,128)(2,1)} %k_ref.7, bf16[512,2048]{1,0:T(8,128)(2,1)} %v_ref.7, bf16[512,2048]{1,0:T(8,128)(2,1)} %get-tuple-element.191.og_ref.refs_3_, ...), custom_call_target="tpu_custom_call" | custom-call | flops 1409286144 | bytes 4718592 | tf_op jit(solution)/shard_map/pallas_call | solution.py:312
  86.4 1.5 %collective-permute-start.10 = (f32[4,128,128]{2,1,0:T(8,128)S(1)}, f32[4,128,128]{2,1,0:T(8,128)S(1)}, u32[]{:S(2)}, u32[]{:S(2)}) collective-permute-start(f32[4,128,128]{2,1,0:T(8,128)S(1)} %bitcast_add_fusion.2), channel_id=1, source_target_pairs={{4,0},{8,4},{12,8},{5,1},{9,5},{13,9},{6,2},{10,6},{14,10},{7,3},{... | collective-permute-start | bytes 786440 | tf_op jit(solution)/shard_map/ppermute | solution.py:62
  87.9 3.7 %collective-permute-start.9 = (f32[16,128]{1,0:T(8,128)S(1)}, f32[16,128]{1,0:T(8,128)S(1)}, u32[]{:S(2)}, u32[]{:S(2)}) collective-permute-start(f32[16,128]{1,0:T(8,128)S(1)} %add.145), channel_id=1, source_target_pairs={{0,8},{4,12},{8,0},{12,4},{1,9},{5,13},{9,1},{13,5},{2,10},{6,14},... | collective-permute-start | bytes 24584 | tf_op jit(solution)/shard_map/ppermute | solution.py:117
  91.6 6.2 %shard_map.100 = (bf16[512,2048]{1,0:T(8,128)(2,1)}, f32[512,2048]{1,0:T(8,128)}, f32[512,2048]{1,0:T(8,128)}) custom-call(bf16[512,2048]{1,0:T(8,128)(2,1)} %refs_0_.8, bf16[512,2048]{1,0:T(8,128)(2,1)} %k_ref.7, bf16[512,2048]{1,0:T(8,128)(2,1)} %v_ref.7, ...), custom_call_target="tpu_custom_call", output_to_operand_aliasing={{0}: (7, {}), {1}: (8, {}), {2}: (9, {})} | custom-call | flops 1409286144 | bytes 4718592 | tf_op jit(solution)/shard_map/pallas_call | solution.py:312
  100.6 6.2 %shard_map.101 = (bf16[512,2048]{1,0:T(8,128)(2,1)}, f32[512,2048]{1,0:T(8,128)}, f32[512,2048]{1,0:T(8,128)}) custom-call(bf16[512,2048]{1,0:T(8,128)(2,1)} %refs_0_.8, bf16[512,2048]{1,0:T(8,128)(2,1)} %k_ref.7, bf16[512,2048]{1,0:T(8,128)(2,1)} %v_ref.7, ...), custom_call_target="tpu_custom_call", output_to_operand_aliasing={{0}: (7, {}), {1}: (8, {}), {2}: (9, {})} | custom-call | flops 1409286144 | bytes 4718592 | tf_op jit(solution)/shard_map/pallas_call | solution.py:312
  110.1 6.2 %shard_map.102 = (bf16[512,2048]{1,0:T(8,128)(2,1)}, f32[512,2048]{1,0:T(8,128)}, f32[512,2048]{1,0:T(8,128)}) custom-call(bf16[512,2048]{1,0:T(8,128)(2,1)} %refs_0_.8, bf16[512,2048]{1,0:T(8,128)(2,1)} %k_ref.7, bf16[512,2048]{1,0:T(8,128)(2,1)} %v_ref.7, ...), custom_call_target="tpu_custom_call", output_to_operand_aliasing={{0}: (7, {}), {1}: (8, {}), {2}: (9, {})} | custom-call | flops 1409286144 | bytes 4718592 | tf_op jit(solution)/shard_map/pallas_call | solution.py:312
  121.4 8.4 %shard_map.103 = (bf16[512,2048]{1,0:T(8,128)(2,1)}, bf16[512,2048]{1,0:T(8,128)(2,1)}) custom-call(bf16[512,2048]{1,0:T(8,128)(2,1)} %k_ref.7, bf16[512,2048]{1,0:T(8,128)(2,1)} %v_ref.7, f32[512,2048]{1,0:T(8,128)} %get-tuple-element.200.kg_ref, f32[512,2048]{1,0:T(8,128)} %get-tuple-element.201.vg_ref, bf16[16,128,128]{2,1,0:T(8,128)(2,1)} %select_convert_fusion.gl_ref, ...), custom_call_target="tpu_custom_call" | custom-call | flops 536870912 | bytes 16777216 | tf_op jit(solution)/shard_map/pallas_call | solution.py:312
  (89 shorter events, 28.4 us)
Async XLA Ops:
  0.6 0.8 copy-start
  1.8 1.2 copy-start.3
  8.8 4.9 %copy-start.1 = (f32[16,128,128]{2,1,0:T(8,128)S(1)}, f32[16,128,128]{2,1,0:T(8,128)}, u32[]{:S(2)}) copy-start(f32[16,128,128]{2,1,0:T(8,128)} %shard_map.93) | copy-start | bytes 3145732
  10.3 2.9 %collective-permute-start = (f32[16,136,128]{2,1,0:T(8,128)S(1)}, f32[16,136,128]{2,1,0:T(8,128)S(1)}, u32[]{:S(2)}, u32[]{:S(2)}) collective-permute-start(f32[16,136,128]{2,1,0:T(8,128)S(1)} %fusion), channel_id=1, source_target_pairs={{0,1},{1,0},{2,3},{3,2},{4,5},{5,4},{6,7},{7,6},{8,9},{9,8},{10,11... | collective-permute-start | bytes 3342344 | tf_op jit(solution)/shard_map/ppermute | solution.py:21
  13.9 5.1 %copy-start.5 = (s32[4]{0:T(128)S(1)}, s32[4]{0:T(128)}, u32[]{:S(2)}) copy-start(s32[4]{0:T(128)} %constant.208.clone.1) | copy-start | bytes 52
  14.2 10.7 %collective-permute-start.1 = (f32[4,128,128]{2,1,0:T(8,128)S(1)}, f32[4,128,128]{2,1,0:T(8,128)S(1)}, u32[]{:S(2)}, u32[]{:S(2)}) collective-permute-start(f32[4,128,128]{2,1,0:T(8,128)S(1)} %bitcast_add_fusion.7), channel_id=1, source_target_pairs={{0,4},{4,8},{8,12},{1,5},{5,9},{9,13},{2,6},{6,10},{10,14},{3,7},{... | collective-permute-start | bytes 786440 | tf_op jit(solution)/shard_map/ppermute | solution.py:62
  25.7 9.4 %collective-permute-start.2 = (f32[4,128,128]{2,1,0:T(8,128)S(1)}, f32[4,128,128]{2,1,0:T(8,128)S(1)}, u32[]{:S(2)}, u32[]{:S(2)}) collective-permute-start(f32[4,128,128]{2,1,0:T(8,128)S(1)} %bitcast_add_fusion.6), channel_id=1, source_target_pairs={{0,4},{4,8},{8,12},{1,5},{5,9},{9,13},{2,6},{6,10},{10,14},{3,7},{... | collective-permute-start | bytes 786440 | tf_op jit(solution)/shard_map/ppermute | solution.py:62
  35.8 9.1 %collective-permute-start.3 = (f32[4,128,128]{2,1,0:T(8,128)S(1)}, f32[4,128,128]{2,1,0:T(8,128)S(1)}, u32[]{:S(2)}, u32[]{:S(2)}) collective-permute-start(f32[4,128,128]{2,1,0:T(8,128)S(1)} %bitcast_add_fusion.5), channel_id=1, source_target_pairs={{0,4},{4,8},{8,12},{1,5},{5,9},{9,13},{2,6},{6,10},{10,14},{3,7},{... | collective-permute-start | bytes 786440 | tf_op jit(solution)/shard_map/ppermute | solution.py:62
  45.7 7.8 %collective-permute-start.4 = (f32[4,128,128]{2,1,0:T(8,128)S(1)}, f32[4,128,128]{2,1,0:T(8,128)S(1)}, u32[]{:S(2)}, u32[]{:S(2)}) collective-permute-start(f32[4,128,128]{2,1,0:T(8,128)S(1)} %bitcast_add_fusion.4), channel_id=1, source_target_pairs={{0,4},{4,8},{8,12},{1,5},{5,9},{9,13},{2,6},{6,10},{10,14},{3,7},{... | collective-permute-start | bytes 786440 | tf_op jit(solution)/shard_map/ppermute | solution.py:62
  54.2 2.0 %collective-permute-start.5 = (f32[8,128,128]{2,1,0:T(8,128)S(1)}, f32[8,128,128]{2,1,0:T(8,128)S(1)}, u32[]{:S(2)}, u32[]{:S(2)}) collective-permute-start(f32[8,128,128]{2,1,0:T(8,128)S(1)} %bitcast.135), channel_id=1, source_target_pairs={{0,1},{1,0},{2,3},{3,2},{4,5},{5,4},{6,7},{7,6},{8,9},{9,8},{10,11... | collective-permute-start | bytes 1572872 | tf_op jit(solution)/shard_map/ppermute | solution.py:21
  66.8 5.7 %copy-start.2 = (f32[16,128,128]{2,1,0:T(8,128)S(1)}, f32[16,128,128]{2,1,0:T(8,128)}, u32[]{:S(2)}) copy-start(f32[16,128,128]{2,1,0:T(8,128)} %get-tuple-element.166) | copy-start | bytes 3145732
  68.3 3.0 %collective-permute-start.6 = (f32[16,136,128]{2,1,0:T(8,128)S(1)}, f32[16,136,128]{2,1,0:T(8,128)}, u32[]{:S(2)}, u32[]{:S(2)}) collective-permute-start(f32[16,136,128]{2,1,0:T(8,128)S(1)} %fusion.2), channel_id=1, source_target_pairs={{0,1},{1,0},{2,3},{3,2},{4,5},{5,4},{6,7},{7,6},{8,9},{9,8},{10,11... | collective-permute-start | bytes 3342344 | tf_op jit(solution)/shard_map/ppermute | solution.py:21
  73.9 1.6 %copy-start.4 = (f32[16,1,128]{2,1,0:T(1,128)S(1)}, f32[16,1,128]{2,1,0:T(1,128)}, u32[]{:S(2)}) copy-start(f32[16,1,128]{2,1,0:T(1,128)} %get-tuple-element.167) | copy-start | bytes 24580
  74.2 11.4 %collective-permute-start.8 = (f32[4,128,128]{2,1,0:T(8,128)S(1)}, f32[4,128,128]{2,1,0:T(8,128)S(1)}, u32[]{:S(2)}, u32[]{:S(2)}) collective-permute-start(f32[4,128,128]{2,1,0:T(8,128)S(1)} %bitcast_add_fusion.3), channel_id=1, source_target_pairs={{4,0},{8,4},{12,8},{5,1},{9,5},{13,9},{6,2},{10,6},{14,10},{7,3},{... | collective-permute-start | bytes 786440 | tf_op jit(solution)/shard_map/ppermute | solution.py:62
  76.3 9.2 %collective-permute-start.7 = (f32[16,128]{1,0:T(8,128)S(1)}, f32[16,128]{1,0:T(8,128)S(1)}, u32[]{:S(2)}, u32[]{:S(2)}) collective-permute-start(f32[16,128]{1,0:T(8,128)S(1)} %bitcast.157), channel_id=1, source_target_pairs={{0,4},{4,0},{8,12},{12,8},{1,5},{5,1},{9,13},{13,9},{2,6},{6,2},{1... | collective-permute-start | bytes 24584 | tf_op jit(solution)/shard_map/ppermute | solution.py:117
  86.4 11.5 %collective-permute-start.10 = (f32[4,128,128]{2,1,0:T(8,128)S(1)}, f32[4,128,128]{2,1,0:T(8,128)S(1)}, u32[]{:S(2)}, u32[]{:S(2)}) collective-permute-start(f32[4,128,128]{2,1,0:T(8,128)S(1)} %bitcast_add_fusion.2), channel_id=1, source_target_pairs={{4,0},{8,4},{12,8},{5,1},{9,5},{13,9},{6,2},{10,6},{14,10},{7,3},{... | collective-permute-start | bytes 786440 | tf_op jit(solution)/shard_map/ppermute | solution.py:62
  87.9 10.0 %collective-permute-start.9 = (f32[16,128]{1,0:T(8,128)S(1)}, f32[16,128]{1,0:T(8,128)S(1)}, u32[]{:S(2)}, u32[]{:S(2)}) collective-permute-start(f32[16,128]{1,0:T(8,128)S(1)} %add.145), channel_id=1, source_target_pairs={{0,8},{4,12},{8,0},{12,4},{1,9},{5,13},{9,1},{13,5},{2,10},{6,14},... | collective-permute-start | bytes 24584 | tf_op jit(solution)/shard_map/ppermute | solution.py:117
  98.6 9.4 %collective-permute-start.11 = (f32[4,128,128]{2,1,0:T(8,128)S(1)}, f32[4,128,128]{2,1,0:T(8,128)S(1)}, u32[]{:S(2)}, u32[]{:S(2)}) collective-permute-start(f32[4,128,128]{2,1,0:T(8,128)S(1)} %bitcast_add_fusion.1), channel_id=1, source_target_pairs={{4,0},{8,4},{12,8},{5,1},{9,5},{13,9},{6,2},{10,6},{14,10},{7,3},{... | collective-permute-start | bytes 786440 | tf_op jit(solution)/shard_map/ppermute | solution.py:62
  108.7 8.9 %collective-permute-start.12 = (f32[4,128,128]{2,1,0:T(8,128)S(1)}, f32[4,128,128]{2,1,0:T(8,128)S(1)}, u32[]{:S(2)}, u32[]{:S(2)}) collective-permute-start(f32[4,128,128]{2,1,0:T(8,128)S(1)} %bitcast_add_fusion), channel_id=1, source_target_pairs={{4,0},{8,4},{12,8},{5,1},{9,5},{13,9},{6,2},{10,6},{14,10},{7,3},{... | collective-permute-start | bytes 786440 | tf_op jit(solution)/shard_map/ppermute | solution.py:62
  118.2 2.0 %collective-permute-start.13 = (f32[8,128,128]{2,1,0:T(8,128)S(1)}, f32[8,128,128]{2,1,0:T(8,128)S(1)}, u32[]{:S(2)}, u32[]{:S(2)}) collective-permute-start(f32[8,128,128]{2,1,0:T(8,128)S(1)} %bitcast.134), channel_id=1, source_target_pairs={{0,1},{1,0},{2,3},{3,2},{4,5},{5,4},{6,7},{7,6},{8,9},{9,8},{10,11... | collective-permute-start | bytes 1572872 | tf_op jit(solution)/shard_map/ppermute | solution.py:21

commit v14 on v13

--- a/solution.py
+++ b/solution.py
@@ -71,9 +71,9 @@
     return prefix.reshape(heads, DH, DH), cover
 
 
-def forward_states(local_state, final_log, cover):
+def forward_states(message, final_log, cover):
     c = lax.axis_index("dp")
-    message = pack_rows(local_state, final_log)
+    local_state = message[:, :DH, :]
     other = swap_dp(message)
     own_state, other_state = local_state, other[:, :DH, :]
     own_fin, other_fin = final_log, other[:, DH, 0]
@@ -89,11 +89,11 @@
     return jnp.where(c == 0, prefix, core_one), cover
 
 
-def backward_states(moment, final_log, gain_part, cover):
+def backward_states(message, final_log, cover):
     c = lax.axis_index("dp")
-    heads = moment.shape[0]
-    gain_rows = gain_part.reshape(heads, DH)
-    message = pack_rows(moment, final_log, gain_rows)
+    heads = message.shape[0]
+    moment = message[:, :DH, :]
+    gain_rows = message[:, DH + 1, :]
     other = swap_dp(message)
     own_m, other_m = moment, other[:, :DH, :]
     own_fin, other_fin = final_log, other[:, DH, 0]
@@ -178,12 +178,21 @@
     return slice(j * DH, (j + 1) * DH)
 
 
+def _pad_rows(*rows):
+    slot = lax.broadcasted_iota(jnp.int32, (PAD, DH), 0)
+    block = jnp.zeros((PAD, DH), jnp.float32)
+    for index, value in enumerate(rows):
+        block = jnp.where(slot == index, jnp.broadcast_to(value, (PAD, DH)), block)
+    return block
+
+
 def local_state_kernel(k_ref, v_ref, cum_ref, cumt_ref, s_ref):
     for j in range(HB):
         cols = _lanes(j)
-        _, _, _, toend = _head_vectors(cum_ref, cumt_ref, j)
+        col, _, _, toend = _head_vectors(cum_ref, cumt_ref, j)
         scaled = (k_ref[:, cols].astype(jnp.float32) * toend).astype(jnp.bfloat16)
-        s_ref[j] = _tn(scaled, v_ref[:, cols])
+        s_ref[j, :DH, :] = _tn(scaled, v_ref[:, cols])
+        s_ref[j, DH:, :] = _pad_rows(col[col.shape[0] - 1 :, :])
 
 
 def _tile_decays(col, row):
@@ -212,10 +221,10 @@
             out_ref[a * size : (a + 1) * size, cols] = total
 
 
-def norm_kernel(q_ref, g_ref, intra_ref, st_ref, cum_ref, cumt_ref, gain_ref, og_ref, m_ref, gp_ref):
+def norm_kernel(q_ref, g_ref, intra_ref, st_ref, cum_ref, cumt_ref, gain_ref, og_ref, m_ref):
     for j in range(HB):
         cols = _lanes(j)
-        _, _, grow, _ = _head_vectors(cum_ref, cumt_ref, j)
+        col, _, grow, _ = _head_vectors(cum_ref, cumt_ref, j)
         q = q_ref[:, cols]
         attended = intra_ref[:, cols] + grow * _nn(q, st_ref[j])
         width = attended.shape[-1]
@@ -228,9 +237,9 @@
             jnp.bfloat16
         )
         og_ref[:, cols] = out_grad
-        gp_ref[j] = jnp.sum(grad_f * normed, axis=0, keepdims=True)
         q_scaled = (q.astype(jnp.float32) * grow).astype(jnp.bfloat16)
-        m_ref[j] = _tn(q_scaled, out_grad)
+        m_ref[j, :DH, :] = _tn(q_scaled, out_grad)
+        m_ref[j, DH:, :] = _pad_rows(col[col.shape[0] - 1 :, :], jnp.sum(grad_f * normed, axis=0, keepdims=True))
 
 
 def grads_kernel(first, hb, q_ref, k_ref, v_ref, og_ref, cum_ref, cumt_ref, st_ref, qg_ref, kg_ref, vg_ref):
@@ -287,12 +296,15 @@
             return pl.BlockSpec((heads, length), lambda i: (0, 0))
         if kind == "gain":
             return pl.BlockSpec((hb, 1, DH), lambda i: (i + first, 0, 0))
+        if kind == "message":
+            return pl.BlockSpec((hb, DH + PAD, DH), lambda i: (i + first, 0, 0))
         return pl.BlockSpec((hb, DH, DH), lambda i: (i + first, 0, 0))
 
     shapes = {
         "rows": (length, heads * DH),
         "gain": (heads, 1, DH),
         "square": (heads, DH, DH),
+        "message": (heads, DH + PAD, DH),
     }
     out_shape = [jax.ShapeDtypeStruct(shapes[kind], dtype) for kind, dtype in outs]
     in_specs = [spec(kind) for kind, _ in ins]
@@ -342,7 +354,7 @@
     (local_state,) = _per_head(
         local_state_kernel,
         [("rows", k), ("rows", v), ("cum", cum), ("cumt", cum_t)],
-        [("square", f32)],
+        [("message", f32)],
         heads, length, small, 2 * rows_bytes,
     )
     def intra_piece(part, done, anchor):
@@ -359,10 +371,10 @@
         local_state, final_log, [functools.partial(intra_piece, p) for p in range(groups)]
     )
     state_low = state_in.astype(bf16)
-    out_grad, moment, gain_part = _per_head(
+    out_grad, moment = _per_head(
         norm_kernel,
         [("rows", q), ("rows", g), ("rows", intra), ("square", state_low), ("cum", cum), ("cumt", cum_t), ("gain", gain_rows)],
-        [("rows", bf16), ("square", f32), ("gain", f32)],
+        [("rows", bf16), ("message", f32)],
         heads, length, 2 * small, 5 * rows_bytes,
     )
     def grads_piece(part, done, anchor):
@@ -376,7 +388,7 @@
         )
 
     grad_state, gain_sum, (query_grad, key_part, value_part) = backward_states(
-        moment, final_log, gain_part.reshape(heads * DH), [functools.partial(grads_piece, p) for p in range(groups)]
+        moment, final_log, [functools.partial(grads_piece, p) for p in range(groups)]
     )
     grad_low = grad_state.astype(bf16)
     key_grad, value_grad = _per_head(

time: 131 us -> 128 us (0.977)
  other arithmetic: 18.8 us -> 16.4 us
    concatenate x2 -> x0, other arithmetic: 2.92 us -> none  [pack_rows(): return jnp.concatenate([core] + pad + [fill], axis=1)]
    select_n x1, other arithmetic: 0.19 us -> 1.52 us  [forward_states(): first = jnp.where(c == 0, own_state, other_state)]
  transfers between devices with their start and end apart: 14 -> 14, of which waited for: 8 -> 8; matrix products, arithmetic and copies ran while one was open for 4% -> 4% of each run, Pallas kernels for 31% -> 32%
where the time goes in v14:
time: 128 us; the launch traced here: 127 us
  Pallas kernels  64.1 us (50%)
  starting transfers between devices  30.3 us (24%)
  other arithmetic  16.4 us (13%)
  waiting for transfers between devices  11.7 us (9%)
  local copies, waits for them, and re-layouts  3.24 us (3%)
    pallas_call x11, Pallas kernels, _per_head(): pl.pallas_call(body, grid=(count,), in_specs=in_specs, out_specs=[spec(ki...  64.1 us
    ppermute x8, starting transfers between devices, chain_scan(): arrived = lax.ppermute(outgoing, 'ctx', perm=perm)  22.8 us
    ppermute x4, waiting for transfers between devices, swap_dp(): return lax.ppermute(x, 'dp', perm=[(0, 1), (1, 0)])  7.01 us
    ppermute x2, starting transfers between devices, gain_step(): return (both[0], both[1] + lax.ppermute(both[1], 'ctx', perm=partners))  6.76 us
    scatter x8, other arithmetic, chain_scan(): prefix = prefix.at[slot].set(jnp.where(valid, arrived, prefix[slot]))  5.2 us
    ppermute x8, waiting for transfers between devices, chain_scan(): arrived = lax.ppermute(outgoing, 'ctx', perm=perm)  4.66 us
    another operation x4, other arithmetic  2.88 us
  transfers between devices with their start and end apart: 14, of which 8 were waited for; matrix products, arithmetic and copies ran while one was open for 4% of the time, Pallas kernels for 32%

profile of v14, /device:TPU:0, one launch (start us, length us, event | category | flops | bytes accessed | tf_op | source)
XLA Modules:
  0.0 127.2 jit_solution(14262995481639841200)
XLA Ops:
  2.7 5.8 %shard_map.93 = f32[16,136,128]{2,1,0:T(8,128)} custom-call(bf16[512,2048]{1,0:T(8,128)(2,1)} %k_ref.7, bf16[512,2048]{1,0:T(8,128)(2,1)} %v_ref.7, f32[512,16]{1,0:T(8,128)} %copy.37.cum_ref.refs_3_.refs_4_, f32[16,512]{1,0:T(8,128)} %bitcast.136), custom_call_target="tpu_custom_call" | custom-call | flops 268435456 | bytes 4194304 | tf_op jit(solution)/shard_map/pallas_call | solution.py:324
  9.9 1.7 %collective-permute-done = f32[16,136,128]{2,1,0:T(8,128)S(1)} collective-permute-done((f32[16,136,128]{2,1,0:T(8,128)}, f32[16,136,128]{2,1,0:T(8,128)S(1)}, u32[]{:S(2)}, u32[]{:S(2)}) %collective-permute-start) | collective-permute-done | bytes 1114144 | tf_op jit(solution)/shard_map/ppermute | solution.py:21
  12.1 1.5 %broadcast_select_fusion.1 = (f32[16,128,128]{2,1,0:T(8,128)S(1)}, f32[16,128,128]{2,1,0:T(8,128)S(1)}, f32[16,128,128]{2,1,0:T(8,128)S(1)}) fusion(pred[]{:T(512)S(6)} %eq.2, f32[16,136,128]{2,1,0:T(8,128)S(1)} %collective-permute-done, f32[16,136,128]{2,1,0:T(8,128)} %shard_map.93), kind=kLoop, calls=%fused_computation.13 | loop fusion | flops 262144 | bytes 5242881 | tf_op jit(solution)/shard_map/jit(_where)/select_n | solution.py:80
  13.8 4.9 %collective-permute-start.1 = (f32[4,128,128]{2,1,0:T(8,128)S(1)}, f32[4,128,128]{2,1,0:T(8,128)S(1)}, u32[]{:S(2)}, u32[]{:S(2)}) collective-permute-start(f32[4,128,128]{2,1,0:T(8,128)S(1)} %bitcast_add_fusion.7), channel_id=1, source_target_pairs={{0,4},{4,8},{8,12},{1,5},{5,9},{9,13},{2,6},{6,10},{10,14},{3,7},{... | collective-permute-start | bytes 786440 | tf_op jit(solution)/shard_map/ppermute | solution.py:62
  19.5 3.9 %shard_map.94.refs_5_ = f32[512,2048]{1,0:T(8,128)} custom-call(bf16[512,2048]{1,0:T(8,128)(2,1)} %refs_0_.8, bf16[512,2048]{1,0:T(8,128)(2,1)} %k_ref.7, bf16[512,2048]{1,0:T(8,128)(2,1)} %v_ref.7, f32[512,16]{1,0:T(8,128)} %copy.37.cum_ref.refs_3_.refs_4_, f32[16,512]{1,0:T(8,128)} %bitcast.137), custom_call_target="tpu_custom_call" | custom-call | flops 536870912 | bytes 2621440 | tf_op jit(solution)/shard_map/pallas_call | solution.py:324
  25.3 4.4 %collective-permute-start.2 = (f32[4,128,128]{2,1,0:T(8,128)S(1)}, f32[4,128,128]{2,1,0:T(8,128)S(1)}, u32[]{:S(2)}, u32[]{:S(2)}) collective-permute-start(f32[4,128,128]{2,1,0:T(8,128)S(1)} %bitcast_add_fusion.6), channel_id=1, source_target_pairs={{0,4},{4,8},{8,12},{1,5},{5,9},{9,13},{2,6},{6,10},{10,14},{3,7},{... | collective-permute-start | bytes 786440 | tf_op jit(solution)/shard_map/ppermute | solution.py:62
  29.8 4.0 %shard_map.95.refs_5_ = f32[512,2048]{1,0:T(8,128)} custom-call(bf16[512,2048]{1,0:T(8,128)(2,1)} %refs_0_.8, bf16[512,2048]{1,0:T(8,128)(2,1)} %k_ref.7, bf16[512,2048]{1,0:T(8,128)(2,1)} %v_ref.7, f32[512,16]{1,0:T(8,128)} %copy.37.cum_ref.refs_3_.refs_4_, f32[16,512]{1,0:T(8,128)} %bitcast.138, ...), custom_call_target="tpu_custom_call", output_to_operand_aliasing={{}: (5, {})} | custom-call | flops 536870912 | bytes 2621440 | tf_op jit(solution)/shard_map/pallas_call | solution.py:324
  35.5 4.4 %collective-permute-start.3 = (f32[4,128,128]{2,1,0:T(8,128)S(1)}, f32[4,128,128]{2,1,0:T(8,128)S(1)}, u32[]{:S(2)}, u32[]{:S(2)}) collective-permute-start(f32[4,128,128]{2,1,0:T(8,128)S(1)} %bitcast_add_fusion.5), channel_id=1, source_target_pairs={{0,4},{4,8},{8,12},{1,5},{5,9},{9,13},{2,6},{6,10},{10,14},{3,7},{... | collective-permute-start | bytes 786440 | tf_op jit(solution)/shard_map/ppermute | solution.py:62
  40.7 3.9 %shard_map.96.refs_5_ = f32[512,2048]{1,0:T(8,128)} custom-call(bf16[512,2048]{1,0:T(8,128)(2,1)} %refs_0_.8, bf16[512,2048]{1,0:T(8,128)(2,1)} %k_ref.7, bf16[512,2048]{1,0:T(8,128)(2,1)} %v_ref.7, f32[512,16]{1,0:T(8,128)} %copy.37.cum_ref.refs_3_.refs_4_, f32[16,512]{1,0:T(8,128)} %bitcast.139, ...), custom_call_target="tpu_custom_call", output_to_operand_aliasing={{}: (5, {})} | custom-call | flops 536870912 | bytes 2621440 | tf_op jit(solution)/shard_map/pallas_call | solution.py:324
  45.4 3.8 %collective-permute-start.4 = (f32[4,128,128]{2,1,0:T(8,128)S(1)}, f32[4,128,128]{2,1,0:T(8,128)S(1)}, u32[]{:S(2)}, u32[]{:S(2)}) collective-permute-start(f32[4,128,128]{2,1,0:T(8,128)S(1)} %bitcast_add_fusion.4), channel_id=1, source_target_pairs={{0,4},{4,8},{8,12},{1,5},{5,9},{9,13},{2,6},{6,10},{10,14},{3,7},{... | collective-permute-start | bytes 786440 | tf_op jit(solution)/shard_map/ppermute | solution.py:62
  49.2 4.0 %shard_map.97.intra_ref = f32[512,2048]{1,0:T(8,128)} custom-call(bf16[512,2048]{1,0:T(8,128)(2,1)} %refs_0_.8, bf16[512,2048]{1,0:T(8,128)(2,1)} %k_ref.7, bf16[512,2048]{1,0:T(8,128)(2,1)} %v_ref.7, f32[512,16]{1,0:T(8,128)} %copy.37.cum_ref.refs_3_.refs_4_, f32[16,512]{1,0:T(8,128)} %bitcast.140, ...), custom_call_target="tpu_custom_call", output_to_operand_aliasing={{}: (5, {})} | custom-call | flops 536870912 | bytes 2621440 | tf_op jit(solution)/shard_map/pallas_call | solution.py:324
  54.0 1.9 %collective-permute-done.5 = f32[8,128,128]{2,1,0:T(8,128)S(1)} collective-permute-done((f32[8,128,128]{2,1,0:T(8,128)S(1)}, f32[8,128,128]{2,1,0:T(8,128)S(1)}, u32[]{:S(2)}, u32[]{:S(2)}) %collective-permute-start.5) | collective-permute-done | bytes 524320 | tf_op jit(solution)/shard_map/ppermute | solution.py:21
  57.0 9.4 %shard_map.98 = (bf16[512,2048]{1,0:T(8,128)(2,1)}, f32[16,136,128]{2,1,0:T(8,128)}) custom-call(bf16[512,2048]{1,0:T(8,128)(2,1)} %refs_0_.8, bf16[512,2048]{1,0:T(8,128)(2,1)} %g_ref.1, f32[512,2048]{1,0:T(8,128)} %shard_map.97.intra_ref, bf16[16,128,128]{2,1,0:T(8,128)(2,1)} %select_convert_fusion.1.st_ref.refs_6_, ...), custom_call_target="tpu_custom_call" | custom-call | flops 536870912 | bytes 10485760 | tf_op jit(solution)/shard_map/pallas_call | solution.py:324
  67.3 2.1 %collective-permute-done.6 = f32[16,136,128]{2,1,0:T(8,128)S(1)} collective-permute-done((f32[16,136,128]{2,1,0:T(8,128)}, f32[16,136,128]{2,1,0:T(8,128)S(1)}, u32[]{:S(2)}, u32[]{:S(2)}) %collective-permute-start.6) | collective-permute-done | bytes 1114144 | tf_op jit(solution)/shard_map/ppermute | solution.py:21
  69.9 1.5 %fusion.29 = (f32[16,128,128]{2,1,0:T(8,128)S(1)}, f32[16,128,128]{2,1,0:T(8,128)S(1)}, f32[16,128,128]{2,1,0:T(8,128)S(1)}) fusion(f32[16,136,128]{2,1,0:T(8,128)} %get-tuple-element.165, f32[16,136,128]{2,1,0:T(8,128)S(1)} %collective-permute-done.6, pred[]{:T(512)S(6)} %eq.2), kind=kLoop, calls=%fused_computation.133 | loop fusion | flops 262144 | bytes 5242881 | tf_op jit(solution)/shard_map/slice | solution.py:95
  73.8 3.0 %collective-permute-start.7 = (f32[16,128]{1,0:T(8,128)S(1)}, f32[16,128]{1,0:T(8,128)S(1)}, u32[]{:S(2)}, u32[]{:S(2)}) collective-permute-start(f32[16,128]{1,0:T(8,128)S(1)} %bitcast.157), channel_id=1, source_target_pairs={{0,4},{4,0},{8,12},{12,8},{1,5},{5,1},{9,13},{13,9},{2,6},{6,2},{1... | collective-permute-start | bytes 24584 | tf_op jit(solution)/shard_map/ppermute | solution.py:117
  76.8 6.2 %shard_map.99 = (bf16[512,2048]{1,0:T(8,128)(2,1)}, f32[512,2048]{1,0:T(8,128)}, f32[512,2048]{1,0:T(8,128)}) custom-call(bf16[512,2048]{1,0:T(8,128)(2,1)} %refs_0_.8, bf16[512,2048]{1,0:T(8,128)(2,1)} %k_ref.7, bf16[512,2048]{1,0:T(8,128)(2,1)} %v_ref.7, bf16[512,2048]{1,0:T(8,128)(2,1)} %get-tuple-element.189.og_ref.refs_3_, ...), custom_call_target="tpu_custom_call" | custom-call | flops 1409286144 | bytes 4718592 | tf_op jit(solution)/shard_map/pallas_call | solution.py:324
  83.8 1.5 %collective-permute-start.10 = (f32[4,128,128]{2,1,0:T(8,128)S(1)}, f32[4,128,128]{2,1,0:T(8,128)S(1)}, u32[]{:S(2)}, u32[]{:S(2)}) collective-permute-start(f32[4,128,128]{2,1,0:T(8,128)S(1)} %bitcast_add_fusion.2), channel_id=1, source_target_pairs={{4,0},{8,4},{12,8},{5,1},{9,5},{13,9},{6,2},{10,6},{14,10},{7,3},{... | collective-permute-start | bytes 786440 | tf_op jit(solution)/shard_map/ppermute | solution.py:62
  85.3 3.7 %collective-permute-start.9 = (f32[16,128]{1,0:T(8,128)S(1)}, f32[16,128]{1,0:T(8,128)S(1)}, u32[]{:S(2)}, u32[]{:S(2)}) collective-permute-start(f32[16,128]{1,0:T(8,128)S(1)} %add.145), channel_id=1, source_target_pairs={{0,8},{4,12},{8,0},{12,4},{1,9},{5,13},{9,1},{13,5},{2,10},{6,14},... | collective-permute-start | bytes 24584 | tf_op jit(solution)/shard_map/ppermute | solution.py:117
  89.0 6.2 %shard_map.100 = (bf16[512,2048]{1,0:T(8,128)(2,1)}, f32[512,2048]{1,0:T(8,128)}, f32[512,2048]{1,0:T(8,128)}) custom-call(bf16[512,2048]{1,0:T(8,128)(2,1)} %refs_0_.8, bf16[512,2048]{1,0:T(8,128)(2,1)} %k_ref.7, bf16[512,2048]{1,0:T(8,128)(2,1)} %v_ref.7, ...), custom_call_target="tpu_custom_call", output_to_operand_aliasing={{0}: (7, {}), {1}: (8, {}), {2}: (9, {})} | custom-call | flops 1409286144 | bytes 4718592 | tf_op jit(solution)/shard_map/pallas_call | solution.py:324
  98.0 6.2 %shard_map.101 = (bf16[512,2048]{1,0:T(8,128)(2,1)}, f32[512,2048]{1,0:T(8,128)}, f32[512,2048]{1,0:T(8,128)}) custom-call(bf16[512,2048]{1,0:T(8,128)(2,1)} %refs_0_.8, bf16[512,2048]{1,0:T(8,128)(2,1)} %k_ref.7, bf16[512,2048]{1,0:T(8,128)(2,1)} %v_ref.7, ...), custom_call_target="tpu_custom_call", output_to_operand_aliasing={{0}: (7, {}), {1}: (8, {}), {2}: (9, {})} | custom-call | flops 1409286144 | bytes 4718592 | tf_op jit(solution)/shard_map/pallas_call | solution.py:324
  107.4 6.2 %shard_map.102 = (bf16[512,2048]{1,0:T(8,128)(2,1)}, f32[512,2048]{1,0:T(8,128)}, f32[512,2048]{1,0:T(8,128)}) custom-call(bf16[512,2048]{1,0:T(8,128)(2,1)} %refs_0_.8, bf16[512,2048]{1,0:T(8,128)(2,1)} %k_ref.7, bf16[512,2048]{1,0:T(8,128)(2,1)} %v_ref.7, ...), custom_call_target="tpu_custom_call", output_to_operand_aliasing={{0}: (7, {}), {1}: (8, {}), {2}: (9, {})} | custom-call | flops 1409286144 | bytes 4718592 | tf_op jit(solution)/shard_map/pallas_call | solution.py:324
  113.6 1.3 %collective-permute-done.12 = f32[4,128,128]{2,1,0:T(8,128)S(1)} collective-permute-done((f32[4,128,128]{2,1,0:T(8,128)S(1)}, f32[4,128,128]{2,1,0:T(8,128)S(1)}, u32[]{:S(2)}, u32[]{:S(2)}) %collective-permute-start.12) | collective-permute-done | bytes 262176 | tf_op jit(solution)/shard_map/ppermute | solution.py:62
  118.8 8.4 %shard_map.103 = (bf16[512,2048]{1,0:T(8,128)(2,1)}, bf16[512,2048]{1,0:T(8,128)(2,1)}) custom-call(bf16[512,2048]{1,0:T(8,128)(2,1)} %k_ref.7, bf16[512,2048]{1,0:T(8,128)(2,1)} %v_ref.7, f32[512,2048]{1,0:T(8,128)} %get-tuple-element.198.kg_ref, f32[512,2048]{1,0:T(8,128)} %get-tuple-element.199.vg_ref, bf16[16,128,128]{2,1,0:T(8,128)(2,1)} %select_convert_fusion.gl_ref, ...), custom_call_target="tpu_custom_call" | custom-call | flops 536870912 | bytes 16777216 | tf_op jit(solution)/shard_map/pallas_call | solution.py:324
  (76 shorter events, 26.2 us)
Async XLA Ops:
  0.6 0.8 copy-start
  1.8 0.9 copy-start.1
  8.6 3.0 %collective-permute-start = (f32[16,136,128]{2,1,0:T(8,128)}, f32[16,136,128]{2,1,0:T(8,128)S(1)}, u32[]{:S(2)}, u32[]{:S(2)}) collective-permute-start(f32[16,136,128]{2,1,0:T(8,128)} %shard_map.93), channel_id=1, source_target_pairs={{0,1},{1,0},{2,3},{3,2},{4,5},{5,4},{6,7},{7,6},{8,9},{9,8},{10,11... | collective-permute-start | bytes 3342344 | tf_op jit(solution)/shard_map/ppermute | solution.py:21
  13.6 5.1 %copy-start.2 = (s32[4]{0:T(128)S(1)}, s32[4]{0:T(128)}, u32[]{:S(2)}) copy-start(s32[4]{0:T(128)} %constant.206.clone.1) | copy-start | bytes 52
  13.8 10.7 %collective-permute-start.1 = (f32[4,128,128]{2,1,0:T(8,128)S(1)}, f32[4,128,128]{2,1,0:T(8,128)S(1)}, u32[]{:S(2)}, u32[]{:S(2)}) collective-permute-start(f32[4,128,128]{2,1,0:T(8,128)S(1)} %bitcast_add_fusion.7), channel_id=1, source_target_pairs={{0,4},{4,8},{8,12},{1,5},{5,9},{9,13},{2,6},{6,10},{10,14},{3,7},{... | collective-permute-start | bytes 786440 | tf_op jit(solution)/shard_map/ppermute | solution.py:62
  25.3 9.4 %collective-permute-start.2 = (f32[4,128,128]{2,1,0:T(8,128)S(1)}, f32[4,128,128]{2,1,0:T(8,128)S(1)}, u32[]{:S(2)}, u32[]{:S(2)}) collective-permute-start(f32[4,128,128]{2,1,0:T(8,128)S(1)} %bitcast_add_fusion.6), channel_id=1, source_target_pairs={{0,4},{4,8},{8,12},{1,5},{5,9},{9,13},{2,6},{6,10},{10,14},{3,7},{... | collective-permute-start | bytes 786440 | tf_op jit(solution)/shard_map/ppermute | solution.py:62
  35.5 9.1 %collective-permute-start.3 = (f32[4,128,128]{2,1,0:T(8,128)S(1)}, f32[4,128,128]{2,1,0:T(8,128)S(1)}, u32[]{:S(2)}, u32[]{:S(2)}) collective-permute-start(f32[4,128,128]{2,1,0:T(8,128)S(1)} %bitcast_add_fusion.5), channel_id=1, source_target_pairs={{0,4},{4,8},{8,12},{1,5},{5,9},{9,13},{2,6},{6,10},{10,14},{3,7},{... | collective-permute-start | bytes 786440 | tf_op jit(solution)/shard_map/ppermute | solution.py:62
  45.4 7.8 %collective-permute-start.4 = (f32[4,128,128]{2,1,0:T(8,128)S(1)}, f32[4,128,128]{2,1,0:T(8,128)S(1)}, u32[]{:S(2)}, u32[]{:S(2)}) collective-permute-start(f32[4,128,128]{2,1,0:T(8,128)S(1)} %bitcast_add_fusion.4), channel_id=1, source_target_pairs={{0,4},{4,8},{8,12},{1,5},{5,9},{9,13},{2,6},{6,10},{10,14},{3,7},{... | collective-permute-start | bytes 786440 | tf_op jit(solution)/shard_map/ppermute | solution.py:62
  53.9 2.0 %collective-permute-start.5 = (f32[8,128,128]{2,1,0:T(8,128)S(1)}, f32[8,128,128]{2,1,0:T(8,128)S(1)}, u32[]{:S(2)}, u32[]{:S(2)}) collective-permute-start(f32[8,128,128]{2,1,0:T(8,128)S(1)} %bitcast.135), channel_id=1, source_target_pairs={{0,1},{1,0},{2,3},{3,2},{4,5},{5,4},{6,7},{7,6},{8,9},{9,8},{10,11... | collective-permute-start | bytes 1572872 | tf_op jit(solution)/shard_map/ppermute | solution.py:21
  66.4 3.0 %collective-permute-start.6 = (f32[16,136,128]{2,1,0:T(8,128)}, f32[16,136,128]{2,1,0:T(8,128)S(1)}, u32[]{:S(2)}, u32[]{:S(2)}) collective-permute-start(f32[16,136,128]{2,1,0:T(8,128)} %get-tuple-element.165), channel_id=1, source_target_pairs={{0,1},{1,0},{2,3},{3,2},{4,5},{5,4},{6,7},{7,6},{8,9},{9,8},{10,11... | collective-permute-start | bytes 3342344 | tf_op jit(solution)/shard_map/ppermute | solution.py:21
  71.6 11.4 %collective-permute-start.8 = (f32[4,128,128]{2,1,0:T(8,128)S(1)}, f32[4,128,128]{2,1,0:T(8,128)S(1)}, u32[]{:S(2)}, u32[]{:S(2)}) collective-permute-start(f32[4,128,128]{2,1,0:T(8,128)S(1)} %bitcast_add_fusion.3), channel_id=1, source_target_pairs={{4,0},{8,4},{12,8},{5,1},{9,5},{13,9},{6,2},{10,6},{14,10},{7,3},{... | collective-permute-start | bytes 786440 | tf_op jit(solution)/shard_map/ppermute | solution.py:62
  73.8 9.2 %collective-permute-start.7 = (f32[16,128]{1,0:T(8,128)S(1)}, f32[16,128]{1,0:T(8,128)S(1)}, u32[]{:S(2)}, u32[]{:S(2)}) collective-permute-start(f32[16,128]{1,0:T(8,128)S(1)} %bitcast.157), channel_id=1, source_target_pairs={{0,4},{4,0},{8,12},{12,8},{1,5},{5,1},{9,13},{13,9},{2,6},{6,2},{1... | collective-permute-start | bytes 24584 | tf_op jit(solution)/shard_map/ppermute | solution.py:117
  83.8 11.5 %collective-permute-start.10 = (f32[4,128,128]{2,1,0:T(8,128)S(1)}, f32[4,128,128]{2,1,0:T(8,128)S(1)}, u32[]{:S(2)}, u32[]{:S(2)}) collective-permute-start(f32[4,128,128]{2,1,0:T(8,128)S(1)} %bitcast_add_fusion.2), channel_id=1, source_target_pairs={{4,0},{8,4},{12,8},{5,1},{9,5},{13,9},{6,2},{10,6},{14,10},{7,3},{... | collective-permute-start | bytes 786440 | tf_op jit(solution)/shard_map/ppermute | solution.py:62
  85.3 9.9 %collective-permute-start.9 = (f32[16,128]{1,0:T(8,128)S(1)}, f32[16,128]{1,0:T(8,128)S(1)}, u32[]{:S(2)}, u32[]{:S(2)}) collective-permute-start(f32[16,128]{1,0:T(8,128)S(1)} %add.145), channel_id=1, source_target_pairs={{0,8},{4,12},{8,0},{12,4},{1,9},{5,13},{9,1},{13,5},{2,10},{6,14},... | collective-permute-start | bytes 24584 | tf_op jit(solution)/shard_map/ppermute | solution.py:117
  96.0 9.4 %collective-permute-start.11 = (f32[4,128,128]{2,1,0:T(8,128)S(1)}, f32[4,128,128]{2,1,0:T(8,128)S(1)}, u32[]{:S(2)}, u32[]{:S(2)}) collective-permute-start(f32[4,128,128]{2,1,0:T(8,128)S(1)} %bitcast_add_fusion.1), channel_id=1, source_target_pairs={{4,0},{8,4},{12,8},{5,1},{9,5},{13,9},{6,2},{10,6},{14,10},{7,3},{... | collective-permute-start | bytes 786440 | tf_op jit(solution)/shard_map/ppermute | solution.py:62
  106.1 8.9 %collective-permute-start.12 = (f32[4,128,128]{2,1,0:T(8,128)S(1)}, f32[4,128,128]{2,1,0:T(8,128)S(1)}, u32[]{:S(2)}, u32[]{:S(2)}) collective-permute-start(f32[4,128,128]{2,1,0:T(8,128)S(1)} %bitcast_add_fusion), channel_id=1, source_target_pairs={{4,0},{8,4},{12,8},{5,1},{9,5},{13,9},{6,2},{10,6},{14,10},{7,3},{... | collective-permute-start | bytes 786440 | tf_op jit(solution)/shard_map/ppermute | solution.py:62
  115.6 2.0 %collective-permute-start.13 = (f32[8,128,128]{2,1,0:T(8,128)S(1)}, f32[8,128,128]{2,1,0:T(8,128)S(1)}, u32[]{:S(2)}, u32[]{:S(2)}) collective-permute-start(f32[8,128,128]{2,1,0:T(8,128)S(1)} %bitcast.134), channel_id=1, source_target_pairs={{0,1},{1,0},{2,3},{3,2},{4,5},{5,4},{6,7},{7,6},{8,9},{9,8},{10,11... | collective-permute-start | bytes 1572872 | tf_op jit(solution)/shard_map/ppermute | solution.py:21

commit v15 on v14

--- a/solution.py
+++ b/solution.py
@@ -186,10 +186,10 @@
     return block
 
 
-def local_state_kernel(k_ref, v_ref, cum_ref, cumt_ref, s_ref):
-    for j in range(HB):
+def local_state_kernel(hb, k_ref, v_ref, cum_ref, cumt_ref, s_ref):
+    for j in range(hb):
         cols = _lanes(j)
-        col, _, _, toend = _head_vectors(cum_ref, cumt_ref, j)
+        col, _, _, toend = _head_vectors(cum_ref, cumt_ref, j, 0, hb)
         scaled = (k_ref[:, cols].astype(jnp.float32) * toend).astype(jnp.bfloat16)
         s_ref[j, :DH, :] = _tn(scaled, v_ref[:, cols])
         s_ref[j, DH:, :] = _pad_rows(col[col.shape[0] - 1 :, :])
@@ -280,8 +280,11 @@
         vo_ref[:, cols] = (vg_ref[:, cols] + toend * _nn(k_ref[:, cols], grad_low)).astype(jnp.bfloat16)
 
 
-def _per_head(kernel, ins, outs, heads, length, flops, nbytes, exps=0, part=None, into=None):
+def _per_head(kernel, ins, outs, heads, length, flops, nbytes, exps=0, part=None, into=None, wide=False):
     hb = HB if part is None else HB // PIECE_STEPS
+    if wide:
+        hb = min(2 * HB, heads)
+        kernel = functools.partial(kernel, hb)
     groups = heads // hb
     first, count = (0, groups) if part is None else (part * PIECE_STEPS, PIECE_STEPS)
     if part is not None:
@@ -355,7 +358,7 @@
         local_state_kernel,
         [("rows", k), ("rows", v), ("cum", cum), ("cumt", cum_t)],
         [("message", f32)],
-        heads, length, small, 2 * rows_bytes,
+        heads, length, small, 2 * rows_bytes, wide=True,
     )
     def intra_piece(part, done, anchor):
         q_tied, _ = lax.optimization_barrier((q, anchor))

time: 128 us -> 127 us (level)
  no operation moved by 1% of the time
where the time goes in v15:
time: 127 us; the launch traced here: 126 us
  Pallas kernels  63.1 us (50%)
  starting transfers between devices  30.3 us (24%)
  other arithmetic  16.4 us (13%)
  waiting for transfers between devices  11.7 us (9%)
  local copies, waits for them, and re-layouts  3.24 us (3%)
    pallas_call x11, Pallas kernels, _per_head(): pl.pallas_call(body, grid=(count,), in_specs=in_specs, out_specs=[spec(ki...  63.1 us
    ppermute x8, starting transfers between devices, chain_scan(): arrived = lax.ppermute(outgoing, 'ctx', perm=perm)  22.8 us
    ppermute x4, waiting for transfers between devices, swap_dp(): return lax.ppermute(x, 'dp', perm=[(0, 1), (1, 0)])  7.01 us
    ppermute x2, starting transfers between devices, gain_step(): return (both[0], both[1] + lax.ppermute(both[1], 'ctx', perm=partners))  6.75 us
    scatter x8, other arithmetic, chain_scan(): prefix = prefix.at[slot].set(jnp.where(valid, arrived, prefix[slot]))  5.2 us
    ppermute x8, waiting for transfers between devices, chain_scan(): arrived = lax.ppermute(outgoing, 'ctx', perm=perm)  4.65 us
    another operation x4, other arithmetic  2.88 us
  transfers between devices with their start and end apart: 14, of which 8 were waited for; matrix products, arithmetic and copies ran while one was open for 4% of the time, Pallas kernels for 32%

profile of v15, /device:TPU:0, one launch (start us, length us, event | category | flops | bytes accessed | tf_op | source)
XLA Modules:
  0.0 126.2 jit_solution(13487074392287787992)
XLA Ops:
  2.7 4.8 %shard_map.93 = f32[16,136,128]{2,1,0:T(8,128)} custom-call(bf16[512,2048]{1,0:T(8,128)(2,1)} %k_ref.7, bf16[512,2048]{1,0:T(8,128)(2,1)} %v_ref.7, f32[512,16]{1,0:T(8,128)} %copy.37.cum_ref.refs_3_.refs_4_, f32[16,512]{1,0:T(8,128)} %bitcast.136), custom_call_target="tpu_custom_call" | custom-call | flops 268435456 | bytes 4194304 | tf_op jit(solution)/shard_map/pallas_call | solution.py:327
  8.8 1.7 %collective-permute-done = f32[16,136,128]{2,1,0:T(8,128)S(1)} collective-permute-done((f32[16,136,128]{2,1,0:T(8,128)}, f32[16,136,128]{2,1,0:T(8,128)S(1)}, u32[]{:S(2)}, u32[]{:S(2)}) %collective-permute-start) | collective-permute-done | bytes 1114144 | tf_op jit(solution)/shard_map/ppermute | solution.py:21
  11.0 1.5 %broadcast_select_fusion.1 = (f32[16,128,128]{2,1,0:T(8,128)S(1)}, f32[16,128,128]{2,1,0:T(8,128)S(1)}, f32[16,128,128]{2,1,0:T(8,128)S(1)}) fusion(pred[]{:T(512)S(6)} %eq.2, f32[16,136,128]{2,1,0:T(8,128)S(1)} %collective-permute-done, f32[16,136,128]{2,1,0:T(8,128)} %shard_map.93), kind=kLoop, calls=%fused_computation.13 | loop fusion | flops 262144 | bytes 5242881 | tf_op jit(solution)/shard_map/jit(_where)/select_n | solution.py:80
  12.8 4.9 %collective-permute-start.1 = (f32[4,128,128]{2,1,0:T(8,128)S(1)}, f32[4,128,128]{2,1,0:T(8,128)S(1)}, u32[]{:S(2)}, u32[]{:S(2)}) collective-permute-start(f32[4,128,128]{2,1,0:T(8,128)S(1)} %bitcast_add_fusion.7), channel_id=1, source_target_pairs={{0,4},{4,8},{8,12},{1,5},{5,9},{9,13},{2,6},{6,10},{10,14},{3,7},{... | collective-permute-start | bytes 786440 | tf_op jit(solution)/shard_map/ppermute | solution.py:62
  18.4 3.9 %shard_map.94.refs_5_ = f32[512,2048]{1,0:T(8,128)} custom-call(bf16[512,2048]{1,0:T(8,128)(2,1)} %refs_0_.8, bf16[512,2048]{1,0:T(8,128)(2,1)} %k_ref.7, bf16[512,2048]{1,0:T(8,128)(2,1)} %v_ref.7, f32[512,16]{1,0:T(8,128)} %copy.37.cum_ref.refs_3_.refs_4_, f32[16,512]{1,0:T(8,128)} %bitcast.137), custom_call_target="tpu_custom_call" | custom-call | flops 536870912 | bytes 2621440 | tf_op jit(solution)/shard_map/pallas_call | solution.py:327
  24.3 4.4 %collective-permute-start.2 = (f32[4,128,128]{2,1,0:T(8,128)S(1)}, f32[4,128,128]{2,1,0:T(8,128)S(1)}, u32[]{:S(2)}, u32[]{:S(2)}) collective-permute-start(f32[4,128,128]{2,1,0:T(8,128)S(1)} %bitcast_add_fusion.6), channel_id=1, source_target_pairs={{0,4},{4,8},{8,12},{1,5},{5,9},{9,13},{2,6},{6,10},{10,14},{3,7},{... | collective-permute-start | bytes 786440 | tf_op jit(solution)/shard_map/ppermute | solution.py:62
  28.7 4.0 %shard_map.95.refs_5_ = f32[512,2048]{1,0:T(8,128)} custom-call(bf16[512,2048]{1,0:T(8,128)(2,1)} %refs_0_.8, bf16[512,2048]{1,0:T(8,128)(2,1)} %k_ref.7, bf16[512,2048]{1,0:T(8,128)(2,1)} %v_ref.7, f32[512,16]{1,0:T(8,128)} %copy.37.cum_ref.refs_3_.refs_4_, f32[16,512]{1,0:T(8,128)} %bitcast.138, ...), custom_call_target="tpu_custom_call", output_to_operand_aliasing={{}: (5, {})} | custom-call | flops 536870912 | bytes 2621440 | tf_op jit(solution)/shard_map/pallas_call | solution.py:327
  34.5 4.4 %collective-permute-start.3 = (f32[4,128,128]{2,1,0:T(8,128)S(1)}, f32[4,128,128]{2,1,0:T(8,128)S(1)}, u32[]{:S(2)}, u32[]{:S(2)}) collective-permute-start(f32[4,128,128]{2,1,0:T(8,128)S(1)} %bitcast_add_fusion.5), channel_id=1, source_target_pairs={{0,4},{4,8},{8,12},{1,5},{5,9},{9,13},{2,6},{6,10},{10,14},{3,7},{... | collective-permute-start | bytes 786440 | tf_op jit(solution)/shard_map/ppermute | solution.py:62
  39.6 3.9 %shard_map.96.refs_5_ = f32[512,2048]{1,0:T(8,128)} custom-call(bf16[512,2048]{1,0:T(8,128)(2,1)} %refs_0_.8, bf16[512,2048]{1,0:T(8,128)(2,1)} %k_ref.7, bf16[512,2048]{1,0:T(8,128)(2,1)} %v_ref.7, f32[512,16]{1,0:T(8,128)} %copy.37.cum_ref.refs_3_.refs_4_, f32[16,512]{1,0:T(8,128)} %bitcast.139, ...), custom_call_target="tpu_custom_call", output_to_operand_aliasing={{}: (5, {})} | custom-call | flops 536870912 | bytes 2621440 | tf_op jit(solution)/shard_map/pallas_call | solution.py:327
  44.3 3.8 %collective-permute-start.4 = (f32[4,128,128]{2,1,0:T(8,128)S(1)}, f32[4,128,128]{2,1,0:T(8,128)S(1)}, u32[]{:S(2)}, u32[]{:S(2)}) collective-permute-start(f32[4,128,128]{2,1,0:T(8,128)S(1)} %bitcast_add_fusion.4), channel_id=1, source_target_pairs={{0,4},{4,8},{8,12},{1,5},{5,9},{9,13},{2,6},{6,10},{10,14},{3,7},{... | collective-permute-start | bytes 786440 | tf_op jit(solution)/shard_map/ppermute | solution.py:62
  48.2 4.0 %shard_map.97.intra_ref = f32[512,2048]{1,0:T(8,128)} custom-call(bf16[512,2048]{1,0:T(8,128)(2,1)} %refs_0_.8, bf16[512,2048]{1,0:T(8,128)(2,1)} %k_ref.7, bf16[512,2048]{1,0:T(8,128)(2,1)} %v_ref.7, f32[512,16]{1,0:T(8,128)} %copy.37.cum_ref.refs_3_.refs_4_, f32[16,512]{1,0:T(8,128)} %bitcast.140, ...), custom_call_target="tpu_custom_call", output_to_operand_aliasing={{}: (5, {})} | custom-call | flops 536870912 | bytes 2621440 | tf_op jit(solution)/shard_map/pallas_call | solution.py:327
  52.9 1.9 %collective-permute-done.5 = f32[8,128,128]{2,1,0:T(8,128)S(1)} collective-permute-done((f32[8,128,128]{2,1,0:T(8,128)S(1)}, f32[8,128,128]{2,1,0:T(8,128)S(1)}, u32[]{:S(2)}, u32[]{:S(2)}) %collective-permute-start.5) | collective-permute-done | bytes 524320 | tf_op jit(solution)/shard_map/ppermute | solution.py:21
  56.0 9.4 %shard_map.98 = (bf16[512,2048]{1,0:T(8,128)(2,1)}, f32[16,136,128]{2,1,0:T(8,128)}) custom-call(bf16[512,2048]{1,0:T(8,128)(2,1)} %refs_0_.8, bf16[512,2048]{1,0:T(8,128)(2,1)} %g_ref.1, f32[512,2048]{1,0:T(8,128)} %shard_map.97.intra_ref, bf16[16,128,128]{2,1,0:T(8,128)(2,1)} %select_convert_fusion.1.st_ref.refs_6_, ...), custom_call_target="tpu_custom_call" | custom-call | flops 536870912 | bytes 10485760 | tf_op jit(solution)/shard_map/pallas_call | solution.py:327
  66.2 2.1 %collective-permute-done.6 = f32[16,136,128]{2,1,0:T(8,128)S(1)} collective-permute-done((f32[16,136,128]{2,1,0:T(8,128)}, f32[16,136,128]{2,1,0:T(8,128)S(1)}, u32[]{:S(2)}, u32[]{:S(2)}) %collective-permute-start.6) | collective-permute-done | bytes 1114144 | tf_op jit(solution)/shard_map/ppermute | solution.py:21
  68.8 1.5 %fusion.29 = (f32[16,128,128]{2,1,0:T(8,128)S(1)}, f32[16,128,128]{2,1,0:T(8,128)S(1)}, f32[16,128,128]{2,1,0:T(8,128)S(1)}) fusion(f32[16,136,128]{2,1,0:T(8,128)} %get-tuple-element.165, f32[16,136,128]{2,1,0:T(8,128)S(1)} %collective-permute-done.6, pred[]{:T(512)S(6)} %eq.2), kind=kLoop, calls=%fused_computation.133 | loop fusion | flops 262144 | bytes 5242881 | tf_op jit(solution)/shard_map/slice | solution.py:95
  72.7 3.0 %collective-permute-start.7 = (f32[16,128]{1,0:T(8,128)S(1)}, f32[16,128]{1,0:T(8,128)S(1)}, u32[]{:S(2)}, u32[]{:S(2)}) collective-permute-start(f32[16,128]{1,0:T(8,128)S(1)} %bitcast.157), channel_id=1, source_target_pairs={{0,4},{4,0},{8,12},{12,8},{1,5},{5,1},{9,13},{13,9},{2,6},{6,2},{1... | collective-permute-start | bytes 24584 | tf_op jit(solution)/shard_map/ppermute | solution.py:117
  75.7 6.2 %shard_map.99 = (bf16[512,2048]{1,0:T(8,128)(2,1)}, f32[512,2048]{1,0:T(8,128)}, f32[512,2048]{1,0:T(8,128)}) custom-call(bf16[512,2048]{1,0:T(8,128)(2,1)} %refs_0_.8, bf16[512,2048]{1,0:T(8,128)(2,1)} %k_ref.7, bf16[512,2048]{1,0:T(8,128)(2,1)} %v_ref.7, bf16[512,2048]{1,0:T(8,128)(2,1)} %get-tuple-element.189.og_ref.refs_3_, ...), custom_call_target="tpu_custom_call" | custom-call | flops 1409286144 | bytes 4718592 | tf_op jit(solution)/shard_map/pallas_call | solution.py:327
  82.7 1.5 %collective-permute-start.10 = (f32[4,128,128]{2,1,0:T(8,128)S(1)}, f32[4,128,128]{2,1,0:T(8,128)S(1)}, u32[]{:S(2)}, u32[]{:S(2)}) collective-permute-start(f32[4,128,128]{2,1,0:T(8,128)S(1)} %bitcast_add_fusion.2), channel_id=1, source_target_pairs={{4,0},{8,4},{12,8},{5,1},{9,5},{13,9},{6,2},{10,6},{14,10},{7,3},{... | collective-permute-start | bytes 786440 | tf_op jit(solution)/shard_map/ppermute | solution.py:62
  84.2 3.7 %collective-permute-start.9 = (f32[16,128]{1,0:T(8,128)S(1)}, f32[16,128]{1,0:T(8,128)S(1)}, u32[]{:S(2)}, u32[]{:S(2)}) collective-permute-start(f32[16,128]{1,0:T(8,128)S(1)} %add.145), channel_id=1, source_target_pairs={{0,8},{4,12},{8,0},{12,4},{1,9},{5,13},{9,1},{13,5},{2,10},{6,14},... | collective-permute-start | bytes 24584 | tf_op jit(solution)/shard_map/ppermute | solution.py:117
  87.9 6.2 %shard_map.100 = (bf16[512,2048]{1,0:T(8,128)(2,1)}, f32[512,2048]{1,0:T(8,128)}, f32[512,2048]{1,0:T(8,128)}) custom-call(bf16[512,2048]{1,0:T(8,128)(2,1)} %refs_0_.8, bf16[512,2048]{1,0:T(8,128)(2,1)} %k_ref.7, bf16[512,2048]{1,0:T(8,128)(2,1)} %v_ref.7, ...), custom_call_target="tpu_custom_call", output_to_operand_aliasing={{0}: (7, {}), {1}: (8, {}), {2}: (9, {})} | custom-call | flops 1409286144 | bytes 4718592 | tf_op jit(solution)/shard_map/pallas_call | solution.py:327
  96.9 6.2 %shard_map.101 = (bf16[512,2048]{1,0:T(8,128)(2,1)}, f32[512,2048]{1,0:T(8,128)}, f32[512,2048]{1,0:T(8,128)}) custom-call(bf16[512,2048]{1,0:T(8,128)(2,1)} %refs_0_.8, bf16[512,2048]{1,0:T(8,128)(2,1)} %k_ref.7, bf16[512,2048]{1,0:T(8,128)(2,1)} %v_ref.7, ...), custom_call_target="tpu_custom_call", output_to_operand_aliasing={{0}: (7, {}), {1}: (8, {}), {2}: (9, {})} | custom-call | flops 1409286144 | bytes 4718592 | tf_op jit(solution)/shard_map/pallas_call | solution.py:327
  106.4 6.2 %shard_map.102 = (bf16[512,2048]{1,0:T(8,128)(2,1)}, f32[512,2048]{1,0:T(8,128)}, f32[512,2048]{1,0:T(8,128)}) custom-call(bf16[512,2048]{1,0:T(8,128)(2,1)} %refs_0_.8, bf16[512,2048]{1,0:T(8,128)(2,1)} %k_ref.7, bf16[512,2048]{1,0:T(8,128)(2,1)} %v_ref.7, ...), custom_call_target="tpu_custom_call", output_to_operand_aliasing={{0}: (7, {}), {1}: (8, {}), {2}: (9, {})} | custom-call | flops 1409286144 | bytes 4718592 | tf_op jit(solution)/shard_map/pallas_call | solution.py:327
  112.5 1.3 %collective-permute-done.12 = f32[4,128,128]{2,1,0:T(8,128)S(1)} collective-permute-done((f32[4,128,128]{2,1,0:T(8,128)S(1)}, f32[4,128,128]{2,1,0:T(8,128)S(1)}, u32[]{:S(2)}, u32[]{:S(2)}) %collective-permute-start.12) | collective-permute-done | bytes 262176 | tf_op jit(solution)/shard_map/ppermute | solution.py:62
  117.7 8.4 %shard_map.103 = (bf16[512,2048]{1,0:T(8,128)(2,1)}, bf16[512,2048]{1,0:T(8,128)(2,1)}) custom-call(bf16[512,2048]{1,0:T(8,128)(2,1)} %k_ref.7, bf16[512,2048]{1,0:T(8,128)(2,1)} %v_ref.7, f32[512,2048]{1,0:T(8,128)} %get-tuple-element.198.kg_ref, f32[512,2048]{1,0:T(8,128)} %get-tuple-element.199.vg_ref, bf16[16,128,128]{2,1,0:T(8,128)(2,1)} %select_convert_fusion.gl_ref, ...), custom_call_target="tpu_custom_call" | custom-call | flops 536870912 | bytes 16777216 | tf_op jit(solution)/shard_map/pallas_call | solution.py:327
  (76 shorter events, 26.2 us)
Async XLA Ops:
  0.6 0.8 copy-start
  1.8 0.9 copy-start.1
  7.5 3.0 %collective-permute-start = (f32[16,136,128]{2,1,0:T(8,128)}, f32[16,136,128]{2,1,0:T(8,128)S(1)}, u32[]{:S(2)}, u32[]{:S(2)}) collective-permute-start(f32[16,136,128]{2,1,0:T(8,128)} %shard_map.93), channel_id=1, source_target_pairs={{0,1},{1,0},{2,3},{3,2},{4,5},{5,4},{6,7},{7,6},{8,9},{9,8},{10,11... | collective-permute-start | bytes 3342344 | tf_op jit(solution)/shard_map/ppermute | solution.py:21
  12.5 5.1 %copy-start.2 = (s32[4]{0:T(128)S(1)}, s32[4]{0:T(128)}, u32[]{:S(2)}) copy-start(s32[4]{0:T(128)} %constant.206.clone.1) | copy-start | bytes 52
  12.8 10.7 %collective-permute-start.1 = (f32[4,128,128]{2,1,0:T(8,128)S(1)}, f32[4,128,128]{2,1,0:T(8,128)S(1)}, u32[]{:S(2)}, u32[]{:S(2)}) collective-permute-start(f32[4,128,128]{2,1,0:T(8,128)S(1)} %bitcast_add_fusion.7), channel_id=1, source_target_pairs={{0,4},{4,8},{8,12},{1,5},{5,9},{9,13},{2,6},{6,10},{10,14},{3,7},{... | collective-permute-start | bytes 786440 | tf_op jit(solution)/shard_map/ppermute | solution.py:62
  24.3 9.4 %collective-permute-start.2 = (f32[4,128,128]{2,1,0:T(8,128)S(1)}, f32[4,128,128]{2,1,0:T(8,128)S(1)}, u32[]{:S(2)}, u32[]{:S(2)}) collective-permute-start(f32[4,128,128]{2,1,0:T(8,128)S(1)} %bitcast_add_fusion.6), channel_id=1, source_target_pairs={{0,4},{4,8},{8,12},{1,5},{5,9},{9,13},{2,6},{6,10},{10,14},{3,7},{... | collective-permute-start | bytes 786440 | tf_op jit(solution)/shard_map/ppermute | solution.py:62
  34.5 9.1 %collective-permute-start.3 = (f32[4,128,128]{2,1,0:T(8,128)S(1)}, f32[4,128,128]{2,1,0:T(8,128)S(1)}, u32[]{:S(2)}, u32[]{:S(2)}) collective-permute-start(f32[4,128,128]{2,1,0:T(8,128)S(1)} %bitcast_add_fusion.5), channel_id=1, source_target_pairs={{0,4},{4,8},{8,12},{1,5},{5,9},{9,13},{2,6},{6,10},{10,14},{3,7},{... | collective-permute-start | bytes 786440 | tf_op jit(solution)/shard_map/ppermute | solution.py:62
  44.3 7.8 %collective-permute-start.4 = (f32[4,128,128]{2,1,0:T(8,128)S(1)}, f32[4,128,128]{2,1,0:T(8,128)S(1)}, u32[]{:S(2)}, u32[]{:S(2)}) collective-permute-start(f32[4,128,128]{2,1,0:T(8,128)S(1)} %bitcast_add_fusion.4), channel_id=1, source_target_pairs={{0,4},{4,8},{8,12},{1,5},{5,9},{9,13},{2,6},{6,10},{10,14},{3,7},{... | collective-permute-start | bytes 786440 | tf_op jit(solution)/shard_map/ppermute | solution.py:62
  52.8 2.0 %collective-permute-start.5 = (f32[8,128,128]{2,1,0:T(8,128)S(1)}, f32[8,128,128]{2,1,0:T(8,128)S(1)}, u32[]{:S(2)}, u32[]{:S(2)}) collective-permute-start(f32[8,128,128]{2,1,0:T(8,128)S(1)} %bitcast.135), channel_id=1, source_target_pairs={{0,1},{1,0},{2,3},{3,2},{4,5},{5,4},{6,7},{7,6},{8,9},{9,8},{10,11... | collective-permute-start | bytes 1572872 | tf_op jit(solution)/shard_map/ppermute | solution.py:21
  65.4 3.0 %collective-permute-start.6 = (f32[16,136,128]{2,1,0:T(8,128)}, f32[16,136,128]{2,1,0:T(8,128)S(1)}, u32[]{:S(2)}, u32[]{:S(2)}) collective-permute-start(f32[16,136,128]{2,1,0:T(8,128)} %get-tuple-element.165), channel_id=1, source_target_pairs={{0,1},{1,0},{2,3},{3,2},{4,5},{5,4},{6,7},{7,6},{8,9},{9,8},{10,11... | collective-permute-start | bytes 3342344 | tf_op jit(solution)/shard_map/ppermute | solution.py:21
  70.5 11.4 %collective-permute-start.8 = (f32[4,128,128]{2,1,0:T(8,128)S(1)}, f32[4,128,128]{2,1,0:T(8,128)S(1)}, u32[]{:S(2)}, u32[]{:S(2)}) collective-permute-start(f32[4,128,128]{2,1,0:T(8,128)S(1)} %bitcast_add_fusion.3), channel_id=1, source_target_pairs={{4,0},{8,4},{12,8},{5,1},{9,5},{13,9},{6,2},{10,6},{14,10},{7,3},{... | collective-permute-start | bytes 786440 | tf_op jit(solution)/shard_map/ppermute | solution.py:62
  72.7 9.2 %collective-permute-start.7 = (f32[16,128]{1,0:T(8,128)S(1)}, f32[16,128]{1,0:T(8,128)S(1)}, u32[]{:S(2)}, u32[]{:S(2)}) collective-permute-start(f32[16,128]{1,0:T(8,128)S(1)} %bitcast.157), channel_id=1, source_target_pairs={{0,4},{4,0},{8,12},{12,8},{1,5},{5,1},{9,13},{13,9},{2,6},{6,2},{1... | collective-permute-start | bytes 24584 | tf_op jit(solution)/shard_map/ppermute | solution.py:117
  82.7 11.5 %collective-permute-start.10 = (f32[4,128,128]{2,1,0:T(8,128)S(1)}, f32[4,128,128]{2,1,0:T(8,128)S(1)}, u32[]{:S(2)}, u32[]{:S(2)}) collective-permute-start(f32[4,128,128]{2,1,0:T(8,128)S(1)} %bitcast_add_fusion.2), channel_id=1, source_target_pairs={{4,0},{8,4},{12,8},{5,1},{9,5},{13,9},{6,2},{10,6},{14,10},{7,3},{... | collective-permute-start | bytes 786440 | tf_op jit(solution)/shard_map/ppermute | solution.py:62
  84.2 9.9 %collective-permute-start.9 = (f32[16,128]{1,0:T(8,128)S(1)}, f32[16,128]{1,0:T(8,128)S(1)}, u32[]{:S(2)}, u32[]{:S(2)}) collective-permute-start(f32[16,128]{1,0:T(8,128)S(1)} %add.145), channel_id=1, source_target_pairs={{0,8},{4,12},{8,0},{12,4},{1,9},{5,13},{9,1},{13,5},{2,10},{6,14},... | collective-permute-start | bytes 24584 | tf_op jit(solution)/shard_map/ppermute | solution.py:117
  94.9 9.4 %collective-permute-start.11 = (f32[4,128,128]{2,1,0:T(8,128)S(1)}, f32[4,128,128]{2,1,0:T(8,128)S(1)}, u32[]{:S(2)}, u32[]{:S(2)}) collective-permute-start(f32[4,128,128]{2,1,0:T(8,128)S(1)} %bitcast_add_fusion.1), channel_id=1, source_target_pairs={{4,0},{8,4},{12,8},{5,1},{9,5},{13,9},{6,2},{10,6},{14,10},{7,3},{... | collective-permute-start | bytes 786440 | tf_op jit(solution)/shard_map/ppermute | solution.py:62
  105.0 8.9 %collective-permute-start.12 = (f32[4,128,128]{2,1,0:T(8,128)S(1)}, f32[4,128,128]{2,1,0:T(8,128)S(1)}, u32[]{:S(2)}, u32[]{:S(2)}) collective-permute-start(f32[4,128,128]{2,1,0:T(8,128)S(1)} %bitcast_add_fusion), channel_id=1, source_target_pairs={{4,0},{8,4},{12,8},{5,1},{9,5},{13,9},{6,2},{10,6},{14,10},{7,3},{... | collective-permute-start | bytes 786440 | tf_op jit(solution)/shard_map/ppermute | solution.py:62
  114.6 2.0 %collective-permute-start.13 = (f32[8,128,128]{2,1,0:T(8,128)S(1)}, f32[8,128,128]{2,1,0:T(8,128)S(1)}, u32[]{:S(2)}, u32[]{:S(2)}) collective-permute-start(f32[8,128,128]{2,1,0:T(8,128)S(1)} %bitcast.134), channel_id=1, source_target_pairs={{0,1},{1,0},{2,3},{3,2},{4,5},{5,4},{6,7},{7,6},{8,9},{9,8},{10,11... | collective-permute-start | bytes 1572872 | tf_op jit(solution)/shard_map/ppermute | solution.py:21

commit v16 on v15

--- a/solution.py
+++ b/solution.py
@@ -81,9 +81,9 @@
     second = jnp.where(c == 0, other_state, own_state)
     fin_first = jnp.where(c == 0, own_fin, other_fin)
     fin_second = jnp.where(c == 0, other_fin, own_fin)
-    chip_state = jnp.exp(fin_second)[:, None, None] * first + second
-    chip_decay = fin_first + fin_second
-    prefix_half, cover = chain_scan(halves(chip_state, c), halves(chip_decay, c), False, cover)
+    chip_half = jnp.exp(halves(fin_second, c))[:, None, None] * halves(first, c) + halves(second, c)
+    decay_half = halves(fin_first, c) + halves(fin_second, c)
+    prefix_half, cover = chain_scan(chip_half, decay_half, False, cover)
     prefix = join_halves(prefix_half, swap_dp(prefix_half), c)
     core_one = jnp.exp(fin_first)[:, None, None] * prefix + first
     return jnp.where(c == 0, prefix, core_one), cover
@@ -102,8 +102,8 @@
     fin_first = jnp.where(c == 0, own_fin, other_fin)
     fin_second = jnp.where(c == 0, other_fin, own_fin)
     chip_gain = gain_rows + other[:, DH + 1, :]
-    chip_state = first + jnp.exp(fin_first)[:, None, None] * second
-    chip_decay = fin_first + fin_second
+    chip_half = halves(first, c) + jnp.exp(halves(fin_first, c))[:, None, None] * halves(second, c)
+    decay_half = halves(fin_first, c) + halves(fin_second, c)
     chips = lax.axis_size("ctx")
 
     def grads_step(piece, both, anchor):
@@ -128,7 +128,7 @@
         else:
             steps.append(gain_round)
     suffix_half, (cover, gain_total) = chain_scan(
-        halves(chip_state, c), halves(chip_decay, c), True, steps, (None, chip_gain)
+        chip_half, decay_half, True, steps, (None, chip_gain)
     )
     suffix = join_halves(suffix_half, swap_dp(suffix_half), c)
     core_zero = second + jnp.exp(fin_second)[:, None, None] * suffix

time: 127 us -> 127 us (level)
    select_n x0 -> x3, other arithmetic: none -> 1.53 us  [the longest x1 1.52 us: backward_states(): second = jnp.where(c == 0, other_m, own_m)]
    slice x1 -> x0, other arithmetic: 1.52 us -> none  [backward_states(): moment = message[:, :DH, :]]
where the time goes in v16:
time: 127 us; the launch traced here: 126 us
  Pallas kernels  63.1 us (50%)
  starting transfers between devices  30.3 us (24%)
  other arithmetic  17 us (13%)
  waiting for transfers between devices  11.5 us (9%)
  local copies, waits for them, and re-layouts  2.93 us (2%)
    pallas_call x11, Pallas kernels, _per_head(): pl.pallas_call(body, grid=(count,), in_specs=in_specs, out_specs=[spec(ki...  63.1 us
    ppermute x8, starting transfers between devices, chain_scan(): arrived = lax.ppermute(outgoing, 'ctx', perm=perm)  22.8 us
    ppermute x4, waiting for transfers between devices, swap_dp(): return lax.ppermute(x, 'dp', perm=[(0, 1), (1, 0)])  6.95 us
    ppermute x2, starting transfers between devices, gain_step(): return (both[0], both[1] + lax.ppermute(both[1], 'ctx', perm=partners))  6.71 us
    scatter x8, other arithmetic, chain_scan(): prefix = prefix.at[slot].set(jnp.where(valid, arrived, prefix[slot]))  5.43 us
    ppermute x8, waiting for transfers between devices, chain_scan(): arrived = lax.ppermute(outgoing, 'ctx', perm=perm)  4.59 us
    another operation x4, other arithmetic  3.03 us
  transfers between devices with their start and end apart: 14, of which 8 were waited for; matrix products, arithmetic and copies ran while one was open for 4% of the time, Pallas kernels for 32%

profile of v16, /device:TPU:0, one launch (start us, length us, event | category | flops | bytes accessed | tf_op | source)
XLA Modules:
  0.0 126.2 jit_solution(6428723845724200741)
XLA Ops:
  2.7 4.8 %shard_map.93 = f32[16,136,128]{2,1,0:T(8,128)} custom-call(bf16[512,2048]{1,0:T(8,128)(2,1)} %k_ref.7, bf16[512,2048]{1,0:T(8,128)(2,1)} %v_ref.7, f32[512,16]{1,0:T(8,128)} %copy.35.cum_ref.refs_3_.refs_4_, f32[16,512]{1,0:T(8,128)} %bitcast.134), custom_call_target="tpu_custom_call" | custom-call | flops 268435456 | bytes 4194304 | tf_op jit(solution)/shard_map/pallas_call | solution.py:327
  8.8 1.7 %collective-permute-done = f32[16,136,128]{2,1,0:T(8,128)S(1)} collective-permute-done((f32[16,136,128]{2,1,0:T(8,128)}, f32[16,136,128]{2,1,0:T(8,128)S(1)}, u32[]{:S(2)}, u32[]{:S(2)}) %collective-permute-start) | collective-permute-done | bytes 1114144 | tf_op jit(solution)/shard_map/ppermute | solution.py:21
  10.9 1.5 %broadcast_select_fusion.1 = (f32[16,128,128]{2,1,0:T(8,128)S(1)}, f32[16,128,128]{2,1,0:T(8,128)S(1)}, f32[16,128,128]{2,1,0:T(8,128)S(1)}) fusion(pred[]{:T(512)S(6)} %eq.2, f32[16,136,128]{2,1,0:T(8,128)S(1)} %collective-permute-done, f32[16,136,128]{2,1,0:T(8,128)} %shard_map.93), kind=kLoop, calls=%fused_computation.11 | loop fusion | flops 262144 | bytes 5242881 | tf_op jit(solution)/shard_map/jit(_where)/select_n | solution.py:80
  12.7 4.9 %collective-permute-start.1 = (f32[4,128,128]{2,1,0:T(8,128)S(1)}, f32[4,128,128]{2,1,0:T(8,128)S(1)}, u32[]{:S(2)}, u32[]{:S(2)}) collective-permute-start(f32[4,128,128]{2,1,0:T(8,128)S(1)} %bitcast_add_fusion.7), channel_id=1, source_target_pairs={{0,4},{4,8},{8,12},{1,5},{5,9},{9,13},{2,6},{6,10},{10,14},{3,7},{... | collective-permute-start | bytes 786440 | tf_op jit(solution)/shard_map/ppermute | solution.py:62
  18.4 3.9 %shard_map.94.refs_5_ = f32[512,2048]{1,0:T(8,128)} custom-call(bf16[512,2048]{1,0:T(8,128)(2,1)} %refs_0_.8, bf16[512,2048]{1,0:T(8,128)(2,1)} %k_ref.7, bf16[512,2048]{1,0:T(8,128)(2,1)} %v_ref.7, f32[512,16]{1,0:T(8,128)} %copy.35.cum_ref.refs_3_.refs_4_, f32[16,512]{1,0:T(8,128)} %bitcast.135), custom_call_target="tpu_custom_call" | custom-call | flops 536870912 | bytes 2621440 | tf_op jit(solution)/shard_map/pallas_call | solution.py:327
  24.3 4.4 %collective-permute-start.2 = (f32[4,128,128]{2,1,0:T(8,128)S(1)}, f32[4,128,128]{2,1,0:T(8,128)S(1)}, u32[]{:S(2)}, u32[]{:S(2)}) collective-permute-start(f32[4,128,128]{2,1,0:T(8,128)S(1)} %bitcast_add_fusion.6), channel_id=1, source_target_pairs={{0,4},{4,8},{8,12},{1,5},{5,9},{9,13},{2,6},{6,10},{10,14},{3,7},{... | collective-permute-start | bytes 786440 | tf_op jit(solution)/shard_map/ppermute | solution.py:62
  28.7 4.0 %shard_map.95.refs_5_ = f32[512,2048]{1,0:T(8,128)} custom-call(bf16[512,2048]{1,0:T(8,128)(2,1)} %refs_0_.8, bf16[512,2048]{1,0:T(8,128)(2,1)} %k_ref.7, bf16[512,2048]{1,0:T(8,128)(2,1)} %v_ref.7, f32[512,16]{1,0:T(8,128)} %copy.35.cum_ref.refs_3_.refs_4_, f32[16,512]{1,0:T(8,128)} %bitcast.136, ...), custom_call_target="tpu_custom_call", output_to_operand_aliasing={{}: (5, {})} | custom-call | flops 536870912 | bytes 2621440 | tf_op jit(solution)/shard_map/pallas_call | solution.py:327
  34.5 4.4 %collective-permute-start.3 = (f32[4,128,128]{2,1,0:T(8,128)S(1)}, f32[4,128,128]{2,1,0:T(8,128)S(1)}, u32[]{:S(2)}, u32[]{:S(2)}) collective-permute-start(f32[4,128,128]{2,1,0:T(8,128)S(1)} %bitcast_add_fusion.5), channel_id=1, source_target_pairs={{0,4},{4,8},{8,12},{1,5},{5,9},{9,13},{2,6},{6,10},{10,14},{3,7},{... | collective-permute-start | bytes 786440 | tf_op jit(solution)/shard_map/ppermute | solution.py:62
  39.6 3.9 %shard_map.96.refs_5_ = f32[512,2048]{1,0:T(8,128)} custom-call(bf16[512,2048]{1,0:T(8,128)(2,1)} %refs_0_.8, bf16[512,2048]{1,0:T(8,128)(2,1)} %k_ref.7, bf16[512,2048]{1,0:T(8,128)(2,1)} %v_ref.7, f32[512,16]{1,0:T(8,128)} %copy.35.cum_ref.refs_3_.refs_4_, f32[16,512]{1,0:T(8,128)} %bitcast.137, ...), custom_call_target="tpu_custom_call", output_to_operand_aliasing={{}: (5, {})} | custom-call | flops 536870912 | bytes 2621440 | tf_op jit(solution)/shard_map/pallas_call | solution.py:327
  44.3 3.8 %collective-permute-start.4 = (f32[4,128,128]{2,1,0:T(8,128)S(1)}, f32[4,128,128]{2,1,0:T(8,128)S(1)}, u32[]{:S(2)}, u32[]{:S(2)}) collective-permute-start(f32[4,128,128]{2,1,0:T(8,128)S(1)} %bitcast_add_fusion.4), channel_id=1, source_target_pairs={{0,4},{4,8},{8,12},{1,5},{5,9},{9,13},{2,6},{6,10},{10,14},{3,7},{... | collective-permute-start | bytes 786440 | tf_op jit(solution)/shard_map/ppermute | solution.py:62
  48.2 4.0 %shard_map.97.intra_ref = f32[512,2048]{1,0:T(8,128)} custom-call(bf16[512,2048]{1,0:T(8,128)(2,1)} %refs_0_.8, bf16[512,2048]{1,0:T(8,128)(2,1)} %k_ref.7, bf16[512,2048]{1,0:T(8,128)(2,1)} %v_ref.7, f32[512,16]{1,0:T(8,128)} %copy.35.cum_ref.refs_3_.refs_4_, f32[16,512]{1,0:T(8,128)} %bitcast.138, ...), custom_call_target="tpu_custom_call", output_to_operand_aliasing={{}: (5, {})} | custom-call | flops 536870912 | bytes 2621440 | tf_op jit(solution)/shard_map/pallas_call | solution.py:327
  53.0 1.9 %collective-permute-done.5 = f32[8,128,128]{2,1,0:T(8,128)S(1)} collective-permute-done((f32[8,128,128]{2,1,0:T(8,128)S(1)}, f32[8,128,128]{2,1,0:T(8,128)S(1)}, u32[]{:S(2)}, u32[]{:S(2)}) %collective-permute-start.5) | collective-permute-done | bytes 524320 | tf_op jit(solution)/shard_map/ppermute | solution.py:21
  56.0 9.4 %shard_map.98 = (bf16[512,2048]{1,0:T(8,128)(2,1)}, f32[16,136,128]{2,1,0:T(8,128)}) custom-call(bf16[512,2048]{1,0:T(8,128)(2,1)} %refs_0_.8, bf16[512,2048]{1,0:T(8,128)(2,1)} %g_ref.1, f32[512,2048]{1,0:T(8,128)} %shard_map.97.intra_ref, bf16[16,128,128]{2,1,0:T(8,128)(2,1)} %select_convert_fusion.1.st_ref.refs_6_, ...), custom_call_target="tpu_custom_call" | custom-call | flops 536870912 | bytes 10485760 | tf_op jit(solution)/shard_map/pallas_call | solution.py:327
  66.3 2.0 %collective-permute-done.6 = f32[16,136,128]{2,1,0:T(8,128)S(1)} collective-permute-done((f32[16,136,128]{2,1,0:T(8,128)}, f32[16,136,128]{2,1,0:T(8,128)S(1)}, u32[]{:S(2)}, u32[]{:S(2)}) %collective-permute-start.6) | collective-permute-done | bytes 1114144 | tf_op jit(solution)/shard_map/ppermute | solution.py:21
  68.8 1.5 %broadcast_select_fusion = (f32[16,128,128]{2,1,0:T(8,128)S(1)}, f32[16,128,128]{2,1,0:T(8,128)S(1)}, f32[16,128,128]{2,1,0:T(8,128)S(1)}) fusion(pred[]{:T(512)S(6)} %eq.2, f32[16,136,128]{2,1,0:T(8,128)S(1)} %collective-permute-done.6, f32[16,136,128]{2,1,0:T(8,128)} %get-tuple-element.165), kind=kLoop, calls=%fused_computation.10 | loop fusion | flops 262144 | bytes 5242881 | tf_op jit(solution)/shard_map/jit(_where)/select_n | solution.py:101
  72.7 3.0 %collective-permute-start.7 = (f32[16,128]{1,0:T(8,128)S(1)}, f32[16,128]{1,0:T(8,128)S(1)}, u32[]{:S(2)}, u32[]{:S(2)}) collective-permute-start(f32[16,128]{1,0:T(8,128)S(1)} %bitcast.155), channel_id=1, source_target_pairs={{0,4},{4,0},{8,12},{12,8},{1,5},{5,1},{9,13},{13,9},{2,6},{6,2},{1... | collective-permute-start | bytes 24584 | tf_op jit(solution)/shard_map/ppermute | solution.py:117
  75.7 6.2 %shard_map.99 = (bf16[512,2048]{1,0:T(8,128)(2,1)}, f32[512,2048]{1,0:T(8,128)}, f32[512,2048]{1,0:T(8,128)}) custom-call(bf16[512,2048]{1,0:T(8,128)(2,1)} %refs_0_.8, bf16[512,2048]{1,0:T(8,128)(2,1)} %k_ref.7, bf16[512,2048]{1,0:T(8,128)(2,1)} %v_ref.7, bf16[512,2048]{1,0:T(8,128)(2,1)} %get-tuple-element.189.og_ref.refs_3_, ...), custom_call_target="tpu_custom_call" | custom-call | flops 1409286144 | bytes 4718592 | tf_op jit(solution)/shard_map/pallas_call | solution.py:327
  82.6 1.5 %collective-permute-start.10 = (f32[4,128,128]{2,1,0:T(8,128)S(1)}, f32[4,128,128]{2,1,0:T(8,128)S(1)}, u32[]{:S(2)}, u32[]{:S(2)}) collective-permute-start(f32[4,128,128]{2,1,0:T(8,128)S(1)} %bitcast_add_fusion.2), channel_id=1, source_target_pairs={{4,0},{8,4},{12,8},{5,1},{9,5},{13,9},{6,2},{10,6},{14,10},{7,3},{... | collective-permute-start | bytes 786440 | tf_op jit(solution)/shard_map/ppermute | solution.py:62
  84.1 3.7 %collective-permute-start.9 = (f32[16,128]{1,0:T(8,128)S(1)}, f32[16,128]{1,0:T(8,128)S(1)}, u32[]{:S(2)}, u32[]{:S(2)}) collective-permute-start(f32[16,128]{1,0:T(8,128)S(1)} %add.151), channel_id=1, source_target_pairs={{0,8},{4,12},{8,0},{12,4},{1,9},{5,13},{9,1},{13,5},{2,10},{6,14},... | collective-permute-start | bytes 24584 | tf_op jit(solution)/shard_map/ppermute | solution.py:117
  87.8 6.2 %shard_map.100 = (bf16[512,2048]{1,0:T(8,128)(2,1)}, f32[512,2048]{1,0:T(8,128)}, f32[512,2048]{1,0:T(8,128)}) custom-call(bf16[512,2048]{1,0:T(8,128)(2,1)} %refs_0_.8, bf16[512,2048]{1,0:T(8,128)(2,1)} %k_ref.7, bf16[512,2048]{1,0:T(8,128)(2,1)} %v_ref.7, ...), custom_call_target="tpu_custom_call", output_to_operand_aliasing={{0}: (7, {}), {1}: (8, {}), {2}: (9, {})} | custom-call | flops 1409286144 | bytes 4718592 | tf_op jit(solution)/shard_map/pallas_call | solution.py:327
  96.9 6.2 %shard_map.101 = (bf16[512,2048]{1,0:T(8,128)(2,1)}, f32[512,2048]{1,0:T(8,128)}, f32[512,2048]{1,0:T(8,128)}) custom-call(bf16[512,2048]{1,0:T(8,128)(2,1)} %refs_0_.8, bf16[512,2048]{1,0:T(8,128)(2,1)} %k_ref.7, bf16[512,2048]{1,0:T(8,128)(2,1)} %v_ref.7, ...), custom_call_target="tpu_custom_call", output_to_operand_aliasing={{0}: (7, {}), {1}: (8, {}), {2}: (9, {})} | custom-call | flops 1409286144 | bytes 4718592 | tf_op jit(solution)/shard_map/pallas_call | solution.py:327
  106.4 6.2 %shard_map.102 = (bf16[512,2048]{1,0:T(8,128)(2,1)}, f32[512,2048]{1,0:T(8,128)}, f32[512,2048]{1,0:T(8,128)}) custom-call(bf16[512,2048]{1,0:T(8,128)(2,1)} %refs_0_.8, bf16[512,2048]{1,0:T(8,128)(2,1)} %k_ref.7, bf16[512,2048]{1,0:T(8,128)(2,1)} %v_ref.7, ...), custom_call_target="tpu_custom_call", output_to_operand_aliasing={{0}: (7, {}), {1}: (8, {}), {2}: (9, {})} | custom-call | flops 1409286144 | bytes 4718592 | tf_op jit(solution)/shard_map/pallas_call | solution.py:327
  112.6 1.3 %collective-permute-done.12 = f32[4,128,128]{2,1,0:T(8,128)S(1)} collective-permute-done((f32[4,128,128]{2,1,0:T(8,128)S(1)}, f32[4,128,128]{2,1,0:T(8,128)S(1)}, u32[]{:S(2)}, u32[]{:S(2)}) %collective-permute-start.12) | collective-permute-done | bytes 262176 | tf_op jit(solution)/shard_map/ppermute | solution.py:62
  117.8 8.4 %shard_map.103 = (bf16[512,2048]{1,0:T(8,128)(2,1)}, bf16[512,2048]{1,0:T(8,128)(2,1)}) custom-call(bf16[512,2048]{1,0:T(8,128)(2,1)} %k_ref.7, bf16[512,2048]{1,0:T(8,128)(2,1)} %v_ref.7, f32[512,2048]{1,0:T(8,128)} %get-tuple-element.198.kg_ref, f32[512,2048]{1,0:T(8,128)} %get-tuple-element.199.vg_ref, bf16[16,128,128]{2,1,0:T(8,128)(2,1)} %select_convert_fusion.gl_ref, ...), custom_call_target="tpu_custom_call" | custom-call | flops 536870912 | bytes 16777216 | tf_op jit(solution)/shard_map/pallas_call | solution.py:327
  (74 shorter events, 26.4 us)
Async XLA Ops:
  0.6 0.8 copy-start
  1.8 0.9 copy-start.1
  7.5 3.0 %collective-permute-start = (f32[16,136,128]{2,1,0:T(8,128)}, f32[16,136,128]{2,1,0:T(8,128)S(1)}, u32[]{:S(2)}, u32[]{:S(2)}) collective-permute-start(f32[16,136,128]{2,1,0:T(8,128)} %shard_map.93), channel_id=1, source_target_pairs={{0,1},{1,0},{2,3},{3,2},{4,5},{5,4},{6,7},{7,6},{8,9},{9,8},{10,11... | collective-permute-start | bytes 3342344 | tf_op jit(solution)/shard_map/ppermute | solution.py:21
  12.4 5.1 %copy-start.2 = (s32[4]{0:T(128)S(1)}, s32[4]{0:T(128)}, u32[]{:S(2)}) copy-start(s32[4]{0:T(128)} %constant.206.clone.1) | copy-start | bytes 52
  12.7 10.7 %collective-permute-start.1 = (f32[4,128,128]{2,1,0:T(8,128)S(1)}, f32[4,128,128]{2,1,0:T(8,128)S(1)}, u32[]{:S(2)}, u32[]{:S(2)}) collective-permute-start(f32[4,128,128]{2,1,0:T(8,128)S(1)} %bitcast_add_fusion.7), channel_id=1, source_target_pairs={{0,4},{4,8},{8,12},{1,5},{5,9},{9,13},{2,6},{6,10},{10,14},{3,7},{... | collective-permute-start | bytes 786440 | tf_op jit(solution)/shard_map/ppermute | solution.py:62
  24.3 9.4 %collective-permute-start.2 = (f32[4,128,128]{2,1,0:T(8,128)S(1)}, f32[4,128,128]{2,1,0:T(8,128)S(1)}, u32[]{:S(2)}, u32[]{:S(2)}) collective-permute-start(f32[4,128,128]{2,1,0:T(8,128)S(1)} %bitcast_add_fusion.6), channel_id=1, source_target_pairs={{0,4},{4,8},{8,12},{1,5},{5,9},{9,13},{2,6},{6,10},{10,14},{3,7},{... | collective-permute-start | bytes 786440 | tf_op jit(solution)/shard_map/ppermute | solution.py:62
  34.5 9.1 %collective-permute-start.3 = (f32[4,128,128]{2,1,0:T(8,128)S(1)}, f32[4,128,128]{2,1,0:T(8,128)S(1)}, u32[]{:S(2)}, u32[]{:S(2)}) collective-permute-start(f32[4,128,128]{2,1,0:T(8,128)S(1)} %bitcast_add_fusion.5), channel_id=1, source_target_pairs={{0,4},{4,8},{8,12},{1,5},{5,9},{9,13},{2,6},{6,10},{10,14},{3,7},{... | collective-permute-start | bytes 786440 | tf_op jit(solution)/shard_map/ppermute | solution.py:62
  44.3 7.8 %collective-permute-start.4 = (f32[4,128,128]{2,1,0:T(8,128)S(1)}, f32[4,128,128]{2,1,0:T(8,128)S(1)}, u32[]{:S(2)}, u32[]{:S(2)}) collective-permute-start(f32[4,128,128]{2,1,0:T(8,128)S(1)} %bitcast_add_fusion.4), channel_id=1, source_target_pairs={{0,4},{4,8},{8,12},{1,5},{5,9},{9,13},{2,6},{6,10},{10,14},{3,7},{... | collective-permute-start | bytes 786440 | tf_op jit(solution)/shard_map/ppermute | solution.py:62
  52.9 2.0 %collective-permute-start.5 = (f32[8,128,128]{2,1,0:T(8,128)S(1)}, f32[8,128,128]{2,1,0:T(8,128)S(1)}, u32[]{:S(2)}, u32[]{:S(2)}) collective-permute-start(f32[8,128,128]{2,1,0:T(8,128)S(1)} %bitcast.133), channel_id=1, source_target_pairs={{0,1},{1,0},{2,3},{3,2},{4,5},{5,4},{6,7},{7,6},{8,9},{9,8},{10,11... | collective-permute-start | bytes 1572872 | tf_op jit(solution)/shard_map/ppermute | solution.py:21
  65.4 3.0 %collective-permute-start.6 = (f32[16,136,128]{2,1,0:T(8,128)}, f32[16,136,128]{2,1,0:T(8,128)S(1)}, u32[]{:S(2)}, u32[]{:S(2)}) collective-permute-start(f32[16,136,128]{2,1,0:T(8,128)} %get-tuple-element.165), channel_id=1, source_target_pairs={{0,1},{1,0},{2,3},{3,2},{4,5},{5,4},{6,7},{7,6},{8,9},{9,8},{10,11... | collective-permute-start | bytes 3342344 | tf_op jit(solution)/shard_map/ppermute | solution.py:21
  70.5 11.3 %collective-permute-start.8 = (f32[4,128,128]{2,1,0:T(8,128)S(1)}, f32[4,128,128]{2,1,0:T(8,128)S(1)}, u32[]{:S(2)}, u32[]{:S(2)}) collective-permute-start(f32[4,128,128]{2,1,0:T(8,128)S(1)} %bitcast_add_fusion.3), channel_id=1, source_target_pairs={{4,0},{8,4},{12,8},{5,1},{9,5},{13,9},{6,2},{10,6},{14,10},{7,3},{... | collective-permute-start | bytes 786440 | tf_op jit(solution)/shard_map/ppermute | solution.py:62
  72.7 9.1 %collective-permute-start.7 = (f32[16,128]{1,0:T(8,128)S(1)}, f32[16,128]{1,0:T(8,128)S(1)}, u32[]{:S(2)}, u32[]{:S(2)}) collective-permute-start(f32[16,128]{1,0:T(8,128)S(1)} %bitcast.155), channel_id=1, source_target_pairs={{0,4},{4,0},{8,12},{12,8},{1,5},{5,1},{9,13},{13,9},{2,6},{6,2},{1... | collective-permute-start | bytes 24584 | tf_op jit(solution)/shard_map/ppermute | solution.py:117
  82.6 11.4 %collective-permute-start.10 = (f32[4,128,128]{2,1,0:T(8,128)S(1)}, f32[4,128,128]{2,1,0:T(8,128)S(1)}, u32[]{:S(2)}, u32[]{:S(2)}) collective-permute-start(f32[4,128,128]{2,1,0:T(8,128)S(1)} %bitcast_add_fusion.2), channel_id=1, source_target_pairs={{4,0},{8,4},{12,8},{5,1},{9,5},{13,9},{6,2},{10,6},{14,10},{7,3},{... | collective-permute-start | bytes 786440 | tf_op jit(solution)/shard_map/ppermute | solution.py:62
  84.1 9.9 %collective-permute-start.9 = (f32[16,128]{1,0:T(8,128)S(1)}, f32[16,128]{1,0:T(8,128)S(1)}, u32[]{:S(2)}, u32[]{:S(2)}) collective-permute-start(f32[16,128]{1,0:T(8,128)S(1)} %add.151), channel_id=1, source_target_pairs={{0,8},{4,12},{8,0},{12,4},{1,9},{5,13},{9,1},{13,5},{2,10},{6,14},... | collective-permute-start | bytes 24584 | tf_op jit(solution)/shard_map/ppermute | solution.py:117
  94.9 9.4 %collective-permute-start.11 = (f32[4,128,128]{2,1,0:T(8,128)S(1)}, f32[4,128,128]{2,1,0:T(8,128)S(1)}, u32[]{:S(2)}, u32[]{:S(2)}) collective-permute-start(f32[4,128,128]{2,1,0:T(8,128)S(1)} %bitcast_add_fusion.1), channel_id=1, source_target_pairs={{4,0},{8,4},{12,8},{5,1},{9,5},{13,9},{6,2},{10,6},{14,10},{7,3},{... | collective-permute-start | bytes 786440 | tf_op jit(solution)/shard_map/ppermute | solution.py:62
  105.1 8.9 %collective-permute-start.12 = (f32[4,128,128]{2,1,0:T(8,128)S(1)}, f32[4,128,128]{2,1,0:T(8,128)S(1)}, u32[]{:S(2)}, u32[]{:S(2)}) collective-permute-start(f32[4,128,128]{2,1,0:T(8,128)S(1)} %bitcast_add_fusion), channel_id=1, source_target_pairs={{4,0},{8,4},{12,8},{5,1},{9,5},{13,9},{6,2},{10,6},{14,10},{7,3},{... | collective-permute-start | bytes 786440 | tf_op jit(solution)/shard_map/ppermute | solution.py:62
  114.6 2.0 %collective-permute-start.13 = (f32[8,128,128]{2,1,0:T(8,128)S(1)}, f32[8,128,128]{2,1,0:T(8,128)S(1)}, u32[]{:S(2)}, u32[]{:S(2)}) collective-permute-start(f32[8,128,128]{2,1,0:T(8,128)S(1)} %bitcast.132), channel_id=1, source_target_pairs={{0,1},{1,0},{2,3},{3,2},{4,5},{5,4},{6,7},{7,6},{8,9},{9,8},{10,11... | collective-permute-start | bytes 1572872 | tf_op jit(solution)/shard_map/ppermute | solution.py:21

commit v17 on v15

--- a/solution.py
+++ b/solution.py
@@ -283,7 +283,7 @@
 def _per_head(kernel, ins, outs, heads, length, flops, nbytes, exps=0, part=None, into=None, wide=False):
     hb = HB if part is None else HB // PIECE_STEPS
     if wide:
-        hb = min(2 * HB, heads)
+        hb = min(4 * HB, heads)
         kernel = functools.partial(kernel, hb)
     groups = heads // hb
     first, count = (0, groups) if part is None else (part * PIECE_STEPS, PIECE_STEPS)

time: 127 us -> 128 us (level)
  no operation moved by 1% of the time
where the time goes in v17:
time: 128 us; the launch traced here: 127 us
  Pallas kernels  63.6 us (50%)
  starting transfers between devices  30.3 us (24%)
  other arithmetic  16.4 us (13%)
  waiting for transfers between devices  11.7 us (9%)
  local copies, waits for them, and re-layouts  3.24 us (3%)
    pallas_call x11, Pallas kernels, _per_head(): pl.pallas_call(body, grid=(count,), in_specs=in_specs, out_specs=[spec(ki...  63.6 us
    ppermute x8, starting transfers between devices, chain_scan(): arrived = lax.ppermute(outgoing, 'ctx', perm=perm)  22.8 us
    ppermute x4, waiting for transfers between devices, swap_dp(): return lax.ppermute(x, 'dp', perm=[(0, 1), (1, 0)])  7.01 us
    ppermute x2, starting transfers between devices, gain_step(): return (both[0], both[1] + lax.ppermute(both[1], 'ctx', perm=partners))  6.76 us
    scatter x8, other arithmetic, chain_scan(): prefix = prefix.at[slot].set(jnp.where(valid, arrived, prefix[slot]))  5.2 us
    ppermute x8, waiting for transfers between devices, chain_scan(): arrived = lax.ppermute(outgoing, 'ctx', perm=perm)  4.66 us
    another operation x4, other arithmetic  2.88 us
  transfers between devices with their start and end apart: 14, of which 8 were waited for; matrix products, arithmetic and copies ran while one was open for 4% of the time, Pallas kernels for 32%

profile of v17, /device:TPU:0, one launch (start us, length us, event | category | flops | bytes accessed | tf_op | source)
XLA Modules:
  0.0 126.7 jit_solution(815492131050434552)
XLA Ops:
  2.7 5.3 %shard_map.93 = f32[16,136,128]{2,1,0:T(8,128)} custom-call(bf16[512,2048]{1,0:T(8,128)(2,1)} %k_ref.7, bf16[512,2048]{1,0:T(8,128)(2,1)} %v_ref.7, f32[512,16]{1,0:T(8,128)} %copy.37.cum_ref.refs_3_.refs_4_, f32[16,512]{1,0:T(8,128)} %bitcast.136), custom_call_target="tpu_custom_call" | custom-call | flops 268435456 | bytes 4194304 | tf_op jit(solution)/shard_map/pallas_call | solution.py:327
  9.3 1.7 %collective-permute-done = f32[16,136,128]{2,1,0:T(8,128)S(1)} collective-permute-done((f32[16,136,128]{2,1,0:T(8,128)}, f32[16,136,128]{2,1,0:T(8,128)S(1)}, u32[]{:S(2)}, u32[]{:S(2)}) %collective-permute-start) | collective-permute-done | bytes 1114144 | tf_op jit(solution)/shard_map/ppermute | solution.py:21
  11.5 1.5 %broadcast_select_fusion.1 = (f32[16,128,128]{2,1,0:T(8,128)S(1)}, f32[16,128,128]{2,1,0:T(8,128)S(1)}, f32[16,128,128]{2,1,0:T(8,128)S(1)}) fusion(pred[]{:T(512)S(6)} %eq.2, f32[16,136,128]{2,1,0:T(8,128)S(1)} %collective-permute-done, f32[16,136,128]{2,1,0:T(8,128)} %shard_map.93), kind=kLoop, calls=%fused_computation.13 | loop fusion | flops 262144 | bytes 5242881 | tf_op jit(solution)/shard_map/jit(_where)/select_n | solution.py:80
  13.3 4.9 %collective-permute-start.1 = (f32[4,128,128]{2,1,0:T(8,128)S(1)}, f32[4,128,128]{2,1,0:T(8,128)S(1)}, u32[]{:S(2)}, u32[]{:S(2)}) collective-permute-start(f32[4,128,128]{2,1,0:T(8,128)S(1)} %bitcast_add_fusion.7), channel_id=1, source_target_pairs={{0,4},{4,8},{8,12},{1,5},{5,9},{9,13},{2,6},{6,10},{10,14},{3,7},{... | collective-permute-start | bytes 786440 | tf_op jit(solution)/shard_map/ppermute | solution.py:62
  18.9 3.9 %shard_map.94.refs_5_ = f32[512,2048]{1,0:T(8,128)} custom-call(bf16[512,2048]{1,0:T(8,128)(2,1)} %refs_0_.8, bf16[512,2048]{1,0:T(8,128)(2,1)} %k_ref.7, bf16[512,2048]{1,0:T(8,128)(2,1)} %v_ref.7, f32[512,16]{1,0:T(8,128)} %copy.37.cum_ref.refs_3_.refs_4_, f32[16,512]{1,0:T(8,128)} %bitcast.137), custom_call_target="tpu_custom_call" | custom-call | flops 536870912 | bytes 2621440 | tf_op jit(solution)/shard_map/pallas_call | solution.py:327
  24.8 4.4 %collective-permute-start.2 = (f32[4,128,128]{2,1,0:T(8,128)S(1)}, f32[4,128,128]{2,1,0:T(8,128)S(1)}, u32[]{:S(2)}, u32[]{:S(2)}) collective-permute-start(f32[4,128,128]{2,1,0:T(8,128)S(1)} %bitcast_add_fusion.6), channel_id=1, source_target_pairs={{0,4},{4,8},{8,12},{1,5},{5,9},{9,13},{2,6},{6,10},{10,14},{3,7},{... | collective-permute-start | bytes 786440 | tf_op jit(solution)/shard_map/ppermute | solution.py:62
  29.2 4.0 %shard_map.95.refs_5_ = f32[512,2048]{1,0:T(8,128)} custom-call(bf16[512,2048]{1,0:T(8,128)(2,1)} %refs_0_.8, bf16[512,2048]{1,0:T(8,128)(2,1)} %k_ref.7, bf16[512,2048]{1,0:T(8,128)(2,1)} %v_ref.7, f32[512,16]{1,0:T(8,128)} %copy.37.cum_ref.refs_3_.refs_4_, f32[16,512]{1,0:T(8,128)} %bitcast.138, ...), custom_call_target="tpu_custom_call", output_to_operand_aliasing={{}: (5, {})} | custom-call | flops 536870912 | bytes 2621440 | tf_op jit(solution)/shard_map/pallas_call | solution.py:327
  35.0 4.4 %collective-permute-start.3 = (f32[4,128,128]{2,1,0:T(8,128)S(1)}, f32[4,128,128]{2,1,0:T(8,128)S(1)}, u32[]{:S(2)}, u32[]{:S(2)}) collective-permute-start(f32[4,128,128]{2,1,0:T(8,128)S(1)} %bitcast_add_fusion.5), channel_id=1, source_target_pairs={{0,4},{4,8},{8,12},{1,5},{5,9},{9,13},{2,6},{6,10},{10,14},{3,7},{... | collective-permute-start | bytes 786440 | tf_op jit(solution)/shard_map/ppermute | solution.py:62
  40.1 3.9 %shard_map.96.refs_5_ = f32[512,2048]{1,0:T(8,128)} custom-call(bf16[512,2048]{1,0:T(8,128)(2,1)} %refs_0_.8, bf16[512,2048]{1,0:T(8,128)(2,1)} %k_ref.7, bf16[512,2048]{1,0:T(8,128)(2,1)} %v_ref.7, f32[512,16]{1,0:T(8,128)} %copy.37.cum_ref.refs_3_.refs_4_, f32[16,512]{1,0:T(8,128)} %bitcast.139, ...), custom_call_target="tpu_custom_call", output_to_operand_aliasing={{}: (5, {})} | custom-call | flops 536870912 | bytes 2621440 | tf_op jit(solution)/shard_map/pallas_call | solution.py:327
  44.8 3.8 %collective-permute-start.4 = (f32[4,128,128]{2,1,0:T(8,128)S(1)}, f32[4,128,128]{2,1,0:T(8,128)S(1)}, u32[]{:S(2)}, u32[]{:S(2)}) collective-permute-start(f32[4,128,128]{2,1,0:T(8,128)S(1)} %bitcast_add_fusion.4), channel_id=1, source_target_pairs={{0,4},{4,8},{8,12},{1,5},{5,9},{9,13},{2,6},{6,10},{10,14},{3,7},{... | collective-permute-start | bytes 786440 | tf_op jit(solution)/shard_map/ppermute | solution.py:62
  48.7 4.0 %shard_map.97.intra_ref = f32[512,2048]{1,0:T(8,128)} custom-call(bf16[512,2048]{1,0:T(8,128)(2,1)} %refs_0_.8, bf16[512,2048]{1,0:T(8,128)(2,1)} %k_ref.7, bf16[512,2048]{1,0:T(8,128)(2,1)} %v_ref.7, f32[512,16]{1,0:T(8,128)} %copy.37.cum_ref.refs_3_.refs_4_, f32[16,512]{1,0:T(8,128)} %bitcast.140, ...), custom_call_target="tpu_custom_call", output_to_operand_aliasing={{}: (5, {})} | custom-call | flops 536870912 | bytes 2621440 | tf_op jit(solution)/shard_map/pallas_call | solution.py:327
  53.4 1.9 %collective-permute-done.5 = f32[8,128,128]{2,1,0:T(8,128)S(1)} collective-permute-done((f32[8,128,128]{2,1,0:T(8,128)S(1)}, f32[8,128,128]{2,1,0:T(8,128)S(1)}, u32[]{:S(2)}, u32[]{:S(2)}) %collective-permute-start.5) | collective-permute-done | bytes 524320 | tf_op jit(solution)/shard_map/ppermute | solution.py:21
  56.5 9.4 %shard_map.98 = (bf16[512,2048]{1,0:T(8,128)(2,1)}, f32[16,136,128]{2,1,0:T(8,128)}) custom-call(bf16[512,2048]{1,0:T(8,128)(2,1)} %refs_0_.8, bf16[512,2048]{1,0:T(8,128)(2,1)} %g_ref.1, f32[512,2048]{1,0:T(8,128)} %shard_map.97.intra_ref, bf16[16,128,128]{2,1,0:T(8,128)(2,1)} %select_convert_fusion.1.st_ref.refs_6_, ...), custom_call_target="tpu_custom_call" | custom-call | flops 536870912 | bytes 10485760 | tf_op jit(solution)/shard_map/pallas_call | solution.py:327
  66.7 2.1 %collective-permute-done.6 = f32[16,136,128]{2,1,0:T(8,128)S(1)} collective-permute-done((f32[16,136,128]{2,1,0:T(8,128)}, f32[16,136,128]{2,1,0:T(8,128)S(1)}, u32[]{:S(2)}, u32[]{:S(2)}) %collective-permute-start.6) | collective-permute-done | bytes 1114144 | tf_op jit(solution)/shard_map/ppermute | solution.py:21
  69.3 1.5 %fusion.29 = (f32[16,128,128]{2,1,0:T(8,128)S(1)}, f32[16,128,128]{2,1,0:T(8,128)S(1)}, f32[16,128,128]{2,1,0:T(8,128)S(1)}) fusion(f32[16,136,128]{2,1,0:T(8,128)} %get-tuple-element.165, f32[16,136,128]{2,1,0:T(8,128)S(1)} %collective-permute-done.6, pred[]{:T(512)S(6)} %eq.2), kind=kLoop, calls=%fused_computation.133 | loop fusion | flops 262144 | bytes 5242881 | tf_op jit(solution)/shard_map/slice | solution.py:95
  71.1 1.5 %collective-permute-start.8 = (f32[4,128,128]{2,1,0:T(8,128)S(1)}, f32[4,128,128]{2,1,0:T(8,128)S(1)}, u32[]{:S(2)}, u32[]{:S(2)}) collective-permute-start(f32[4,128,128]{2,1,0:T(8,128)S(1)} %bitcast_add_fusion.3), channel_id=1, source_target_pairs={{4,0},{8,4},{12,8},{5,1},{9,5},{13,9},{6,2},{10,6},{14,10},{7,3},{... | collective-permute-start | bytes 786440 | tf_op jit(solution)/shard_map/ppermute | solution.py:62
  73.4 3.0 %collective-permute-start.7 = (f32[16,128]{1,0:T(8,128)S(1)}, f32[16,128]{1,0:T(8,128)S(1)}, u32[]{:S(2)}, u32[]{:S(2)}) collective-permute-start(f32[16,128]{1,0:T(8,128)S(1)} %bitcast.157), channel_id=1, source_target_pairs={{0,4},{4,0},{8,12},{12,8},{1,5},{5,1},{9,13},{13,9},{2,6},{6,2},{1... | collective-permute-start | bytes 24584 | tf_op jit(solution)/shard_map/ppermute | solution.py:117
  76.4 6.2 %shard_map.99 = (bf16[512,2048]{1,0:T(8,128)(2,1)}, f32[512,2048]{1,0:T(8,128)}, f32[512,2048]{1,0:T(8,128)}) custom-call(bf16[512,2048]{1,0:T(8,128)(2,1)} %refs_0_.8, bf16[512,2048]{1,0:T(8,128)(2,1)} %k_ref.7, bf16[512,2048]{1,0:T(8,128)(2,1)} %v_ref.7, bf16[512,2048]{1,0:T(8,128)(2,1)} %get-tuple-element.189.og_ref.refs_3_, ...), custom_call_target="tpu_custom_call" | custom-call | flops 1409286144 | bytes 4718592 | tf_op jit(solution)/shard_map/pallas_call | solution.py:327
  84.7 3.7 %collective-permute-start.9 = (f32[16,128]{1,0:T(8,128)S(1)}, f32[16,128]{1,0:T(8,128)S(1)}, u32[]{:S(2)}, u32[]{:S(2)}) collective-permute-start(f32[16,128]{1,0:T(8,128)S(1)} %add.145), channel_id=1, source_target_pairs={{0,8},{4,12},{8,0},{12,4},{1,9},{5,13},{9,1},{13,5},{2,10},{6,14},... | collective-permute-start | bytes 24584 | tf_op jit(solution)/shard_map/ppermute | solution.py:117
  88.5 6.2 %shard_map.100 = (bf16[512,2048]{1,0:T(8,128)(2,1)}, f32[512,2048]{1,0:T(8,128)}, f32[512,2048]{1,0:T(8,128)}) custom-call(bf16[512,2048]{1,0:T(8,128)(2,1)} %refs_0_.8, bf16[512,2048]{1,0:T(8,128)(2,1)} %k_ref.7, bf16[512,2048]{1,0:T(8,128)(2,1)} %v_ref.7, ...), custom_call_target="tpu_custom_call", output_to_operand_aliasing={{0}: (7, {}), {1}: (8, {}), {2}: (9, {})} | custom-call | flops 1409286144 | bytes 4718592 | tf_op jit(solution)/shard_map/pallas_call | solution.py:327
  97.4 6.2 %shard_map.101 = (bf16[512,2048]{1,0:T(8,128)(2,1)}, f32[512,2048]{1,0:T(8,128)}, f32[512,2048]{1,0:T(8,128)}) custom-call(bf16[512,2048]{1,0:T(8,128)(2,1)} %refs_0_.8, bf16[512,2048]{1,0:T(8,128)(2,1)} %k_ref.7, bf16[512,2048]{1,0:T(8,128)(2,1)} %v_ref.7, ...), custom_call_target="tpu_custom_call", output_to_operand_aliasing={{0}: (7, {}), {1}: (8, {}), {2}: (9, {})} | custom-call | flops 1409286144 | bytes 4718592 | tf_op jit(solution)/shard_map/pallas_call | solution.py:327
  106.9 6.2 %shard_map.102 = (bf16[512,2048]{1,0:T(8,128)(2,1)}, f32[512,2048]{1,0:T(8,128)}, f32[512,2048]{1,0:T(8,128)}) custom-call(bf16[512,2048]{1,0:T(8,128)(2,1)} %refs_0_.8, bf16[512,2048]{1,0:T(8,128)(2,1)} %k_ref.7, bf16[512,2048]{1,0:T(8,128)(2,1)} %v_ref.7, ...), custom_call_target="tpu_custom_call", output_to_operand_aliasing={{0}: (7, {}), {1}: (8, {}), {2}: (9, {})} | custom-call | flops 1409286144 | bytes 4718592 | tf_op jit(solution)/shard_map/pallas_call | solution.py:327
  113.0 1.3 %collective-permute-done.12 = f32[4,128,128]{2,1,0:T(8,128)S(1)} collective-permute-done((f32[4,128,128]{2,1,0:T(8,128)S(1)}, f32[4,128,128]{2,1,0:T(8,128)S(1)}, u32[]{:S(2)}, u32[]{:S(2)}) %collective-permute-start.12) | collective-permute-done | bytes 262176 | tf_op jit(solution)/shard_map/ppermute | solution.py:62
  118.2 8.4 %shard_map.103 = (bf16[512,2048]{1,0:T(8,128)(2,1)}, bf16[512,2048]{1,0:T(8,128)(2,1)}) custom-call(bf16[512,2048]{1,0:T(8,128)(2,1)} %k_ref.7, bf16[512,2048]{1,0:T(8,128)(2,1)} %v_ref.7, f32[512,2048]{1,0:T(8,128)} %get-tuple-element.198.kg_ref, f32[512,2048]{1,0:T(8,128)} %get-tuple-element.199.vg_ref, bf16[16,128,128]{2,1,0:T(8,128)(2,1)} %select_convert_fusion.gl_ref, ...), custom_call_target="tpu_custom_call" | custom-call | flops 536870912 | bytes 16777216 | tf_op jit(solution)/shard_map/pallas_call | solution.py:327
  (76 shorter events, 26.2 us)
Async XLA Ops:
  0.6 0.8 copy-start
  1.8 0.9 copy-start.1
  8.0 3.0 %collective-permute-start = (f32[16,136,128]{2,1,0:T(8,128)}, f32[16,136,128]{2,1,0:T(8,128)S(1)}, u32[]{:S(2)}, u32[]{:S(2)}) collective-permute-start(f32[16,136,128]{2,1,0:T(8,128)} %shard_map.93), channel_id=1, source_target_pairs={{0,1},{1,0},{2,3},{3,2},{4,5},{5,4},{6,7},{7,6},{8,9},{9,8},{10,11... | collective-permute-start | bytes 3342344 | tf_op jit(solution)/shard_map/ppermute | solution.py:21
  13.0 5.1 %copy-start.2 = (s32[4]{0:T(128)S(1)}, s32[4]{0:T(128)}, u32[]{:S(2)}) copy-start(s32[4]{0:T(128)} %constant.206.clone.1) | copy-start | bytes 52
  13.3 10.7 %collective-permute-start.1 = (f32[4,128,128]{2,1,0:T(8,128)S(1)}, f32[4,128,128]{2,1,0:T(8,128)S(1)}, u32[]{:S(2)}, u32[]{:S(2)}) collective-permute-start(f32[4,128,128]{2,1,0:T(8,128)S(1)} %bitcast_add_fusion.7), channel_id=1, source_target_pairs={{0,4},{4,8},{8,12},{1,5},{5,9},{9,13},{2,6},{6,10},{10,14},{3,7},{... | collective-permute-start | bytes 786440 | tf_op jit(solution)/shard_map/ppermute | solution.py:62
  24.8 9.4 %collective-permute-start.2 = (f32[4,128,128]{2,1,0:T(8,128)S(1)}, f32[4,128,128]{2,1,0:T(8,128)S(1)}, u32[]{:S(2)}, u32[]{:S(2)}) collective-permute-start(f32[4,128,128]{2,1,0:T(8,128)S(1)} %bitcast_add_fusion.6), channel_id=1, source_target_pairs={{0,4},{4,8},{8,12},{1,5},{5,9},{9,13},{2,6},{6,10},{10,14},{3,7},{... | collective-permute-start | bytes 786440 | tf_op jit(solution)/shard_map/ppermute | solution.py:62
  35.0 9.1 %collective-permute-start.3 = (f32[4,128,128]{2,1,0:T(8,128)S(1)}, f32[4,128,128]{2,1,0:T(8,128)S(1)}, u32[]{:S(2)}, u32[]{:S(2)}) collective-permute-start(f32[4,128,128]{2,1,0:T(8,128)S(1)} %bitcast_add_fusion.5), channel_id=1, source_target_pairs={{0,4},{4,8},{8,12},{1,5},{5,9},{9,13},{2,6},{6,10},{10,14},{3,7},{... | collective-permute-start | bytes 786440 | tf_op jit(solution)/shard_map/ppermute | solution.py:62
  44.8 7.8 %collective-permute-start.4 = (f32[4,128,128]{2,1,0:T(8,128)S(1)}, f32[4,128,128]{2,1,0:T(8,128)S(1)}, u32[]{:S(2)}, u32[]{:S(2)}) collective-permute-start(f32[4,128,128]{2,1,0:T(8,128)S(1)} %bitcast_add_fusion.4), channel_id=1, source_target_pairs={{0,4},{4,8},{8,12},{1,5},{5,9},{9,13},{2,6},{6,10},{10,14},{3,7},{... | collective-permute-start | bytes 786440 | tf_op jit(solution)/shard_map/ppermute | solution.py:62
  53.3 2.0 %collective-permute-start.5 = (f32[8,128,128]{2,1,0:T(8,128)S(1)}, f32[8,128,128]{2,1,0:T(8,128)S(1)}, u32[]{:S(2)}, u32[]{:S(2)}) collective-permute-start(f32[8,128,128]{2,1,0:T(8,128)S(1)} %bitcast.135), channel_id=1, source_target_pairs={{0,1},{1,0},{2,3},{3,2},{4,5},{5,4},{6,7},{7,6},{8,9},{9,8},{10,11... | collective-permute-start | bytes 1572872 | tf_op jit(solution)/shard_map/ppermute | solution.py:21
  65.9 3.0 %collective-permute-start.6 = (f32[16,136,128]{2,1,0:T(8,128)}, f32[16,136,128]{2,1,0:T(8,128)S(1)}, u32[]{:S(2)}, u32[]{:S(2)}) collective-permute-start(f32[16,136,128]{2,1,0:T(8,128)} %get-tuple-element.165), channel_id=1, source_target_pairs={{0,1},{1,0},{2,3},{3,2},{4,5},{5,4},{6,7},{7,6},{8,9},{9,8},{10,11... | collective-permute-start | bytes 3342344 | tf_op jit(solution)/shard_map/ppermute | solution.py:21
  71.1 11.5 %collective-permute-start.8 = (f32[4,128,128]{2,1,0:T(8,128)S(1)}, f32[4,128,128]{2,1,0:T(8,128)S(1)}, u32[]{:S(2)}, u32[]{:S(2)}) collective-permute-start(f32[4,128,128]{2,1,0:T(8,128)S(1)} %bitcast_add_fusion.3), channel_id=1, source_target_pairs={{4,0},{8,4},{12,8},{5,1},{9,5},{13,9},{6,2},{10,6},{14,10},{7,3},{... | collective-permute-start | bytes 786440 | tf_op jit(solution)/shard_map/ppermute | solution.py:62
  73.4 9.2 %collective-permute-start.7 = (f32[16,128]{1,0:T(8,128)S(1)}, f32[16,128]{1,0:T(8,128)S(1)}, u32[]{:S(2)}, u32[]{:S(2)}) collective-permute-start(f32[16,128]{1,0:T(8,128)S(1)} %bitcast.157), channel_id=1, source_target_pairs={{0,4},{4,0},{8,12},{12,8},{1,5},{5,1},{9,13},{13,9},{2,6},{6,2},{1... | collective-permute-start | bytes 24584 | tf_op jit(solution)/shard_map/ppermute | solution.py:117
  83.4 11.3 %collective-permute-start.10 = (f32[4,128,128]{2,1,0:T(8,128)S(1)}, f32[4,128,128]{2,1,0:T(8,128)S(1)}, u32[]{:S(2)}, u32[]{:S(2)}) collective-permute-start(f32[4,128,128]{2,1,0:T(8,128)S(1)} %bitcast_add_fusion.2), channel_id=1, source_target_pairs={{4,0},{8,4},{12,8},{5,1},{9,5},{13,9},{6,2},{10,6},{14,10},{7,3},{... | collective-permute-start | bytes 786440 | tf_op jit(solution)/shard_map/ppermute | solution.py:62
  84.7 9.9 %collective-permute-start.9 = (f32[16,128]{1,0:T(8,128)S(1)}, f32[16,128]{1,0:T(8,128)S(1)}, u32[]{:S(2)}, u32[]{:S(2)}) collective-permute-start(f32[16,128]{1,0:T(8,128)S(1)} %add.145), channel_id=1, source_target_pairs={{0,8},{4,12},{8,0},{12,4},{1,9},{5,13},{9,1},{13,5},{2,10},{6,14},... | collective-permute-start | bytes 24584 | tf_op jit(solution)/shard_map/ppermute | solution.py:117
  95.4 9.4 %collective-permute-start.11 = (f32[4,128,128]{2,1,0:T(8,128)S(1)}, f32[4,128,128]{2,1,0:T(8,128)S(1)}, u32[]{:S(2)}, u32[]{:S(2)}) collective-permute-start(f32[4,128,128]{2,1,0:T(8,128)S(1)} %bitcast_add_fusion.1), channel_id=1, source_target_pairs={{4,0},{8,4},{12,8},{5,1},{9,5},{13,9},{6,2},{10,6},{14,10},{7,3},{... | collective-permute-start | bytes 786440 | tf_op jit(solution)/shard_map/ppermute | solution.py:62
  105.5 8.9 %collective-permute-start.12 = (f32[4,128,128]{2,1,0:T(8,128)S(1)}, f32[4,128,128]{2,1,0:T(8,128)S(1)}, u32[]{:S(2)}, u32[]{:S(2)}) collective-permute-start(f32[4,128,128]{2,1,0:T(8,128)S(1)} %bitcast_add_fusion), channel_id=1, source_target_pairs={{4,0},{8,4},{12,8},{5,1},{9,5},{13,9},{6,2},{10,6},{14,10},{7,3},{... | collective-permute-start | bytes 786440 | tf_op jit(solution)/shard_map/ppermute | solution.py:62
  115.1 2.0 %collective-permute-start.13 = (f32[8,128,128]{2,1,0:T(8,128)S(1)}, f32[8,128,128]{2,1,0:T(8,128)S(1)}, u32[]{:S(2)}, u32[]{:S(2)}) collective-permute-start(f32[8,128,128]{2,1,0:T(8,128)S(1)} %bitcast.134), channel_id=1, source_target_pairs={{0,1},{1,0},{2,3},{3,2},{4,5},{5,4},{6,7},{7,6},{8,9},{9,8},{10,11... | collective-permute-start | bytes 1572872 | tf_op jit(solution)/shard_map/ppermute | solution.py:21
